TPU v7x, 256 devices: a whole 4x4x8 slice. The times are simulated.
256 devices in a mesh: section: 8 (over x, core), blk: 32 (over y, z).
Axes of the slice: x: 4, y: 4, z: 8, core: 2. Of those that a mesh axis runs over, the one named last changes fastest.
Arguments:
- features: bfloat16 [4, 16384, 256], P(None, 'blk'), may hold values from -6 to 6
- tile_values: bfloat16 [4, 2560, 128, 128], P(None, 'blk'), may hold values from -1 to 1
- tile_rows: int32 [4, 2560], P(None, 'blk'), may hold values from 0 to 127, as said below
- tile_cols: int32 [4, 2560], P(None, 'blk'), may hold values from 0 to 127, as said below
- tile_count: int32 [4, 32], P(None, 'blk'), may hold values from 10 to 80, as said below
- degrees: int32 [4, 16384], P(None, 'blk'), may hold values from 16 to 64
- self_weight: bfloat16 [8, 256, 256], P('section'), may hold values from -0.375 to 0.375
- neighbour_weight: bfloat16 [8, 256, 256], P('section'), may hold values from -0.375 to 0.375
Outputs:
- layer_outputs: bfloat16 [8, 4, 16384, 256], P('section', None, 'blk')
Inputs may be any that keep to these rules, and one draw needn't show every extreme that they name: `tile_rows`: slot k names a row block of its own blk index: between 4 * (k div 80) and 4 * (k div 80) + 3. `tile_cols`: slot k names a column block of a blk index at most 2 away from k div 80, counting around the axis; the 80 slots of one blk index name distinct row and column block pairs. `tile_count`: in every batch some blk index has all 80 slots live.
All inputs are finite; a program needn't handle non-finite values.
Results may differ from a plain program's by a relative error of at most 0.017.
Values may be sent and summed in bfloat16 or wider, within the bound.
No kernel may reach another device: no remote copies, remote signals or barrier semaphores. Data moves between devices by JAX's collectives and lax.ppermute only.
A program may use at most 64 MiB of HBM per device.

v0:
```python
import jax
import jax.numpy as jnp
from jax import lax
from jax.sharding import PartitionSpec as P

REACH = 2


def from_behind(x, axis, by):
    peers = lax.axis_size(axis)
    return lax.ppermute(x, axis, [(i, (i + by) % peers) for i in range(peers)])


def shortened(x):

    def short(part):
        return part.astype(jnp.bfloat16) if part.dtype == jnp.float32 else part

    return jax.tree.map(short, x)


def passed_along(x, axis, by):
    peers = lax.axis_size(axis)
    pairs = [(i, i + by) for i in range(peers) if 0 <= i + by < peers]
    return lax.ppermute(x, axis, pairs)


def body(
    features, tile_values, tile_rows, tile_cols, tile_count, degrees, self_weight, neighbour_weight
):
    batch_total = features.shape[0]
    rows_dev = features.shape[1]
    feature_width = features.shape[2]
    block_size = tile_values.shape[2]
    slot_total = tile_values.shape[1]
    blocks_dev = rows_dev // block_size
    window_span = 2 * REACH + 1
    band_width = window_span * blocks_dev
    blk_count = lax.axis_size("blk")
    blk_index = lax.axis_index("blk")
    section_index = lax.axis_index("section")
    section_count = lax.axis_size("section")

    def gather_window(hidden):
        nearby = []
        for offset in (1, -1):
            nearby.append(from_behind(hidden, "blk", offset))
        distant = []
        for position, offset in enumerate((1, -1)):
            distant.append(from_behind(shortened(nearby[position]), "blk", offset))
        return jnp.concatenate([distant[0], nearby[0], hidden, nearby[1], distant[1]], axis=0)

    def aggregate(window, values, rows, cols, count):
        column_dev = cols // blocks_dev
        shifted = jnp.mod(column_dev - blk_index + REACH, blk_count)
        column_local = shifted * blocks_dev + jnp.mod(cols, blocks_dev)
        row_local = rows - blk_index * blocks_dev
        panels = window.reshape(band_width, block_size, feature_width)
        alive = jnp.arange(slot_total, dtype=jnp.int32) < count
        target = row_local * band_width + column_local
        placing = (
            (target[None, :] == jnp.arange(blocks_dev * band_width, dtype=jnp.int32)[:, None])
            & alive[None, :]
        ).astype(jnp.bfloat16)
        slab = jnp.dot(
            placing,
            values.reshape(slot_total, block_size * block_size),
            preferred_element_type=jnp.float32,
        ).astype(jnp.bfloat16)
        slab = slab.reshape(blocks_dev, band_width, block_size, block_size)
        summed = jnp.einsum("rcij,cjf->rif", slab, panels, preferred_element_type=jnp.float32)
        return summed.reshape(rows_dev, feature_width)

    def node_layer(hidden, batch, self_matrix, neighbour_matrix):
        values = lax.dynamic_index_in_dim(tile_values, batch, 0, keepdims=False)
        rows = lax.dynamic_index_in_dim(tile_rows, batch, 0, keepdims=False)
        cols = lax.dynamic_index_in_dim(tile_cols, batch, 0, keepdims=False)
        count = lax.dynamic_index_in_dim(tile_count, batch, 0, keepdims=False)[0]
        degree = lax.dynamic_index_in_dim(degrees, batch, 0, keepdims=False)
        window = gather_window(hidden)
        summed = aggregate(window, values, rows, cols, count)
        neighbour_mean = (summed / degree.astype(jnp.float32)[:, None]).astype(jnp.bfloat16)
        combined = jnp.dot(hidden, self_matrix, preferred_element_type=jnp.float32) + jnp.dot(
            neighbour_mean, neighbour_matrix, preferred_element_type=jnp.float32
        )
        active = jnp.maximum(combined, 0.0)
        scale = lax.rsqrt(jnp.mean(active * active, axis=-1, keepdims=True) + 1e-05)
        return (active * scale).astype(jnp.bfloat16)

    turn_total = batch_total + section_count - 1
    self_matrix = self_weight[0]
    neighbour_matrix = neighbour_weight[0]

    def advance(turn_index, state):
        incoming, stored = state
        batch = turn_index - section_index
        clamped = jnp.clip(batch, 0, batch_total - 1)
        valid = (batch >= 0) & (batch < batch_total)
        first_input = lax.dynamic_index_in_dim(features, clamped, 0, keepdims=False)
        hidden = jnp.where(section_index == 0, first_input, incoming)
        result = node_layer(hidden, clamped, self_matrix, neighbour_matrix)
        previous = lax.dynamic_index_in_dim(stored, clamped, 0, keepdims=False)
        stored = lax.dynamic_update_index_in_dim(
            stored, jnp.where(valid, result, previous), clamped, 0
        )
        incoming = passed_along(result, "section", 1)
        return (incoming, stored)

    incoming = jnp.zeros((rows_dev, feature_width), jnp.bfloat16)
    stored = jnp.zeros((batch_total, rows_dev, feature_width), jnp.bfloat16)
    incoming, stored = lax.fori_loop(0, turn_total, advance, (incoming, stored))
    return stored[None]


def solution(mesh):
    return jax.shard_map(
        body,
        mesh=mesh,
        in_specs=(
            P(None, "blk", None),
            P(None, "blk", None, None),
            P(None, "blk"),
            P(None, "blk"),
            P(None, "blk"),
            P(None, "blk"),
            P("section", None, None),
            P("section", None, None),
        ),
        out_specs=P("section", None, "blk", None),
        check_vma=False,
    )
```

profile of v0, /device:TPU:1, one launch (start us, length us, event | category | flops | bytes accessed | tf_op | source)
XLA Modules:
  0.0 476.5 jit_solution(1530251505906914177)
XLA Ops:
  1.0 474.6 %while.18 = (s32[]{:T(128)}, bf16[512,256]{0,1:T(8,128)(2,1)}, bf16[4,512,256]{2,1,0:T(8,128)(2,1)S(1)}, pred[]{:T(512)}, s32[]{:T(128)}, /*index=5*/bf16[4,512,...) while((s32[]{:T(128)}, bf16[512,256]{0,1:T(8,128)(2,1)}, ...), condition=%wide.region_2.3_spmd, body=%wide.region_0.2_spmd.sunk | while | flops 1017659904 | bytes 48512980 | solution.py:111
  5.7 6.5 %collective-permute-start.2 = (bf16[512,256]{1,0:T(8,128)(2,1)S(1)}, bf16[512,256]{1,0:T(8,128)(2,1)}, u32[]{:S(2)}, u32[]{:S(2)}) collective-permute-start(bf16[512,256]{1,0:T(8,128)(2,1)S(1)} %bitcast_select_fusion.3), channel_id=1, source_target_pairs={{0,31},{1,0},{2,1},{3,2},{4,3},{5,4},{6,5},{7,6},{8,7},{9,8},{10,9... | collective-permute-start | bytes 786440 | tf_op jit(solution)/shard_map/while/body/eval_jaxpr/ppermute | solution.py:11
  21.3 4.8 %collective-permute-start.3 = (bf16[512,256]{1,0:T(8,128)(2,1)}, bf16[512,256]{1,0:T(8,128)(2,1)S(1)}, u32[]{:S(2)}, u32[]{:S(2)}) collective-permute-start(bf16[512,256]{1,0:T(8,128)(2,1)} %collective-permute-done.2), channel_id=1, source_target_pairs={{0,31},{1,0},{2,1},{3,2},{4,3},{5,4},{6,5},{7,6},{8,7},{9,8},{10,9... | collective-permute-start | bytes 786440 | tf_op jit(solution)/shard_map/while/body/eval_jaxpr/ppermute | solution.py:11
  39.9 4.9 %collective-permute-start.4 = (bf16[512,256]{0,1:T(8,128)(2,1)S(1)}, bf16[512,256]{0,1:T(8,128)(2,1)}, u32[]{:S(2)}, u32[]{:S(2)}) collective-permute-start(bf16[512,256]{0,1:T(8,128)(2,1)S(1)} %get-tuple-element.550), channel_id=1, source_target_pairs={{0,32},{32,64},{64,96},{96,128},{128,160},{160,192},{192,224},{1,3... | collective-permute-start | bytes 786440 | tf_op jit(solution)/shard_map/while/body/eval_jaxpr/ppermute | solution.py:25
  50.5 4.8 %collective-permute-start.2 = (bf16[512,256]{1,0:T(8,128)(2,1)S(1)}, bf16[512,256]{1,0:T(8,128)(2,1)}, u32[]{:S(2)}, u32[]{:S(2)}) collective-permute-start(bf16[512,256]{1,0:T(8,128)(2,1)S(1)} %bitcast_select_fusion.3), channel_id=1, source_target_pairs={{0,31},{1,0},{2,1},{3,2},{4,3},{5,4},{6,5},{7,6},{8,7},{9,8},{10,9... | collective-permute-start | bytes 786440 | tf_op jit(solution)/shard_map/while/body/eval_jaxpr/ppermute | solution.py:11
  81.4 6.4 %collective-permute-start.4 = (bf16[512,256]{0,1:T(8,128)(2,1)S(1)}, bf16[512,256]{0,1:T(8,128)(2,1)}, u32[]{:S(2)}, u32[]{:S(2)}) collective-permute-start(bf16[512,256]{0,1:T(8,128)(2,1)S(1)} %get-tuple-element.550), channel_id=1, source_target_pairs={{0,32},{32,64},{64,96},{96,128},{128,160},{160,192},{192,224},{1,3... | collective-permute-start | bytes 786440 | tf_op jit(solution)/shard_map/while/body/eval_jaxpr/ppermute | solution.py:25
  93.5 4.8 %collective-permute-start.2 = (bf16[512,256]{1,0:T(8,128)(2,1)S(1)}, bf16[512,256]{1,0:T(8,128)(2,1)}, u32[]{:S(2)}, u32[]{:S(2)}) collective-permute-start(bf16[512,256]{1,0:T(8,128)(2,1)S(1)} %bitcast_select_fusion.3), channel_id=1, source_target_pairs={{0,31},{1,0},{2,1},{3,2},{4,3},{5,4},{6,5},{7,6},{8,7},{9,8},{10,9... | collective-permute-start | bytes 786440 | tf_op jit(solution)/shard_map/while/body/eval_jaxpr/ppermute | solution.py:11
  124.3 6.2 %collective-permute-start.4 = (bf16[512,256]{0,1:T(8,128)(2,1)S(1)}, bf16[512,256]{0,1:T(8,128)(2,1)}, u32[]{:S(2)}, u32[]{:S(2)}) collective-permute-start(bf16[512,256]{0,1:T(8,128)(2,1)S(1)} %get-tuple-element.550), channel_id=1, source_target_pairs={{0,32},{32,64},{64,96},{96,128},{128,160},{160,192},{192,224},{1,3... | collective-permute-start | bytes 786440 | tf_op jit(solution)/shard_map/while/body/eval_jaxpr/ppermute | solution.py:25
  136.2 4.8 %collective-permute-start.2 = (bf16[512,256]{1,0:T(8,128)(2,1)S(1)}, bf16[512,256]{1,0:T(8,128)(2,1)}, u32[]{:S(2)}, u32[]{:S(2)}) collective-permute-start(bf16[512,256]{1,0:T(8,128)(2,1)S(1)} %bitcast_select_fusion.3), channel_id=1, source_target_pairs={{0,31},{1,0},{2,1},{3,2},{4,3},{5,4},{6,5},{7,6},{8,7},{9,8},{10,9... | collective-permute-start | bytes 786440 | tf_op jit(solution)/shard_map/while/body/eval_jaxpr/ppermute | solution.py:11
  167.0 6.2 %collective-permute-start.4 = (bf16[512,256]{0,1:T(8,128)(2,1)S(1)}, bf16[512,256]{0,1:T(8,128)(2,1)}, u32[]{:S(2)}, u32[]{:S(2)}) collective-permute-start(bf16[512,256]{0,1:T(8,128)(2,1)S(1)} %get-tuple-element.550), channel_id=1, source_target_pairs={{0,32},{32,64},{64,96},{96,128},{128,160},{160,192},{192,224},{1,3... | collective-permute-start | bytes 786440 | tf_op jit(solution)/shard_map/while/body/eval_jaxpr/ppermute | solution.py:25
  178.9 4.8 %collective-permute-start.2 = (bf16[512,256]{1,0:T(8,128)(2,1)S(1)}, bf16[512,256]{1,0:T(8,128)(2,1)}, u32[]{:S(2)}, u32[]{:S(2)}) collective-permute-start(bf16[512,256]{1,0:T(8,128)(2,1)S(1)} %bitcast_select_fusion.3), channel_id=1, source_target_pairs={{0,31},{1,0},{2,1},{3,2},{4,3},{5,4},{6,5},{7,6},{8,7},{9,8},{10,9... | collective-permute-start | bytes 786440 | tf_op jit(solution)/shard_map/while/body/eval_jaxpr/ppermute | solution.py:11
  209.8 6.2 %collective-permute-start.4 = (bf16[512,256]{0,1:T(8,128)(2,1)S(1)}, bf16[512,256]{0,1:T(8,128)(2,1)}, u32[]{:S(2)}, u32[]{:S(2)}) collective-permute-start(bf16[512,256]{0,1:T(8,128)(2,1)S(1)} %get-tuple-element.550), channel_id=1, source_target_pairs={{0,32},{32,64},{64,96},{96,128},{128,160},{160,192},{192,224},{1,3... | collective-permute-start | bytes 786440 | tf_op jit(solution)/shard_map/while/body/eval_jaxpr/ppermute | solution.py:25
  221.6 4.8 %collective-permute-start.2 = (bf16[512,256]{1,0:T(8,128)(2,1)S(1)}, bf16[512,256]{1,0:T(8,128)(2,1)}, u32[]{:S(2)}, u32[]{:S(2)}) collective-permute-start(bf16[512,256]{1,0:T(8,128)(2,1)S(1)} %bitcast_select_fusion.3), channel_id=1, source_target_pairs={{0,31},{1,0},{2,1},{3,2},{4,3},{5,4},{6,5},{7,6},{8,7},{9,8},{10,9... | collective-permute-start | bytes 786440 | tf_op jit(solution)/shard_map/while/body/eval_jaxpr/ppermute | solution.py:11
  252.5 6.2 %collective-permute-start.4 = (bf16[512,256]{0,1:T(8,128)(2,1)S(1)}, bf16[512,256]{0,1:T(8,128)(2,1)}, u32[]{:S(2)}, u32[]{:S(2)}) collective-permute-start(bf16[512,256]{0,1:T(8,128)(2,1)S(1)} %get-tuple-element.550), channel_id=1, source_target_pairs={{0,32},{32,64},{64,96},{96,128},{128,160},{160,192},{192,224},{1,3... | collective-permute-start | bytes 786440 | tf_op jit(solution)/shard_map/while/body/eval_jaxpr/ppermute | solution.py:25
  264.3 4.8 %collective-permute-start.2 = (bf16[512,256]{1,0:T(8,128)(2,1)S(1)}, bf16[512,256]{1,0:T(8,128)(2,1)}, u32[]{:S(2)}, u32[]{:S(2)}) collective-permute-start(bf16[512,256]{1,0:T(8,128)(2,1)S(1)} %bitcast_select_fusion.3), channel_id=1, source_target_pairs={{0,31},{1,0},{2,1},{3,2},{4,3},{5,4},{6,5},{7,6},{8,7},{9,8},{10,9... | collective-permute-start | bytes 786440 | tf_op jit(solution)/shard_map/while/body/eval_jaxpr/ppermute | solution.py:11
  295.2 6.2 %collective-permute-start.4 = (bf16[512,256]{0,1:T(8,128)(2,1)S(1)}, bf16[512,256]{0,1:T(8,128)(2,1)}, u32[]{:S(2)}, u32[]{:S(2)}) collective-permute-start(bf16[512,256]{0,1:T(8,128)(2,1)S(1)} %get-tuple-element.550), channel_id=1, source_target_pairs={{0,32},{32,64},{64,96},{96,128},{128,160},{160,192},{192,224},{1,3... | collective-permute-start | bytes 786440 | tf_op jit(solution)/shard_map/while/body/eval_jaxpr/ppermute | solution.py:25
  307.0 4.8 %collective-permute-start.2 = (bf16[512,256]{1,0:T(8,128)(2,1)S(1)}, bf16[512,256]{1,0:T(8,128)(2,1)}, u32[]{:S(2)}, u32[]{:S(2)}) collective-permute-start(bf16[512,256]{1,0:T(8,128)(2,1)S(1)} %bitcast_select_fusion.3), channel_id=1, source_target_pairs={{0,31},{1,0},{2,1},{3,2},{4,3},{5,4},{6,5},{7,6},{8,7},{9,8},{10,9... | collective-permute-start | bytes 786440 | tf_op jit(solution)/shard_map/while/body/eval_jaxpr/ppermute | solution.py:11
  337.9 6.2 %collective-permute-start.4 = (bf16[512,256]{0,1:T(8,128)(2,1)S(1)}, bf16[512,256]{0,1:T(8,128)(2,1)}, u32[]{:S(2)}, u32[]{:S(2)}) collective-permute-start(bf16[512,256]{0,1:T(8,128)(2,1)S(1)} %get-tuple-element.550), channel_id=1, source_target_pairs={{0,32},{32,64},{64,96},{96,128},{128,160},{160,192},{192,224},{1,3... | collective-permute-start | bytes 786440 | tf_op jit(solution)/shard_map/while/body/eval_jaxpr/ppermute | solution.py:25
  349.7 4.8 %collective-permute-start.2 = (bf16[512,256]{1,0:T(8,128)(2,1)S(1)}, bf16[512,256]{1,0:T(8,128)(2,1)}, u32[]{:S(2)}, u32[]{:S(2)}) collective-permute-start(bf16[512,256]{1,0:T(8,128)(2,1)S(1)} %bitcast_select_fusion.3), channel_id=1, source_target_pairs={{0,31},{1,0},{2,1},{3,2},{4,3},{5,4},{6,5},{7,6},{8,7},{9,8},{10,9... | collective-permute-start | bytes 786440 | tf_op jit(solution)/shard_map/while/body/eval_jaxpr/ppermute | solution.py:11
  380.6 6.2 %collective-permute-start.4 = (bf16[512,256]{0,1:T(8,128)(2,1)S(1)}, bf16[512,256]{0,1:T(8,128)(2,1)}, u32[]{:S(2)}, u32[]{:S(2)}) collective-permute-start(bf16[512,256]{0,1:T(8,128)(2,1)S(1)} %get-tuple-element.550), channel_id=1, source_target_pairs={{0,32},{32,64},{64,96},{96,128},{128,160},{160,192},{192,224},{1,3... | collective-permute-start | bytes 786440 | tf_op jit(solution)/shard_map/while/body/eval_jaxpr/ppermute | solution.py:25
  392.5 4.8 %collective-permute-start.2 = (bf16[512,256]{1,0:T(8,128)(2,1)S(1)}, bf16[512,256]{1,0:T(8,128)(2,1)}, u32[]{:S(2)}, u32[]{:S(2)}) collective-permute-start(bf16[512,256]{1,0:T(8,128)(2,1)S(1)} %bitcast_select_fusion.3), channel_id=1, source_target_pairs={{0,31},{1,0},{2,1},{3,2},{4,3},{5,4},{6,5},{7,6},{8,7},{9,8},{10,9... | collective-permute-start | bytes 786440 | tf_op jit(solution)/shard_map/while/body/eval_jaxpr/ppermute | solution.py:11
  423.3 6.2 %collective-permute-start.4 = (bf16[512,256]{0,1:T(8,128)(2,1)S(1)}, bf16[512,256]{0,1:T(8,128)(2,1)}, u32[]{:S(2)}, u32[]{:S(2)}) collective-permute-start(bf16[512,256]{0,1:T(8,128)(2,1)S(1)} %get-tuple-element.550), channel_id=1, source_target_pairs={{0,32},{32,64},{64,96},{96,128},{128,160},{160,192},{192,224},{1,3... | collective-permute-start | bytes 786440 | tf_op jit(solution)/shard_map/while/body/eval_jaxpr/ppermute | solution.py:25
  435.2 4.8 %collective-permute-start.2 = (bf16[512,256]{1,0:T(8,128)(2,1)S(1)}, bf16[512,256]{1,0:T(8,128)(2,1)}, u32[]{:S(2)}, u32[]{:S(2)}) collective-permute-start(bf16[512,256]{1,0:T(8,128)(2,1)S(1)} %bitcast_select_fusion.3), channel_id=1, source_target_pairs={{0,31},{1,0},{2,1},{3,2},{4,3},{5,4},{6,5},{7,6},{8,7},{9,8},{10,9... | collective-permute-start | bytes 786440 | tf_op jit(solution)/shard_map/while/body/eval_jaxpr/ppermute | solution.py:11
  466.0 6.2 %collective-permute-start.4 = (bf16[512,256]{0,1:T(8,128)(2,1)S(1)}, bf16[512,256]{0,1:T(8,128)(2,1)}, u32[]{:S(2)}, u32[]{:S(2)}) collective-permute-start(bf16[512,256]{0,1:T(8,128)(2,1)S(1)} %get-tuple-element.550), channel_id=1, source_target_pairs={{0,32},{32,64},{64,96},{96,128},{128,160},{160,192},{192,224},{1,3... | collective-permute-start | bytes 786440 | tf_op jit(solution)/shard_map/while/body/eval_jaxpr/ppermute | solution.py:25
  (414 shorter events, 348.7 us)
Async XLA Ops:
  3.2 15.1 %collective-permute-start = (bf16[512,256]{1,0:T(8,128)(2,1)S(1)}, bf16[512,256]{1,0:T(8,128)(2,1)}, u32[]{:S(2)}, u32[]{:S(2)}) collective-permute-start(bf16[512,256]{1,0:T(8,128)(2,1)S(1)} %bitcast_select_fusion.3), channel_id=1, source_target_pairs={{0,1},{1,2},{2,3},{3,4},{4,5},{5,6},{6,7},{7,8},{8,9},{9,10},{10,1... | collective-permute-start | bytes 786440 | tf_op jit(solution)/shard_map/while/body/eval_jaxpr/ppermute | solution.py:11
  5.7 15.6 %collective-permute-start.2 = (bf16[512,256]{1,0:T(8,128)(2,1)S(1)}, bf16[512,256]{1,0:T(8,128)(2,1)}, u32[]{:S(2)}, u32[]{:S(2)}) collective-permute-start(bf16[512,256]{1,0:T(8,128)(2,1)S(1)} %bitcast_select_fusion.3), channel_id=1, source_target_pairs={{0,31},{1,0},{2,1},{3,2},{4,3},{5,4},{6,5},{7,6},{8,7},{9,8},{10,9... | collective-permute-start | bytes 786440 | tf_op jit(solution)/shard_map/while/body/eval_jaxpr/ppermute | solution.py:11
  21.3 13.3 %collective-permute-start.3 = (bf16[512,256]{1,0:T(8,128)(2,1)}, bf16[512,256]{1,0:T(8,128)(2,1)S(1)}, u32[]{:S(2)}, u32[]{:S(2)}) collective-permute-start(bf16[512,256]{1,0:T(8,128)(2,1)} %collective-permute-done.2), channel_id=1, source_target_pairs={{0,31},{1,0},{2,1},{3,2},{4,3},{5,4},{6,5},{7,6},{8,7},{9,8},{10,9... | collective-permute-start | bytes 786440 | tf_op jit(solution)/shard_map/while/body/eval_jaxpr/ppermute | solution.py:11
  50.5 13.8 %collective-permute-start.2 = (bf16[512,256]{1,0:T(8,128)(2,1)S(1)}, bf16[512,256]{1,0:T(8,128)(2,1)}, u32[]{:S(2)}, u32[]{:S(2)}) collective-permute-start(bf16[512,256]{1,0:T(8,128)(2,1)S(1)} %bitcast_select_fusion.3), channel_id=1, source_target_pairs={{0,31},{1,0},{2,1},{3,2},{4,3},{5,4},{6,5},{7,6},{8,7},{9,8},{10,9... | collective-permute-start | bytes 786440 | tf_op jit(solution)/shard_map/while/body/eval_jaxpr/ppermute | solution.py:11
  64.3 11.8 %collective-permute-start.3 = (bf16[512,256]{1,0:T(8,128)(2,1)}, bf16[512,256]{1,0:T(8,128)(2,1)S(1)}, u32[]{:S(2)}, u32[]{:S(2)}) collective-permute-start(bf16[512,256]{1,0:T(8,128)(2,1)} %collective-permute-done.2), channel_id=1, source_target_pairs={{0,31},{1,0},{2,1},{3,2},{4,3},{5,4},{6,5},{7,6},{8,7},{9,8},{10,9... | collective-permute-start | bytes 786440 | tf_op jit(solution)/shard_map/while/body/eval_jaxpr/ppermute | solution.py:11
  93.4 11.0 %collective-permute-start = (bf16[512,256]{1,0:T(8,128)(2,1)S(1)}, bf16[512,256]{1,0:T(8,128)(2,1)}, u32[]{:S(2)}, u32[]{:S(2)}) collective-permute-start(bf16[512,256]{1,0:T(8,128)(2,1)S(1)} %bitcast_select_fusion.3), channel_id=1, source_target_pairs={{0,1},{1,2},{2,3},{3,4},{4,5},{5,6},{6,7},{7,8},{8,9},{9,10},{10,1... | collective-permute-start | bytes 786440 | tf_op jit(solution)/shard_map/while/body/eval_jaxpr/ppermute | solution.py:11
  93.5 13.8 %collective-permute-start.2 = (bf16[512,256]{1,0:T(8,128)(2,1)S(1)}, bf16[512,256]{1,0:T(8,128)(2,1)}, u32[]{:S(2)}, u32[]{:S(2)}) collective-permute-start(bf16[512,256]{1,0:T(8,128)(2,1)S(1)} %bitcast_select_fusion.3), channel_id=1, source_target_pairs={{0,31},{1,0},{2,1},{3,2},{4,3},{5,4},{6,5},{7,6},{8,7},{9,8},{10,9... | collective-permute-start | bytes 786440 | tf_op jit(solution)/shard_map/while/body/eval_jaxpr/ppermute | solution.py:11
  107.3 11.7 %collective-permute-start.3 = (bf16[512,256]{1,0:T(8,128)(2,1)}, bf16[512,256]{1,0:T(8,128)(2,1)S(1)}, u32[]{:S(2)}, u32[]{:S(2)}) collective-permute-start(bf16[512,256]{1,0:T(8,128)(2,1)} %collective-permute-done.2), channel_id=1, source_target_pairs={{0,31},{1,0},{2,1},{3,2},{4,3},{5,4},{6,5},{7,6},{8,7},{9,8},{10,9... | collective-permute-start | bytes 786440 | tf_op jit(solution)/shard_map/while/body/eval_jaxpr/ppermute | solution.py:11
  136.2 13.8 %collective-permute-start.2 = (bf16[512,256]{1,0:T(8,128)(2,1)S(1)}, bf16[512,256]{1,0:T(8,128)(2,1)}, u32[]{:S(2)}, u32[]{:S(2)}) collective-permute-start(bf16[512,256]{1,0:T(8,128)(2,1)S(1)} %bitcast_select_fusion.3), channel_id=1, source_target_pairs={{0,31},{1,0},{2,1},{3,2},{4,3},{5,4},{6,5},{7,6},{8,7},{9,8},{10,9... | collective-permute-start | bytes 786440 | tf_op jit(solution)/shard_map/while/body/eval_jaxpr/ppermute | solution.py:11
  150.0 11.7 %collective-permute-start.3 = (bf16[512,256]{1,0:T(8,128)(2,1)}, bf16[512,256]{1,0:T(8,128)(2,1)S(1)}, u32[]{:S(2)}, u32[]{:S(2)}) collective-permute-start(bf16[512,256]{1,0:T(8,128)(2,1)} %collective-permute-done.2), channel_id=1, source_target_pairs={{0,31},{1,0},{2,1},{3,2},{4,3},{5,4},{6,5},{7,6},{8,7},{9,8},{10,9... | collective-permute-start | bytes 786440 | tf_op jit(solution)/shard_map/while/body/eval_jaxpr/ppermute | solution.py:11
  178.9 13.8 %collective-permute-start.2 = (bf16[512,256]{1,0:T(8,128)(2,1)S(1)}, bf16[512,256]{1,0:T(8,128)(2,1)}, u32[]{:S(2)}, u32[]{:S(2)}) collective-permute-start(bf16[512,256]{1,0:T(8,128)(2,1)S(1)} %bitcast_select_fusion.3), channel_id=1, source_target_pairs={{0,31},{1,0},{2,1},{3,2},{4,3},{5,4},{6,5},{7,6},{8,7},{9,8},{10,9... | collective-permute-start | bytes 786440 | tf_op jit(solution)/shard_map/while/body/eval_jaxpr/ppermute | solution.py:11
  192.7 11.7 %collective-permute-start.3 = (bf16[512,256]{1,0:T(8,128)(2,1)}, bf16[512,256]{1,0:T(8,128)(2,1)S(1)}, u32[]{:S(2)}, u32[]{:S(2)}) collective-permute-start(bf16[512,256]{1,0:T(8,128)(2,1)} %collective-permute-done.2), channel_id=1, source_target_pairs={{0,31},{1,0},{2,1},{3,2},{4,3},{5,4},{6,5},{7,6},{8,7},{9,8},{10,9... | collective-permute-start | bytes 786440 | tf_op jit(solution)/shard_map/while/body/eval_jaxpr/ppermute | solution.py:11
  221.6 13.8 %collective-permute-start.2 = (bf16[512,256]{1,0:T(8,128)(2,1)S(1)}, bf16[512,256]{1,0:T(8,128)(2,1)}, u32[]{:S(2)}, u32[]{:S(2)}) collective-permute-start(bf16[512,256]{1,0:T(8,128)(2,1)S(1)} %bitcast_select_fusion.3), channel_id=1, source_target_pairs={{0,31},{1,0},{2,1},{3,2},{4,3},{5,4},{6,5},{7,6},{8,7},{9,8},{10,9... | collective-permute-start | bytes 786440 | tf_op jit(solution)/shard_map/while/body/eval_jaxpr/ppermute | solution.py:11
  235.5 11.7 %collective-permute-start.3 = (bf16[512,256]{1,0:T(8,128)(2,1)}, bf16[512,256]{1,0:T(8,128)(2,1)S(1)}, u32[]{:S(2)}, u32[]{:S(2)}) collective-permute-start(bf16[512,256]{1,0:T(8,128)(2,1)} %collective-permute-done.2), channel_id=1, source_target_pairs={{0,31},{1,0},{2,1},{3,2},{4,3},{5,4},{6,5},{7,6},{8,7},{9,8},{10,9... | collective-permute-start | bytes 786440 | tf_op jit(solution)/shard_map/while/body/eval_jaxpr/ppermute | solution.py:11
  264.3 13.8 %collective-permute-start.2 = (bf16[512,256]{1,0:T(8,128)(2,1)S(1)}, bf16[512,256]{1,0:T(8,128)(2,1)}, u32[]{:S(2)}, u32[]{:S(2)}) collective-permute-start(bf16[512,256]{1,0:T(8,128)(2,1)S(1)} %bitcast_select_fusion.3), channel_id=1, source_target_pairs={{0,31},{1,0},{2,1},{3,2},{4,3},{5,4},{6,5},{7,6},{8,7},{9,8},{10,9... | collective-permute-start | bytes 786440 | tf_op jit(solution)/shard_map/while/body/eval_jaxpr/ppermute | solution.py:11
  278.2 11.7 %collective-permute-start.3 = (bf16[512,256]{1,0:T(8,128)(2,1)}, bf16[512,256]{1,0:T(8,128)(2,1)S(1)}, u32[]{:S(2)}, u32[]{:S(2)}) collective-permute-start(bf16[512,256]{1,0:T(8,128)(2,1)} %collective-permute-done.2), channel_id=1, source_target_pairs={{0,31},{1,0},{2,1},{3,2},{4,3},{5,4},{6,5},{7,6},{8,7},{9,8},{10,9... | collective-permute-start | bytes 786440 | tf_op jit(solution)/shard_map/while/body/eval_jaxpr/ppermute | solution.py:11
  307.0 13.8 %collective-permute-start.2 = (bf16[512,256]{1,0:T(8,128)(2,1)S(1)}, bf16[512,256]{1,0:T(8,128)(2,1)}, u32[]{:S(2)}, u32[]{:S(2)}) collective-permute-start(bf16[512,256]{1,0:T(8,128)(2,1)S(1)} %bitcast_select_fusion.3), channel_id=1, source_target_pairs={{0,31},{1,0},{2,1},{3,2},{4,3},{5,4},{6,5},{7,6},{8,7},{9,8},{10,9... | collective-permute-start | bytes 786440 | tf_op jit(solution)/shard_map/while/body/eval_jaxpr/ppermute | solution.py:11
  320.9 11.7 %collective-permute-start.3 = (bf16[512,256]{1,0:T(8,128)(2,1)}, bf16[512,256]{1,0:T(8,128)(2,1)S(1)}, u32[]{:S(2)}, u32[]{:S(2)}) collective-permute-start(bf16[512,256]{1,0:T(8,128)(2,1)} %collective-permute-done.2), channel_id=1, source_target_pairs={{0,31},{1,0},{2,1},{3,2},{4,3},{5,4},{6,5},{7,6},{8,7},{9,8},{10,9... | collective-permute-start | bytes 786440 | tf_op jit(solution)/shard_map/while/body/eval_jaxpr/ppermute | solution.py:11
  349.7 13.8 %collective-permute-start.2 = (bf16[512,256]{1,0:T(8,128)(2,1)S(1)}, bf16[512,256]{1,0:T(8,128)(2,1)}, u32[]{:S(2)}, u32[]{:S(2)}) collective-permute-start(bf16[512,256]{1,0:T(8,128)(2,1)S(1)} %bitcast_select_fusion.3), channel_id=1, source_target_pairs={{0,31},{1,0},{2,1},{3,2},{4,3},{5,4},{6,5},{7,6},{8,7},{9,8},{10,9... | collective-permute-start | bytes 786440 | tf_op jit(solution)/shard_map/while/body/eval_jaxpr/ppermute | solution.py:11
  363.6 11.7 %collective-permute-start.3 = (bf16[512,256]{1,0:T(8,128)(2,1)}, bf16[512,256]{1,0:T(8,128)(2,1)S(1)}, u32[]{:S(2)}, u32[]{:S(2)}) collective-permute-start(bf16[512,256]{1,0:T(8,128)(2,1)} %collective-permute-done.2), channel_id=1, source_target_pairs={{0,31},{1,0},{2,1},{3,2},{4,3},{5,4},{6,5},{7,6},{8,7},{9,8},{10,9... | collective-permute-start | bytes 786440 | tf_op jit(solution)/shard_map/while/body/eval_jaxpr/ppermute | solution.py:11
  392.5 13.8 %collective-permute-start.2 = (bf16[512,256]{1,0:T(8,128)(2,1)S(1)}, bf16[512,256]{1,0:T(8,128)(2,1)}, u32[]{:S(2)}, u32[]{:S(2)}) collective-permute-start(bf16[512,256]{1,0:T(8,128)(2,1)S(1)} %bitcast_select_fusion.3), channel_id=1, source_target_pairs={{0,31},{1,0},{2,1},{3,2},{4,3},{5,4},{6,5},{7,6},{8,7},{9,8},{10,9... | collective-permute-start | bytes 786440 | tf_op jit(solution)/shard_map/while/body/eval_jaxpr/ppermute | solution.py:11
  406.3 11.7 %collective-permute-start.3 = (bf16[512,256]{1,0:T(8,128)(2,1)}, bf16[512,256]{1,0:T(8,128)(2,1)S(1)}, u32[]{:S(2)}, u32[]{:S(2)}) collective-permute-start(bf16[512,256]{1,0:T(8,128)(2,1)} %collective-permute-done.2), channel_id=1, source_target_pairs={{0,31},{1,0},{2,1},{3,2},{4,3},{5,4},{6,5},{7,6},{8,7},{9,8},{10,9... | collective-permute-start | bytes 786440 | tf_op jit(solution)/shard_map/while/body/eval_jaxpr/ppermute | solution.py:11
  435.2 13.8 %collective-permute-start.2 = (bf16[512,256]{1,0:T(8,128)(2,1)S(1)}, bf16[512,256]{1,0:T(8,128)(2,1)}, u32[]{:S(2)}, u32[]{:S(2)}) collective-permute-start(bf16[512,256]{1,0:T(8,128)(2,1)S(1)} %bitcast_select_fusion.3), channel_id=1, source_target_pairs={{0,31},{1,0},{2,1},{3,2},{4,3},{5,4},{6,5},{7,6},{8,7},{9,8},{10,9... | collective-permute-start | bytes 786440 | tf_op jit(solution)/shard_map/while/body/eval_jaxpr/ppermute | solution.py:11
  449.0 11.7 %collective-permute-start.3 = (bf16[512,256]{1,0:T(8,128)(2,1)}, bf16[512,256]{1,0:T(8,128)(2,1)S(1)}, u32[]{:S(2)}, u32[]{:S(2)}) collective-permute-start(bf16[512,256]{1,0:T(8,128)(2,1)} %collective-permute-done.2), channel_id=1, source_target_pairs={{0,31},{1,0},{2,1},{3,2},{4,3},{5,4},{6,5},{7,6},{8,7},{9,8},{10,9... | collective-permute-start | bytes 786440 | tf_op jit(solution)/shard_map/while/body/eval_jaxpr/ppermute | solution.py:11
  (67 other events, 653.2 us)
where the time goes:
time: 480 us; the launch traced here: 477 us
  starting transfers between devices  178 us (37%)
  local copies, waits for them, and re-layouts  129 us (27%)
  matrix products  71 us (15%)
  waiting for transfers between devices  49.4 us (10%)
  other arithmetic  47 us (10%)
    ppermute x44, starting transfers between devices, from_behind(): return lax.ppermute(x, axis, [(i, (i + by) % peers) for i in range(peers)])  111 us
    while x121, local copies, waits for them, and re-layouts  70.9 us
    ppermute x11, starting transfers between devices, passed_along(): return lax.ppermute(x, axis, pairs)  67.2 us
    dot_general x11, matrix products, node_layer(): jnp.dot(neighbour_mean, neighbour_matrix, preferred_element_type=jnp.floa...  36.7 us
    ppermute x11, waiting for transfers between devices, passed_along(): return lax.ppermute(x, axis, pairs)  34.2 us
    dynamic_slice x11, local copies, waits for them, and re-layouts, node_layer(): values = lax.dynamic_index_in_dim(tile_values, batch, 0, keepdims=False)  22.6 us
    dot_general x11, matrix products, aggregate(): jnp.dot(placing, values.reshape(slot_total, block_size * block_size), pre...  22.5 us
    ppermute x44, waiting for transfers between devices, from_behind(): return lax.ppermute(x, axis, [(i, (i + by) % peers) for i in range(peers)])  15.1 us
  transfers between devices with their start and end apart: 55, of which 22 were waited for; matrix products, arithmetic and copies ran while one was open for 34% of the time, Pallas kernels for 0%

commit v1 on v0

v1 whole, which is shorter than its diff:
```python
import jax
import jax.numpy as jnp
from jax import lax
from jax.sharding import PartitionSpec as P

REACH = 2


def body(
    features, tile_values, tile_rows, tile_cols, tile_count, degrees, self_weight, neighbour_weight
):
    batch_total, rows_dev, feature_width = features.shape
    slot_total, block_size = tile_values.shape[1], tile_values.shape[2]
    blocks_dev = rows_dev // block_size
    window_span = 2 * REACH + 1
    band_width = window_span * blocks_dev
    blk_count = lax.axis_size("blk")
    section_count = lax.axis_size("section")
    layer_total = section_count
    blk_index = lax.axis_index("blk")
    section_index = lax.axis_index("section")

    self_all = lax.all_gather(self_weight[0], "section")
    neighbour_all = lax.all_gather(neighbour_weight[0], "section")

    group = section_count // batch_total
    workers = [group * m + group - 1 for m in range(batch_total)]
    batch = section_index // group

    def halo(x, by):
        pairs = []
        for s in workers:
            for b in range(blk_count):
                pairs.append((s * blk_count + b, s * blk_count + (b + by) % blk_count))
        return lax.ppermute(x, ("section", "blk"), pairs)

    values = lax.dynamic_index_in_dim(tile_values, batch, 0, keepdims=False)
    rows = lax.dynamic_index_in_dim(tile_rows, batch, 0, keepdims=False)
    cols = lax.dynamic_index_in_dim(tile_cols, batch, 0, keepdims=False)
    count = lax.dynamic_index_in_dim(tile_count, batch, 0, keepdims=False)[0]
    degree = lax.dynamic_index_in_dim(degrees, batch, 0, keepdims=False)
    hidden = lax.dynamic_index_in_dim(features, batch, 0, keepdims=False)

    column_dev = cols // blocks_dev
    shifted = jnp.mod(column_dev - blk_index + REACH, blk_count)
    column_local = shifted * blocks_dev + jnp.mod(cols, blocks_dev)
    row_local = rows - blk_index * blocks_dev
    alive = jnp.arange(slot_total, dtype=jnp.int32) < count
    target = row_local * band_width + column_local
    placing = (
        (target[None, :] == jnp.arange(blocks_dev * band_width, dtype=jnp.int32)[:, None])
        & alive[None, :]
    ).astype(jnp.bfloat16)
    slab = jnp.dot(
        placing,
        values.reshape(slot_total, block_size * block_size),
        preferred_element_type=jnp.float32,
    ).astype(jnp.bfloat16)
    band = (
        slab.reshape(blocks_dev, band_width, block_size, block_size)
        .transpose(0, 2, 1, 3)
        .reshape(rows_dev, window_span, rows_dev)
    )
    degree_f = degree.astype(jnp.float32)[:, None]

    outputs = []
    for level in range(layer_total):
        up1 = halo(hidden, 1)
        down1 = halo(hidden, -1)
        up2 = halo(up1, 1)
        down2 = halo(down1, -1)
        parts = [up2, up1, hidden, down1, down2]
        summed = jnp.dot(band[:, REACH, :], hidden, preferred_element_type=jnp.float32)
        for position in (REACH - 1, REACH + 1, REACH - 2, REACH + 2):
            summed = summed + jnp.dot(
                band[:, position, :], parts[position], preferred_element_type=jnp.float32
            )
        neighbour_mean = (summed / degree_f).astype(jnp.bfloat16)
        combined = jnp.dot(hidden, self_all[level], preferred_element_type=jnp.float32) + jnp.dot(
            neighbour_mean, neighbour_all[level], preferred_element_type=jnp.float32
        )
        active = jnp.maximum(combined, 0.0)
        scale = lax.rsqrt(jnp.mean(active * active, axis=-1, keepdims=True) + 1e-05)
        hidden = (active * scale).astype(jnp.bfloat16)
        outputs.append(hidden)

    gathered = []
    for m in range(batch_total):
        slot = jnp.zeros((rows_dev, feature_width), jnp.bfloat16)
        for level in range(layer_total):
            source = workers[m]
            if source == level:
                arrived = outputs[level]
            else:
                arrived = lax.ppermute(outputs[level], "section", [(source, level)])
            slot = jnp.where(section_index == level, arrived, slot)
        gathered.append(slot)
    return jnp.stack(gathered)[None]


def solution(mesh):
    return jax.shard_map(
        body,
        mesh=mesh,
        in_specs=(
            P(None, "blk", None),
            P(None, "blk", None, None),
            P(None, "blk"),
            P(None, "blk"),
            P(None, "blk"),
            P(None, "blk"),
            P("section", None, None),
            P("section", None, None),
        ),
        out_specs=P("section", None, "blk", None),
        check_vma=False,
    )
```

time: 480 us -> 337 us (0.70)
  the two profiles are of different devices: /device:TPU:1 before, /device:TPU:7 now
where the time goes in v1:
time: 337 us; the launch traced here: 335 us
  starting transfers between devices  174 us (52%)
  matrix products  68 us (20%)
  waiting for transfers between devices  47.5 us (14%)
  local copies, waits for them, and re-layouts  17.1 us (5%)
  between operations  14.5 us (4%)
  other arithmetic  13.4 us (4%)
    ppermute x32, starting transfers between devices, halo(): return lax.ppermute(x, ('section', 'blk'), pairs)  141 us
    ppermute x28, starting transfers between devices, body(): arrived = lax.ppermute(outputs[level], 'section', [(source, level)])  33.5 us
    dot_general x24, matrix products, body(): jnp.dot(band[:, position, :], parts[position], preferred_element_type=jnp...  21.7 us
    dot_general x8, matrix products, body(): jnp.dot(neighbour_mean, neighbour_all[level], preferred_element_type=jnp....  21.6 us
    ppermute x32, waiting for transfers between devices, halo(): return lax.ppermute(x, ('section', 'blk'), pairs)  17.9 us
    ppermute x28, waiting for transfers between devices, body(): arrived = lax.ppermute(outputs[level], 'section', [(source, level)])  17.5 us
    dot_general x8, matrix products, body(): jnp.dot(hidden, self_all[level], preferred_element_type=jnp.float32)  16.1 us
    all_gather x1, waiting for transfers between devices, body(): neighbour_all = lax.all_gather(neighbour_weight[0], 'section')  11.3 us
  transfers between devices with their start and end apart: 62, of which 12 were waited for; matrix products, arithmetic and copies ran while one was open for 27% of the time, Pallas kernels for 0%

profile of v1, /device:TPU:7, one launch (start us, length us, event | category | flops | bytes accessed | tf_op | source)
XLA Modules:
  0.0 334.8 jit_solution(220431325574392672)
XLA Ops:
  7.8 3.5 %collective-permute-start = (bf16[512,256]{1,0:T(8,128)(2,1)S(1)}, bf16[512,256]{1,0:T(8,128)(2,1)}, u32[]{:S(2)}, u32[]{:S(2)}) collective-permute-start(bf16[512,256]{1,0:T(8,128)(2,1)S(1)} %dynamic-slice_bitcast_fusion), channel_id=1, source_target_pairs={{32,33},{33,34},{34,35},{35,36},{36,37},{37,38},{38,39},{39,40},{4... | collective-permute-start | bytes 786440 | tf_op jit(solution)/shard_map/ppermute | solution.py:35
  11.3 8.3 %collective-permute-start.1 = (bf16[512,256]{1,0:T(8,128)(2,1)S(1)}, bf16[512,256]{1,0:T(8,128)(2,1)}, u32[]{:S(2)}, u32[]{:S(2)}) collective-permute-start(bf16[512,256]{1,0:T(8,128)(2,1)S(1)} %dynamic-slice_bitcast_fusion), channel_id=1, source_target_pairs={{32,63},{33,32},{34,33},{35,34},{36,35},{37,36},{38,37},{39,38},{4... | collective-permute-start | bytes 786440 | tf_op jit(solution)/shard_map/ppermute | solution.py:35
  29.4 5.3 %copy.17 = bf16[4,20,128,128]{2,0,3,1:T(4,128)(2,1)} copy(bf16[4,20,128,128]{3,2,1,0:T(8,128)(2,1)} %bitcast.256) | data formatting | bytes 5242880 | tf_op jit(solution)/shard_map/reshape | solution.py:60
  34.7 3.7 %reshape.87 = bf16[512,5,512]{0,2,1:T(8,128)(2,1)S(1)} reshape(bf16[4,128,20,128]{1,0,3,2:T(4,128)(2,1)} %bitcast.257) | data formatting | bytes 5242880 | tf_op jit(solution)/shard_map/reshape | solution.py:62
  38.8 3.3 collective-permute-start.3
  52.9 11.3 %all-gather.5.cloned.1.call-done = bf16[8,256,256]{2,1,0:T(8,128)(2,1)} async-done(((bf16[1,256,256]{2,1,0:T(8,128)(2,1)}), bf16[8,256,256]{2,1,0:T(8,128)(2,1)}) %all-gather.5.cloned.1.call-update) | async-done | bytes 1048592 | tf_op jit(solution)/shard_map/all_gather | solution.py:24
  71.2 5.9 %collective-permute-start.5 = (bf16[512,256]{0,1:T(8,128)(2,1)S(1)}, bf16[512,256]{0,1:T(8,128)(2,1)S(1)}, u32[]{:S(2)}, u32[]{:S(2)}) collective-permute-start(bf16[512,256]{0,1:T(8,128)(2,1)S(1)} %multiply_convert_fusion.7), channel_id=1, source_target_pairs={{32,63},{33,32},{34,33},{35,34},{36,35},{37,36},{38,37},{39,38},{4... | collective-permute-start | bytes 786440 | tf_op jit(solution)/shard_map/ppermute | solution.py:35
  85.1 6.7 %collective-permute-start.7 = (bf16[512,256]{0,1:T(8,128)(2,1)S(1)}, bf16[512,256]{0,1:T(8,128)(2,1)S(1)}, u32[]{:S(2)}, u32[]{:S(2)}) collective-permute-start(bf16[512,256]{0,1:T(8,128)(2,1)S(1)} %collective-permute-done.5), channel_id=1, source_target_pairs={{32,63},{33,32},{34,33},{35,34},{36,35},{37,36},{38,37},{39,38},{4... | collective-permute-start | bytes 786440 | tf_op jit(solution)/shard_map/ppermute | solution.py:35
  101.1 7.1 %collective-permute-start.9 = (bf16[512,256]{0,1:T(8,128)(2,1)}, bf16[512,256]{0,1:T(8,128)(2,1)S(1)}, u32[]{:S(2)}, u32[]{:S(2)}) collective-permute-start(bf16[512,256]{0,1:T(8,128)(2,1)} %multiply_convert_fusion.6), channel_id=1, source_target_pairs={{32,63},{33,32},{34,33},{35,34},{36,35},{37,36},{38,37},{39,38},{4... | collective-permute-start | bytes 786440 | tf_op jit(solution)/shard_map/ppermute | solution.py:35
  108.2 4.5 %collective-permute-start.58 = (bf16[512,256]{0,1:T(8,128)(2,1)}, bf16[512,256]{0,1:T(8,128)(2,1)}, u32[]{:S(2)}, u32[]{:S(2)}) collective-permute-start(bf16[512,256]{0,1:T(8,128)(2,1)} %multiply_convert_fusion.6), channel_id=1, source_target_pairs={{224,32},{225,33},{226,34},{227,35},{228,36},{229,37},{230,38},{23... | collective-permute-start | bytes 786440 | tf_op jit(solution)/shard_map/ppermute | solution.py:95
  118.4 6.7 %collective-permute-start.11 = (bf16[512,256]{0,1:T(8,128)(2,1)S(1)}, bf16[512,256]{0,1:T(8,128)(2,1)S(1)}, u32[]{:S(2)}, u32[]{:S(2)}) collective-permute-start(bf16[512,256]{0,1:T(8,128)(2,1)S(1)} %collective-permute-done.9), channel_id=1, source_target_pairs={{32,63},{33,32},{34,33},{35,34},{36,35},{37,36},{38,37},{39,38},{4... | collective-permute-start | bytes 786440 | tf_op jit(solution)/shard_map/ppermute | solution.py:35
  134.4 7.1 %collective-permute-start.13 = (bf16[512,256]{0,1:T(8,128)(2,1)S(1)}, bf16[512,256]{0,1:T(8,128)(2,1)S(1)}, u32[]{:S(2)}, u32[]{:S(2)}) collective-permute-start(bf16[512,256]{0,1:T(8,128)(2,1)S(1)} %multiply_convert_fusion.5), channel_id=1, source_target_pairs={{32,63},{33,32},{34,33},{35,34},{36,35},{37,36},{38,37},{39,38},{4... | collective-permute-start | bytes 786440 | tf_op jit(solution)/shard_map/ppermute | solution.py:35
  146.2 6.9 %collective-permute-start.15 = (bf16[512,256]{0,1:T(8,128)(2,1)S(1)}, bf16[512,256]{0,1:T(8,128)(2,1)S(1)}, u32[]{:S(2)}, u32[]{:S(2)}) collective-permute-start(bf16[512,256]{0,1:T(8,128)(2,1)S(1)} %collective-permute-done.13), channel_id=1, source_target_pairs={{32,63},{33,32},{34,33},{35,34},{36,35},{37,36},{38,37},{39,38},{4... | collective-permute-start | bytes 786440 | tf_op jit(solution)/shard_map/ppermute | solution.py:35
  163.2 7.1 %collective-permute-start.17 = (bf16[512,256]{0,1:T(8,128)(2,1)S(1)}, bf16[512,256]{0,1:T(8,128)(2,1)S(1)}, u32[]{:S(2)}, u32[]{:S(2)}) collective-permute-start(bf16[512,256]{0,1:T(8,128)(2,1)S(1)} %multiply_convert_fusion.4), channel_id=1, source_target_pairs={{32,63},{33,32},{34,33},{35,34},{36,35},{37,36},{38,37},{39,38},{4... | collective-permute-start | bytes 786440 | tf_op jit(solution)/shard_map/ppermute | solution.py:35
  175.0 6.7 %collective-permute-start.19 = (bf16[512,256]{0,1:T(8,128)(2,1)S(1)}, bf16[512,256]{0,1:T(8,128)(2,1)S(1)}, u32[]{:S(2)}, u32[]{:S(2)}) collective-permute-start(bf16[512,256]{0,1:T(8,128)(2,1)S(1)} %collective-permute-done.17), channel_id=1, source_target_pairs={{32,63},{33,32},{34,33},{35,34},{36,35},{37,36},{38,37},{39,38},{4... | collective-permute-start | bytes 786440 | tf_op jit(solution)/shard_map/ppermute | solution.py:35
  192.7 7.1 %collective-permute-start.21 = (bf16[512,256]{0,1:T(8,128)(2,1)}, bf16[512,256]{0,1:T(8,128)(2,1)S(1)}, u32[]{:S(2)}, u32[]{:S(2)}) collective-permute-start(bf16[512,256]{0,1:T(8,128)(2,1)} %multiply_convert_fusion.3), channel_id=1, source_target_pairs={{32,63},{33,32},{34,33},{35,34},{36,35},{37,36},{38,37},{39,38},{4... | collective-permute-start | bytes 786440 | tf_op jit(solution)/shard_map/ppermute | solution.py:35
  205.5 6.7 %collective-permute-start.23 = (bf16[512,256]{0,1:T(8,128)(2,1)S(1)}, bf16[512,256]{0,1:T(8,128)(2,1)S(1)}, u32[]{:S(2)}, u32[]{:S(2)}) collective-permute-start(bf16[512,256]{0,1:T(8,128)(2,1)S(1)} %collective-permute-done.21), channel_id=1, source_target_pairs={{32,63},{33,32},{34,33},{35,34},{36,35},{37,36},{38,37},{39,38},{4... | collective-permute-start | bytes 786440 | tf_op jit(solution)/shard_map/ppermute | solution.py:35
  223.2 7.1 %collective-permute-start.25 = (bf16[512,256]{0,1:T(8,128)(2,1)}, bf16[512,256]{0,1:T(8,128)(2,1)S(1)}, u32[]{:S(2)}, u32[]{:S(2)}) collective-permute-start(bf16[512,256]{0,1:T(8,128)(2,1)} %multiply_convert_fusion.2), channel_id=1, source_target_pairs={{32,63},{33,32},{34,33},{35,34},{36,35},{37,36},{38,37},{39,38},{4... | collective-permute-start | bytes 786440 | tf_op jit(solution)/shard_map/ppermute | solution.py:35
  236.1 6.7 %collective-permute-start.27 = (bf16[512,256]{0,1:T(8,128)(2,1)S(1)}, bf16[512,256]{0,1:T(8,128)(2,1)S(1)}, u32[]{:S(2)}, u32[]{:S(2)}) collective-permute-start(bf16[512,256]{0,1:T(8,128)(2,1)S(1)} %collective-permute-done.25), channel_id=1, source_target_pairs={{32,63},{33,32},{34,33},{35,34},{36,35},{37,36},{38,37},{39,38},{4... | collective-permute-start | bytes 786440 | tf_op jit(solution)/shard_map/ppermute | solution.py:35
  253.8 7.1 %collective-permute-start.29 = (bf16[512,256]{0,1:T(8,128)(2,1)}, bf16[512,256]{0,1:T(8,128)(2,1)S(1)}, u32[]{:S(2)}, u32[]{:S(2)}) collective-permute-start(bf16[512,256]{0,1:T(8,128)(2,1)} %multiply_convert_fusion.1), channel_id=1, source_target_pairs={{32,63},{33,32},{34,33},{35,34},{36,35},{37,36},{38,37},{39,38},{4... | collective-permute-start | bytes 786440 | tf_op jit(solution)/shard_map/ppermute | solution.py:35
  266.6 6.7 %collective-permute-start.31 = (bf16[512,256]{0,1:T(8,128)(2,1)S(1)}, bf16[512,256]{0,1:T(8,128)(2,1)S(1)}, u32[]{:S(2)}, u32[]{:S(2)}) collective-permute-start(bf16[512,256]{0,1:T(8,128)(2,1)S(1)} %collective-permute-done.29), channel_id=1, source_target_pairs={{32,63},{33,32},{34,33},{35,34},{36,35},{37,36},{38,37},{39,38},{4... | collective-permute-start | bytes 786440 | tf_op jit(solution)/shard_map/ppermute | solution.py:35
  303.2 5.9 %collective-permute-done.32 = bf16[512,256]{0,1:T(8,128)(2,1)S(1)} collective-permute-done((bf16[512,256]{0,1:T(8,128)(2,1)S(1)}, bf16[512,256]{0,1:T(8,128)(2,1)S(1)}, u32[]{:S(2)}, u32[]{:S(2)}) %collective-permute-start.32) | collective-permute-done | bytes 262176 | tf_op jit(solution)/shard_map/ppermute | solution.py:95
  313.3 5.2 %collective-permute-done.39 = bf16[512,256]{0,1:T(8,128)(2,1)S(1)} collective-permute-done((bf16[512,256]{0,1:T(8,128)(2,1)S(1)}, bf16[512,256]{0,1:T(8,128)(2,1)S(1)}, u32[]{:S(2)}, u32[]{:S(2)}) %collective-permute-start.39) | collective-permute-done | bytes 262176 | tf_op jit(solution)/shard_map/ppermute | solution.py:95
  319.9 6.4 %collective-permute-done.46 = bf16[512,256]{0,1:T(8,128)(2,1)S(1)} collective-permute-done((bf16[512,256]{0,1:T(8,128)(2,1)S(1)}, bf16[512,256]{0,1:T(8,128)(2,1)S(1)}, u32[]{:S(2)}, u32[]{:S(2)}) %collective-permute-start.46) | collective-permute-done | bytes 262176 | tf_op jit(solution)/shard_map/ppermute | solution.py:95
  (195 shorter events, 167.1 us)
Async XLA Ops:
  6.5 41.4 %all-gather.3.cloned.1.call-start = ((), (), s32[]{:S(2)}) async-start(), calls=%async_computation | async-start | bytes 1179648 | tf_op jit(solution)/shard_map/all_gather | solution.py:23
  7.3 57.0 %all-gather.5.cloned.1.call-start = ((), (), s32[]{:S(2)}) async-start(), calls=%async_computation.1 | async-start | bytes 1179648 | tf_op jit(solution)/shard_map/all_gather | solution.py:24
  7.8 34.4 %collective-permute-start = (bf16[512,256]{1,0:T(8,128)(2,1)S(1)}, bf16[512,256]{1,0:T(8,128)(2,1)}, u32[]{:S(2)}, u32[]{:S(2)}) collective-permute-start(bf16[512,256]{1,0:T(8,128)(2,1)S(1)} %dynamic-slice_bitcast_fusion), channel_id=1, source_target_pairs={{32,33},{33,34},{34,35},{35,36},{36,37},{37,38},{38,39},{39,40},{4... | collective-permute-start | bytes 786440 | tf_op jit(solution)/shard_map/ppermute | solution.py:35
  11.3 27.5 %collective-permute-start.1 = (bf16[512,256]{1,0:T(8,128)(2,1)S(1)}, bf16[512,256]{1,0:T(8,128)(2,1)}, u32[]{:S(2)}, u32[]{:S(2)}) collective-permute-start(bf16[512,256]{1,0:T(8,128)(2,1)S(1)} %dynamic-slice_bitcast_fusion), channel_id=1, source_target_pairs={{32,63},{33,32},{34,33},{35,34},{36,35},{37,36},{38,37},{39,38},{4... | collective-permute-start | bytes 786440 | tf_op jit(solution)/shard_map/ppermute | solution.py:35
  68.0 14.8 %collective-permute-start.4 = (bf16[512,256]{0,1:T(8,128)(2,1)S(1)}, bf16[512,256]{0,1:T(8,128)(2,1)S(1)}, u32[]{:S(2)}, u32[]{:S(2)}) collective-permute-start(bf16[512,256]{0,1:T(8,128)(2,1)S(1)} %multiply_convert_fusion.7), channel_id=1, source_target_pairs={{32,33},{33,34},{34,35},{35,36},{36,37},{37,38},{38,39},{39,40},{4... | collective-permute-start | bytes 786440 | tf_op jit(solution)/shard_map/ppermute | solution.py:35
  71.2 13.9 %collective-permute-start.5 = (bf16[512,256]{0,1:T(8,128)(2,1)S(1)}, bf16[512,256]{0,1:T(8,128)(2,1)S(1)}, u32[]{:S(2)}, u32[]{:S(2)}) collective-permute-start(bf16[512,256]{0,1:T(8,128)(2,1)S(1)} %multiply_convert_fusion.7), channel_id=1, source_target_pairs={{32,63},{33,32},{34,33},{35,34},{36,35},{37,36},{38,37},{39,38},{4... | collective-permute-start | bytes 786440 | tf_op jit(solution)/shard_map/ppermute | solution.py:35
  77.1 202.6 %collective-permute-start.59 = (bf16[512,256]{0,1:T(8,128)(2,1)S(1)}, bf16[512,256]{0,1:T(8,128)(2,1)}, u32[]{:S(2)}, u32[]{:S(2)}) collective-permute-start(bf16[512,256]{0,1:T(8,128)(2,1)S(1)} %multiply_convert_fusion.7), channel_id=1, source_target_pairs={{224,0},{225,1},{226,2},{227,3},{228,4},{229,5},{230,6},{231,7},{2... | collective-permute-start | bytes 786440 | tf_op jit(solution)/shard_map/ppermute | solution.py:95
  79.1 202.6 %collective-permute-start.38 = (bf16[512,256]{0,1:T(8,128)(2,1)S(1)}, bf16[512,256]{0,1:T(8,128)(2,1)}, u32[]{:S(2)}, u32[]{:S(2)}) collective-permute-start(bf16[512,256]{0,1:T(8,128)(2,1)S(1)} %multiply_convert_fusion.7), channel_id=1, source_target_pairs={{32,0},{33,1},{34,2},{35,3},{36,4},{37,5},{38,6},{39,7},{40,8},{41... | collective-permute-start | bytes 786440 | tf_op jit(solution)/shard_map/ppermute | solution.py:95
  82.8 13.4 %collective-permute-start.6 = (bf16[512,256]{0,1:T(8,128)(2,1)S(1)}, bf16[512,256]{0,1:T(8,128)(2,1)}, u32[]{:S(2)}, u32[]{:S(2)}) collective-permute-start(bf16[512,256]{0,1:T(8,128)(2,1)S(1)} %collective-permute-done.4), channel_id=1, source_target_pairs={{32,33},{33,34},{34,35},{35,36},{36,37},{37,38},{38,39},{39,40},{4... | collective-permute-start | bytes 786440 | tf_op jit(solution)/shard_map/ppermute | solution.py:35
  99.2 16.9 %collective-permute-start.8 = (bf16[512,256]{0,1:T(8,128)(2,1)}, bf16[512,256]{0,1:T(8,128)(2,1)S(1)}, u32[]{:S(2)}, u32[]{:S(2)}) collective-permute-start(bf16[512,256]{0,1:T(8,128)(2,1)} %multiply_convert_fusion.6), channel_id=1, source_target_pairs={{32,33},{33,34},{34,35},{35,36},{36,37},{37,38},{38,39},{39,40},{4... | collective-permute-start | bytes 786440 | tf_op jit(solution)/shard_map/ppermute | solution.py:35
  101.1 17.3 %collective-permute-start.9 = (bf16[512,256]{0,1:T(8,128)(2,1)}, bf16[512,256]{0,1:T(8,128)(2,1)S(1)}, u32[]{:S(2)}, u32[]{:S(2)}) collective-permute-start(bf16[512,256]{0,1:T(8,128)(2,1)} %multiply_convert_fusion.6), channel_id=1, source_target_pairs={{32,63},{33,32},{34,33},{35,34},{36,35},{37,36},{38,37},{39,38},{4... | collective-permute-start | bytes 786440 | tf_op jit(solution)/shard_map/ppermute | solution.py:35
  108.2 175.5 %collective-permute-start.58 = (bf16[512,256]{0,1:T(8,128)(2,1)}, bf16[512,256]{0,1:T(8,128)(2,1)}, u32[]{:S(2)}, u32[]{:S(2)}) collective-permute-start(bf16[512,256]{0,1:T(8,128)(2,1)} %multiply_convert_fusion.6), channel_id=1, source_target_pairs={{224,32},{225,33},{226,34},{227,35},{228,36},{229,37},{230,38},{23... | collective-permute-start | bytes 786440 | tf_op jit(solution)/shard_map/ppermute | solution.py:95
  116.1 12.6 %collective-permute-start.10 = (bf16[512,256]{0,1:T(8,128)(2,1)S(1)}, bf16[512,256]{0,1:T(8,128)(2,1)}, u32[]{:S(2)}, u32[]{:S(2)}) collective-permute-start(bf16[512,256]{0,1:T(8,128)(2,1)S(1)} %collective-permute-done.8), channel_id=1, source_target_pairs={{32,33},{33,34},{34,35},{35,36},{36,37},{37,38},{38,39},{39,40},{4... | collective-permute-start | bytes 786440 | tf_op jit(solution)/shard_map/ppermute | solution.py:35
  143.9 13.5 %collective-permute-start.14 = (bf16[512,256]{0,1:T(8,128)(2,1)S(1)}, bf16[512,256]{0,1:T(8,128)(2,1)S(1)}, u32[]{:S(2)}, u32[]{:S(2)}) collective-permute-start(bf16[512,256]{0,1:T(8,128)(2,1)S(1)} %collective-permute-done.12), channel_id=1, source_target_pairs={{32,33},{33,34},{34,35},{35,36},{36,37},{37,38},{38,39},{39,40},{4... | collective-permute-start | bytes 786440 | tf_op jit(solution)/shard_map/ppermute | solution.py:35
  172.6 13.5 %collective-permute-start.18 = (bf16[512,256]{0,1:T(8,128)(2,1)S(1)}, bf16[512,256]{0,1:T(8,128)(2,1)}, u32[]{:S(2)}, u32[]{:S(2)}) collective-permute-start(bf16[512,256]{0,1:T(8,128)(2,1)S(1)} %collective-permute-done.16), channel_id=1, source_target_pairs={{32,33},{33,34},{34,35},{35,36},{36,37},{37,38},{38,39},{39,40},{4... | collective-permute-start | bytes 786440 | tf_op jit(solution)/shard_map/ppermute | solution.py:35
  190.8 12.4 %collective-permute-start.20 = (bf16[512,256]{0,1:T(8,128)(2,1)}, bf16[512,256]{0,1:T(8,128)(2,1)S(1)}, u32[]{:S(2)}, u32[]{:S(2)}) collective-permute-start(bf16[512,256]{0,1:T(8,128)(2,1)} %multiply_convert_fusion.3), channel_id=1, source_target_pairs={{32,33},{33,34},{34,35},{35,36},{36,37},{37,38},{38,39},{39,40},{4... | collective-permute-start | bytes 786440 | tf_op jit(solution)/shard_map/ppermute | solution.py:35
  192.7 12.8 %collective-permute-start.21 = (bf16[512,256]{0,1:T(8,128)(2,1)}, bf16[512,256]{0,1:T(8,128)(2,1)S(1)}, u32[]{:S(2)}, u32[]{:S(2)}) collective-permute-start(bf16[512,256]{0,1:T(8,128)(2,1)} %multiply_convert_fusion.3), channel_id=1, source_target_pairs={{32,63},{33,32},{34,33},{35,34},{36,35},{37,36},{38,37},{39,38},{4... | collective-permute-start | bytes 786440 | tf_op jit(solution)/shard_map/ppermute | solution.py:35
  203.2 13.5 %collective-permute-start.22 = (bf16[512,256]{0,1:T(8,128)(2,1)S(1)}, bf16[512,256]{0,1:T(8,128)(2,1)}, u32[]{:S(2)}, u32[]{:S(2)}) collective-permute-start(bf16[512,256]{0,1:T(8,128)(2,1)S(1)} %collective-permute-done.20), channel_id=1, source_target_pairs={{32,33},{33,34},{34,35},{35,36},{36,37},{37,38},{38,39},{39,40},{4... | collective-permute-start | bytes 786440 | tf_op jit(solution)/shard_map/ppermute | solution.py:35
  221.3 12.4 %collective-permute-start.24 = (bf16[512,256]{0,1:T(8,128)(2,1)}, bf16[512,256]{0,1:T(8,128)(2,1)S(1)}, u32[]{:S(2)}, u32[]{:S(2)}) collective-permute-start(bf16[512,256]{0,1:T(8,128)(2,1)} %multiply_convert_fusion.2), channel_id=1, source_target_pairs={{32,33},{33,34},{34,35},{35,36},{36,37},{37,38},{38,39},{39,40},{4... | collective-permute-start | bytes 786440 | tf_op jit(solution)/shard_map/ppermute | solution.py:35
  223.2 12.8 %collective-permute-start.25 = (bf16[512,256]{0,1:T(8,128)(2,1)}, bf16[512,256]{0,1:T(8,128)(2,1)S(1)}, u32[]{:S(2)}, u32[]{:S(2)}) collective-permute-start(bf16[512,256]{0,1:T(8,128)(2,1)} %multiply_convert_fusion.2), channel_id=1, source_target_pairs={{32,63},{33,32},{34,33},{35,34},{36,35},{37,36},{38,37},{39,38},{4... | collective-permute-start | bytes 786440 | tf_op jit(solution)/shard_map/ppermute | solution.py:35
  233.8 13.5 %collective-permute-start.26 = (bf16[512,256]{0,1:T(8,128)(2,1)S(1)}, bf16[512,256]{0,1:T(8,128)(2,1)}, u32[]{:S(2)}, u32[]{:S(2)}) collective-permute-start(bf16[512,256]{0,1:T(8,128)(2,1)S(1)} %collective-permute-done.24), channel_id=1, source_target_pairs={{32,33},{33,34},{34,35},{35,36},{36,37},{37,38},{38,39},{39,40},{4... | collective-permute-start | bytes 786440 | tf_op jit(solution)/shard_map/ppermute | solution.py:35
  253.8 12.8 %collective-permute-start.29 = (bf16[512,256]{0,1:T(8,128)(2,1)}, bf16[512,256]{0,1:T(8,128)(2,1)S(1)}, u32[]{:S(2)}, u32[]{:S(2)}) collective-permute-start(bf16[512,256]{0,1:T(8,128)(2,1)} %multiply_convert_fusion.1), channel_id=1, source_target_pairs={{32,63},{33,32},{34,33},{35,34},{36,35},{37,36},{38,37},{39,38},{4... | collective-permute-start | bytes 786440 | tf_op jit(solution)/shard_map/ppermute | solution.py:35
  264.3 21.5 %collective-permute-start.30 = (bf16[512,256]{0,1:T(8,128)(2,1)S(1)}, bf16[512,256]{0,1:T(8,128)(2,1)S(1)}, u32[]{:S(2)}, u32[]{:S(2)}) collective-permute-start(bf16[512,256]{0,1:T(8,128)(2,1)S(1)} %collective-permute-done.28), channel_id=1, source_target_pairs={{32,33},{33,34},{34,35},{35,36},{36,37},{37,38},{38,39},{39,40},{4... | collective-permute-start | bytes 786440 | tf_op jit(solution)/shard_map/ppermute | solution.py:35
  276.6 14.7 %collective-permute-start.57 = (bf16[512,256]{0,1:T(8,128)(2,1)S(1)}, bf16[512,256]{0,1:T(8,128)(2,1)}, u32[]{:S(2)}, u32[]{:S(2)}) collective-permute-start(bf16[512,256]{0,1:T(8,128)(2,1)S(1)} %multiply_convert_fusion.5), channel_id=1, source_target_pairs={{224,64},{225,65},{226,66},{227,67},{228,68},{229,69},{230,70},{23... | collective-permute-start | bytes 786440 | tf_op jit(solution)/shard_map/ppermute | solution.py:95
  (45 other events, 432.8 us)
Sparse Core Ops, SparseCore 0:
  9.2 27.4 all-gather.2
  38.6 25.6 all-gather.4

commit v2 on v1

--- a/solution.py
+++ b/solution.py
@@ -20,8 +20,9 @@
     blk_index = lax.axis_index("blk")
     section_index = lax.axis_index("section")
 
-    self_all = lax.all_gather(self_weight[0], "section")
-    neighbour_all = lax.all_gather(neighbour_weight[0], "section")
+    weights_all = lax.all_gather(jnp.stack([self_weight[0], neighbour_weight[0]]), "section")
+    self_all = weights_all[:, 0]
+    neighbour_all = weights_all[:, 1]
 
     group = section_count // batch_total
     workers = [group * m + group - 1 for m in range(batch_total)]
@@ -84,17 +85,22 @@
         hidden = (active * scale).astype(jnp.bfloat16)
         outputs.append(hidden)
 
-    gathered = []
-    for m in range(batch_total):
-        slot = jnp.zeros((rows_dev, feature_width), jnp.bfloat16)
-        for level in range(layer_total):
-            source = workers[m]
-            if source == level:
-                arrived = outputs[level]
-            else:
-                arrived = lax.ppermute(outputs[level], "section", [(source, level)])
-            slot = jnp.where(section_index == level, arrived, slot)
-        gathered.append(slot)
+    arrived = []
+    for shift in range(section_count):
+        candidates = [(w + shift) % section_count for w in workers]
+        sending = outputs[candidates[0]]
+        for w, level in zip(workers[1:], candidates[1:]):
+            sending = jnp.where(section_index == w, outputs[level], sending)
+        if shift == 0:
+            arrived.append(sending)
+        else:
+            pairs = [(w, (w + shift) % section_count) for w in workers]
+            arrived.append(lax.ppermute(sending, "section", pairs))
+    arrived = jnp.stack(arrived)
+    gathered = [
+        lax.dynamic_index_in_dim(arrived, (section_index - w) % section_count, 0, keepdims=False)
+        for w in workers
+    ]
     return jnp.stack(gathered)[None]
 
 

time: 337 us -> 286 us (0.85)
  the two profiles are of different devices: /device:TPU:7 before, /device:TPU:1 now
where the time goes in v2:
time: 286 us; the launch traced here: 283 us
  starting transfers between devices  130 us (45%)
  matrix products  68 us (24%)
  waiting for transfers between devices  38.7 us (14%)
  local copies, waits for them, and re-layouts  20.1 us (7%)
  between operations  14.5 us (5%)
  other arithmetic  11.3 us (4%)
    ppermute x32, starting transfers between devices, halo(): return lax.ppermute(x, ('section', 'blk'), pairs)  112 us
    ppermute x32, waiting for transfers between devices, halo(): return lax.ppermute(x, ('section', 'blk'), pairs)  33.9 us
    dot_general x24, matrix products, body(): jnp.dot(band[:, position, :], parts[position], preferred_element_type=jnp...  30.3 us
    ppermute x7, starting transfers between devices, body(): arrived.append(lax.ppermute(sending, 'section', pairs))  17.9 us
    dot_general x8, matrix products, body(): jnp.dot(neighbour_mean, neighbour_all[level], preferred_element_type=jnp....  15.8 us
    dot_general x8, matrix products, body(): jnp.dot(hidden, self_all[level], preferred_element_type=jnp.float32)  11 us
    dot_general x8, matrix products, body(): jnp.dot(band[:, REACH, :], hidden, preferred_element_type=jnp.float32)  8.99 us
    select_n x4, other arithmetic, body(): sending = jnp.where(section_index == w, outputs[level], sending)  6.85 us
  transfers between devices with their start and end apart: 40, of which 10 were waited for; matrix products, arithmetic and copies ran while one was open for 27% of the time, Pallas kernels for 0%

profile of v2, /device:TPU:1, one launch (start us, length us, event | category | flops | bytes accessed | tf_op | source)
XLA Modules:
  0.0 283.0 jit_solution(10916462579513807213)
XLA Ops:
  8.4 10.8 %collective-permute-start.1 = (bf16[512,256]{1,0:T(8,128)(2,1)S(1)}, bf16[512,256]{1,0:T(8,128)(2,1)S(1)}, u32[]{:S(2)}, u32[]{:S(2)}) collective-permute-start(bf16[512,256]{1,0:T(8,128)(2,1)S(1)} %dynamic-slice_bitcast_fusion), channel_id=1, source_target_pairs={{32,63},{33,32},{34,33},{35,34},{36,35},{37,36},{38,37},{39,38},{4... | collective-permute-start | bytes 786440 | tf_op jit(solution)/shard_map/ppermute | solution.py:36
  30.8 5.3 %copy.17 = bf16[4,20,128,128]{2,0,3,1:T(4,128)(2,1)} copy(bf16[4,20,128,128]{3,2,1,0:T(8,128)(2,1)} %bitcast.265) | data formatting | bytes 5242880 | tf_op jit(solution)/shard_map/reshape | solution.py:61
  36.1 3.8 %reshape.119 = bf16[512,5,512]{0,2,1:T(8,128)(2,1)S(1)} reshape(bf16[4,128,20,128]{1,0,3,2:T(4,128)(2,1)} %bitcast.266) | data formatting | bytes 5242880 | tf_op jit(solution)/shard_map/reshape | solution.py:63
  40.3 6.6 %collective-permute-start.3 = (bf16[512,256]{1,0:T(8,128)(2,1)S(1)}, bf16[512,256]{1,0:T(8,128)(2,1)S(1)}, u32[]{:S(2)}, u32[]{:S(2)}) collective-permute-start(bf16[512,256]{1,0:T(8,128)(2,1)S(1)} %collective-permute-done.1), channel_id=1, source_target_pairs={{32,63},{33,32},{34,33},{35,34},{36,35},{37,36},{38,37},{39,38},{4... | collective-permute-start | bytes 786440 | tf_op jit(solution)/shard_map/ppermute | solution.py:36
  53.5 4.0 %collective-permute-done.2 = bf16[512,256]{1,0:T(8,128)(2,1)} collective-permute-done((bf16[512,256]{1,0:T(8,128)(2,1)S(1)}, bf16[512,256]{1,0:T(8,128)(2,1)}, u32[]{:S(2)}, u32[]{:S(2)}) %collective-permute-start.2) | collective-permute-done | bytes 262176 | tf_op jit(solution)/shard_map/ppermute | solution.py:36
  59.6 3.0 %collective-permute-start.5 = (bf16[512,256]{0,1:T(8,128)(2,1)S(1)}, bf16[512,256]{0,1:T(8,128)(2,1)S(1)}, u32[]{:S(2)}, u32[]{:S(2)}) collective-permute-start(bf16[512,256]{0,1:T(8,128)(2,1)S(1)} %multiply_convert_fusion.7), channel_id=1, source_target_pairs={{32,63},{33,32},{34,33},{35,34},{36,35},{37,36},{38,37},{39,38},{4... | collective-permute-start | bytes 786440 | tf_op jit(solution)/shard_map/ppermute | solution.py:36
  67.5 6.3 %collective-permute-start.7 = (bf16[512,256]{0,1:T(8,128)(2,1)S(1)}, bf16[512,256]{0,1:T(8,128)(2,1)S(1)}, u32[]{:S(2)}, u32[]{:S(2)}) collective-permute-start(bf16[512,256]{0,1:T(8,128)(2,1)S(1)} %collective-permute-done.5), channel_id=1, source_target_pairs={{32,63},{33,32},{34,33},{35,34},{36,35},{37,36},{38,37},{39,38},{4... | collective-permute-start | bytes 786440 | tf_op jit(solution)/shard_map/ppermute | solution.py:36
  80.0 4.3 %collective-permute-done.6 = bf16[512,256]{0,1:T(8,128)(2,1)S(1)} collective-permute-done((bf16[512,256]{0,1:T(8,128)(2,1)S(1)}, bf16[512,256]{0,1:T(8,128)(2,1)S(1)}, u32[]{:S(2)}, u32[]{:S(2)}) %collective-permute-start.6) | collective-permute-done | bytes 262176 | tf_op jit(solution)/shard_map/ppermute | solution.py:36
  93.9 5.7 %collective-permute-start.11 = (bf16[512,256]{0,1:T(8,128)(2,1)S(1)}, bf16[512,256]{0,1:T(8,128)(2,1)S(1)}, u32[]{:S(2)}, u32[]{:S(2)}) collective-permute-start(bf16[512,256]{0,1:T(8,128)(2,1)S(1)} %collective-permute-done.9), channel_id=1, source_target_pairs={{32,63},{33,32},{34,33},{35,34},{36,35},{37,36},{38,37},{39,38},{4... | collective-permute-start | bytes 786440 | tf_op jit(solution)/shard_map/ppermute | solution.py:36
  105.8 4.3 %collective-permute-done.10 = bf16[512,256]{0,1:T(8,128)(2,1)S(1)} collective-permute-done((bf16[512,256]{0,1:T(8,128)(2,1)S(1)}, bf16[512,256]{0,1:T(8,128)(2,1)S(1)}, u32[]{:S(2)}, u32[]{:S(2)}) %collective-permute-start.10) | collective-permute-done | bytes 262176 | tf_op jit(solution)/shard_map/ppermute | solution.py:36
  119.7 5.7 %collective-permute-start.15 = (bf16[512,256]{0,1:T(8,128)(2,1)S(1)}, bf16[512,256]{0,1:T(8,128)(2,1)S(1)}, u32[]{:S(2)}, u32[]{:S(2)}) collective-permute-start(bf16[512,256]{0,1:T(8,128)(2,1)S(1)} %collective-permute-done.13), channel_id=1, source_target_pairs={{32,63},{33,32},{34,33},{35,34},{36,35},{37,36},{38,37},{39,38},{4... | collective-permute-start | bytes 786440 | tf_op jit(solution)/shard_map/ppermute | solution.py:36
  131.7 4.1 %collective-permute-done.14 = bf16[512,256]{0,1:T(8,128)(2,1)S(1)} collective-permute-done((bf16[512,256]{0,1:T(8,128)(2,1)S(1)}, bf16[512,256]{0,1:T(8,128)(2,1)S(1)}, u32[]{:S(2)}, u32[]{:S(2)}) %collective-permute-start.14) | collective-permute-done | bytes 262176 | tf_op jit(solution)/shard_map/ppermute | solution.py:36
  145.5 5.9 %collective-permute-start.19 = (bf16[512,256]{0,1:T(8,128)(2,1)S(1)}, bf16[512,256]{0,1:T(8,128)(2,1)S(1)}, u32[]{:S(2)}, u32[]{:S(2)}) collective-permute-start(bf16[512,256]{0,1:T(8,128)(2,1)S(1)} %collective-permute-done.17), channel_id=1, source_target_pairs={{32,63},{33,32},{34,33},{35,34},{36,35},{37,36},{38,37},{39,38},{4... | collective-permute-start | bytes 786440 | tf_op jit(solution)/shard_map/ppermute | solution.py:36
  157.5 4.3 %collective-permute-done.18 = bf16[512,256]{0,1:T(8,128)(2,1)S(1)} collective-permute-done((bf16[512,256]{0,1:T(8,128)(2,1)S(1)}, bf16[512,256]{0,1:T(8,128)(2,1)S(1)}, u32[]{:S(2)}, u32[]{:S(2)}) %collective-permute-start.18) | collective-permute-done | bytes 262176 | tf_op jit(solution)/shard_map/ppermute | solution.py:36
  171.4 5.7 %collective-permute-start.23 = (bf16[512,256]{0,1:T(8,128)(2,1)S(1)}, bf16[512,256]{0,1:T(8,128)(2,1)S(1)}, u32[]{:S(2)}, u32[]{:S(2)}) collective-permute-start(bf16[512,256]{0,1:T(8,128)(2,1)S(1)} %collective-permute-done.21), channel_id=1, source_target_pairs={{32,63},{33,32},{34,33},{35,34},{36,35},{37,36},{38,37},{39,38},{4... | collective-permute-start | bytes 786440 | tf_op jit(solution)/shard_map/ppermute | solution.py:36
  183.3 4.4 %collective-permute-done.22 = bf16[512,256]{0,1:T(8,128)(2,1)} collective-permute-done((bf16[512,256]{0,1:T(8,128)(2,1)S(1)}, bf16[512,256]{0,1:T(8,128)(2,1)}, u32[]{:S(2)}, u32[]{:S(2)}) %collective-permute-start.22) | collective-permute-done | bytes 262176 | tf_op jit(solution)/shard_map/ppermute | solution.py:36
  197.4 5.6 %collective-permute-start.27 = (bf16[512,256]{0,1:T(8,128)(2,1)S(1)}, bf16[512,256]{0,1:T(8,128)(2,1)S(1)}, u32[]{:S(2)}, u32[]{:S(2)}) collective-permute-start(bf16[512,256]{0,1:T(8,128)(2,1)S(1)} %collective-permute-done.25), channel_id=1, source_target_pairs={{32,63},{33,32},{34,33},{35,34},{36,35},{37,36},{38,37},{39,38},{4... | collective-permute-start | bytes 786440 | tf_op jit(solution)/shard_map/ppermute | solution.py:36
  209.2 4.4 %collective-permute-done.26 = bf16[512,256]{0,1:T(8,128)(2,1)} collective-permute-done((bf16[512,256]{0,1:T(8,128)(2,1)S(1)}, bf16[512,256]{0,1:T(8,128)(2,1)}, u32[]{:S(2)}, u32[]{:S(2)}) %collective-permute-start.26) | collective-permute-done | bytes 262176 | tf_op jit(solution)/shard_map/ppermute | solution.py:36
  234.7 5.6 %collective-permute-start.31 = (bf16[512,256]{0,1:T(8,128)(2,1)S(1)}, bf16[512,256]{0,1:T(8,128)(2,1)S(1)}, u32[]{:S(2)}, u32[]{:S(2)}) collective-permute-start(bf16[512,256]{0,1:T(8,128)(2,1)S(1)} %collective-permute-done.29), channel_id=1, source_target_pairs={{32,63},{33,32},{34,33},{35,34},{36,35},{37,36},{38,37},{39,38},{4... | collective-permute-start | bytes 786440 | tf_op jit(solution)/shard_map/ppermute | solution.py:36
  246.9 4.0 %collective-permute-done.30 = bf16[512,256]{0,1:T(8,128)(2,1)} collective-permute-done((bf16[512,256]{0,1:T(8,128)(2,1)S(1)}, bf16[512,256]{0,1:T(8,128)(2,1)}, u32[]{:S(2)}, u32[]{:S(2)}) %collective-permute-start.30) | collective-permute-done | bytes 262176 | tf_op jit(solution)/shard_map/ppermute | solution.py:36
  255.6 3.2 %collective-permute-start.33 = (bf16[512,256]{0,1:T(8,128)(2,1)S(1)}, bf16[512,256]{0,1:T(8,128)(2,1)S(1)}, u32[]{:S(2)}, u32[]{:S(2)}) collective-permute-start(bf16[512,256]{0,1:T(8,128)(2,1)S(1)} %get-tuple-element.17), channel_id=1, source_target_pairs={{32,96},{96,160},{160,224},{224,32},{33,97},{97,161},{161,225},{22... | collective-permute-start | bytes 786440 | tf_op jit(solution)/shard_map/ppermute | solution.py:98
  259.0 3.3 %collective-permute-start.37 = (bf16[512,256]{0,1:T(8,128)(2,1)S(1)}, bf16[512,256]{0,1:T(8,128)(2,1)S(1)}, u32[]{:S(2)}, u32[]{:S(2)}) collective-permute-start(bf16[512,256]{0,1:T(8,128)(2,1)S(1)} %get-tuple-element.7), channel_id=1, source_target_pairs={{32,224},{96,32},{160,96},{224,160},{33,225},{97,33},{161,97},{225... | collective-permute-start | bytes 786440 | tf_op jit(solution)/shard_map/ppermute | solution.py:98
  263.9 3.4 %collective-permute-start.35 = (bf16[512,256]{0,1:T(8,128)(2,1)S(1)}, bf16[512,256]{0,1:T(8,128)(2,1)S(1)}, u32[]{:S(2)}, u32[]{:S(2)}) collective-permute-start(bf16[512,256]{0,1:T(8,128)(2,1)S(1)} %get-tuple-element.16), channel_id=1, source_target_pairs={{32,160},{96,224},{160,32},{224,96},{33,161},{97,225},{161,33},{22... | collective-permute-start | bytes 786440 | tf_op jit(solution)/shard_map/ppermute | solution.py:98
  268.4 4.2 %collective-permute-done.35 = bf16[512,256]{0,1:T(8,128)(2,1)S(1)} collective-permute-done((bf16[512,256]{0,1:T(8,128)(2,1)S(1)}, bf16[512,256]{0,1:T(8,128)(2,1)S(1)}, u32[]{:S(2)}, u32[]{:S(2)}) %collective-permute-start.35) | collective-permute-done | bytes 262176 | tf_op jit(solution)/shard_map/ppermute | solution.py:98
  (167 shorter events, 150.5 us)
Async XLA Ops:
  6.5 45.0 %all-gather.3.cloned.1.call-start = ((), (), s32[]{:S(2)}) async-start(), calls=%async_computation | async-start | bytes 2359296 | tf_op jit(solution)/shard_map/all_gather | solution.py:23
  8.4 31.9 %collective-permute-start.1 = (bf16[512,256]{1,0:T(8,128)(2,1)S(1)}, bf16[512,256]{1,0:T(8,128)(2,1)S(1)}, u32[]{:S(2)}, u32[]{:S(2)}) collective-permute-start(bf16[512,256]{1,0:T(8,128)(2,1)S(1)} %dynamic-slice_bitcast_fusion), channel_id=1, source_target_pairs={{32,63},{33,32},{34,33},{35,34},{36,35},{37,36},{38,37},{39,38},{4... | collective-permute-start | bytes 786440 | tf_op jit(solution)/shard_map/ppermute | solution.py:36
  19.2 27.7 %collective-permute-start = (bf16[512,256]{1,0:T(8,128)(2,1)S(1)}, bf16[512,256]{1,0:T(8,128)(2,1)S(1)}, u32[]{:S(2)}, u32[]{:S(2)}) collective-permute-start(bf16[512,256]{1,0:T(8,128)(2,1)S(1)} %dynamic-slice_bitcast_fusion), channel_id=1, source_target_pairs={{32,33},{33,34},{34,35},{35,36},{36,37},{37,38},{38,39},{39,40},{4... | collective-permute-start | bytes 786440 | tf_op jit(solution)/shard_map/ppermute | solution.py:36
  46.9 10.5 %collective-permute-start.2 = (bf16[512,256]{1,0:T(8,128)(2,1)S(1)}, bf16[512,256]{1,0:T(8,128)(2,1)}, u32[]{:S(2)}, u32[]{:S(2)}) collective-permute-start(bf16[512,256]{1,0:T(8,128)(2,1)S(1)} %collective-permute-done), channel_id=1, source_target_pairs={{32,33},{33,34},{34,35},{35,36},{36,37},{37,38},{38,39},{39,40},{4... | collective-permute-start | bytes 786440 | tf_op jit(solution)/shard_map/ppermute | solution.py:36
  62.6 11.2 %collective-permute-start.4 = (bf16[512,256]{0,1:T(8,128)(2,1)S(1)}, bf16[512,256]{0,1:T(8,128)(2,1)S(1)}, u32[]{:S(2)}, u32[]{:S(2)}) collective-permute-start(bf16[512,256]{0,1:T(8,128)(2,1)S(1)} %multiply_convert_fusion.7), channel_id=1, source_target_pairs={{32,33},{33,34},{34,35},{35,36},{36,37},{37,38},{38,39},{39,40},{4... | collective-permute-start | bytes 786440 | tf_op jit(solution)/shard_map/ppermute | solution.py:36
  67.5 11.1 %collective-permute-start.7 = (bf16[512,256]{0,1:T(8,128)(2,1)S(1)}, bf16[512,256]{0,1:T(8,128)(2,1)S(1)}, u32[]{:S(2)}, u32[]{:S(2)}) collective-permute-start(bf16[512,256]{0,1:T(8,128)(2,1)S(1)} %collective-permute-done.5), channel_id=1, source_target_pairs={{32,63},{33,32},{34,33},{35,34},{36,35},{37,36},{38,37},{39,38},{4... | collective-permute-start | bytes 786440 | tf_op jit(solution)/shard_map/ppermute | solution.py:36
  88.4 11.2 %collective-permute-start.8 = (bf16[512,256]{0,1:T(8,128)(2,1)S(1)}, bf16[512,256]{0,1:T(8,128)(2,1)S(1)}, u32[]{:S(2)}, u32[]{:S(2)}) collective-permute-start(bf16[512,256]{0,1:T(8,128)(2,1)S(1)} %multiply_convert_fusion.6), channel_id=1, source_target_pairs={{32,33},{33,34},{34,35},{35,36},{36,37},{37,38},{38,39},{39,40},{4... | collective-permute-start | bytes 786440 | tf_op jit(solution)/shard_map/ppermute | solution.py:36
  114.2 11.2 %collective-permute-start.12 = (bf16[512,256]{0,1:T(8,128)(2,1)S(1)}, bf16[512,256]{0,1:T(8,128)(2,1)S(1)}, u32[]{:S(2)}, u32[]{:S(2)}) collective-permute-start(bf16[512,256]{0,1:T(8,128)(2,1)S(1)} %multiply_convert_fusion.5), channel_id=1, source_target_pairs={{32,33},{33,34},{34,35},{35,36},{36,37},{37,38},{38,39},{39,40},{4... | collective-permute-start | bytes 786440 | tf_op jit(solution)/shard_map/ppermute | solution.py:36
  119.7 10.6 %collective-permute-start.15 = (bf16[512,256]{0,1:T(8,128)(2,1)S(1)}, bf16[512,256]{0,1:T(8,128)(2,1)S(1)}, u32[]{:S(2)}, u32[]{:S(2)}) collective-permute-start(bf16[512,256]{0,1:T(8,128)(2,1)S(1)} %collective-permute-done.13), channel_id=1, source_target_pairs={{32,63},{33,32},{34,33},{35,34},{36,35},{37,36},{38,37},{39,38},{4... | collective-permute-start | bytes 786440 | tf_op jit(solution)/shard_map/ppermute | solution.py:36
  140.2 11.2 %collective-permute-start.16 = (bf16[512,256]{0,1:T(8,128)(2,1)S(1)}, bf16[512,256]{0,1:T(8,128)(2,1)S(1)}, u32[]{:S(2)}, u32[]{:S(2)}) collective-permute-start(bf16[512,256]{0,1:T(8,128)(2,1)S(1)} %multiply_convert_fusion.4), channel_id=1, source_target_pairs={{32,33},{33,34},{34,35},{35,36},{36,37},{37,38},{38,39},{39,40},{4... | collective-permute-start | bytes 786440 | tf_op jit(solution)/shard_map/ppermute | solution.py:36
  145.5 10.6 %collective-permute-start.19 = (bf16[512,256]{0,1:T(8,128)(2,1)S(1)}, bf16[512,256]{0,1:T(8,128)(2,1)S(1)}, u32[]{:S(2)}, u32[]{:S(2)}) collective-permute-start(bf16[512,256]{0,1:T(8,128)(2,1)S(1)} %collective-permute-done.17), channel_id=1, source_target_pairs={{32,63},{33,32},{34,33},{35,34},{36,35},{37,36},{38,37},{39,38},{4... | collective-permute-start | bytes 786440 | tf_op jit(solution)/shard_map/ppermute | solution.py:36
  165.9 11.2 %collective-permute-start.20 = (bf16[512,256]{0,1:T(8,128)(2,1)S(1)}, bf16[512,256]{0,1:T(8,128)(2,1)S(1)}, u32[]{:S(2)}, u32[]{:S(2)}) collective-permute-start(bf16[512,256]{0,1:T(8,128)(2,1)S(1)} %multiply_convert_fusion.3), channel_id=1, source_target_pairs={{32,33},{33,34},{34,35},{35,36},{36,37},{37,38},{38,39},{39,40},{4... | collective-permute-start | bytes 786440 | tf_op jit(solution)/shard_map/ppermute | solution.py:36
  171.4 10.5 %collective-permute-start.23 = (bf16[512,256]{0,1:T(8,128)(2,1)S(1)}, bf16[512,256]{0,1:T(8,128)(2,1)S(1)}, u32[]{:S(2)}, u32[]{:S(2)}) collective-permute-start(bf16[512,256]{0,1:T(8,128)(2,1)S(1)} %collective-permute-done.21), channel_id=1, source_target_pairs={{32,63},{33,32},{34,33},{35,34},{36,35},{37,36},{38,37},{39,38},{4... | collective-permute-start | bytes 786440 | tf_op jit(solution)/shard_map/ppermute | solution.py:36
  177.2 10.5 %collective-permute-start.22 = (bf16[512,256]{0,1:T(8,128)(2,1)S(1)}, bf16[512,256]{0,1:T(8,128)(2,1)}, u32[]{:S(2)}, u32[]{:S(2)}) collective-permute-start(bf16[512,256]{0,1:T(8,128)(2,1)S(1)} %collective-permute-done.20), channel_id=1, source_target_pairs={{32,33},{33,34},{34,35},{35,36},{36,37},{37,38},{38,39},{39,40},{4... | collective-permute-start | bytes 786440 | tf_op jit(solution)/shard_map/ppermute | solution.py:36
  191.8 11.2 %collective-permute-start.24 = (bf16[512,256]{0,1:T(8,128)(2,1)S(1)}, bf16[512,256]{0,1:T(8,128)(2,1)S(1)}, u32[]{:S(2)}, u32[]{:S(2)}) collective-permute-start(bf16[512,256]{0,1:T(8,128)(2,1)S(1)} %multiply_convert_fusion.2), channel_id=1, source_target_pairs={{32,33},{33,34},{34,35},{35,36},{36,37},{37,38},{38,39},{39,40},{4... | collective-permute-start | bytes 786440 | tf_op jit(solution)/shard_map/ppermute | solution.py:36
  203.0 10.5 %collective-permute-start.26 = (bf16[512,256]{0,1:T(8,128)(2,1)S(1)}, bf16[512,256]{0,1:T(8,128)(2,1)}, u32[]{:S(2)}, u32[]{:S(2)}) collective-permute-start(bf16[512,256]{0,1:T(8,128)(2,1)S(1)} %collective-permute-done.24), channel_id=1, source_target_pairs={{32,33},{33,34},{34,35},{35,36},{36,37},{37,38},{38,39},{39,40},{4... | collective-permute-start | bytes 786440 | tf_op jit(solution)/shard_map/ppermute | solution.py:36
  221.1 13.6 %collective-permute-start.29 = (bf16[512,256]{0,1:T(8,128)(2,1)S(1)}, bf16[512,256]{0,1:T(8,128)(2,1)S(1)}, u32[]{:S(2)}, u32[]{:S(2)}) collective-permute-start(bf16[512,256]{0,1:T(8,128)(2,1)S(1)} %get-tuple-element.6), channel_id=1, source_target_pairs={{32,63},{33,32},{34,33},{35,34},{36,35},{37,36},{38,37},{39,38},{4... | collective-permute-start | bytes 786440 | tf_op jit(solution)/shard_map/ppermute | solution.py:36
  223.4 16.9 %collective-permute-start.28 = (bf16[512,256]{0,1:T(8,128)(2,1)S(1)}, bf16[512,256]{0,1:T(8,128)(2,1)S(1)}, u32[]{:S(2)}, u32[]{:S(2)}) collective-permute-start(bf16[512,256]{0,1:T(8,128)(2,1)S(1)} %get-tuple-element.6), channel_id=1, source_target_pairs={{32,33},{33,34},{34,35},{35,36},{36,37},{37,38},{38,39},{39,40},{4... | collective-permute-start | bytes 786440 | tf_op jit(solution)/shard_map/ppermute | solution.py:36
  228.4 44.2 %collective-permute-start.36 = (bf16[512,256]{0,1:T(8,128)(2,1)S(1)}, bf16[512,256]{0,1:T(8,128)(2,1)}, u32[]{:S(2)}, u32[]{:S(2)}) collective-permute-start(bf16[512,256]{0,1:T(8,128)(2,1)S(1)} %get-tuple-element.13), channel_id=1, source_target_pairs={{32,192},{96,0},{160,64},{224,128},{33,193},{97,1},{161,65},{225,1... | collective-permute-start | bytes 786440 | tf_op jit(solution)/shard_map/ppermute | solution.py:98
  230.4 37.0 %collective-permute-start.34 = (bf16[512,256]{0,1:T(8,128)(2,1)}, bf16[512,256]{0,1:T(8,128)(2,1)}, u32[]{:S(2)}, u32[]{:S(2)}) collective-permute-start(bf16[512,256]{0,1:T(8,128)(2,1)} %get-tuple-element.14), channel_id=1, source_target_pairs={{32,128},{96,192},{160,0},{224,64},{33,129},{97,193},{161,1},{225,... | collective-permute-start | bytes 786440 | tf_op jit(solution)/shard_map/ppermute | solution.py:98
  232.3 26.7 %collective-permute-start.32 = (bf16[512,256]{0,1:T(8,128)(2,1)}, bf16[512,256]{0,1:T(8,128)(2,1)}, u32[]{:S(2)}, u32[]{:S(2)}) collective-permute-start(bf16[512,256]{0,1:T(8,128)(2,1)} %get-tuple-element.15), channel_id=1, source_target_pairs={{32,64},{96,128},{160,192},{224,0},{33,65},{97,129},{161,193},{225... | collective-permute-start | bytes 786440 | tf_op jit(solution)/shard_map/ppermute | solution.py:98
  240.3 10.5 %collective-permute-start.30 = (bf16[512,256]{0,1:T(8,128)(2,1)S(1)}, bf16[512,256]{0,1:T(8,128)(2,1)}, u32[]{:S(2)}, u32[]{:S(2)}) collective-permute-start(bf16[512,256]{0,1:T(8,128)(2,1)S(1)} %collective-permute-done.28), channel_id=1, source_target_pairs={{32,33},{33,34},{34,35},{35,36},{36,37},{37,38},{38,39},{39,40},{4... | collective-permute-start | bytes 786440 | tf_op jit(solution)/shard_map/ppermute | solution.py:36
  243.7 29.8 %collective-permute-start.38 = (bf16[512,256]{0,1:T(8,128)(2,1)}, bf16[512,256]{0,1:T(8,128)(2,1)}, u32[]{:S(2)}, u32[]{:S(2)}) collective-permute-start(bf16[512,256]{0,1:T(8,128)(2,1)} %get-tuple-element.5), channel_id=1, source_target_pairs={{32,0},{96,64},{160,128},{224,192},{33,1},{97,65},{161,129},{225,1... | collective-permute-start | bytes 786440 | tf_op jit(solution)/shard_map/ppermute | solution.py:98
  259.0 14.5 %collective-permute-start.37 = (bf16[512,256]{0,1:T(8,128)(2,1)S(1)}, bf16[512,256]{0,1:T(8,128)(2,1)S(1)}, u32[]{:S(2)}, u32[]{:S(2)}) collective-permute-start(bf16[512,256]{0,1:T(8,128)(2,1)S(1)} %get-tuple-element.7), channel_id=1, source_target_pairs={{32,224},{96,32},{160,96},{224,160},{33,225},{97,33},{161,97},{225... | collective-permute-start | bytes 786440 | tf_op jit(solution)/shard_map/ppermute | solution.py:98
  (27 other events, 314.2 us)
Sparse Core Ops, SparseCore 0:
  9.2 31.9 all-gather.2

commit v3 on v2

--- a/solution.py
+++ b/solution.py
@@ -68,8 +68,8 @@
     for level in range(layer_total):
         up1 = halo(hidden, 1)
         down1 = halo(hidden, -1)
-        up2 = halo(up1, 1)
-        down2 = halo(down1, -1)
+        up2 = halo(hidden, 2)
+        down2 = halo(hidden, -2)
         parts = [up2, up1, hidden, down1, down2]
         summed = jnp.dot(band[:, REACH, :], hidden, preferred_element_type=jnp.float32)
         for position in (REACH - 1, REACH + 1, REACH - 2, REACH + 2):

time: 286 us -> 306 us (1.070)
  matrix products: 68 us -> 77.4 us
  starting transfers between devices: 130 us -> 136 us
  waiting for transfers between devices: 38.7 us -> 43.7 us
    dot_general x24, matrix products: 30.3 us -> 37.9 us  [body(): jnp.dot(band[:, position, :], parts[position], preferred_element_type=jnp...]
    ppermute x32, starting transfers between devices: 112 us -> 118 us  [halo(): return lax.ppermute(x, ('section', 'blk'), pairs)]
    ppermute x32, waiting for transfers between devices: 33.9 us -> 38.9 us  [halo(): return lax.ppermute(x, ('section', 'blk'), pairs)]
  transfers between devices with their start and end apart: 40 -> 40, of which waited for: 10 -> 9; matrix products, arithmetic and copies ran while one was open for 27% -> 28% of each run, Pallas kernels for 0% -> 0%
where the time goes in v3:
time: 306 us; the launch traced here: 303 us
  starting transfers between devices  136 us (44%)
  matrix products  77.4 us (25%)
  waiting for transfers between devices  43.7 us (14%)
  local copies, waits for them, and re-layouts  20.1 us (7%)
  between operations  14.4 us (5%)
  other arithmetic  11.4 us (4%)
    ppermute x32, starting transfers between devices, halo(): return lax.ppermute(x, ('section', 'blk'), pairs)  118 us
    ppermute x32, waiting for transfers between devices, halo(): return lax.ppermute(x, ('section', 'blk'), pairs)  38.9 us
    dot_general x24, matrix products, body(): jnp.dot(band[:, position, :], parts[position], preferred_element_type=jnp...  37.9 us
    ppermute x7, starting transfers between devices, body(): arrived.append(lax.ppermute(sending, 'section', pairs))  17.9 us
    dot_general x8, matrix products, body(): jnp.dot(neighbour_mean, neighbour_all[level], preferred_element_type=jnp....  16.8 us
    dot_general x8, matrix products, body(): jnp.dot(hidden, self_all[level], preferred_element_type=jnp.float32)  11.8 us
    dot_general x8, matrix products, body(): jnp.dot(band[:, REACH, :], hidden, preferred_element_type=jnp.float32)  8.99 us
    select_n x4, other arithmetic, body(): sending = jnp.where(section_index == w, outputs[level], sending)  6.85 us
  transfers between devices with their start and end apart: 40, of which 9 were waited for; matrix products, arithmetic and copies ran while one was open for 28% of the time, Pallas kernels for 0%

profile of v3, /device:TPU:1, one launch (start us, length us, event | category | flops | bytes accessed | tf_op | source)
XLA Modules:
  0.0 302.9 jit_solution(7303979409654663695)
XLA Ops:
  8.4 11.2 %collective-permute-start.3 = (bf16[512,256]{1,0:T(8,128)(2,1)S(1)}, bf16[512,256]{1,0:T(8,128)(2,1)}, u32[]{:S(2)}, u32[]{:S(2)}) collective-permute-start(bf16[512,256]{1,0:T(8,128)(2,1)S(1)} %dynamic-slice_bitcast_fusion), channel_id=1, source_target_pairs={{32,62},{33,63},{34,32},{35,33},{36,34},{37,35},{38,36},{39,37},{4... | collective-permute-start | bytes 786440 | tf_op jit(solution)/shard_map/ppermute | solution.py:36
  21.5 7.1 %collective-permute-start.1 = (bf16[512,256]{1,0:T(8,128)(2,1)S(1)}, bf16[512,256]{1,0:T(8,128)(2,1)S(1)}, u32[]{:S(2)}, u32[]{:S(2)}) collective-permute-start(bf16[512,256]{1,0:T(8,128)(2,1)S(1)} %dynamic-slice_bitcast_fusion), channel_id=1, source_target_pairs={{32,63},{33,32},{34,33},{35,34},{36,35},{37,36},{38,37},{39,38},{4... | collective-permute-start | bytes 786440 | tf_op jit(solution)/shard_map/ppermute | solution.py:36
  40.4 5.3 %copy.17 = bf16[4,20,128,128]{2,0,3,1:T(4,128)(2,1)} copy(bf16[4,20,128,128]{3,2,1,0:T(8,128)(2,1)} %bitcast.265) | data formatting | bytes 5242880 | tf_op jit(solution)/shard_map/reshape | solution.py:61
  65.7 10.0 %collective-permute-start.5 = (bf16[512,256]{0,1:T(8,128)(2,1)S(1)}, bf16[512,256]{0,1:T(8,128)(2,1)S(1)}, u32[]{:S(2)}, u32[]{:S(2)}) collective-permute-start(bf16[512,256]{0,1:T(8,128)(2,1)S(1)} %multiply_convert_fusion.7), channel_id=1, source_target_pairs={{32,63},{33,32},{34,33},{35,34},{36,35},{37,36},{38,37},{39,38},{4... | collective-permute-start | bytes 786440 | tf_op jit(solution)/shard_map/ppermute | solution.py:36
  80.2 5.9 %collective-permute-done.4 = bf16[512,256]{0,1:T(8,128)(2,1)S(1)} collective-permute-done((bf16[512,256]{0,1:T(8,128)(2,1)S(1)}, bf16[512,256]{0,1:T(8,128)(2,1)S(1)}, u32[]{:S(2)}, u32[]{:S(2)}) %collective-permute-start.4) | collective-permute-done | bytes 262176 | tf_op jit(solution)/shard_map/ppermute | solution.py:36
  94.0 4.3 %collective-permute-start.10 = (bf16[512,256]{0,1:T(8,128)(2,1)S(1)}, bf16[512,256]{0,1:T(8,128)(2,1)S(1)}, u32[]{:S(2)}, u32[]{:S(2)}) collective-permute-start(bf16[512,256]{0,1:T(8,128)(2,1)S(1)} %multiply_convert_fusion.6), channel_id=1, source_target_pairs={{32,34},{33,35},{34,36},{35,37},{36,38},{37,39},{38,40},{39,41},{4... | collective-permute-start | bytes 786440 | tf_op jit(solution)/shard_map/ppermute | solution.py:36
  98.3 4.8 %collective-permute-start.9 = (bf16[512,256]{0,1:T(8,128)(2,1)S(1)}, bf16[512,256]{0,1:T(8,128)(2,1)S(1)}, u32[]{:S(2)}, u32[]{:S(2)}) collective-permute-start(bf16[512,256]{0,1:T(8,128)(2,1)S(1)} %multiply_convert_fusion.6), channel_id=1, source_target_pairs={{32,63},{33,32},{34,33},{35,34},{36,35},{37,36},{38,37},{39,38},{4... | collective-permute-start | bytes 786440 | tf_op jit(solution)/shard_map/ppermute | solution.py:36
  107.6 5.9 %collective-permute-done.8 = bf16[512,256]{0,1:T(8,128)(2,1)S(1)} collective-permute-done((bf16[512,256]{0,1:T(8,128)(2,1)S(1)}, bf16[512,256]{0,1:T(8,128)(2,1)S(1)}, u32[]{:S(2)}, u32[]{:S(2)}) %collective-permute-start.8) | collective-permute-done | bytes 262176 | tf_op jit(solution)/shard_map/ppermute | solution.py:36
  121.4 4.3 %collective-permute-start.14 = (bf16[512,256]{0,1:T(8,128)(2,1)S(1)}, bf16[512,256]{0,1:T(8,128)(2,1)S(1)}, u32[]{:S(2)}, u32[]{:S(2)}) collective-permute-start(bf16[512,256]{0,1:T(8,128)(2,1)S(1)} %multiply_convert_fusion.5), channel_id=1, source_target_pairs={{32,34},{33,35},{34,36},{35,37},{36,38},{37,39},{38,40},{39,41},{4... | collective-permute-start | bytes 786440 | tf_op jit(solution)/shard_map/ppermute | solution.py:36
  125.7 4.8 %collective-permute-start.13 = (bf16[512,256]{0,1:T(8,128)(2,1)S(1)}, bf16[512,256]{0,1:T(8,128)(2,1)S(1)}, u32[]{:S(2)}, u32[]{:S(2)}) collective-permute-start(bf16[512,256]{0,1:T(8,128)(2,1)S(1)} %multiply_convert_fusion.5), channel_id=1, source_target_pairs={{32,63},{33,32},{34,33},{35,34},{36,35},{37,36},{38,37},{39,38},{4... | collective-permute-start | bytes 786440 | tf_op jit(solution)/shard_map/ppermute | solution.py:36
  135.2 5.8 %collective-permute-done.12 = bf16[512,256]{0,1:T(8,128)(2,1)S(1)} collective-permute-done((bf16[512,256]{0,1:T(8,128)(2,1)S(1)}, bf16[512,256]{0,1:T(8,128)(2,1)S(1)}, u32[]{:S(2)}, u32[]{:S(2)}) %collective-permute-start.12) | collective-permute-done | bytes 262176 | tf_op jit(solution)/shard_map/ppermute | solution.py:36
  149.8 4.3 %collective-permute-start.18 = (bf16[512,256]{0,1:T(8,128)(2,1)S(1)}, bf16[512,256]{0,1:T(8,128)(2,1)S(1)}, u32[]{:S(2)}, u32[]{:S(2)}) collective-permute-start(bf16[512,256]{0,1:T(8,128)(2,1)S(1)} %multiply_convert_fusion.4), channel_id=1, source_target_pairs={{32,34},{33,35},{34,36},{35,37},{36,38},{37,39},{38,40},{39,41},{4... | collective-permute-start | bytes 786440 | tf_op jit(solution)/shard_map/ppermute | solution.py:36
  154.0 4.8 %collective-permute-start.17 = (bf16[512,256]{0,1:T(8,128)(2,1)S(1)}, bf16[512,256]{0,1:T(8,128)(2,1)S(1)}, u32[]{:S(2)}, u32[]{:S(2)}) collective-permute-start(bf16[512,256]{0,1:T(8,128)(2,1)S(1)} %multiply_convert_fusion.4), channel_id=1, source_target_pairs={{32,63},{33,32},{34,33},{35,34},{36,35},{37,36},{38,37},{39,38},{4... | collective-permute-start | bytes 786440 | tf_op jit(solution)/shard_map/ppermute | solution.py:36
  163.3 5.9 %collective-permute-done.16 = bf16[512,256]{0,1:T(8,128)(2,1)S(1)} collective-permute-done((bf16[512,256]{0,1:T(8,128)(2,1)S(1)}, bf16[512,256]{0,1:T(8,128)(2,1)S(1)}, u32[]{:S(2)}, u32[]{:S(2)}) %collective-permute-start.16) | collective-permute-done | bytes 262176 | tf_op jit(solution)/shard_map/ppermute | solution.py:36
  179.0 4.3 %collective-permute-start.22 = (bf16[512,256]{0,1:T(8,128)(2,1)S(1)}, bf16[512,256]{0,1:T(8,128)(2,1)S(1)}, u32[]{:S(2)}, u32[]{:S(2)}) collective-permute-start(bf16[512,256]{0,1:T(8,128)(2,1)S(1)} %multiply_convert_fusion.3), channel_id=1, source_target_pairs={{32,34},{33,35},{34,36},{35,37},{36,38},{37,39},{38,40},{39,41},{4... | collective-permute-start | bytes 786440 | tf_op jit(solution)/shard_map/ppermute | solution.py:36
  183.3 4.8 %collective-permute-start.21 = (bf16[512,256]{0,1:T(8,128)(2,1)S(1)}, bf16[512,256]{0,1:T(8,128)(2,1)S(1)}, u32[]{:S(2)}, u32[]{:S(2)}) collective-permute-start(bf16[512,256]{0,1:T(8,128)(2,1)S(1)} %multiply_convert_fusion.3), channel_id=1, source_target_pairs={{32,63},{33,32},{34,33},{35,34},{36,35},{37,36},{38,37},{39,38},{4... | collective-permute-start | bytes 786440 | tf_op jit(solution)/shard_map/ppermute | solution.py:36
  193.4 5.2 %collective-permute-done.20 = bf16[512,256]{0,1:T(8,128)(2,1)S(1)} collective-permute-done((bf16[512,256]{0,1:T(8,128)(2,1)S(1)}, bf16[512,256]{0,1:T(8,128)(2,1)S(1)}, u32[]{:S(2)}, u32[]{:S(2)}) %collective-permute-start.20) | collective-permute-done | bytes 262176 | tf_op jit(solution)/shard_map/ppermute | solution.py:36
  207.4 4.3 %collective-permute-start.26 = (bf16[512,256]{0,1:T(8,128)(2,1)S(1)}, bf16[512,256]{0,1:T(8,128)(2,1)S(1)}, u32[]{:S(2)}, u32[]{:S(2)}) collective-permute-start(bf16[512,256]{0,1:T(8,128)(2,1)S(1)} %multiply_convert_fusion.2), channel_id=1, source_target_pairs={{32,34},{33,35},{34,36},{35,37},{36,38},{37,39},{38,40},{39,41},{4... | collective-permute-start | bytes 786440 | tf_op jit(solution)/shard_map/ppermute | solution.py:36
  211.7 4.9 %collective-permute-start.25 = (bf16[512,256]{0,1:T(8,128)(2,1)S(1)}, bf16[512,256]{0,1:T(8,128)(2,1)}, u32[]{:S(2)}, u32[]{:S(2)}) collective-permute-start(bf16[512,256]{0,1:T(8,128)(2,1)S(1)} %multiply_convert_fusion.2), channel_id=1, source_target_pairs={{32,63},{33,32},{34,33},{35,34},{36,35},{37,36},{38,37},{39,38},{4... | collective-permute-start | bytes 786440 | tf_op jit(solution)/shard_map/ppermute | solution.py:36
  221.1 5.9 %collective-permute-done.24 = bf16[512,256]{0,1:T(8,128)(2,1)S(1)} collective-permute-done((bf16[512,256]{0,1:T(8,128)(2,1)S(1)}, bf16[512,256]{0,1:T(8,128)(2,1)S(1)}, u32[]{:S(2)}, u32[]{:S(2)}) %collective-permute-start.24) | collective-permute-done | bytes 262176 | tf_op jit(solution)/shard_map/ppermute | solution.py:36
  241.6 4.3 %collective-permute-start.30 = (bf16[512,256]{0,1:T(8,128)(2,1)S(1)}, bf16[512,256]{0,1:T(8,128)(2,1)S(1)}, u32[]{:S(2)}, u32[]{:S(2)}) collective-permute-start(bf16[512,256]{0,1:T(8,128)(2,1)S(1)} %get-tuple-element.6), channel_id=1, source_target_pairs={{32,34},{33,35},{34,36},{35,37},{36,38},{37,39},{38,40},{39,41},{4... | collective-permute-start | bytes 786440 | tf_op jit(solution)/shard_map/ppermute | solution.py:36
  245.9 4.8 %collective-permute-start.29 = (bf16[512,256]{0,1:T(8,128)(2,1)S(1)}, bf16[512,256]{0,1:T(8,128)(2,1)}, u32[]{:S(2)}, u32[]{:S(2)}) collective-permute-start(bf16[512,256]{0,1:T(8,128)(2,1)S(1)} %get-tuple-element.6), channel_id=1, source_target_pairs={{32,63},{33,32},{34,33},{35,34},{36,35},{37,36},{38,37},{39,38},{4... | collective-permute-start | bytes 786440 | tf_op jit(solution)/shard_map/ppermute | solution.py:36
  256.9 4.2 %collective-permute-done.28 = bf16[512,256]{0,1:T(8,128)(2,1)S(1)} collective-permute-done((bf16[512,256]{0,1:T(8,128)(2,1)S(1)}, bf16[512,256]{0,1:T(8,128)(2,1)S(1)}, u32[]{:S(2)}, u32[]{:S(2)}) %collective-permute-start.28) | collective-permute-done | bytes 262176 | tf_op jit(solution)/shard_map/ppermute | solution.py:36
  288.3 4.2 %collective-permute-done.35 = bf16[512,256]{0,1:T(8,128)(2,1)S(1)} collective-permute-done((bf16[512,256]{0,1:T(8,128)(2,1)S(1)}, bf16[512,256]{0,1:T(8,128)(2,1)S(1)}, u32[]{:S(2)}, u32[]{:S(2)}) %collective-permute-start.35) | collective-permute-done | bytes 262176 | tf_op jit(solution)/shard_map/ppermute | solution.py:98
  (169 shorter events, 157.4 us)
Async XLA Ops:
  6.5 48.8 %all-gather.3.cloned.1.call-start = ((), (), s32[]{:S(2)}) async-start(), calls=%async_computation | async-start | bytes 2359296 | tf_op jit(solution)/shard_map/all_gather | solution.py:23
  8.4 42.8 %collective-permute-start.3 = (bf16[512,256]{1,0:T(8,128)(2,1)S(1)}, bf16[512,256]{1,0:T(8,128)(2,1)}, u32[]{:S(2)}, u32[]{:S(2)}) collective-permute-start(bf16[512,256]{1,0:T(8,128)(2,1)S(1)} %dynamic-slice_bitcast_fusion), channel_id=1, source_target_pairs={{32,62},{33,63},{34,32},{35,33},{36,34},{37,35},{38,36},{39,37},{4... | collective-permute-start | bytes 786440 | tf_op jit(solution)/shard_map/ppermute | solution.py:36
  19.6 33.6 %collective-permute-start.2 = (bf16[512,256]{1,0:T(8,128)(2,1)S(1)}, bf16[512,256]{1,0:T(8,128)(2,1)}, u32[]{:S(2)}, u32[]{:S(2)}) collective-permute-start(bf16[512,256]{1,0:T(8,128)(2,1)S(1)} %dynamic-slice_bitcast_fusion), channel_id=1, source_target_pairs={{32,34},{33,35},{34,36},{35,37},{36,38},{37,39},{38,40},{39,41},{4... | collective-permute-start | bytes 786440 | tf_op jit(solution)/shard_map/ppermute | solution.py:36
  21.5 35.8 %collective-permute-start.1 = (bf16[512,256]{1,0:T(8,128)(2,1)S(1)}, bf16[512,256]{1,0:T(8,128)(2,1)S(1)}, u32[]{:S(2)}, u32[]{:S(2)}) collective-permute-start(bf16[512,256]{1,0:T(8,128)(2,1)S(1)} %dynamic-slice_bitcast_fusion), channel_id=1, source_target_pairs={{32,63},{33,32},{34,33},{35,34},{36,35},{37,36},{38,37},{39,38},{4... | collective-permute-start | bytes 786440 | tf_op jit(solution)/shard_map/ppermute | solution.py:36
  28.7 21.2 %collective-permute-start = (bf16[512,256]{1,0:T(8,128)(2,1)S(1)}, bf16[512,256]{1,0:T(8,128)(2,1)S(1)}, u32[]{:S(2)}, u32[]{:S(2)}) collective-permute-start(bf16[512,256]{1,0:T(8,128)(2,1)S(1)} %dynamic-slice_bitcast_fusion), channel_id=1, source_target_pairs={{32,33},{33,34},{34,35},{35,36},{36,37},{37,38},{38,39},{39,40},{4... | collective-permute-start | bytes 786440 | tf_op jit(solution)/shard_map/ppermute | solution.py:36
  59.5 28.0 %collective-permute-start.7 = (bf16[512,256]{0,1:T(8,128)(2,1)S(1)}, bf16[512,256]{0,1:T(8,128)(2,1)S(1)}, u32[]{:S(2)}, u32[]{:S(2)}) collective-permute-start(bf16[512,256]{0,1:T(8,128)(2,1)S(1)} %multiply_convert_fusion.7), channel_id=1, source_target_pairs={{32,62},{33,63},{34,32},{35,33},{36,34},{37,35},{38,36},{39,37},{4... | collective-permute-start | bytes 786440 | tf_op jit(solution)/shard_map/ppermute | solution.py:36
  63.4 25.6 %collective-permute-start.6 = (bf16[512,256]{0,1:T(8,128)(2,1)S(1)}, bf16[512,256]{0,1:T(8,128)(2,1)S(1)}, u32[]{:S(2)}, u32[]{:S(2)}) collective-permute-start(bf16[512,256]{0,1:T(8,128)(2,1)S(1)} %multiply_convert_fusion.7), channel_id=1, source_target_pairs={{32,34},{33,35},{34,36},{35,37},{36,38},{37,39},{38,40},{39,41},{4... | collective-permute-start | bytes 786440 | tf_op jit(solution)/shard_map/ppermute | solution.py:36
  65.7 24.6 %collective-permute-start.5 = (bf16[512,256]{0,1:T(8,128)(2,1)S(1)}, bf16[512,256]{0,1:T(8,128)(2,1)S(1)}, u32[]{:S(2)}, u32[]{:S(2)}) collective-permute-start(bf16[512,256]{0,1:T(8,128)(2,1)S(1)} %multiply_convert_fusion.7), channel_id=1, source_target_pairs={{32,63},{33,32},{34,33},{35,34},{36,35},{37,36},{38,37},{39,38},{4... | collective-permute-start | bytes 786440 | tf_op jit(solution)/shard_map/ppermute | solution.py:36
  92.1 22.8 %collective-permute-start.11 = (bf16[512,256]{0,1:T(8,128)(2,1)S(1)}, bf16[512,256]{0,1:T(8,128)(2,1)S(1)}, u32[]{:S(2)}, u32[]{:S(2)}) collective-permute-start(bf16[512,256]{0,1:T(8,128)(2,1)S(1)} %multiply_convert_fusion.6), channel_id=1, source_target_pairs={{32,62},{33,63},{34,32},{35,33},{36,34},{37,35},{38,36},{39,37},{4... | collective-permute-start | bytes 786440 | tf_op jit(solution)/shard_map/ppermute | solution.py:36
  94.0 22.3 %collective-permute-start.10 = (bf16[512,256]{0,1:T(8,128)(2,1)S(1)}, bf16[512,256]{0,1:T(8,128)(2,1)S(1)}, u32[]{:S(2)}, u32[]{:S(2)}) collective-permute-start(bf16[512,256]{0,1:T(8,128)(2,1)S(1)} %multiply_convert_fusion.6), channel_id=1, source_target_pairs={{32,34},{33,35},{34,36},{35,37},{36,38},{37,39},{38,40},{39,41},{4... | collective-permute-start | bytes 786440 | tf_op jit(solution)/shard_map/ppermute | solution.py:36
  119.5 22.8 %collective-permute-start.15 = (bf16[512,256]{0,1:T(8,128)(2,1)S(1)}, bf16[512,256]{0,1:T(8,128)(2,1)S(1)}, u32[]{:S(2)}, u32[]{:S(2)}) collective-permute-start(bf16[512,256]{0,1:T(8,128)(2,1)S(1)} %multiply_convert_fusion.5), channel_id=1, source_target_pairs={{32,62},{33,63},{34,32},{35,33},{36,34},{37,35},{38,36},{39,37},{4... | collective-permute-start | bytes 786440 | tf_op jit(solution)/shard_map/ppermute | solution.py:36
  121.4 22.3 %collective-permute-start.14 = (bf16[512,256]{0,1:T(8,128)(2,1)S(1)}, bf16[512,256]{0,1:T(8,128)(2,1)S(1)}, u32[]{:S(2)}, u32[]{:S(2)}) collective-permute-start(bf16[512,256]{0,1:T(8,128)(2,1)S(1)} %multiply_convert_fusion.5), channel_id=1, source_target_pairs={{32,34},{33,35},{34,36},{35,37},{36,38},{37,39},{38,40},{39,41},{4... | collective-permute-start | bytes 786440 | tf_op jit(solution)/shard_map/ppermute | solution.py:36
  147.8 22.8 %collective-permute-start.19 = (bf16[512,256]{0,1:T(8,128)(2,1)S(1)}, bf16[512,256]{0,1:T(8,128)(2,1)S(1)}, u32[]{:S(2)}, u32[]{:S(2)}) collective-permute-start(bf16[512,256]{0,1:T(8,128)(2,1)S(1)} %multiply_convert_fusion.4), channel_id=1, source_target_pairs={{32,62},{33,63},{34,32},{35,33},{36,34},{37,35},{38,36},{39,37},{4... | collective-permute-start | bytes 786440 | tf_op jit(solution)/shard_map/ppermute | solution.py:36
  149.8 23.1 %collective-permute-start.18 = (bf16[512,256]{0,1:T(8,128)(2,1)S(1)}, bf16[512,256]{0,1:T(8,128)(2,1)S(1)}, u32[]{:S(2)}, u32[]{:S(2)}) collective-permute-start(bf16[512,256]{0,1:T(8,128)(2,1)S(1)} %multiply_convert_fusion.4), channel_id=1, source_target_pairs={{32,34},{33,35},{34,36},{35,37},{36,38},{37,39},{38,40},{39,41},{4... | collective-permute-start | bytes 786440 | tf_op jit(solution)/shard_map/ppermute | solution.py:36
  177.1 22.8 %collective-permute-start.23 = (bf16[512,256]{0,1:T(8,128)(2,1)S(1)}, bf16[512,256]{0,1:T(8,128)(2,1)S(1)}, u32[]{:S(2)}, u32[]{:S(2)}) collective-permute-start(bf16[512,256]{0,1:T(8,128)(2,1)S(1)} %multiply_convert_fusion.3), channel_id=1, source_target_pairs={{32,62},{33,63},{34,32},{35,33},{36,34},{37,35},{38,36},{39,37},{4... | collective-permute-start | bytes 786440 | tf_op jit(solution)/shard_map/ppermute | solution.py:36
  179.0 23.2 %collective-permute-start.22 = (bf16[512,256]{0,1:T(8,128)(2,1)S(1)}, bf16[512,256]{0,1:T(8,128)(2,1)S(1)}, u32[]{:S(2)}, u32[]{:S(2)}) collective-permute-start(bf16[512,256]{0,1:T(8,128)(2,1)S(1)} %multiply_convert_fusion.3), channel_id=1, source_target_pairs={{32,34},{33,35},{34,36},{35,37},{36,38},{37,39},{38,40},{39,41},{4... | collective-permute-start | bytes 786440 | tf_op jit(solution)/shard_map/ppermute | solution.py:36
  205.5 22.9 %collective-permute-start.27 = (bf16[512,256]{0,1:T(8,128)(2,1)S(1)}, bf16[512,256]{0,1:T(8,128)(2,1)S(1)}, u32[]{:S(2)}, u32[]{:S(2)}) collective-permute-start(bf16[512,256]{0,1:T(8,128)(2,1)S(1)} %multiply_convert_fusion.2), channel_id=1, source_target_pairs={{32,62},{33,63},{34,32},{35,33},{36,34},{37,35},{38,36},{39,37},{4... | collective-permute-start | bytes 786440 | tf_op jit(solution)/shard_map/ppermute | solution.py:36
  207.4 22.4 %collective-permute-start.26 = (bf16[512,256]{0,1:T(8,128)(2,1)S(1)}, bf16[512,256]{0,1:T(8,128)(2,1)S(1)}, u32[]{:S(2)}, u32[]{:S(2)}) collective-permute-start(bf16[512,256]{0,1:T(8,128)(2,1)S(1)} %multiply_convert_fusion.2), channel_id=1, source_target_pairs={{32,34},{33,35},{34,36},{35,37},{36,38},{37,39},{38,40},{39,41},{4... | collective-permute-start | bytes 786440 | tf_op jit(solution)/shard_map/ppermute | solution.py:36
  239.7 24.5 %collective-permute-start.31 = (bf16[512,256]{0,1:T(8,128)(2,1)S(1)}, bf16[512,256]{0,1:T(8,128)(2,1)S(1)}, u32[]{:S(2)}, u32[]{:S(2)}) collective-permute-start(bf16[512,256]{0,1:T(8,128)(2,1)S(1)} %get-tuple-element.6), channel_id=1, source_target_pairs={{32,62},{33,63},{34,32},{35,33},{36,34},{37,35},{38,36},{39,37},{4... | collective-permute-start | bytes 786440 | tf_op jit(solution)/shard_map/ppermute | solution.py:36
  241.6 25.8 %collective-permute-start.30 = (bf16[512,256]{0,1:T(8,128)(2,1)S(1)}, bf16[512,256]{0,1:T(8,128)(2,1)S(1)}, u32[]{:S(2)}, u32[]{:S(2)}) collective-permute-start(bf16[512,256]{0,1:T(8,128)(2,1)S(1)} %get-tuple-element.6), channel_id=1, source_target_pairs={{32,34},{33,35},{34,36},{35,37},{36,38},{37,39},{38,40},{39,41},{4... | collective-permute-start | bytes 786440 | tf_op jit(solution)/shard_map/ppermute | solution.py:36
  245.9 24.7 %collective-permute-start.29 = (bf16[512,256]{0,1:T(8,128)(2,1)S(1)}, bf16[512,256]{0,1:T(8,128)(2,1)}, u32[]{:S(2)}, u32[]{:S(2)}) collective-permute-start(bf16[512,256]{0,1:T(8,128)(2,1)S(1)} %get-tuple-element.6), channel_id=1, source_target_pairs={{32,63},{33,32},{34,33},{35,34},{36,35},{37,36},{38,37},{39,38},{4... | collective-permute-start | bytes 786440 | tf_op jit(solution)/shard_map/ppermute | solution.py:36
  254.6 37.9 %collective-permute-start.36 = (bf16[512,256]{0,1:T(8,128)(2,1)S(1)}, bf16[512,256]{0,1:T(8,128)(2,1)}, u32[]{:S(2)}, u32[]{:S(2)}) collective-permute-start(bf16[512,256]{0,1:T(8,128)(2,1)S(1)} %get-tuple-element.13), channel_id=1, source_target_pairs={{32,192},{96,0},{160,64},{224,128},{33,193},{97,1},{161,65},{225,1... | collective-permute-start | bytes 786440 | tf_op jit(solution)/shard_map/ppermute | solution.py:98
  261.1 26.2 %collective-permute-start.34 = (bf16[512,256]{0,1:T(8,128)(2,1)}, bf16[512,256]{0,1:T(8,128)(2,1)}, u32[]{:S(2)}, u32[]{:S(2)}) collective-permute-start(bf16[512,256]{0,1:T(8,128)(2,1)} %get-tuple-element.14), channel_id=1, source_target_pairs={{32,128},{96,192},{160,0},{224,64},{33,129},{97,193},{161,1},{225,... | collective-permute-start | bytes 786440 | tf_op jit(solution)/shard_map/ppermute | solution.py:98
  267.4 26.1 %collective-permute-start.38 = (bf16[512,256]{0,1:T(8,128)(2,1)}, bf16[512,256]{0,1:T(8,128)(2,1)}, u32[]{:S(2)}, u32[]{:S(2)}) collective-permute-start(bf16[512,256]{0,1:T(8,128)(2,1)} %get-tuple-element.5), channel_id=1, source_target_pairs={{32,0},{96,64},{160,128},{224,192},{33,1},{97,65},{161,129},{225,1... | collective-permute-start | bytes 786440 | tf_op jit(solution)/shard_map/ppermute | solution.py:98
  (28 other events, 421.1 us)
Sparse Core Ops, SparseCore 0:
  9.2 31.9 all-gather.2

commit v4 on v2

--- a/solution.py
+++ b/solution.py
@@ -1,9 +1,70 @@
 import jax
 import jax.numpy as jnp
 from jax import lax
+from jax.experimental import pallas as pl
+from jax.experimental.pallas import tpu as pltpu
 from jax.sharding import PartitionSpec as P
 
 REACH = 2
+
+
+def _band_kernel(rows_ref, cols_ref, count_ref, values_ref, band_ref):
+    block = values_ref.shape[1]
+    band_ref[...] = jnp.zeros(band_ref.shape, band_ref.dtype)
+
+    def place(k, carry):
+        r = pl.multiple_of(rows_ref[k] * block, block)
+        c = pl.multiple_of(cols_ref[k] * block, block)
+        band_ref[pl.ds(r, block), pl.ds(c, block)] = values_ref[k]
+        return carry
+
+    lax.fori_loop(0, count_ref[0], place, 0)
+
+
+def build_band(row_local, column_local, count, values, rows_dev, band_cols):
+    return pl.pallas_call(
+        _band_kernel,
+        out_shape=jax.ShapeDtypeStruct((rows_dev, band_cols), values.dtype),
+        in_specs=[pl.BlockSpec(memory_space=pltpu.SMEM)] * 3
+        + [pl.BlockSpec(memory_space=pltpu.VMEM)],
+        out_specs=pl.BlockSpec(memory_space=pltpu.VMEM),
+    )(row_local, column_local, count, values)
+
+
+def _layer_kernel(band_ref, p0, p1, p2, p3, p4, degree_ref, ws_ref, wn_ref, out_ref):
+    rows = p2.shape[0]
+    parts = (p0, p1, p2, p3, p4)
+    summed = jnp.dot(
+        band_ref[:, pl.ds(2 * rows, rows)], p2[...], preferred_element_type=jnp.float32
+    )
+    for position in (1, 3, 0, 4):
+        summed = summed + jnp.dot(
+            band_ref[:, pl.ds(position * rows, rows)],
+            parts[position][...],
+            preferred_element_type=jnp.float32,
+        )
+    neighbour_mean = (summed / degree_ref[...]).astype(jnp.bfloat16)
+    combined = jnp.dot(p2[...], ws_ref[...], preferred_element_type=jnp.float32) + jnp.dot(
+        neighbour_mean, wn_ref[...], preferred_element_type=jnp.float32
+    )
+    active = jnp.maximum(combined, 0.0)
+    scale = lax.rsqrt(jnp.mean(active * active, axis=-1, keepdims=True) + 1e-05)
+    out_ref[...] = (active * scale).astype(out_ref.dtype)
+
+
+def run_layer(band, parts, degree_f, ws, wn):
+    rows, width = parts[2].shape
+    return pl.pallas_call(
+        _layer_kernel,
+        out_shape=jax.ShapeDtypeStruct((rows, width), jnp.bfloat16),
+        in_specs=[pl.BlockSpec(memory_space=pltpu.VMEM)] * 9,
+        out_specs=pl.BlockSpec(memory_space=pltpu.VMEM),
+        cost_estimate=pl.CostEstimate(
+            flops=2 * rows * band.shape[1] * width + 4 * rows * width * width,
+            bytes_accessed=band.size * 2 + 6 * rows * width * 2,
+            transcendentals=rows,
+        ),
+    )(band, *parts, degree_f, ws, wn)
 
 
 def body(
@@ -46,21 +107,13 @@
     shifted = jnp.mod(column_dev - blk_index + REACH, blk_count)
     column_local = shifted * blocks_dev + jnp.mod(cols, blocks_dev)
     row_local = rows - blk_index * blocks_dev
-    alive = jnp.arange(slot_total, dtype=jnp.int32) < count
-    target = row_local * band_width + column_local
-    placing = (
-        (target[None, :] == jnp.arange(blocks_dev * band_width, dtype=jnp.int32)[:, None])
-        & alive[None, :]
-    ).astype(jnp.bfloat16)
-    slab = jnp.dot(
-        placing,
-        values.reshape(slot_total, block_size * block_size),
-        preferred_element_type=jnp.float32,
-    ).astype(jnp.bfloat16)
-    band = (
-        slab.reshape(blocks_dev, band_width, block_size, block_size)
-        .transpose(0, 2, 1, 3)
-        .reshape(rows_dev, window_span, rows_dev)
+    band = build_band(
+        jnp.clip(row_local, 0, blocks_dev - 1),
+        jnp.clip(column_local, 0, band_width - 1),
+        jnp.clip(count, 0, slot_total).reshape(1),
+        values,
+        rows_dev,
+        band_width * block_size,
     )
     degree_f = degree.astype(jnp.float32)[:, None]
 
@@ -71,18 +124,7 @@
         up2 = halo(up1, 1)
         down2 = halo(down1, -1)
         parts = [up2, up1, hidden, down1, down2]
-        summed = jnp.dot(band[:, REACH, :], hidden, preferred_element_type=jnp.float32)
-        for position in (REACH - 1, REACH + 1, REACH - 2, REACH + 2):
-            summed = summed + jnp.dot(
-                band[:, position, :], parts[position], preferred_element_type=jnp.float32
-            )
-        neighbour_mean = (summed / degree_f).astype(jnp.bfloat16)
-        combined = jnp.dot(hidden, self_all[level], preferred_element_type=jnp.float32) + jnp.dot(
-            neighbour_mean, neighbour_all[level], preferred_element_type=jnp.float32
-        )
-        active = jnp.maximum(combined, 0.0)
-        scale = lax.rsqrt(jnp.mean(active * active, axis=-1, keepdims=True) + 1e-05)
-        hidden = (active * scale).astype(jnp.bfloat16)
+        hidden = run_layer(band, parts, degree_f, self_all[level], neighbour_all[level])
         outputs.append(hidden)
 
     arrived = []

time: 286 us -> 285 us (level)
  matrix products: 68 us -> 0 us
  Pallas kernels: 0 us -> 37.6 us
  starting transfers between devices: 130 us -> 164 us
  local copies, waits for them, and re-layouts: 20.1 us -> 17.1 us
    dot_general x49 -> x0, matrix products: 68 us -> none  [the longest x24 30.3 us: body(): jnp.dot(band[:, position, :], parts[position], preferred_element_type=jnp...]
    pallas_call x0 -> x9, Pallas kernels: none -> 37.6 us  [the longest x8 34.1 us: run_layer(): pl.pallas_call(_layer_kernel, out_shape=jax.ShapeDtypeStruct((rows, width...]
    ppermute x32, starting transfers between devices: 112 us -> 145 us  [halo(): return lax.ppermute(x, ('section', 'blk'), pairs)]
    reshape x2 -> x0, local copies, waits for them, and re-layouts: 9.07 us -> none  [the longest x1 5.31 us: body(): slab.reshape(blocks_dev, band_width, block_size, block_size)]
    squeeze x0 -> x2, local copies, waits for them, and re-layouts: none -> 6.57 us  [the longest x1 3.57 us: body(): values = lax.dynamic_index_in_dim(tile_values, batch, 0, keepdims=False)]
    ppermute x32, waiting for transfers between devices: 33.9 us -> 39 us  [halo(): return lax.ppermute(x, ('section', 'blk'), pairs)]
    select_n x4 -> x2, other arithmetic: 6.85 us -> 2.12 us  [body(): sending = jnp.where(section_index == w, outputs[level], sending)]
    dynamic_slice x2 -> x0, local copies, waits for them, and re-layouts: 3.39 us -> none  [the longest x1 2.14 us: body(): values = lax.dynamic_index_in_dim(tile_values, batch, 0, keepdims=False)]
  transfers between devices with their start and end apart: 40 -> 40, of which waited for: 10 -> 21; matrix products, arithmetic and copies ran while one was open for 27% -> 6% of each run, Pallas kernels for 0% -> 3%
where the time goes in v4:
time: 285 us; the launch traced here: 284 us
  starting transfers between devices  164 us (58%)
  waiting for transfers between devices  40.7 us (14%)
  Pallas kernels  37.6 us (13%)
  local copies, waits for them, and re-layouts  17.1 us (6%)
  between operations  14.9 us (5%)
  other arithmetic  9.7 us (3%)
    ppermute x32, starting transfers between devices, halo(): return lax.ppermute(x, ('section', 'blk'), pairs)  145 us
    ppermute x32, waiting for transfers between devices, halo(): return lax.ppermute(x, ('section', 'blk'), pairs)  39 us
    pallas_call x8, Pallas kernels, run_layer(): pl.pallas_call(_layer_kernel, out_shape=jax.ShapeDtypeStruct((rows, width...  34.1 us
    ppermute x7, starting transfers between devices, body(): arrived.append(lax.ppermute(sending, 'section', pairs))  19 us
    unnamed x86, local copies, waits for them, and re-layouts  8.63 us
  transfers between devices with their start and end apart: 40, of which 21 were waited for; matrix products, arithmetic and copies ran while one was open for 6% of the time, Pallas kernels for 3%

profile of v4, /device:TPU:1, one launch (start us, length us, event | category | flops | bytes accessed | tf_op | source)
XLA Modules:
  0.0 283.5 jit_solution(17248172743345944946)
XLA Ops:
  8.4 4.4 %collective-permute-start = (bf16[512,256]{1,0:T(8,128)(2,1)S(1)}, bf16[512,256]{1,0:T(8,128)(2,1)S(1)}, u32[]{:S(2)}, u32[]{:S(2)}) collective-permute-start(bf16[512,256]{1,0:T(8,128)(2,1)S(1)} %dynamic-slice_bitcast_fusion.1.p2), channel_id=1, source_target_pairs={{32,33},{33,34},{34,35},{35,36},{36,37},{37,38},{38,39},{39,40},{4... | collective-permute-start | bytes 786440 | tf_op jit(solution)/shard_map/ppermute | solution.py:97
  12.8 8.3 %collective-permute-start.2 = (bf16[512,256]{1,0:T(8,128)(2,1)S(1)}, bf16[512,256]{1,0:T(8,128)(2,1)S(1)}, u32[]{:S(2)}, u32[]{:S(2)}) collective-permute-start(bf16[512,256]{1,0:T(8,128)(2,1)S(1)} %dynamic-slice_bitcast_fusion.1.p2), channel_id=1, source_target_pairs={{32,63},{33,32},{34,33},{35,34},{36,35},{37,36},{38,37},{39,38},{4... | collective-permute-start | bytes 786440 | tf_op jit(solution)/shard_map/ppermute | solution.py:97
  36.3 6.7 %collective-permute-start.3 = (bf16[512,256]{1,0:T(8,128)(2,1)S(1)}, bf16[512,256]{1,0:T(8,128)(2,1)S(1)}, u32[]{:S(2)}, u32[]{:S(2)}) collective-permute-start(bf16[512,256]{1,0:T(8,128)(2,1)S(1)} %collective-permute-done.2.p3), channel_id=1, source_target_pairs={{32,63},{33,32},{34,33},{35,34},{36,35},{37,36},{38,37},{39,38},{4... | collective-permute-start | bytes 786440 | tf_op jit(solution)/shard_map/ppermute | solution.py:97
  53.1 7.1 %collective-permute-start.6 = (bf16[512,256]{1,0:T(8,128)(2,1)}, bf16[512,256]{1,0:T(8,128)(2,1)S(1)}, u32[]{:S(2)}, u32[]{:S(2)}) collective-permute-start(bf16[512,256]{1,0:T(8,128)(2,1)} %shard_map.83.p2), channel_id=1, source_target_pairs={{32,63},{33,32},{34,33},{35,34},{36,35},{37,36},{38,37},{39,38},{4... | collective-permute-start | bytes 786440 | tf_op jit(solution)/shard_map/ppermute | solution.py:97
  64.2 6.7 %collective-permute-start.7 = (bf16[512,256]{1,0:T(8,128)(2,1)S(1)}, bf16[512,256]{1,0:T(8,128)(2,1)S(1)}, u32[]{:S(2)}, u32[]{:S(2)}) collective-permute-start(bf16[512,256]{1,0:T(8,128)(2,1)S(1)} %collective-permute-done.6.p3), channel_id=1, source_target_pairs={{32,63},{33,32},{34,33},{35,34},{36,35},{37,36},{38,37},{39,38},{4... | collective-permute-start | bytes 786440 | tf_op jit(solution)/shard_map/ppermute | solution.py:97
  79.1 7.1 %collective-permute-start.10 = (bf16[512,256]{1,0:T(8,128)(2,1)}, bf16[512,256]{1,0:T(8,128)(2,1)S(1)}, u32[]{:S(2)}, u32[]{:S(2)}) collective-permute-start(bf16[512,256]{1,0:T(8,128)(2,1)} %shard_map.84.p2), channel_id=1, source_target_pairs={{32,63},{33,32},{34,33},{35,34},{36,35},{37,36},{38,37},{39,38},{4... | collective-permute-start | bytes 786440 | tf_op jit(solution)/shard_map/ppermute | solution.py:97
  89.9 7.0 %collective-permute-start.11 = (bf16[512,256]{1,0:T(8,128)(2,1)S(1)}, bf16[512,256]{1,0:T(8,128)(2,1)S(1)}, u32[]{:S(2)}, u32[]{:S(2)}) collective-permute-start(bf16[512,256]{1,0:T(8,128)(2,1)S(1)} %collective-permute-done.10.p3), channel_id=1, source_target_pairs={{32,63},{33,32},{34,33},{35,34},{36,35},{37,36},{38,37},{39,38},{4... | collective-permute-start | bytes 786440 | tf_op jit(solution)/shard_map/ppermute | solution.py:97
  100.2 7.2 %collective-permute-done.9.p0 = bf16[512,256]{1,0:T(8,128)(2,1)S(1)} collective-permute-done((bf16[512,256]{1,0:T(8,128)(2,1)S(1)}, bf16[512,256]{1,0:T(8,128)(2,1)S(1)}, u32[]{:S(2)}, u32[]{:S(2)}) %collective-permute-start.9) | collective-permute-done | bytes 262176 | tf_op jit(solution)/shard_map/ppermute | solution.py:97
  108.1 4.2 %shard_map.85.p2 = bf16[512,256]{1,0:T(8,128)(2,1)} custom-call(bf16[512,2560]{1,0:T(8,128)(2,1)} %shard_map.82.band_ref, bf16[512,256]{1,0:T(8,128)(2,1)} %copy-done.35, bf16[512,256]{1,0:T(8,128)(2,1)} %copy-done.23, bf16[512,256]{1,0:T(8,128)(2,1)} %shard_map.84.p2, bf16[512,256]{1,0:T(8,128)(2,1)} %copy-done.17, bf16[512,256]{1,0:T(8,128)(2,1)} %copy-done.29, ...), custom_call_target="tpu_custom_call" | custom-call | flops 805306368 | bytes 4194304 | tf_op jit(solution)/shard_map/pallas_call | solution.py:57
  114.2 6.7 %collective-permute-start.14 = (bf16[512,256]{1,0:T(8,128)(2,1)}, bf16[512,256]{1,0:T(8,128)(2,1)S(1)}, u32[]{:S(2)}, u32[]{:S(2)}) collective-permute-start(bf16[512,256]{1,0:T(8,128)(2,1)} %shard_map.85.p2), channel_id=1, source_target_pairs={{32,63},{33,32},{34,33},{35,34},{36,35},{37,36},{38,37},{39,38},{4... | collective-permute-start | bytes 786440 | tf_op jit(solution)/shard_map/ppermute | solution.py:97
  124.9 6.7 %collective-permute-start.15 = (bf16[512,256]{1,0:T(8,128)(2,1)S(1)}, bf16[512,256]{1,0:T(8,128)(2,1)S(1)}, u32[]{:S(2)}, u32[]{:S(2)}) collective-permute-start(bf16[512,256]{1,0:T(8,128)(2,1)S(1)} %collective-permute-done.14.p3), channel_id=1, source_target_pairs={{32,63},{33,32},{34,33},{35,34},{36,35},{37,36},{38,37},{39,38},{4... | collective-permute-start | bytes 786440 | tf_op jit(solution)/shard_map/ppermute | solution.py:97
  135.6 4.3 %shard_map.86.p2 = bf16[512,256]{1,0:T(8,128)(2,1)} custom-call(bf16[512,2560]{1,0:T(8,128)(2,1)} %shard_map.82.band_ref, bf16[512,256]{1,0:T(8,128)(2,1)} %copy-done.30, bf16[512,256]{1,0:T(8,128)(2,1)} %copy-done.18, bf16[512,256]{1,0:T(8,128)(2,1)} %shard_map.85.p2, bf16[512,256]{1,0:T(8,128)(2,1)} %copy-done.24, bf16[512,256]{1,0:T(8,128)(2,1)} %copy-done.36, ...), custom_call_target="tpu_custom_call" | custom-call | flops 805306368 | bytes 4194304 | tf_op jit(solution)/shard_map/pallas_call | solution.py:57
  141.8 7.1 %collective-permute-start.18 = (bf16[512,256]{1,0:T(8,128)(2,1)}, bf16[512,256]{1,0:T(8,128)(2,1)S(1)}, u32[]{:S(2)}, u32[]{:S(2)}) collective-permute-start(bf16[512,256]{1,0:T(8,128)(2,1)} %shard_map.86.p2), channel_id=1, source_target_pairs={{32,63},{33,32},{34,33},{35,34},{36,35},{37,36},{38,37},{39,38},{4... | collective-permute-start | bytes 786440 | tf_op jit(solution)/shard_map/ppermute | solution.py:97
  152.9 6.7 %collective-permute-start.19 = (bf16[512,256]{1,0:T(8,128)(2,1)S(1)}, bf16[512,256]{1,0:T(8,128)(2,1)S(1)}, u32[]{:S(2)}, u32[]{:S(2)}) collective-permute-start(bf16[512,256]{1,0:T(8,128)(2,1)S(1)} %collective-permute-done.18.p3), channel_id=1, source_target_pairs={{32,63},{33,32},{34,33},{35,34},{36,35},{37,36},{38,37},{39,38},{4... | collective-permute-start | bytes 786440 | tf_op jit(solution)/shard_map/ppermute | solution.py:97
  169.7 7.1 %collective-permute-start.22 = (bf16[512,256]{1,0:T(8,128)(2,1)}, bf16[512,256]{1,0:T(8,128)(2,1)S(1)}, u32[]{:S(2)}, u32[]{:S(2)}) collective-permute-start(bf16[512,256]{1,0:T(8,128)(2,1)} %shard_map.87.p2), channel_id=1, source_target_pairs={{32,63},{33,32},{34,33},{35,34},{36,35},{37,36},{38,37},{39,38},{4... | collective-permute-start | bytes 786440 | tf_op jit(solution)/shard_map/ppermute | solution.py:97
  180.8 6.7 %collective-permute-start.23 = (bf16[512,256]{1,0:T(8,128)(2,1)S(1)}, bf16[512,256]{1,0:T(8,128)(2,1)S(1)}, u32[]{:S(2)}, u32[]{:S(2)}) collective-permute-start(bf16[512,256]{1,0:T(8,128)(2,1)S(1)} %collective-permute-done.22.p3), channel_id=1, source_target_pairs={{32,63},{33,32},{34,33},{35,34},{36,35},{37,36},{38,37},{39,38},{4... | collective-permute-start | bytes 786440 | tf_op jit(solution)/shard_map/ppermute | solution.py:97
  191.5 4.2 %shard_map.88.p2 = bf16[512,256]{1,0:T(8,128)(2,1)} custom-call(bf16[512,2560]{1,0:T(8,128)(2,1)} %shard_map.82.band_ref, bf16[512,256]{1,0:T(8,128)(2,1)} %copy-done.32, bf16[512,256]{1,0:T(8,128)(2,1)} %copy-done.20, bf16[512,256]{1,0:T(8,128)(2,1)} %shard_map.87.p2, bf16[512,256]{1,0:T(8,128)(2,1)} %copy-done.26, bf16[512,256]{1,0:T(8,128)(2,1)} %copy-done.38, ...), custom_call_target="tpu_custom_call" | custom-call | flops 805306368 | bytes 4194304 | tf_op jit(solution)/shard_map/pallas_call | solution.py:57
  197.6 7.1 %collective-permute-start.26 = (bf16[512,256]{1,0:T(8,128)(2,1)}, bf16[512,256]{1,0:T(8,128)(2,1)S(1)}, u32[]{:S(2)}, u32[]{:S(2)}) collective-permute-start(bf16[512,256]{1,0:T(8,128)(2,1)} %shard_map.88.p2), channel_id=1, source_target_pairs={{32,63},{33,32},{34,33},{35,34},{36,35},{37,36},{38,37},{39,38},{4... | collective-permute-start | bytes 786440 | tf_op jit(solution)/shard_map/ppermute | solution.py:97
  208.7 6.7 %collective-permute-start.27 = (bf16[512,256]{1,0:T(8,128)(2,1)S(1)}, bf16[512,256]{1,0:T(8,128)(2,1)S(1)}, u32[]{:S(2)}, u32[]{:S(2)}) collective-permute-start(bf16[512,256]{1,0:T(8,128)(2,1)S(1)} %collective-permute-done.26.p3), channel_id=1, source_target_pairs={{32,63},{33,32},{34,33},{35,34},{36,35},{37,36},{38,37},{39,38},{4... | collective-permute-start | bytes 786440 | tf_op jit(solution)/shard_map/ppermute | solution.py:97
  219.4 4.3 %shard_map.89.p2 = bf16[512,256]{1,0:T(8,128)(2,1)} custom-call(bf16[512,2560]{1,0:T(8,128)(2,1)} %shard_map.82.band_ref, bf16[512,256]{1,0:T(8,128)(2,1)} %copy-done.33, bf16[512,256]{1,0:T(8,128)(2,1)} %copy-done.21, bf16[512,256]{1,0:T(8,128)(2,1)} %shard_map.88.p2, bf16[512,256]{1,0:T(8,128)(2,1)} %copy-done.27, bf16[512,256]{1,0:T(8,128)(2,1)} %copy-done.39, ...), custom_call_target="tpu_custom_call" | custom-call | flops 805306368 | bytes 4194304 | tf_op jit(solution)/shard_map/pallas_call | solution.py:57
  225.7 7.1 %collective-permute-start.30 = (bf16[512,256]{1,0:T(8,128)(2,1)}, bf16[512,256]{1,0:T(8,128)(2,1)S(1)}, u32[]{:S(2)}, u32[]{:S(2)}) collective-permute-start(bf16[512,256]{1,0:T(8,128)(2,1)} %shard_map.89.p2), channel_id=1, source_target_pairs={{32,63},{33,32},{34,33},{35,34},{36,35},{37,36},{38,37},{39,38},{4... | collective-permute-start | bytes 786440 | tf_op jit(solution)/shard_map/ppermute | solution.py:97
  236.8 6.7 %collective-permute-start.31 = (bf16[512,256]{1,0:T(8,128)(2,1)S(1)}, bf16[512,256]{1,0:T(8,128)(2,1)S(1)}, u32[]{:S(2)}, u32[]{:S(2)}) collective-permute-start(bf16[512,256]{1,0:T(8,128)(2,1)S(1)} %collective-permute-done.30.p3), channel_id=1, source_target_pairs={{32,63},{33,32},{34,33},{35,34},{36,35},{37,36},{38,37},{39,38},{4... | collective-permute-start | bytes 786440 | tf_op jit(solution)/shard_map/ppermute | solution.py:97
  253.3 4.3 %shard_map.90 = bf16[512,256]{1,0:T(8,128)(2,1)} custom-call(bf16[512,2560]{1,0:T(8,128)(2,1)} %shard_map.82.band_ref, bf16[512,256]{1,0:T(8,128)(2,1)} %copy-done.12, bf16[512,256]{1,0:T(8,128)(2,1)} %copy-done.8, bf16[512,256]{1,0:T(8,128)(2,1)} %shard_map.89.p2, bf16[512,256]{1,0:T(8,128)(2,1)} %copy-done.9, bf16[512,256]{1,0:T(8,128)(2,1)} %copy-done.13, ...), custom_call_target="tpu_custom_call" | custom-call | flops 805306368 | bytes 4194304 | tf_op jit(solution)/shard_map/pallas_call | solution.py:57
  262.1 4.3 %collective-permute-start.35 = (bf16[512,256]{1,0:T(8,128)(2,1)S(1)}, bf16[512,256]{1,0:T(8,128)(2,1)S(1)}, u32[]{:S(2)}, u32[]{:S(2)}) collective-permute-start(bf16[512,256]{1,0:T(8,128)(2,1)S(1)} %get-tuple-element.30), channel_id=1, source_target_pairs={{32,160},{96,224},{160,32},{224,96},{33,161},{97,225},{161,33},{22... | collective-permute-start | bytes 786440 | tf_op jit(solution)/shard_map/ppermute | solution.py:140
  (167 shorter events, 119.9 us)
Async XLA Ops:
  6.5 36.4 %all-gather.3.cloned.1.call-start = ((), (), s32[]{:S(2)}) async-start(), calls=%async_computation | async-start | bytes 2359296 | tf_op jit(solution)/shard_map/all_gather | solution.py:84
  8.4 25.9 %collective-permute-start = (bf16[512,256]{1,0:T(8,128)(2,1)S(1)}, bf16[512,256]{1,0:T(8,128)(2,1)S(1)}, u32[]{:S(2)}, u32[]{:S(2)}) collective-permute-start(bf16[512,256]{1,0:T(8,128)(2,1)S(1)} %dynamic-slice_bitcast_fusion.1.p2), channel_id=1, source_target_pairs={{32,33},{33,34},{34,35},{35,36},{36,37},{37,38},{38,39},{39,40},{4... | collective-permute-start | bytes 786440 | tf_op jit(solution)/shard_map/ppermute | solution.py:97
  12.8 23.5 %collective-permute-start.2 = (bf16[512,256]{1,0:T(8,128)(2,1)S(1)}, bf16[512,256]{1,0:T(8,128)(2,1)S(1)}, u32[]{:S(2)}, u32[]{:S(2)}) collective-permute-start(bf16[512,256]{1,0:T(8,128)(2,1)S(1)} %dynamic-slice_bitcast_fusion.1.p2), channel_id=1, source_target_pairs={{32,63},{33,32},{34,33},{35,34},{36,35},{37,36},{38,37},{39,38},{4... | collective-permute-start | bytes 786440 | tf_op jit(solution)/shard_map/ppermute | solution.py:97
  34.3 11.7 %collective-permute-start.1 = (bf16[512,256]{1,0:T(8,128)(2,1)S(1)}, bf16[512,256]{1,0:T(8,128)(2,1)S(1)}, u32[]{:S(2)}, u32[]{:S(2)}) collective-permute-start(bf16[512,256]{1,0:T(8,128)(2,1)S(1)} %collective-permute-done.p1), channel_id=1, source_target_pairs={{32,33},{33,34},{34,35},{35,36},{36,37},{37,38},{38,39},{39,40},{4... | collective-permute-start | bytes 786440 | tf_op jit(solution)/shard_map/ppermute | solution.py:97
  51.2 11.1 %collective-permute-start.4 = (bf16[512,256]{1,0:T(8,128)(2,1)}, bf16[512,256]{1,0:T(8,128)(2,1)S(1)}, u32[]{:S(2)}, u32[]{:S(2)}) collective-permute-start(bf16[512,256]{1,0:T(8,128)(2,1)} %shard_map.83.p2), channel_id=1, source_target_pairs={{32,33},{33,34},{34,35},{35,36},{36,37},{37,38},{38,39},{39,40},{4... | collective-permute-start | bytes 786440 | tf_op jit(solution)/shard_map/ppermute | solution.py:97
  53.1 11.1 %collective-permute-start.6 = (bf16[512,256]{1,0:T(8,128)(2,1)}, bf16[512,256]{1,0:T(8,128)(2,1)S(1)}, u32[]{:S(2)}, u32[]{:S(2)}) collective-permute-start(bf16[512,256]{1,0:T(8,128)(2,1)} %shard_map.83.p2), channel_id=1, source_target_pairs={{32,63},{33,32},{34,33},{35,34},{36,35},{37,36},{38,37},{39,38},{4... | collective-permute-start | bytes 786440 | tf_op jit(solution)/shard_map/ppermute | solution.py:97
  79.1 10.7 %collective-permute-start.10 = (bf16[512,256]{1,0:T(8,128)(2,1)}, bf16[512,256]{1,0:T(8,128)(2,1)S(1)}, u32[]{:S(2)}, u32[]{:S(2)}) collective-permute-start(bf16[512,256]{1,0:T(8,128)(2,1)} %shard_map.84.p2), channel_id=1, source_target_pairs={{32,63},{33,32},{34,33},{35,34},{36,35},{37,36},{38,37},{39,38},{4... | collective-permute-start | bytes 786440 | tf_op jit(solution)/shard_map/ppermute | solution.py:97
  86.3 10.6 %collective-permute-start.8 = (bf16[512,256]{1,0:T(8,128)(2,1)}, bf16[512,256]{1,0:T(8,128)(2,1)S(1)}, u32[]{:S(2)}, u32[]{:S(2)}) collective-permute-start(bf16[512,256]{1,0:T(8,128)(2,1)} %shard_map.84.p2), channel_id=1, source_target_pairs={{32,33},{33,34},{34,35},{35,36},{36,37},{37,38},{38,39},{39,40},{4... | collective-permute-start | bytes 786440 | tf_op jit(solution)/shard_map/ppermute | solution.py:97
  112.3 10.6 %collective-permute-start.12 = (bf16[512,256]{1,0:T(8,128)(2,1)}, bf16[512,256]{1,0:T(8,128)(2,1)S(1)}, u32[]{:S(2)}, u32[]{:S(2)}) collective-permute-start(bf16[512,256]{1,0:T(8,128)(2,1)} %shard_map.85.p2), channel_id=1, source_target_pairs={{32,33},{33,34},{34,35},{35,36},{36,37},{37,38},{38,39},{39,40},{4... | collective-permute-start | bytes 786440 | tf_op jit(solution)/shard_map/ppermute | solution.py:97
  114.2 10.6 %collective-permute-start.14 = (bf16[512,256]{1,0:T(8,128)(2,1)}, bf16[512,256]{1,0:T(8,128)(2,1)S(1)}, u32[]{:S(2)}, u32[]{:S(2)}) collective-permute-start(bf16[512,256]{1,0:T(8,128)(2,1)} %shard_map.85.p2), channel_id=1, source_target_pairs={{32,63},{33,32},{34,33},{35,34},{36,35},{37,36},{38,37},{39,38},{4... | collective-permute-start | bytes 786440 | tf_op jit(solution)/shard_map/ppermute | solution.py:97
  139.8 11.1 %collective-permute-start.16 = (bf16[512,256]{1,0:T(8,128)(2,1)}, bf16[512,256]{1,0:T(8,128)(2,1)S(1)}, u32[]{:S(2)}, u32[]{:S(2)}) collective-permute-start(bf16[512,256]{1,0:T(8,128)(2,1)} %shard_map.86.p2), channel_id=1, source_target_pairs={{32,33},{33,34},{34,35},{35,36},{36,37},{37,38},{38,39},{39,40},{4... | collective-permute-start | bytes 786440 | tf_op jit(solution)/shard_map/ppermute | solution.py:97
  141.8 11.1 %collective-permute-start.18 = (bf16[512,256]{1,0:T(8,128)(2,1)}, bf16[512,256]{1,0:T(8,128)(2,1)S(1)}, u32[]{:S(2)}, u32[]{:S(2)}) collective-permute-start(bf16[512,256]{1,0:T(8,128)(2,1)} %shard_map.86.p2), channel_id=1, source_target_pairs={{32,63},{33,32},{34,33},{35,34},{36,35},{37,36},{38,37},{39,38},{4... | collective-permute-start | bytes 786440 | tf_op jit(solution)/shard_map/ppermute | solution.py:97
  167.8 11.1 %collective-permute-start.20 = (bf16[512,256]{1,0:T(8,128)(2,1)}, bf16[512,256]{1,0:T(8,128)(2,1)S(1)}, u32[]{:S(2)}, u32[]{:S(2)}) collective-permute-start(bf16[512,256]{1,0:T(8,128)(2,1)} %shard_map.87.p2), channel_id=1, source_target_pairs={{32,33},{33,34},{34,35},{35,36},{36,37},{37,38},{38,39},{39,40},{4... | collective-permute-start | bytes 786440 | tf_op jit(solution)/shard_map/ppermute | solution.py:97
  169.7 11.1 %collective-permute-start.22 = (bf16[512,256]{1,0:T(8,128)(2,1)}, bf16[512,256]{1,0:T(8,128)(2,1)S(1)}, u32[]{:S(2)}, u32[]{:S(2)}) collective-permute-start(bf16[512,256]{1,0:T(8,128)(2,1)} %shard_map.87.p2), channel_id=1, source_target_pairs={{32,63},{33,32},{34,33},{35,34},{36,35},{37,36},{38,37},{39,38},{4... | collective-permute-start | bytes 786440 | tf_op jit(solution)/shard_map/ppermute | solution.py:97
  195.7 11.1 %collective-permute-start.24 = (bf16[512,256]{1,0:T(8,128)(2,1)}, bf16[512,256]{1,0:T(8,128)(2,1)S(1)}, u32[]{:S(2)}, u32[]{:S(2)}) collective-permute-start(bf16[512,256]{1,0:T(8,128)(2,1)} %shard_map.88.p2), channel_id=1, source_target_pairs={{32,33},{33,34},{34,35},{35,36},{36,37},{37,38},{38,39},{39,40},{4... | collective-permute-start | bytes 786440 | tf_op jit(solution)/shard_map/ppermute | solution.py:97
  197.6 11.1 %collective-permute-start.26 = (bf16[512,256]{1,0:T(8,128)(2,1)}, bf16[512,256]{1,0:T(8,128)(2,1)S(1)}, u32[]{:S(2)}, u32[]{:S(2)}) collective-permute-start(bf16[512,256]{1,0:T(8,128)(2,1)} %shard_map.88.p2), channel_id=1, source_target_pairs={{32,63},{33,32},{34,33},{35,34},{36,35},{37,36},{38,37},{39,38},{4... | collective-permute-start | bytes 786440 | tf_op jit(solution)/shard_map/ppermute | solution.py:97
  223.7 11.1 %collective-permute-start.28 = (bf16[512,256]{1,0:T(8,128)(2,1)}, bf16[512,256]{1,0:T(8,128)(2,1)S(1)}, u32[]{:S(2)}, u32[]{:S(2)}) collective-permute-start(bf16[512,256]{1,0:T(8,128)(2,1)} %shard_map.89.p2), channel_id=1, source_target_pairs={{32,33},{33,34},{34,35},{35,36},{36,37},{37,38},{38,39},{39,40},{4... | collective-permute-start | bytes 786440 | tf_op jit(solution)/shard_map/ppermute | solution.py:97
  225.7 11.1 %collective-permute-start.30 = (bf16[512,256]{1,0:T(8,128)(2,1)}, bf16[512,256]{1,0:T(8,128)(2,1)S(1)}, u32[]{:S(2)}, u32[]{:S(2)}) collective-permute-start(bf16[512,256]{1,0:T(8,128)(2,1)} %shard_map.89.p2), channel_id=1, source_target_pairs={{32,63},{33,32},{34,33},{35,34},{36,35},{37,36},{38,37},{39,38},{4... | collective-permute-start | bytes 786440 | tf_op jit(solution)/shard_map/ppermute | solution.py:97
  234.8 15.7 %collective-permute-start.29 = (bf16[512,256]{1,0:T(8,128)(2,1)S(1)}, bf16[512,256]{1,0:T(8,128)(2,1)S(1)}, u32[]{:S(2)}, u32[]{:S(2)}) collective-permute-start(bf16[512,256]{1,0:T(8,128)(2,1)S(1)} %collective-permute-done.28.p1), channel_id=1, source_target_pairs={{32,33},{33,34},{34,35},{35,36},{36,37},{37,38},{38,39},{39,40},{4... | collective-permute-start | bytes 786440 | tf_op jit(solution)/shard_map/ppermute | solution.py:97
  236.8 15.8 %collective-permute-start.31 = (bf16[512,256]{1,0:T(8,128)(2,1)S(1)}, bf16[512,256]{1,0:T(8,128)(2,1)S(1)}, u32[]{:S(2)}, u32[]{:S(2)}) collective-permute-start(bf16[512,256]{1,0:T(8,128)(2,1)S(1)} %collective-permute-done.30.p3), channel_id=1, source_target_pairs={{32,63},{33,32},{34,33},{35,34},{36,35},{37,36},{38,37},{39,38},{4... | collective-permute-start | bytes 786440 | tf_op jit(solution)/shard_map/ppermute | solution.py:97
  244.6 17.5 %collective-permute-start.32 = (bf16[512,256]{1,0:T(8,128)(2,1)S(1)}, bf16[512,256]{1,0:T(8,128)(2,1)}, u32[]{:S(2)}, u32[]{:S(2)}) collective-permute-start(bf16[512,256]{1,0:T(8,128)(2,1)S(1)} %get-tuple-element.28), channel_id=1, source_target_pairs={{32,64},{96,128},{160,192},{224,0},{33,65},{97,129},{161,193},{225... | collective-permute-start | bytes 786440 | tf_op jit(solution)/shard_map/ppermute | solution.py:140
  246.6 24.3 %collective-permute-start.34 = (bf16[512,256]{1,0:T(8,128)(2,1)S(1)}, bf16[512,256]{1,0:T(8,128)(2,1)}, u32[]{:S(2)}, u32[]{:S(2)}) collective-permute-start(bf16[512,256]{1,0:T(8,128)(2,1)S(1)} %get-tuple-element.27), channel_id=1, source_target_pairs={{32,128},{96,192},{160,0},{224,64},{33,129},{97,193},{161,1},{225,... | collective-permute-start | bytes 786440 | tf_op jit(solution)/shard_map/ppermute | solution.py:140
  248.6 23.3 %collective-permute-start.36 = (bf16[512,256]{1,0:T(8,128)(2,1)S(1)}, bf16[512,256]{1,0:T(8,128)(2,1)}, u32[]{:S(2)}, u32[]{:S(2)}) collective-permute-start(bf16[512,256]{1,0:T(8,128)(2,1)S(1)} %get-tuple-element.26), channel_id=1, source_target_pairs={{32,192},{96,0},{160,64},{224,128},{33,193},{97,1},{161,65},{225,1... | collective-permute-start | bytes 786440 | tf_op jit(solution)/shard_map/ppermute | solution.py:140
  250.6 23.9 %collective-permute-start.38 = (bf16[512,256]{1,0:T(8,128)(2,1)S(1)}, bf16[512,256]{1,0:T(8,128)(2,1)}, u32[]{:S(2)}, u32[]{:S(2)}) collective-permute-start(bf16[512,256]{1,0:T(8,128)(2,1)S(1)} %get-tuple-element.25), channel_id=1, source_target_pairs={{32,0},{96,64},{160,128},{224,192},{33,1},{97,65},{161,129},{225,1... | collective-permute-start | bytes 786440 | tf_op jit(solution)/shard_map/ppermute | solution.py:140
  (56 other events, 484.6 us)
Sparse Core Ops, SparseCore 0:
  9.2 31.9 all-gather.2

commit v5 on v4

--- a/solution.py
+++ b/solution.py
@@ -86,15 +86,20 @@
     neighbour_all = weights_all[:, 1]
 
     group = section_count // batch_total
-    workers = [group * m + group - 1 for m in range(batch_total)]
     batch = section_index // group
+    odd = section_index % 2 == 1
 
-    def halo(x, by):
+    def halo(x, reach):
         pairs = []
-        for s in workers:
+        for s in range(section_count):
+            by = reach if s % 2 == 1 else -reach
             for b in range(blk_count):
                 pairs.append((s * blk_count + b, s * blk_count + (b + by) % blk_count))
         return lax.ppermute(x, ("section", "blk"), pairs)
+
+    def swap(x):
+        pairs = [(s, s ^ 1) for s in range(section_count)]
+        return lax.ppermute(x, "section", pairs)
 
     values = lax.dynamic_index_in_dim(tile_values, batch, 0, keepdims=False)
     rows = lax.dynamic_index_in_dim(tile_rows, batch, 0, keepdims=False)
@@ -105,6 +110,7 @@
 
     column_dev = cols // blocks_dev
     shifted = jnp.mod(column_dev - blk_index + REACH, blk_count)
+    shifted = jnp.where(odd, shifted, 2 * REACH - shifted)
     column_local = shifted * blocks_dev + jnp.mod(cols, blocks_dev)
     row_local = rows - blk_index * blocks_dev
     band = build_band(
@@ -119,29 +125,29 @@
 
     outputs = []
     for level in range(layer_total):
-        up1 = halo(hidden, 1)
-        down1 = halo(hidden, -1)
-        up2 = halo(up1, 1)
-        down2 = halo(down1, -1)
-        parts = [up2, up1, hidden, down1, down2]
+        near = halo(hidden, 1)
+        far = halo(hidden, 2)
+        theirs = swap(jnp.concatenate([near, far], axis=0))
+        parts = [far, near, hidden, theirs[:rows_dev], theirs[rows_dev:]]
         hidden = run_layer(band, parts, degree_f, self_all[level], neighbour_all[level])
         outputs.append(hidden)
 
+    stacked = jnp.stack(outputs)
     arrived = []
-    for shift in range(section_count):
-        candidates = [(w + shift) % section_count for w in workers]
-        sending = outputs[candidates[0]]
-        for w, level in zip(workers[1:], candidates[1:]):
-            sending = jnp.where(section_index == w, outputs[level], sending)
+    for shift in range(0, section_count, group):
+        sending = lax.dynamic_index_in_dim(
+            stacked, (section_index + shift) % section_count, 0, keepdims=False
+        )
         if shift == 0:
             arrived.append(sending)
         else:
-            pairs = [(w, (w + shift) % section_count) for w in workers]
+            pairs = [(s, (s + shift) % section_count) for s in range(section_count)]
             arrived.append(lax.ppermute(sending, "section", pairs))
     arrived = jnp.stack(arrived)
+    chip = section_index // group
     gathered = [
-        lax.dynamic_index_in_dim(arrived, (section_index - w) % section_count, 0, keepdims=False)
-        for w in workers
+        lax.dynamic_index_in_dim(arrived, (chip - m) % batch_total, 0, keepdims=False)
+        for m in range(batch_total)
     ]
     return jnp.stack(gathered)[None]
 

time: 285 us -> 225 us (0.79)
  starting transfers between devices: 164 us -> 19.4 us
  waiting for transfers between devices: 40.7 us -> 127 us
  local copies, waits for them, and re-layouts: 17.1 us -> 23.5 us
  Pallas kernels: 37.6 us -> 33.6 us
    ppermute x32 -> x16, starting transfers between devices: 145 us -> 9.22 us  [halo(): return lax.ppermute(x, ('section', 'blk'), pairs)]
    ppermute x32 -> x16, waiting for transfers between devices: 39 us -> 105 us  [halo(): return lax.ppermute(x, ('section', 'blk'), pairs)]
    ppermute x7 -> x3, starting transfers between devices: 19 us -> 2.82 us  [body(): arrived.append(lax.ppermute(sending, 'section', pairs))]
    ppermute x7 -> x3, waiting for transfers between devices: 1.63 us -> 14 us  [body(): arrived.append(lax.ppermute(sending, 'section', pairs))]
    ppermute x0 -> x8, waiting for transfers between devices: none -> 8.4 us  [swap(): return lax.ppermute(x, 'section', pairs)]
    ppermute x0 -> x8, starting transfers between devices: none -> 7.38 us  [swap(): return lax.ppermute(x, 'section', pairs)]
    slice x0 -> x8, local copies, waits for them, and re-layouts: none -> 5.8 us  [body(): parts = [far, near, hidden, theirs[:rows_dev], theirs[rows_dev:]]]
    pallas_call x8 -> x7, Pallas kernels: 34.1 us -> 29.8 us  [run_layer(): pl.pallas_call(_layer_kernel, out_shape=jax.ShapeDtypeStruct((rows, width...]
  transfers between devices with their start and end apart: 40 -> 28, of which waited for: 21 -> 25; matrix products, arithmetic and copies ran while one was open for 6% -> 6% of each run, Pallas kernels for 3% -> 2%
where the time goes in v5:
time: 225 us
  waiting for transfers between devices  127 us (56%)
  Pallas kernels  33.6 us (15%)
  local copies, waits for them, and re-layouts  23.5 us (10%)
  starting transfers between devices  19.4 us (9%)
  between operations  14.3 us (6%)
  other arithmetic  7.22 us (3%)
    ppermute x16, waiting for transfers between devices, halo(): return lax.ppermute(x, ('section', 'blk'), pairs)  105 us
    pallas_call x7, Pallas kernels, run_layer(): pl.pallas_call(_layer_kernel, out_shape=jax.ShapeDtypeStruct((rows, width...  29.8 us
    ppermute x3, waiting for transfers between devices, body(): arrived.append(lax.ppermute(sending, 'section', pairs))  14 us
    ppermute x16, starting transfers between devices, halo(): return lax.ppermute(x, ('section', 'blk'), pairs)  9.22 us
    ppermute x8, waiting for transfers between devices, swap(): return lax.ppermute(x, 'section', pairs)  8.4 us
    ppermute x8, starting transfers between devices, swap(): return lax.ppermute(x, 'section', pairs)  7.38 us
    slice x8, local copies, waits for them, and re-layouts, body(): parts = [far, near, hidden, theirs[:rows_dev], theirs[rows_dev:]]  5.8 us
    unnamed x57, local copies, waits for them, and re-layouts  5.12 us
  transfers between devices with their start and end apart: 28, of which 25 were waited for; matrix products, arithmetic and copies ran while one was open for 6% of the time, Pallas kernels for 2%

profile of v5, /device:TPU:1, one launch (start us, length us, event | category | flops | bytes accessed | tf_op | source)
XLA Modules:
  0.0 225.1 jit_solution(3582566274077617836)
XLA Ops:
  8.4 3.9 %collective-permute-start = (bf16[512,256]{1,0:T(8,128)(2,1)S(1)}, bf16[512,256]{1,0:T(8,128)(2,1)S(1)}, u32[]{:S(2)}, u32[]{:S(2)}) collective-permute-start(bf16[512,256]{1,0:T(8,128)(2,1)S(1)} %dynamic-slice_bitcast_fusion.4.p2), channel_id=1, source_target_pairs={{0,30},{1,31},{2,0},{3,1},{4,2},{5,3},{6,4},{7,5},{8,6},{9,7},{10,... | collective-permute-start | bytes 786440 | tf_op jit(solution)/shard_map/ppermute | solution.py:98
  14.0 8.2 %collective-permute-done.p0 = bf16[512,256]{1,0:T(8,128)(2,1)S(1)} collective-permute-done((bf16[512,256]{1,0:T(8,128)(2,1)S(1)}, bf16[512,256]{1,0:T(8,128)(2,1)S(1)}, u32[]{:S(2)}, u32[]{:S(2)}) %collective-permute-start) | collective-permute-done | bytes 262176 | tf_op jit(solution)/shard_map/ppermute | solution.py:98
  22.2 4.6 %collective-permute-done.1.p1 = bf16[512,256]{1,0:T(8,128)(2,1)S(1)} collective-permute-done((bf16[512,256]{1,0:T(8,128)(2,1)S(1)}, bf16[512,256]{1,0:T(8,128)(2,1)S(1)}, u32[]{:S(2)}, u32[]{:S(2)}) %collective-permute-start.1) | collective-permute-done | bytes 262176 | tf_op jit(solution)/shard_map/ppermute | solution.py:98
  33.8 3.6 %dynamic-slice_bitcast_fusion.values_ref = bf16[80,128,128]{2,1,0:T(8,128)(2,1)} fusion(bf16[4,80,128,128]{3,2,1,0:T(8,128)(2,1)} %param.9, s32[]{:T(128)S(6)} %select_n.106), kind=kLoop, calls=%fused_computation | loop fusion | bytes 5242884 | tf_op jit(solution)/shard_map/jit(dynamic_index_in_dim)/squeeze | solution.py:104
  37.5 3.8 %shard_map.82.band_ref = bf16[512,2560]{1,0:T(8,128)(2,1)} custom-call(s32[80]{0:T(128)} %fusion.7.rows_ref, s32[80]{0:T(128)} %fusion.8.cols_ref, s32[1]{0:T(128)} %bitcast.2.count_ref, bf16[80,128,128]{2,1,0:T(8,128)(2,1)} %dynamic-slice_bitcast_fusion.values_ref), custom_call_target="tpu_custom_call" | custom-call | tf_op jit(solution)/shard_map/pallas_call | solution.py:25
  44.9 4.2 %shard_map.83.p2 = bf16[512,256]{1,0:T(8,128)(2,1)} custom-call(bf16[512,2560]{1,0:T(8,128)(2,1)} %shard_map.82.band_ref, bf16[512,256]{1,0:T(8,128)(2,1)} %copy-done.12, bf16[512,256]{1,0:T(8,128)(2,1)} %copy-done.13, bf16[512,256]{1,0:T(8,128)(2,1)} %copy-done.9, bf16[512,256]{1,0:T(8,128)(2,1)} %get-tuple-element.44.p3, ...), custom_call_target="tpu_custom_call" | custom-call | flops 805306368 | bytes 4194304 | tf_op jit(solution)/shard_map/pallas_call | solution.py:57
  51.9 7.1 %collective-permute-done.3.p0 = bf16[512,256]{1,0:T(8,128)(2,1)S(1)} collective-permute-done((bf16[512,256]{1,0:T(8,128)(2,1)}, bf16[512,256]{1,0:T(8,128)(2,1)S(1)}, u32[]{:S(2)}, u32[]{:S(2)}) %collective-permute-start.3) | collective-permute-done | bytes 262176 | tf_op jit(solution)/shard_map/ppermute | solution.py:98
  59.0 5.2 %collective-permute-done.4.p1 = bf16[512,256]{1,0:T(8,128)(2,1)S(1)} collective-permute-done((bf16[512,256]{1,0:T(8,128)(2,1)}, bf16[512,256]{1,0:T(8,128)(2,1)S(1)}, u32[]{:S(2)}, u32[]{:S(2)}) %collective-permute-start.4) | collective-permute-done | bytes 262176 | tf_op jit(solution)/shard_map/ppermute | solution.py:98
  67.4 4.2 %shard_map.84.p2 = bf16[512,256]{1,0:T(8,128)(2,1)} custom-call(bf16[512,2560]{1,0:T(8,128)(2,1)} %shard_map.82.band_ref, bf16[512,256]{1,0:T(8,128)(2,1)} %copy-done.14, bf16[512,256]{1,0:T(8,128)(2,1)} %copy-done.19, bf16[512,256]{1,0:T(8,128)(2,1)} %shard_map.83.p2, bf16[512,256]{1,0:T(8,128)(2,1)} %get-tuple-element.42.p3, ...), custom_call_target="tpu_custom_call" | custom-call | flops 805306368 | bytes 4194304 | tf_op jit(solution)/shard_map/pallas_call | solution.py:57
  72.3 9.2 %collective-permute-done.6.p0 = bf16[512,256]{1,0:T(8,128)(2,1)S(1)} collective-permute-done((bf16[512,256]{1,0:T(8,128)(2,1)}, bf16[512,256]{1,0:T(8,128)(2,1)S(1)}, u32[]{:S(2)}, u32[]{:S(2)}) %collective-permute-start.6) | collective-permute-done | bytes 262176 | tf_op jit(solution)/shard_map/ppermute | solution.py:98
  81.5 5.0 %collective-permute-done.7.p1 = bf16[512,256]{1,0:T(8,128)(2,1)S(1)} collective-permute-done((bf16[512,256]{1,0:T(8,128)(2,1)}, bf16[512,256]{1,0:T(8,128)(2,1)S(1)}, u32[]{:S(2)}, u32[]{:S(2)}) %collective-permute-start.7) | collective-permute-done | bytes 262176 | tf_op jit(solution)/shard_map/ppermute | solution.py:98
  89.4 4.2 %shard_map.85.p2 = bf16[512,256]{1,0:T(8,128)(2,1)} custom-call(bf16[512,2560]{1,0:T(8,128)(2,1)} %shard_map.82.band_ref, bf16[512,256]{1,0:T(8,128)(2,1)} %copy-done.15, bf16[512,256]{1,0:T(8,128)(2,1)} %copy-done.20, bf16[512,256]{1,0:T(8,128)(2,1)} %shard_map.84.p2, bf16[512,256]{1,0:T(8,128)(2,1)} %get-tuple-element.40.p3, ...), custom_call_target="tpu_custom_call" | custom-call | flops 805306368 | bytes 4194304 | tf_op jit(solution)/shard_map/pallas_call | solution.py:57
  93.7 12.6 %collective-permute-done.9.p0 = bf16[512,256]{1,0:T(8,128)(2,1)S(1)} collective-permute-done((bf16[512,256]{1,0:T(8,128)(2,1)}, bf16[512,256]{1,0:T(8,128)(2,1)S(1)}, u32[]{:S(2)}, u32[]{:S(2)}) %collective-permute-start.9) | collective-permute-done | bytes 262176 | tf_op jit(solution)/shard_map/ppermute | solution.py:98
  111.9 4.2 %shard_map.86.p2 = bf16[512,256]{1,0:T(8,128)(2,1)} custom-call(bf16[512,2560]{1,0:T(8,128)(2,1)} %shard_map.82.band_ref, bf16[512,256]{1,0:T(8,128)(2,1)} %copy-done.16, bf16[512,256]{1,0:T(8,128)(2,1)} %copy-done.21, bf16[512,256]{1,0:T(8,128)(2,1)} %shard_map.85.p2, bf16[512,256]{1,0:T(8,128)(2,1)} %get-tuple-element.38.p3, ...), custom_call_target="tpu_custom_call" | custom-call | flops 805306368 | bytes 4194304 | tf_op jit(solution)/shard_map/pallas_call | solution.py:57
  116.2 12.5 %collective-permute-done.12.p0 = bf16[512,256]{1,0:T(8,128)(2,1)S(1)} collective-permute-done((bf16[512,256]{1,0:T(8,128)(2,1)}, bf16[512,256]{1,0:T(8,128)(2,1)S(1)}, u32[]{:S(2)}, u32[]{:S(2)}) %collective-permute-start.12) | collective-permute-done | bytes 262176 | tf_op jit(solution)/shard_map/ppermute | solution.py:98
  133.1 4.2 %shard_map.87.p2 = bf16[512,256]{1,0:T(8,128)(2,1)} custom-call(bf16[512,2560]{1,0:T(8,128)(2,1)} %shard_map.82.band_ref, bf16[512,256]{1,0:T(8,128)(2,1)} %copy-done.17, bf16[512,256]{1,0:T(8,128)(2,1)} %copy-done.22, bf16[512,256]{1,0:T(8,128)(2,1)} %shard_map.86.p2, bf16[512,256]{1,0:T(8,128)(2,1)} %get-tuple-element.36.p3, ...), custom_call_target="tpu_custom_call" | custom-call | flops 805306368 | bytes 4194304 | tf_op jit(solution)/shard_map/pallas_call | solution.py:57
  137.4 12.5 %collective-permute-done.15.p0 = bf16[512,256]{1,0:T(8,128)(2,1)S(1)} collective-permute-done((bf16[512,256]{1,0:T(8,128)(2,1)}, bf16[512,256]{1,0:T(8,128)(2,1)S(1)}, u32[]{:S(2)}, u32[]{:S(2)}) %collective-permute-start.15) | collective-permute-done | bytes 262176 | tf_op jit(solution)/shard_map/ppermute | solution.py:98
  153.7 4.3 %shard_map.88.p2 = bf16[512,256]{1,0:T(8,128)(2,1)} custom-call(bf16[512,2560]{1,0:T(8,128)(2,1)} %shard_map.82.band_ref, bf16[512,256]{1,0:T(8,128)(2,1)} %copy-done.18, bf16[512,256]{1,0:T(8,128)(2,1)} %copy-done.23, bf16[512,256]{1,0:T(8,128)(2,1)} %shard_map.87.p2, bf16[512,256]{1,0:T(8,128)(2,1)} %get-tuple-element.34.p3, ...), custom_call_target="tpu_custom_call" | custom-call | flops 805306368 | bytes 4194304 | tf_op jit(solution)/shard_map/pallas_call | solution.py:57
  158.0 12.4 %collective-permute-done.18.p0 = bf16[512,256]{1,0:T(8,128)(2,1)S(1)} collective-permute-done((bf16[512,256]{1,0:T(8,128)(2,1)}, bf16[512,256]{1,0:T(8,128)(2,1)S(1)}, u32[]{:S(2)}, u32[]{:S(2)}) %collective-permute-start.18) | collective-permute-done | bytes 262176 | tf_op jit(solution)/shard_map/ppermute | solution.py:98
  174.5 4.3 %shard_map.89 = bf16[512,256]{1,0:T(8,128)(2,1)} custom-call(bf16[512,2560]{1,0:T(8,128)(2,1)} %shard_map.82.band_ref, bf16[512,256]{1,0:T(8,128)(2,1)} %copy-done.10, bf16[512,256]{1,0:T(8,128)(2,1)} %copy-done.11, bf16[512,256]{1,0:T(8,128)(2,1)} %shard_map.88.p2, bf16[512,256]{1,0:T(8,128)(2,1)} %get-tuple-element.32.p3, ...), custom_call_target="tpu_custom_call" | custom-call | flops 805306368 | bytes 4194304 | tf_op jit(solution)/shard_map/pallas_call | solution.py:57
  180.7 10.2 %collective-permute-done.21 = bf16[512,256]{1,0:T(8,128)(2,1)S(1)} collective-permute-done((bf16[512,256]{1,0:T(8,128)(2,1)}, bf16[512,256]{1,0:T(8,128)(2,1)S(1)}, u32[]{:S(2)}, u32[]{:S(2)}) %collective-permute-start.21) | collective-permute-done | bytes 262176 | tf_op jit(solution)/shard_map/ppermute | solution.py:98
  195.1 3.8 %shard_map.90 = bf16[8,512,256]{2,1,0:T(8,128)(2,1)} fusion(bf16[8,512,256]{2,1,0:T(8,128)(2,1)} %bitcast_dynamic-update-slice_fusion.1, bf16[512,2560]{1,0:T(8,128)(2,1)} %shard_map.82.band_ref, bf16[512,256]{1,0:T(8,128)(2,1)S(1)} %collective-permute-done.21, bf16[512,256]{1,0:T(8,128)(2,1)S(1)} %collective-permute-done.22, ...), kind=kCustom, calls=%fused_computation.12 | custom fusion | bytes 4458496 | tf_op jit(solution)/shard_map/pallas_call | solution.py:57
  203.0 5.1 %collective-permute-done.26 = bf16[512,256]{1,0:T(8,128)(2,1)S(1)} collective-permute-done((bf16[512,256]{1,0:T(8,128)(2,1)S(1)}, bf16[512,256]{1,0:T(8,128)(2,1)S(1)}, u32[]{:S(2)}, u32[]{:S(2)}) %collective-permute-start.26) | collective-permute-done | bytes 262176 | tf_op jit(solution)/shard_map/ppermute | solution.py:145
  210.7 6.2 %collective-permute-done.24 = bf16[512,256]{1,0:T(8,128)(2,1)S(1)} collective-permute-done((bf16[512,256]{1,0:T(8,128)(2,1)S(1)}, bf16[512,256]{1,0:T(8,128)(2,1)S(1)}, u32[]{:S(2)}, u32[]{:S(2)}) %collective-permute-start.24) | collective-permute-done | bytes 262176 | tf_op jit(solution)/shard_map/ppermute | solution.py:145
  (128 shorter events, 55.3 us)
Async XLA Ops:
  6.5 35.5 %all-gather.3.cloned.1.call-start = ((), (), s32[]{:S(2)}) async-start(), calls=%async_computation | async-start | bytes 2359296 | tf_op jit(solution)/shard_map/all_gather | solution.py:84
  8.4 13.7 %collective-permute-start = (bf16[512,256]{1,0:T(8,128)(2,1)S(1)}, bf16[512,256]{1,0:T(8,128)(2,1)S(1)}, u32[]{:S(2)}, u32[]{:S(2)}) collective-permute-start(bf16[512,256]{1,0:T(8,128)(2,1)S(1)} %dynamic-slice_bitcast_fusion.4.p2), channel_id=1, source_target_pairs={{0,30},{1,31},{2,0},{3,1},{4,2},{5,3},{6,4},{7,5},{8,6},{9,7},{10,... | collective-permute-start | bytes 786440 | tf_op jit(solution)/shard_map/ppermute | solution.py:98
  12.3 14.4 %collective-permute-start.1 = (bf16[512,256]{1,0:T(8,128)(2,1)S(1)}, bf16[512,256]{1,0:T(8,128)(2,1)S(1)}, u32[]{:S(2)}, u32[]{:S(2)}) collective-permute-start(bf16[512,256]{1,0:T(8,128)(2,1)S(1)} %dynamic-slice_bitcast_fusion.4.p2), channel_id=1, source_target_pairs={{0,31},{1,0},{2,1},{3,2},{4,3},{5,4},{6,5},{7,6},{8,7},{9,8},{10,9... | collective-permute-start | bytes 786440 | tf_op jit(solution)/shard_map/ppermute | solution.py:98
  26.8 14.4 %collective-permute-start.2 = (bf16[1024,256]{1,0:T(8,128)(2,1)S(1)}, bf16[1024,256]{1,0:T(8,128)(2,1)S(1)}, u32[]{:S(2)}, u32[]{:S(2)}) collective-permute-start(bf16[1024,256]{1,0:T(8,128)(2,1)S(1)} %pad_maximum_fusion.1), channel_id=1, source_target_pairs={{0,32},{32,0},{64,96},{96,64},{128,160},{160,128},{192,224},{224,1... | collective-permute-start | bytes 1572872 | tf_op jit(solution)/shard_map/ppermute | solution.py:102
  49.2 9.8 %collective-permute-start.3 = (bf16[512,256]{1,0:T(8,128)(2,1)}, bf16[512,256]{1,0:T(8,128)(2,1)S(1)}, u32[]{:S(2)}, u32[]{:S(2)}) collective-permute-start(bf16[512,256]{1,0:T(8,128)(2,1)} %shard_map.83.p2), channel_id=1, source_target_pairs={{0,30},{1,31},{2,0},{3,1},{4,2},{5,3},{6,4},{7,5},{8,6},{9,7},{10,... | collective-permute-start | bytes 786440 | tf_op jit(solution)/shard_map/ppermute | solution.py:98
  50.6 13.6 %collective-permute-start.4 = (bf16[512,256]{1,0:T(8,128)(2,1)}, bf16[512,256]{1,0:T(8,128)(2,1)S(1)}, u32[]{:S(2)}, u32[]{:S(2)}) collective-permute-start(bf16[512,256]{1,0:T(8,128)(2,1)} %shard_map.83.p2), channel_id=1, source_target_pairs={{0,31},{1,0},{2,1},{3,2},{4,3},{5,4},{6,5},{7,6},{8,7},{9,8},{10,9... | collective-permute-start | bytes 786440 | tf_op jit(solution)/shard_map/ppermute | solution.py:98
  71.7 9.8 %collective-permute-start.6 = (bf16[512,256]{1,0:T(8,128)(2,1)}, bf16[512,256]{1,0:T(8,128)(2,1)S(1)}, u32[]{:S(2)}, u32[]{:S(2)}) collective-permute-start(bf16[512,256]{1,0:T(8,128)(2,1)} %shard_map.84.p2), channel_id=1, source_target_pairs={{0,30},{1,31},{2,0},{3,1},{4,2},{5,3},{6,4},{7,5},{8,6},{9,7},{10,... | collective-permute-start | bytes 786440 | tf_op jit(solution)/shard_map/ppermute | solution.py:98
  71.7 14.8 %collective-permute-start.7 = (bf16[512,256]{1,0:T(8,128)(2,1)}, bf16[512,256]{1,0:T(8,128)(2,1)S(1)}, u32[]{:S(2)}, u32[]{:S(2)}) collective-permute-start(bf16[512,256]{1,0:T(8,128)(2,1)} %shard_map.84.p2), channel_id=1, source_target_pairs={{0,31},{1,0},{2,1},{3,2},{4,3},{5,4},{6,5},{7,6},{8,7},{9,8},{10,9... | collective-permute-start | bytes 786440 | tf_op jit(solution)/shard_map/ppermute | solution.py:98
  93.7 12.6 %collective-permute-start.9 = (bf16[512,256]{1,0:T(8,128)(2,1)}, bf16[512,256]{1,0:T(8,128)(2,1)S(1)}, u32[]{:S(2)}, u32[]{:S(2)}) collective-permute-start(bf16[512,256]{1,0:T(8,128)(2,1)} %shard_map.85.p2), channel_id=1, source_target_pairs={{0,30},{1,31},{2,0},{3,1},{4,2},{5,3},{6,4},{7,5},{8,6},{9,7},{10,... | collective-permute-start | bytes 786440 | tf_op jit(solution)/shard_map/ppermute | solution.py:98
  93.7 13.6 %collective-permute-start.10 = (bf16[512,256]{1,0:T(8,128)(2,1)}, bf16[512,256]{1,0:T(8,128)(2,1)S(1)}, u32[]{:S(2)}, u32[]{:S(2)}) collective-permute-start(bf16[512,256]{1,0:T(8,128)(2,1)} %shard_map.85.p2), channel_id=1, source_target_pairs={{0,31},{1,0},{2,1},{3,2},{4,3},{5,4},{6,5},{7,6},{8,7},{9,8},{10,9... | collective-permute-start | bytes 786440 | tf_op jit(solution)/shard_map/ppermute | solution.py:98
  107.3 3.8 %collective-permute-start.11 = (bf16[1024,256]{1,0:T(8,128)(2,1)S(1)}, bf16[1024,256]{1,0:T(8,128)(2,1)S(1)}, u32[]{:S(2)}, u32[]{:S(2)}) collective-permute-start(bf16[1024,256]{1,0:T(8,128)(2,1)S(1)} %pad_maximum_fusion.4), channel_id=1, source_target_pairs={{0,32},{32,0},{64,96},{96,64},{128,160},{160,128},{192,224},{224,1... | collective-permute-start | bytes 1572872 | tf_op jit(solution)/shard_map/ppermute | solution.py:102
  116.2 12.5 %collective-permute-start.12 = (bf16[512,256]{1,0:T(8,128)(2,1)}, bf16[512,256]{1,0:T(8,128)(2,1)S(1)}, u32[]{:S(2)}, u32[]{:S(2)}) collective-permute-start(bf16[512,256]{1,0:T(8,128)(2,1)} %shard_map.86.p2), channel_id=1, source_target_pairs={{0,30},{1,31},{2,0},{3,1},{4,2},{5,3},{6,4},{7,5},{8,6},{9,7},{10,... | collective-permute-start | bytes 786440 | tf_op jit(solution)/shard_map/ppermute | solution.py:98
  116.2 13.5 %collective-permute-start.13 = (bf16[512,256]{1,0:T(8,128)(2,1)}, bf16[512,256]{1,0:T(8,128)(2,1)S(1)}, u32[]{:S(2)}, u32[]{:S(2)}) collective-permute-start(bf16[512,256]{1,0:T(8,128)(2,1)} %shard_map.86.p2), channel_id=1, source_target_pairs={{0,31},{1,0},{2,1},{3,2},{4,3},{5,4},{6,5},{7,6},{8,7},{9,8},{10,9... | collective-permute-start | bytes 786440 | tf_op jit(solution)/shard_map/ppermute | solution.py:98
  129.7 2.6 %collective-permute-start.14 = (bf16[1024,256]{1,0:T(8,128)(2,1)S(1)}, bf16[1024,256]{1,0:T(8,128)(2,1)S(1)}, u32[]{:S(2)}, u32[]{:S(2)}) collective-permute-start(bf16[1024,256]{1,0:T(8,128)(2,1)S(1)} %pad_maximum_fusion.5), channel_id=1, source_target_pairs={{0,32},{32,0},{64,96},{96,64},{128,160},{160,128},{192,224},{224,1... | collective-permute-start | bytes 1572872 | tf_op jit(solution)/shard_map/ppermute | solution.py:102
  137.4 12.5 %collective-permute-start.15 = (bf16[512,256]{1,0:T(8,128)(2,1)}, bf16[512,256]{1,0:T(8,128)(2,1)S(1)}, u32[]{:S(2)}, u32[]{:S(2)}) collective-permute-start(bf16[512,256]{1,0:T(8,128)(2,1)} %shard_map.87.p2), channel_id=1, source_target_pairs={{0,30},{1,31},{2,0},{3,1},{4,2},{5,3},{6,4},{7,5},{8,6},{9,7},{10,... | collective-permute-start | bytes 786440 | tf_op jit(solution)/shard_map/ppermute | solution.py:98
  137.4 13.5 %collective-permute-start.16 = (bf16[512,256]{1,0:T(8,128)(2,1)}, bf16[512,256]{1,0:T(8,128)(2,1)S(1)}, u32[]{:S(2)}, u32[]{:S(2)}) collective-permute-start(bf16[512,256]{1,0:T(8,128)(2,1)} %shard_map.87.p2), channel_id=1, source_target_pairs={{0,31},{1,0},{2,1},{3,2},{4,3},{5,4},{6,5},{7,6},{8,7},{9,8},{10,9... | collective-permute-start | bytes 786440 | tf_op jit(solution)/shard_map/ppermute | solution.py:98
  158.0 12.4 %collective-permute-start.18 = (bf16[512,256]{1,0:T(8,128)(2,1)}, bf16[512,256]{1,0:T(8,128)(2,1)S(1)}, u32[]{:S(2)}, u32[]{:S(2)}) collective-permute-start(bf16[512,256]{1,0:T(8,128)(2,1)} %shard_map.88.p2), channel_id=1, source_target_pairs={{0,30},{1,31},{2,0},{3,1},{4,2},{5,3},{6,4},{7,5},{8,6},{9,7},{10,... | collective-permute-start | bytes 786440 | tf_op jit(solution)/shard_map/ppermute | solution.py:98
  158.0 13.7 %collective-permute-start.19 = (bf16[512,256]{1,0:T(8,128)(2,1)}, bf16[512,256]{1,0:T(8,128)(2,1)S(1)}, u32[]{:S(2)}, u32[]{:S(2)}) collective-permute-start(bf16[512,256]{1,0:T(8,128)(2,1)} %shard_map.88.p2), channel_id=1, source_target_pairs={{0,31},{1,0},{2,1},{3,2},{4,3},{5,4},{6,5},{7,6},{8,7},{9,8},{10,9... | collective-permute-start | bytes 786440 | tf_op jit(solution)/shard_map/ppermute | solution.py:98
  178.8 12.0 %collective-permute-start.21 = (bf16[512,256]{1,0:T(8,128)(2,1)}, bf16[512,256]{1,0:T(8,128)(2,1)S(1)}, u32[]{:S(2)}, u32[]{:S(2)}) collective-permute-start(bf16[512,256]{1,0:T(8,128)(2,1)} %shard_map.89), channel_id=1, source_target_pairs={{0,30},{1,31},{2,0},{3,1},{4,2},{5,3},{6,4},{7,5},{8,6},{9,7},{10,... | collective-permute-start | bytes 786440 | tf_op jit(solution)/shard_map/ppermute | solution.py:98
  178.9 13.1 %collective-permute-start.22 = (bf16[512,256]{1,0:T(8,128)(2,1)}, bf16[512,256]{1,0:T(8,128)(2,1)S(1)}, u32[]{:S(2)}, u32[]{:S(2)}) collective-permute-start(bf16[512,256]{1,0:T(8,128)(2,1)} %shard_map.89), channel_id=1, source_target_pairs={{0,31},{1,0},{2,1},{3,2},{4,3},{5,4},{6,5},{7,6},{8,7},{9,8},{10,9... | collective-permute-start | bytes 786440 | tf_op jit(solution)/shard_map/ppermute | solution.py:98
  192.0 3.0 %collective-permute-start.23 = (bf16[1024,256]{1,0:T(8,128)(2,1)S(1)}, bf16[1024,256]{1,0:T(8,128)(2,1)S(1)}, u32[]{:S(2)}, u32[]{:S(2)}) collective-permute-start(bf16[1024,256]{1,0:T(8,128)(2,1)S(1)} %pad_maximum_fusion.8), channel_id=1, source_target_pairs={{0,32},{32,0},{64,96},{96,64},{128,160},{160,128},{192,224},{224,1... | collective-permute-start | bytes 1572872 | tf_op jit(solution)/shard_map/ppermute | solution.py:102
  200.2 7.9 %collective-permute-start.26 = (bf16[512,256]{1,0:T(8,128)(2,1)S(1)}, bf16[512,256]{1,0:T(8,128)(2,1)S(1)}, u32[]{:S(2)}, u32[]{:S(2)}) collective-permute-start(bf16[512,256]{1,0:T(8,128)(2,1)S(1)} %get-tuple-element.6), channel_id=1, source_target_pairs={{0,192},{32,224},{64,0},{96,32},{128,64},{160,96},{192,128},{224,1... | collective-permute-start | bytes 786440 | tf_op jit(solution)/shard_map/ppermute | solution.py:145
  201.6 9.1 %collective-permute-start.25 = (bf16[512,256]{1,0:T(8,128)(2,1)S(1)}, bf16[512,256]{1,0:T(8,128)(2,1)S(1)}, u32[]{:S(2)}, u32[]{:S(2)}) collective-permute-start(bf16[512,256]{1,0:T(8,128)(2,1)S(1)} %get-tuple-element.7), channel_id=1, source_target_pairs={{0,128},{32,160},{64,192},{96,224},{128,0},{160,32},{192,64},{224,... | collective-permute-start | bytes 786440 | tf_op jit(solution)/shard_map/ppermute | solution.py:145
  202.2 14.7 %collective-permute-start.24 = (bf16[512,256]{1,0:T(8,128)(2,1)S(1)}, bf16[512,256]{1,0:T(8,128)(2,1)S(1)}, u32[]{:S(2)}, u32[]{:S(2)}) collective-permute-start(bf16[512,256]{1,0:T(8,128)(2,1)S(1)} %get-tuple-element.8), channel_id=1, source_target_pairs={{0,64},{32,96},{64,128},{96,160},{128,192},{160,224},{192,0},{224,... | collective-permute-start | bytes 786440 | tf_op jit(solution)/shard_map/ppermute | solution.py:145
  (29 other events, 248.5 us)
Sparse Core Ops, SparseCore 0:
  9.2 31.9 all-gather.2

commit v6 on v5

--- a/solution.py
+++ b/solution.py
@@ -31,12 +31,41 @@
     )(row_local, column_local, count, values)
 
 
-def _layer_kernel(band_ref, p0, p1, p2, p3, p4, degree_ref, ws_ref, wn_ref, out_ref):
-    rows = p2.shape[0]
-    parts = (p0, p1, p2, p3, p4)
-    summed = jnp.dot(
-        band_ref[:, pl.ds(2 * rows, rows)], p2[...], preferred_element_type=jnp.float32
-    )
+def _own_kernel(band_ref, hidden_ref, rows_ref, ws_ref, summed_ref, self_ref):
+    summed_ref[...] = jnp.dot(band_ref[...], hidden_ref[...], preferred_element_type=jnp.float32)
+    self_ref[...] = jnp.dot(rows_ref[...], ws_ref[...], preferred_element_type=jnp.float32)
+
+
+def own_part(band, hidden, ws, tile):
+    rows, width = hidden.shape
+    own = REACH
+    f32 = jax.ShapeDtypeStruct((rows, width), jnp.float32)
+    return pl.pallas_call(
+        _own_kernel,
+        out_shape=(f32, f32),
+        grid=(rows // tile,),
+        in_specs=[
+            pl.BlockSpec((tile, rows), lambda i: (i, own)),
+            pl.BlockSpec((rows, width), lambda i: (0, 0)),
+            pl.BlockSpec((tile, width), lambda i: (i, 0)),
+            pl.BlockSpec((width, width), lambda i: (0, 0)),
+        ],
+        out_specs=[
+            pl.BlockSpec((tile, width), lambda i: (i, 0)),
+            pl.BlockSpec((tile, width), lambda i: (i, 0)),
+        ],
+        cost_estimate=pl.CostEstimate(
+            flops=2 * rows * rows * width + 2 * rows * width * width,
+            bytes_accessed=rows * rows * 2 + 2 * rows * width * 2 + 2 * rows * width * 4,
+            transcendentals=0,
+        ),
+    )(band, hidden, hidden, ws)
+
+
+def _layer_kernel(band_ref, p0, p1, p3, p4, own_ref, self_ref, degree_ref, wn_ref, out_ref):
+    rows = p0.shape[0]
+    parts = {0: p0, 1: p1, 3: p3, 4: p4}
+    summed = own_ref[...]
     for position in (1, 3, 0, 4):
         summed = summed + jnp.dot(
             band_ref[:, pl.ds(position * rows, rows)],
@@ -44,7 +73,7 @@
             preferred_element_type=jnp.float32,
         )
     neighbour_mean = (summed / degree_ref[...]).astype(jnp.bfloat16)
-    combined = jnp.dot(p2[...], ws_ref[...], preferred_element_type=jnp.float32) + jnp.dot(
+    combined = self_ref[...] + jnp.dot(
         neighbour_mean, wn_ref[...], preferred_element_type=jnp.float32
     )
     active = jnp.maximum(combined, 0.0)
@@ -52,19 +81,33 @@
     out_ref[...] = (active * scale).astype(out_ref.dtype)
 
 
-def run_layer(band, parts, degree_f, ws, wn):
+def run_layer(band, parts, own, own_self, degree_f, wn, tile):
     rows, width = parts[2].shape
+    band_cols = band.shape[1]
+    whole = pl.BlockSpec((rows, width), lambda i: (0, 0))
+    row_tile = pl.BlockSpec((tile, width), lambda i: (i, 0))
     return pl.pallas_call(
         _layer_kernel,
         out_shape=jax.ShapeDtypeStruct((rows, width), jnp.bfloat16),
-        in_specs=[pl.BlockSpec(memory_space=pltpu.VMEM)] * 9,
-        out_specs=pl.BlockSpec(memory_space=pltpu.VMEM),
+        grid=(rows // tile,),
+        in_specs=[
+            pl.BlockSpec((tile, band_cols), lambda i: (i, 0)),
+            whole,
+            whole,
+            whole,
+            whole,
+            row_tile,
+            row_tile,
+            pl.BlockSpec((tile, 1), lambda i: (i, 0)),
+            pl.BlockSpec((width, width), lambda i: (0, 0)),
+        ],
+        out_specs=row_tile,
         cost_estimate=pl.CostEstimate(
-            flops=2 * rows * band.shape[1] * width + 4 * rows * width * width,
-            bytes_accessed=band.size * 2 + 6 * rows * width * 2,
+            flops=2 * rows * (band_cols - rows) * width + 2 * rows * width * width,
+            bytes_accessed=rows * band_cols * 2 + 6 * rows * width * 2 + 2 * rows * width * 4,
             transcendentals=rows,
         ),
-    )(band, *parts, degree_f, ws, wn)
+    )(band, parts[0], parts[1], parts[3], parts[4], own, own_self, degree_f, wn)
 
 
 def body(
@@ -127,9 +170,9 @@
     for level in range(layer_total):
         near = halo(hidden, 1)
         far = halo(hidden, 2)
-        theirs = swap(jnp.concatenate([near, far], axis=0))
-        parts = [far, near, hidden, theirs[:rows_dev], theirs[rows_dev:]]
-        hidden = run_layer(band, parts, degree_f, self_all[level], neighbour_all[level])
+        own, own_self = own_part(band, hidden, self_all[level], block_size)
+        parts = [far, near, hidden, swap(near), swap(far)]
+        hidden = run_layer(band, parts, own, own_self, degree_f, neighbour_all[level], block_size)
         outputs.append(hidden)
 
     stacked = jnp.stack(outputs)

time: 225 us -> 260 us (1.16)
  Pallas kernels: 33.6 us -> 70.5 us
  waiting for transfers between devices: 127 us -> 102 us
  starting transfers between devices: 19.4 us -> 41.3 us
    pallas_call x0 -> x8, Pallas kernels: none -> 30.4 us  [own_part(): pl.pallas_call(_own_kernel, out_shape=(f32, f32), grid=(rows // tile,), i...]
    ppermute x16, waiting for transfers between devices: 105 us -> 79.6 us  [halo(): return lax.ppermute(x, ('section', 'blk'), pairs)]
    ppermute x8 -> x16, starting transfers between devices: 7.38 us -> 24.7 us  [swap(): return lax.ppermute(x, 'section', pairs)]
    ppermute x8 -> x16, waiting for transfers between devices: 8.4 us -> 0.04 us  [swap(): return lax.ppermute(x, 'section', pairs)]
    all_gather x1, waiting for transfers between devices: 0.01 us -> 8.14 us  [body(): lax.all_gather(jnp.stack([self_weight[0], neighbour_weight[0]]), 'section')]
    pallas_call x7, Pallas kernels: 29.8 us -> 36.5 us  [run_layer(): pl.pallas_call(_layer_kernel, out_shape=jax.ShapeDtypeStruct((rows, width...]
    slice x8 -> x0, local copies, waits for them, and re-layouts: 5.8 us -> none  [body(): parts = [far, near, hidden, theirs[:rows_dev], theirs[rows_dev:]]]
    ppermute x16, starting transfers between devices: 9.22 us -> 13.9 us  [halo(): return lax.ppermute(x, ('section', 'blk'), pairs)]
  transfers between devices with their start and end apart: 28 -> 36, of which waited for: 25 -> 17; matrix products, arithmetic and copies ran while one was open for 6% -> 6% of each run, Pallas kernels for 2% -> 13%
where the time goes in v6:
time: 260 us; the launch traced here: 259 us
  waiting for transfers between devices  102 us (39%)
  Pallas kernels  70.5 us (27%)
  starting transfers between devices  41.3 us (16%)
  local copies, waits for them, and re-layouts  23.2 us (9%)
  between operations  14.4 us (6%)
  other arithmetic  7.46 us (3%)
    ppermute x16, waiting for transfers between devices, halo(): return lax.ppermute(x, ('section', 'blk'), pairs)  79.6 us
    pallas_call x7, Pallas kernels, run_layer(): pl.pallas_call(_layer_kernel, out_shape=jax.ShapeDtypeStruct((rows, width...  36.5 us
    pallas_call x8, Pallas kernels, own_part(): pl.pallas_call(_own_kernel, out_shape=(f32, f32), grid=(rows // tile,), i...  30.4 us
    ppermute x16, starting transfers between devices, swap(): return lax.ppermute(x, 'section', pairs)  24.7 us
    ppermute x3, waiting for transfers between devices, body(): arrived.append(lax.ppermute(sending, 'section', pairs))  13.9 us
    ppermute x16, starting transfers between devices, halo(): return lax.ppermute(x, ('section', 'blk'), pairs)  13.9 us
    unnamed x85, local copies, waits for them, and re-layouts  9.7 us
    all_gather x1, waiting for transfers between devices, body(): lax.all_gather(jnp.stack([self_weight[0], neighbour_weight[0]]), 'section')  8.14 us
  transfers between devices with their start and end apart: 36, of which 17 were waited for; matrix products, arithmetic and copies ran while one was open for 6% of the time, Pallas kernels for 13%

profile of v6, /device:TPU:1, one launch (start us, length us, event | category | flops | bytes accessed | tf_op | source)
XLA Modules:
  0.0 258.6 jit_solution(15991160471974716594)
XLA Ops:
  8.4 3.9 %collective-permute-start = (bf16[512,256]{1,0:T(8,128)(2,1)S(1)}, bf16[512,256]{1,0:T(8,128)(2,1)S(1)}, u32[]{:S(2)}, u32[]{:S(2)}) collective-permute-start(bf16[512,256]{1,0:T(8,128)(2,1)S(1)} %dynamic-slice_bitcast_fusion.4.hidden_ref.rows_ref), channel_id=1, source_target_pairs={{0,30},{1,31},{2,0},{3,1},{4,2},{5,3},{6,4},{7,5},{8,6},{9,7},{10,... | collective-permute-start | bytes 786440 | tf_op jit(solution)/shard_map/ppermute | solution.py:141
  27.1 5.9 %collective-permute-start.2 = (bf16[512,256]{1,0:T(8,128)(2,1)S(1)}, bf16[512,256]{1,0:T(8,128)(2,1)S(1)}, u32[]{:S(2)}, u32[]{:S(2)}) collective-permute-start(bf16[512,256]{1,0:T(8,128)(2,1)S(1)} %collective-permute-done.1.p1), channel_id=1, source_target_pairs={{0,32},{32,0},{64,96},{96,64},{128,160},{160,128},{192,224},{224,1... | collective-permute-start | bytes 786440 | tf_op jit(solution)/shard_map/ppermute | solution.py:145
  33.1 8.1 %all-gather.3.cloned.1.call-done = bf16[16,256,256]{2,1,0:T(8,128)(2,1)} async-done(((bf16[2,256,256]{2,1,0:T(8,128)(2,1)}), bf16[16,256,256]{2,1,0:T(8,128)(2,1)}) %all-gather.3.cloned.1.call-update) | async-done | bytes 2097168 | tf_op jit(solution)/shard_map/all_gather | solution.py:127
  44.2 3.8 %shard_map.83 = (f32[512,256]{1,0:T(8,128)}, f32[512,256]{1,0:T(8,128)}) custom-call(bf16[512,2560]{1,0:T(8,128)(2,1)} %shard_map.82.band_ref, bf16[512,256]{1,0:T(8,128)(2,1)} %copy-done.9, bf16[512,256]{1,0:T(8,128)(2,1)} %copy-done.9, bf16[256,256]{1,0:T(8,128)(2,1)} %get-tuple-element.56.ws_ref), custom_call_target="tpu_custom_call" | custom-call | flops 201326592 | bytes 2097152 | tf_op jit(solution)/shard_map/pallas_call | solution.py:43
  48.9 5.2 %shard_map.84.hidden_ref.rows_ref = bf16[512,256]{1,0:T(8,128)(2,1)} custom-call(bf16[512,2560]{1,0:T(8,128)(2,1)} %shard_map.82.band_ref, bf16[512,256]{1,0:T(8,128)(2,1)} %copy-done.13, bf16[512,256]{1,0:T(8,128)(2,1)} %copy-done.14, bf16[512,256]{1,0:T(8,128)(2,1)} %copy-done.15, bf16[512,256]{1,0:T(8,128)(2,1)} %copy-done.16, ...), custom_call_target="tpu_custom_call" | custom-call | flops 603979776 | bytes 5242880 | tf_op jit(solution)/shard_map/pallas_call | solution.py:89
  57.6 5.6 %collective-permute-done.5.p1 = bf16[512,256]{1,0:T(8,128)(2,1)S(1)} collective-permute-done((bf16[512,256]{1,0:T(8,128)(2,1)}, bf16[512,256]{1,0:T(8,128)(2,1)S(1)}, u32[]{:S(2)}, u32[]{:S(2)}) %collective-permute-start.5) | collective-permute-done | bytes 262176 | tf_op jit(solution)/shard_map/ppermute | solution.py:141
  69.7 3.8 %shard_map.85 = (f32[512,256]{1,0:T(8,128)}, f32[512,256]{1,0:T(8,128)}) custom-call(bf16[512,2560]{1,0:T(8,128)(2,1)} %shard_map.82.band_ref, bf16[512,256]{1,0:T(8,128)(2,1)} %shard_map.84.hidden_ref.rows_ref, bf16[512,256]{1,0:T(8,128)(2,1)} %shard_map.84.hidden_ref.rows_ref, bf16[256,256]{1,0:T(8,128)(2,1)} %get-tuple-element.54.ws_ref), custom_call_target="tpu_custom_call" | custom-call | flops 201326592 | bytes 2097152 | tf_op jit(solution)/shard_map/pallas_call | solution.py:43
  74.3 5.2 %shard_map.86.hidden_ref.rows_ref = bf16[512,256]{1,0:T(8,128)(2,1)} custom-call(bf16[512,2560]{1,0:T(8,128)(2,1)} %shard_map.82.band_ref, bf16[512,256]{1,0:T(8,128)(2,1)} %copy-done.22, bf16[512,256]{1,0:T(8,128)(2,1)} %copy-done.17, bf16[512,256]{1,0:T(8,128)(2,1)} %copy-done.28, bf16[512,256]{1,0:T(8,128)(2,1)} %copy-done.34, ...), custom_call_target="tpu_custom_call" | custom-call | flops 603979776 | bytes 5242880 | tf_op jit(solution)/shard_map/pallas_call | solution.py:89
  80.9 7.5 %collective-permute-done.9.p1 = bf16[512,256]{1,0:T(8,128)(2,1)S(1)} collective-permute-done((bf16[512,256]{1,0:T(8,128)(2,1)}, bf16[512,256]{1,0:T(8,128)(2,1)S(1)}, u32[]{:S(2)}, u32[]{:S(2)}) %collective-permute-start.9) | collective-permute-done | bytes 262176 | tf_op jit(solution)/shard_map/ppermute | solution.py:141
  94.7 3.8 %shard_map.87 = (f32[512,256]{1,0:T(8,128)}, f32[512,256]{1,0:T(8,128)}) custom-call(bf16[512,2560]{1,0:T(8,128)(2,1)} %shard_map.82.band_ref, bf16[512,256]{1,0:T(8,128)(2,1)} %shard_map.86.hidden_ref.rows_ref, bf16[512,256]{1,0:T(8,128)(2,1)} %shard_map.86.hidden_ref.rows_ref, bf16[256,256]{1,0:T(8,128)(2,1)} %get-tuple-element.52.ws_ref), custom_call_target="tpu_custom_call" | custom-call | flops 201326592 | bytes 2097152 | tf_op jit(solution)/shard_map/pallas_call | solution.py:43
  99.3 5.2 %shard_map.88.hidden_ref.rows_ref = bf16[512,256]{1,0:T(8,128)(2,1)} custom-call(bf16[512,2560]{1,0:T(8,128)(2,1)} %shard_map.82.band_ref, bf16[512,256]{1,0:T(8,128)(2,1)} %copy-done.23, bf16[512,256]{1,0:T(8,128)(2,1)} %copy-done.18, bf16[512,256]{1,0:T(8,128)(2,1)} %copy-done.29, bf16[512,256]{1,0:T(8,128)(2,1)} %copy-done.35, ...), custom_call_target="tpu_custom_call" | custom-call | flops 603979776 | bytes 5242880 | tf_op jit(solution)/shard_map/pallas_call | solution.py:89
  105.1 8.5 %collective-permute-done.13.p1 = bf16[512,256]{1,0:T(8,128)(2,1)S(1)} collective-permute-done((bf16[512,256]{1,0:T(8,128)(2,1)}, bf16[512,256]{1,0:T(8,128)(2,1)S(1)}, u32[]{:S(2)}, u32[]{:S(2)}) %collective-permute-start.13) | collective-permute-done | bytes 262176 | tf_op jit(solution)/shard_map/ppermute | solution.py:141
  124.5 5.2 %shard_map.90.hidden_ref.rows_ref = bf16[512,256]{1,0:T(8,128)(2,1)} custom-call(bf16[512,2560]{1,0:T(8,128)(2,1)} %shard_map.82.band_ref, bf16[512,256]{1,0:T(8,128)(2,1)} %copy-done.24, bf16[512,256]{1,0:T(8,128)(2,1)} %copy-done.19, bf16[512,256]{1,0:T(8,128)(2,1)} %copy-done.30, bf16[512,256]{1,0:T(8,128)(2,1)} %copy-done.36, ...), custom_call_target="tpu_custom_call" | custom-call | flops 603979776 | bytes 5242880 | tf_op jit(solution)/shard_map/pallas_call | solution.py:89
  130.3 8.4 %collective-permute-done.17.p1 = bf16[512,256]{1,0:T(8,128)(2,1)S(1)} collective-permute-done((bf16[512,256]{1,0:T(8,128)(2,1)}, bf16[512,256]{1,0:T(8,128)(2,1)S(1)}, u32[]{:S(2)}, u32[]{:S(2)}) %collective-permute-start.17) | collective-permute-done | bytes 262176 | tf_op jit(solution)/shard_map/ppermute | solution.py:141
  149.6 5.2 %shard_map.92.hidden_ref.rows_ref = bf16[512,256]{1,0:T(8,128)(2,1)} custom-call(bf16[512,2560]{1,0:T(8,128)(2,1)} %shard_map.82.band_ref, bf16[512,256]{1,0:T(8,128)(2,1)} %copy-done.25, bf16[512,256]{1,0:T(8,128)(2,1)} %copy-done.20, bf16[512,256]{1,0:T(8,128)(2,1)} %copy-done.31, bf16[512,256]{1,0:T(8,128)(2,1)} %copy-done.37, ...), custom_call_target="tpu_custom_call" | custom-call | flops 603979776 | bytes 5242880 | tf_op jit(solution)/shard_map/pallas_call | solution.py:89
  155.4 8.4 %collective-permute-done.21.p1 = bf16[512,256]{1,0:T(8,128)(2,1)S(1)} collective-permute-done((bf16[512,256]{1,0:T(8,128)(2,1)}, bf16[512,256]{1,0:T(8,128)(2,1)S(1)}, u32[]{:S(2)}, u32[]{:S(2)}) %collective-permute-start.21) | collective-permute-done | bytes 262176 | tf_op jit(solution)/shard_map/ppermute | solution.py:141
  174.7 5.3 %shard_map.94.hidden_ref.rows_ref = bf16[512,256]{1,0:T(8,128)(2,1)} custom-call(bf16[512,2560]{1,0:T(8,128)(2,1)} %shard_map.82.band_ref, bf16[512,256]{1,0:T(8,128)(2,1)} %copy-done.26, bf16[512,256]{1,0:T(8,128)(2,1)} %copy-done.21, bf16[512,256]{1,0:T(8,128)(2,1)} %copy-done.32, bf16[512,256]{1,0:T(8,128)(2,1)} %copy-done.38, ...), custom_call_target="tpu_custom_call" | custom-call | flops 603979776 | bytes 5242880 | tf_op jit(solution)/shard_map/pallas_call | solution.py:89
  180.6 8.2 %collective-permute-done.25.p1 = bf16[512,256]{1,0:T(8,128)(2,1)S(1)} collective-permute-done((bf16[512,256]{1,0:T(8,128)(2,1)}, bf16[512,256]{1,0:T(8,128)(2,1)S(1)}, u32[]{:S(2)}, u32[]{:S(2)}) %collective-permute-start.25) | collective-permute-done | bytes 262176 | tf_op jit(solution)/shard_map/ppermute | solution.py:141
  201.2 5.3 %shard_map.96.hidden_ref.rows_ref = bf16[512,256]{1,0:T(8,128)(2,1)} custom-call(bf16[512,2560]{1,0:T(8,128)(2,1)} %shard_map.82.band_ref, bf16[512,256]{1,0:T(8,128)(2,1)} %copy-done.12, bf16[512,256]{1,0:T(8,128)(2,1)} %copy-done.11, bf16[512,256]{1,0:T(8,128)(2,1)} %copy-done.27, bf16[512,256]{1,0:T(8,128)(2,1)} %copy-done.33, ...), custom_call_target="tpu_custom_call" | custom-call | flops 603979776 | bytes 5242880 | tf_op jit(solution)/shard_map/pallas_call | solution.py:89
  208.8 12.3 %collective-permute-done.29 = bf16[512,256]{1,0:T(8,128)(2,1)S(1)} collective-permute-done((bf16[512,256]{1,0:T(8,128)(2,1)}, bf16[512,256]{1,0:T(8,128)(2,1)S(1)}, u32[]{:S(2)}, u32[]{:S(2)}) %collective-permute-start.29) | collective-permute-done | bytes 262176 | tf_op jit(solution)/shard_map/ppermute | solution.py:141
  223.3 3.8 %shard_map.97 = (f32[512,256]{1,0:T(8,128)}, f32[512,256]{1,0:T(8,128)}) custom-call(bf16[512,2560]{1,0:T(8,128)(2,1)} %shard_map.82.band_ref, bf16[512,256]{1,0:T(8,128)(2,1)} %shard_map.96.hidden_ref.rows_ref, bf16[512,256]{1,0:T(8,128)(2,1)} %shard_map.96.hidden_ref.rows_ref, bf16[256,256]{1,0:T(8,128)(2,1)} %get-tuple-element.42.ws_ref), custom_call_target="tpu_custom_call" | custom-call | flops 201326592 | bytes 2097152 | tf_op jit(solution)/shard_map/pallas_call | solution.py:43
  227.8 4.8 %shard_map.98 = bf16[8,512,256]{2,1,0:T(8,128)(2,1)} fusion(bf16[8,512,256]{2,1,0:T(8,128)(2,1)} %bitcast_dynamic-update-slice_fusion.1, bf16[512,2560]{1,0:T(8,128)(2,1)} %shard_map.82.band_ref, bf16[512,256]{1,0:T(8,128)(2,1)S(1)} %collective-permute-done.28, bf16[512,256]{1,0:T(8,128)(2,1)S(1)} %collective-permute-done.29, ...), kind=kCustom, calls=%fused_computation.4 | custom fusion | bytes 5113856 | tf_op jit(solution)/shard_map/pallas_call | solution.py:89
  236.6 4.7 %collective-permute-done.34 = bf16[512,256]{1,0:T(8,128)(2,1)S(1)} collective-permute-done((bf16[512,256]{1,0:T(8,128)(2,1)S(1)}, bf16[512,256]{1,0:T(8,128)(2,1)S(1)}, u32[]{:S(2)}, u32[]{:S(2)}) %collective-permute-start.34) | collective-permute-done | bytes 262176 | tf_op jit(solution)/shard_map/ppermute | solution.py:188
  243.7 6.7 %collective-permute-done.32 = bf16[512,256]{1,0:T(8,128)(2,1)S(1)} collective-permute-done((bf16[512,256]{1,0:T(8,128)(2,1)S(1)}, bf16[512,256]{1,0:T(8,128)(2,1)S(1)}, u32[]{:S(2)}, u32[]{:S(2)}) %collective-permute-start.32) | collective-permute-done | bytes 262176 | tf_op jit(solution)/shard_map/ppermute | solution.py:188
  (164 shorter events, 99.4 us)
Async XLA Ops:
  6.5 34.7 %all-gather.3.cloned.1.call-start = ((), (), s32[]{:S(2)}) async-start(), calls=%async_computation | async-start | bytes 2359296 | tf_op jit(solution)/shard_map/all_gather | solution.py:127
  8.4 24.6 %collective-permute-start = (bf16[512,256]{1,0:T(8,128)(2,1)S(1)}, bf16[512,256]{1,0:T(8,128)(2,1)S(1)}, u32[]{:S(2)}, u32[]{:S(2)}) collective-permute-start(bf16[512,256]{1,0:T(8,128)(2,1)S(1)} %dynamic-slice_bitcast_fusion.4.hidden_ref.rows_ref), channel_id=1, source_target_pairs={{0,30},{1,31},{2,0},{3,1},{4,2},{5,3},{6,4},{7,5},{8,6},{9,7},{10,... | collective-permute-start | bytes 786440 | tf_op jit(solution)/shard_map/ppermute | solution.py:141
  12.3 14.7 %collective-permute-start.1 = (bf16[512,256]{1,0:T(8,128)(2,1)S(1)}, bf16[512,256]{1,0:T(8,128)(2,1)S(1)}, u32[]{:S(2)}, u32[]{:S(2)}) collective-permute-start(bf16[512,256]{1,0:T(8,128)(2,1)S(1)} %dynamic-slice_bitcast_fusion.4.hidden_ref.rows_ref), channel_id=1, source_target_pairs={{0,31},{1,0},{2,1},{3,2},{4,3},{5,4},{6,5},{7,6},{8,7},{9,8},{10,9... | collective-permute-start | bytes 786440 | tf_op jit(solution)/shard_map/ppermute | solution.py:141
  27.1 21.0 %collective-permute-start.2 = (bf16[512,256]{1,0:T(8,128)(2,1)S(1)}, bf16[512,256]{1,0:T(8,128)(2,1)S(1)}, u32[]{:S(2)}, u32[]{:S(2)}) collective-permute-start(bf16[512,256]{1,0:T(8,128)(2,1)S(1)} %collective-permute-done.1.p1), channel_id=1, source_target_pairs={{0,32},{32,0},{64,96},{96,64},{128,160},{160,128},{192,224},{224,1... | collective-permute-start | bytes 786440 | tf_op jit(solution)/shard_map/ppermute | solution.py:145
  33.0 15.1 %collective-permute-start.3 = (bf16[512,256]{1,0:T(8,128)(2,1)S(1)}, bf16[512,256]{1,0:T(8,128)(2,1)S(1)}, u32[]{:S(2)}, u32[]{:S(2)}) collective-permute-start(bf16[512,256]{1,0:T(8,128)(2,1)S(1)} %collective-permute-done.p0), channel_id=1, source_target_pairs={{0,32},{32,0},{64,96},{96,64},{128,160},{160,128},{192,224},{224,1... | collective-permute-start | bytes 786440 | tf_op jit(solution)/shard_map/ppermute | solution.py:145
  54.1 9.2 %collective-permute-start.5 = (bf16[512,256]{1,0:T(8,128)(2,1)}, bf16[512,256]{1,0:T(8,128)(2,1)S(1)}, u32[]{:S(2)}, u32[]{:S(2)}) collective-permute-start(bf16[512,256]{1,0:T(8,128)(2,1)} %shard_map.84.hidden_ref.rows_ref), channel_id=1, source_target_pairs={{0,31},{1,0},{2,1},{3,2},{4,3},{5,4},{6,5},{7,6},{8,7},{9,8},{10,9... | collective-permute-start | bytes 786440 | tf_op jit(solution)/shard_map/ppermute | solution.py:141
  55.3 12.8 %collective-permute-start.4 = (bf16[512,256]{1,0:T(8,128)(2,1)}, bf16[512,256]{1,0:T(8,128)(2,1)S(1)}, u32[]{:S(2)}, u32[]{:S(2)}) collective-permute-start(bf16[512,256]{1,0:T(8,128)(2,1)} %shard_map.84.hidden_ref.rows_ref), channel_id=1, source_target_pairs={{0,30},{1,31},{2,0},{3,1},{4,2},{5,3},{6,4},{7,5},{8,6},{9,7},{10,... | collective-permute-start | bytes 786440 | tf_op jit(solution)/shard_map/ppermute | solution.py:141
  63.2 10.2 %collective-permute-start.6 = (bf16[512,256]{1,0:T(8,128)(2,1)S(1)}, bf16[512,256]{1,0:T(8,128)(2,1)S(1)}, u32[]{:S(2)}, u32[]{:S(2)}) collective-permute-start(bf16[512,256]{1,0:T(8,128)(2,1)S(1)} %collective-permute-done.5.p1), channel_id=1, source_target_pairs={{0,32},{32,0},{64,96},{96,64},{128,160},{160,128},{192,224},{224,1... | collective-permute-start | bytes 786440 | tf_op jit(solution)/shard_map/ppermute | solution.py:145
  80.0 12.7 %collective-permute-start.8 = (bf16[512,256]{1,0:T(8,128)(2,1)}, bf16[512,256]{1,0:T(8,128)(2,1)S(1)}, u32[]{:S(2)}, u32[]{:S(2)}) collective-permute-start(bf16[512,256]{1,0:T(8,128)(2,1)} %shard_map.86.hidden_ref.rows_ref), channel_id=1, source_target_pairs={{0,30},{1,31},{2,0},{3,1},{4,2},{5,3},{6,4},{7,5},{8,6},{9,7},{10,... | collective-permute-start | bytes 786440 | tf_op jit(solution)/shard_map/ppermute | solution.py:141
  88.4 10.1 %collective-permute-start.10 = (bf16[512,256]{1,0:T(8,128)(2,1)S(1)}, bf16[512,256]{1,0:T(8,128)(2,1)S(1)}, u32[]{:S(2)}, u32[]{:S(2)}) collective-permute-start(bf16[512,256]{1,0:T(8,128)(2,1)S(1)} %collective-permute-done.9.p1), channel_id=1, source_target_pairs={{0,32},{32,0},{64,96},{96,64},{128,160},{160,128},{192,224},{224,1... | collective-permute-start | bytes 786440 | tf_op jit(solution)/shard_map/ppermute | solution.py:145
  104.5 9.1 %collective-permute-start.13 = (bf16[512,256]{1,0:T(8,128)(2,1)}, bf16[512,256]{1,0:T(8,128)(2,1)S(1)}, u32[]{:S(2)}, u32[]{:S(2)}) collective-permute-start(bf16[512,256]{1,0:T(8,128)(2,1)} %shard_map.88.hidden_ref.rows_ref), channel_id=1, source_target_pairs={{0,31},{1,0},{2,1},{3,2},{4,3},{5,4},{6,5},{7,6},{8,7},{9,8},{10,9... | collective-permute-start | bytes 786440 | tf_op jit(solution)/shard_map/ppermute | solution.py:141
  105.1 12.6 %collective-permute-start.12 = (bf16[512,256]{1,0:T(8,128)(2,1)}, bf16[512,256]{1,0:T(8,128)(2,1)S(1)}, u32[]{:S(2)}, u32[]{:S(2)}) collective-permute-start(bf16[512,256]{1,0:T(8,128)(2,1)} %shard_map.88.hidden_ref.rows_ref), channel_id=1, source_target_pairs={{0,30},{1,31},{2,0},{3,1},{4,2},{5,3},{6,4},{7,5},{8,6},{9,7},{10,... | collective-permute-start | bytes 786440 | tf_op jit(solution)/shard_map/ppermute | solution.py:141
  113.6 10.1 %collective-permute-start.14 = (bf16[512,256]{1,0:T(8,128)(2,1)S(1)}, bf16[512,256]{1,0:T(8,128)(2,1)S(1)}, u32[]{:S(2)}, u32[]{:S(2)}) collective-permute-start(bf16[512,256]{1,0:T(8,128)(2,1)S(1)} %collective-permute-done.13.p1), channel_id=1, source_target_pairs={{0,32},{32,0},{64,96},{96,64},{128,160},{160,128},{192,224},{224,1... | collective-permute-start | bytes 786440 | tf_op jit(solution)/shard_map/ppermute | solution.py:145
  129.7 9.0 %collective-permute-start.17 = (bf16[512,256]{1,0:T(8,128)(2,1)}, bf16[512,256]{1,0:T(8,128)(2,1)S(1)}, u32[]{:S(2)}, u32[]{:S(2)}) collective-permute-start(bf16[512,256]{1,0:T(8,128)(2,1)} %shard_map.90.hidden_ref.rows_ref), channel_id=1, source_target_pairs={{0,31},{1,0},{2,1},{3,2},{4,3},{5,4},{6,5},{7,6},{8,7},{9,8},{10,9... | collective-permute-start | bytes 786440 | tf_op jit(solution)/shard_map/ppermute | solution.py:141
  130.3 12.5 %collective-permute-start.16 = (bf16[512,256]{1,0:T(8,128)(2,1)}, bf16[512,256]{1,0:T(8,128)(2,1)S(1)}, u32[]{:S(2)}, u32[]{:S(2)}) collective-permute-start(bf16[512,256]{1,0:T(8,128)(2,1)} %shard_map.90.hidden_ref.rows_ref), channel_id=1, source_target_pairs={{0,30},{1,31},{2,0},{3,1},{4,2},{5,3},{6,4},{7,5},{8,6},{9,7},{10,... | collective-permute-start | bytes 786440 | tf_op jit(solution)/shard_map/ppermute | solution.py:141
  138.7 10.1 %collective-permute-start.18 = (bf16[512,256]{1,0:T(8,128)(2,1)S(1)}, bf16[512,256]{1,0:T(8,128)(2,1)S(1)}, u32[]{:S(2)}, u32[]{:S(2)}) collective-permute-start(bf16[512,256]{1,0:T(8,128)(2,1)S(1)} %collective-permute-done.17.p1), channel_id=1, source_target_pairs={{0,32},{32,0},{64,96},{96,64},{128,160},{160,128},{192,224},{224,1... | collective-permute-start | bytes 786440 | tf_op jit(solution)/shard_map/ppermute | solution.py:145
  154.8 9.1 %collective-permute-start.21 = (bf16[512,256]{1,0:T(8,128)(2,1)}, bf16[512,256]{1,0:T(8,128)(2,1)S(1)}, u32[]{:S(2)}, u32[]{:S(2)}) collective-permute-start(bf16[512,256]{1,0:T(8,128)(2,1)} %shard_map.92.hidden_ref.rows_ref), channel_id=1, source_target_pairs={{0,31},{1,0},{2,1},{3,2},{4,3},{5,4},{6,5},{7,6},{8,7},{9,8},{10,9... | collective-permute-start | bytes 786440 | tf_op jit(solution)/shard_map/ppermute | solution.py:141
  155.4 12.5 %collective-permute-start.20 = (bf16[512,256]{1,0:T(8,128)(2,1)}, bf16[512,256]{1,0:T(8,128)(2,1)S(1)}, u32[]{:S(2)}, u32[]{:S(2)}) collective-permute-start(bf16[512,256]{1,0:T(8,128)(2,1)} %shard_map.92.hidden_ref.rows_ref), channel_id=1, source_target_pairs={{0,30},{1,31},{2,0},{3,1},{4,2},{5,3},{6,4},{7,5},{8,6},{9,7},{10,... | collective-permute-start | bytes 786440 | tf_op jit(solution)/shard_map/ppermute | solution.py:141
  163.8 10.1 %collective-permute-start.22 = (bf16[512,256]{1,0:T(8,128)(2,1)S(1)}, bf16[512,256]{1,0:T(8,128)(2,1)S(1)}, u32[]{:S(2)}, u32[]{:S(2)}) collective-permute-start(bf16[512,256]{1,0:T(8,128)(2,1)S(1)} %collective-permute-done.21.p1), channel_id=1, source_target_pairs={{0,32},{32,0},{64,96},{96,64},{128,160},{160,128},{192,224},{224,1... | collective-permute-start | bytes 786440 | tf_op jit(solution)/shard_map/ppermute | solution.py:145
  180.6 12.5 %collective-permute-start.24 = (bf16[512,256]{1,0:T(8,128)(2,1)}, bf16[512,256]{1,0:T(8,128)(2,1)S(1)}, u32[]{:S(2)}, u32[]{:S(2)}) collective-permute-start(bf16[512,256]{1,0:T(8,128)(2,1)} %shard_map.94.hidden_ref.rows_ref), channel_id=1, source_target_pairs={{0,30},{1,31},{2,0},{3,1},{4,2},{5,3},{6,4},{7,5},{8,6},{9,7},{10,... | collective-permute-start | bytes 786440 | tf_op jit(solution)/shard_map/ppermute | solution.py:141
  188.9 11.5 %collective-permute-start.26 = (bf16[512,256]{1,0:T(8,128)(2,1)S(1)}, bf16[512,256]{1,0:T(8,128)(2,1)S(1)}, u32[]{:S(2)}, u32[]{:S(2)}) collective-permute-start(bf16[512,256]{1,0:T(8,128)(2,1)S(1)} %collective-permute-done.25.p1), channel_id=1, source_target_pairs={{0,32},{32,0},{64,96},{96,64},{128,160},{160,128},{192,224},{224,1... | collective-permute-start | bytes 786440 | tf_op jit(solution)/shard_map/ppermute | solution.py:145
  206.5 16.1 %collective-permute-start.28 = (bf16[512,256]{1,0:T(8,128)(2,1)}, bf16[512,256]{1,0:T(8,128)(2,1)S(1)}, u32[]{:S(2)}, u32[]{:S(2)}) collective-permute-start(bf16[512,256]{1,0:T(8,128)(2,1)} %shard_map.96.hidden_ref.rows_ref), channel_id=1, source_target_pairs={{0,30},{1,31},{2,0},{3,1},{4,2},{5,3},{6,4},{7,5},{8,6},{9,7},{10,... | collective-permute-start | bytes 786440 | tf_op jit(solution)/shard_map/ppermute | solution.py:141
  206.5 14.6 %collective-permute-start.29 = (bf16[512,256]{1,0:T(8,128)(2,1)}, bf16[512,256]{1,0:T(8,128)(2,1)S(1)}, u32[]{:S(2)}, u32[]{:S(2)}) collective-permute-start(bf16[512,256]{1,0:T(8,128)(2,1)} %shard_map.96.hidden_ref.rows_ref), channel_id=1, source_target_pairs={{0,31},{1,0},{2,1},{3,2},{4,3},{5,4},{6,5},{7,6},{8,7},{9,8},{10,9... | collective-permute-start | bytes 786440 | tf_op jit(solution)/shard_map/ppermute | solution.py:141
  235.8 14.6 %collective-permute-start.32 = (bf16[512,256]{1,0:T(8,128)(2,1)S(1)}, bf16[512,256]{1,0:T(8,128)(2,1)S(1)}, u32[]{:S(2)}, u32[]{:S(2)}) collective-permute-start(bf16[512,256]{1,0:T(8,128)(2,1)S(1)} %get-tuple-element.40), channel_id=1, source_target_pairs={{0,64},{32,96},{64,128},{96,160},{128,192},{160,224},{192,0},{224,... | collective-permute-start | bytes 786440 | tf_op jit(solution)/shard_map/ppermute | solution.py:188
  (51 other events, 357.0 us)
Sparse Core Ops, SparseCore 0:
  9.2 31.9 all-gather.2

commit v7 on v5

--- a/solution.py
+++ b/solution.py
@@ -127,8 +127,7 @@
     for level in range(layer_total):
         near = halo(hidden, 1)
         far = halo(hidden, 2)
-        theirs = swap(jnp.concatenate([near, far], axis=0))
-        parts = [far, near, hidden, theirs[:rows_dev], theirs[rows_dev:]]
+        parts = [far, near, hidden, swap(near), swap(far)]
         hidden = run_layer(band, parts, degree_f, self_all[level], neighbour_all[level])
         outputs.append(hidden)
 

time: 225 us -> 226 us (level)
  starting transfers between devices: 19.4 us -> 46.7 us
  waiting for transfers between devices: 127 us -> 102 us
    ppermute x16, waiting for transfers between devices: 105 us -> 76.1 us  [halo(): return lax.ppermute(x, ('section', 'blk'), pairs)]
    ppermute x8 -> x16, starting transfers between devices: 7.38 us -> 29.2 us  [swap(): return lax.ppermute(x, 'section', pairs)]
    all_gather x1, waiting for transfers between devices: 0.01 us -> 7.98 us  [body(): lax.all_gather(jnp.stack([self_weight[0], neighbour_weight[0]]), 'section')]
    slice x8 -> x0, local copies, waits for them, and re-layouts: 5.8 us -> none  [body(): parts = [far, near, hidden, theirs[:rows_dev], theirs[rows_dev:]]]
    ppermute x16, starting transfers between devices: 9.22 us -> 13.6 us  [halo(): return lax.ppermute(x, ('section', 'blk'), pairs)]
    unnamed x57 -> x85, local copies, waits for them, and re-layouts: 5.12 us -> 8.99 us
    ppermute x3, waiting for transfers between devices: 14 us -> 11.1 us  [body(): arrived.append(lax.ppermute(sending, 'section', pairs))]
    ppermute x8 -> x16, waiting for transfers between devices: 8.4 us -> 6.88 us  [swap(): return lax.ppermute(x, 'section', pairs)]
  transfers between devices with their start and end apart: 28 -> 36, of which waited for: 25 -> 24; matrix products, arithmetic and copies ran while one was open for 6% -> 7% of each run, Pallas kernels for 2% -> 2%
where the time goes in v7:
time: 226 us
  waiting for transfers between devices  102 us (45%)
  starting transfers between devices  46.7 us (21%)
  Pallas kernels  33.5 us (15%)
  local copies, waits for them, and re-layouts  21.5 us (10%)
  between operations  14.3 us (6%)
  other arithmetic  7.45 us (3%)
    ppermute x16, waiting for transfers between devices, halo(): return lax.ppermute(x, ('section', 'blk'), pairs)  76.1 us
    pallas_call x7, Pallas kernels, run_layer(): pl.pallas_call(_layer_kernel, out_shape=jax.ShapeDtypeStruct((rows, width...  29.8 us
    ppermute x16, starting transfers between devices, swap(): return lax.ppermute(x, 'section', pairs)  29.2 us
    ppermute x16, starting transfers between devices, halo(): return lax.ppermute(x, ('section', 'blk'), pairs)  13.6 us
    ppermute x3, waiting for transfers between devices, body(): arrived.append(lax.ppermute(sending, 'section', pairs))  11.1 us
    unnamed x85, local copies, waits for them, and re-layouts  8.99 us
    all_gather x1, waiting for transfers between devices, body(): lax.all_gather(jnp.stack([self_weight[0], neighbour_weight[0]]), 'section')  7.98 us
    ppermute x16, waiting for transfers between devices, swap(): return lax.ppermute(x, 'section', pairs)  6.88 us
  transfers between devices with their start and end apart: 36, of which 24 were waited for; matrix products, arithmetic and copies ran while one was open for 7% of the time, Pallas kernels for 2%

profile of v7, /device:TPU:1, one launch (start us, length us, event | category | flops | bytes accessed | tf_op | source)
XLA Modules:
  0.0 225.6 jit_solution(10596168557434490219)
XLA Ops:
  19.9 3.6 %dynamic-slice_bitcast_fusion.values_ref = bf16[80,128,128]{2,1,0:T(8,128)(2,1)} fusion(bf16[4,80,128,128]{3,2,1,0:T(8,128)(2,1)} %param.9, s32[]{:T(128)S(6)} %select_n.106), kind=kLoop, calls=%fused_computation | loop fusion | bytes 5242884 | tf_op jit(solution)/shard_map/jit(dynamic_index_in_dim)/squeeze | solution.py:104
  23.5 3.7 %shard_map.82.band_ref = bf16[512,2560]{1,0:T(8,128)(2,1)} custom-call(s32[80]{0:T(128)} %fusion.7.rows_ref, s32[80]{0:T(128)} %fusion.8.cols_ref, s32[1]{0:T(128)} %bitcast.2.count_ref, bf16[80,128,128]{2,1,0:T(8,128)(2,1)} %dynamic-slice_bitcast_fusion.values_ref), custom_call_target="tpu_custom_call" | custom-call | tf_op jit(solution)/shard_map/pallas_call | solution.py:25
  27.2 5.9 %collective-permute-start.2 = (bf16[512,256]{1,0:T(8,128)(2,1)S(1)}, bf16[512,256]{1,0:T(8,128)(2,1)S(1)}, u32[]{:S(2)}, u32[]{:S(2)}) collective-permute-start(bf16[512,256]{1,0:T(8,128)(2,1)S(1)} %collective-permute-done.1.p1), channel_id=1, source_target_pairs={{0,32},{32,0},{64,96},{96,64},{128,160},{160,128},{192,224},{224,1... | collective-permute-start | bytes 786440 | tf_op jit(solution)/shard_map/ppermute | solution.py:102
  33.3 8.0 %all-gather.3.cloned.1.call-done = bf16[16,256,256]{2,1,0:T(8,128)(2,1)} async-done(((bf16[2,256,256]{2,1,0:T(8,128)(2,1)}), bf16[16,256,256]{2,1,0:T(8,128)(2,1)}) %all-gather.3.cloned.1.call-update) | async-done | bytes 2097168 | tf_op jit(solution)/shard_map/all_gather | solution.py:84
  45.0 4.2 %shard_map.83.p2 = bf16[512,256]{1,0:T(8,128)(2,1)} custom-call(bf16[512,2560]{1,0:T(8,128)(2,1)} %shard_map.82.band_ref, bf16[512,256]{1,0:T(8,128)(2,1)} %copy-done.14, bf16[512,256]{1,0:T(8,128)(2,1)} %copy-done.13, bf16[512,256]{1,0:T(8,128)(2,1)} %copy-done.9, bf16[512,256]{1,0:T(8,128)(2,1)} %copy-done.15, bf16[512,256]{1,0:T(8,128)(2,1)} %copy-done.16, ...), custom_call_target="tpu_custom_call" | custom-call | flops 805306368 | bytes 4194304 | tf_op jit(solution)/shard_map/pallas_call | solution.py:57
  52.8 5.6 %collective-permute-done.5.p1 = bf16[512,256]{1,0:T(8,128)(2,1)S(1)} collective-permute-done((bf16[512,256]{1,0:T(8,128)(2,1)}, bf16[512,256]{1,0:T(8,128)(2,1)S(1)}, u32[]{:S(2)}, u32[]{:S(2)}) %collective-permute-start.5) | collective-permute-done | bytes 262176 | tf_op jit(solution)/shard_map/ppermute | solution.py:98
  66.7 4.2 %shard_map.84.p2 = bf16[512,256]{1,0:T(8,128)(2,1)} custom-call(bf16[512,2560]{1,0:T(8,128)(2,1)} %shard_map.82.band_ref, bf16[512,256]{1,0:T(8,128)(2,1)} %copy-done.22, bf16[512,256]{1,0:T(8,128)(2,1)} %copy-done.17, bf16[512,256]{1,0:T(8,128)(2,1)} %shard_map.83.p2, bf16[512,256]{1,0:T(8,128)(2,1)} %copy-done.28, bf16[512,256]{1,0:T(8,128)(2,1)} %copy-done.34, ...), custom_call_target="tpu_custom_call" | custom-call | flops 805306368 | bytes 4194304 | tf_op jit(solution)/shard_map/pallas_call | solution.py:57
  72.3 7.6 %collective-permute-done.9.p1 = bf16[512,256]{1,0:T(8,128)(2,1)S(1)} collective-permute-done((bf16[512,256]{1,0:T(8,128)(2,1)}, bf16[512,256]{1,0:T(8,128)(2,1)S(1)}, u32[]{:S(2)}, u32[]{:S(2)}) %collective-permute-start.9) | collective-permute-done | bytes 262176 | tf_op jit(solution)/shard_map/ppermute | solution.py:98
  80.8 3.4 %collective-permute-done.8.p0 = bf16[512,256]{1,0:T(8,128)(2,1)S(1)} collective-permute-done((bf16[512,256]{1,0:T(8,128)(2,1)}, bf16[512,256]{1,0:T(8,128)(2,1)S(1)}, u32[]{:S(2)}, u32[]{:S(2)}) %collective-permute-start.8) | collective-permute-done | bytes 262176 | tf_op jit(solution)/shard_map/ppermute | solution.py:98
  88.3 4.2 %shard_map.85.p2 = bf16[512,256]{1,0:T(8,128)(2,1)} custom-call(bf16[512,2560]{1,0:T(8,128)(2,1)} %shard_map.82.band_ref, bf16[512,256]{1,0:T(8,128)(2,1)} %copy-done.23, bf16[512,256]{1,0:T(8,128)(2,1)} %copy-done.18, bf16[512,256]{1,0:T(8,128)(2,1)} %shard_map.84.p2, bf16[512,256]{1,0:T(8,128)(2,1)} %copy-done.29, bf16[512,256]{1,0:T(8,128)(2,1)} %copy-done.35, ...), custom_call_target="tpu_custom_call" | custom-call | flops 805306368 | bytes 4194304 | tf_op jit(solution)/shard_map/pallas_call | solution.py:57
  93.1 8.4 %collective-permute-done.13.p1 = bf16[512,256]{1,0:T(8,128)(2,1)S(1)} collective-permute-done((bf16[512,256]{1,0:T(8,128)(2,1)}, bf16[512,256]{1,0:T(8,128)(2,1)S(1)}, u32[]{:S(2)}, u32[]{:S(2)}) %collective-permute-start.13) | collective-permute-done | bytes 262176 | tf_op jit(solution)/shard_map/ppermute | solution.py:98
  110.0 4.2 %shard_map.86.p2 = bf16[512,256]{1,0:T(8,128)(2,1)} custom-call(bf16[512,2560]{1,0:T(8,128)(2,1)} %shard_map.82.band_ref, bf16[512,256]{1,0:T(8,128)(2,1)} %copy-done.24, bf16[512,256]{1,0:T(8,128)(2,1)} %copy-done.19, bf16[512,256]{1,0:T(8,128)(2,1)} %shard_map.85.p2, bf16[512,256]{1,0:T(8,128)(2,1)} %copy-done.30, bf16[512,256]{1,0:T(8,128)(2,1)} %copy-done.36, ...), custom_call_target="tpu_custom_call" | custom-call | flops 805306368 | bytes 4194304 | tf_op jit(solution)/shard_map/pallas_call | solution.py:57
  114.9 8.4 %collective-permute-done.17.p1 = bf16[512,256]{1,0:T(8,128)(2,1)S(1)} collective-permute-done((bf16[512,256]{1,0:T(8,128)(2,1)}, bf16[512,256]{1,0:T(8,128)(2,1)S(1)}, u32[]{:S(2)}, u32[]{:S(2)}) %collective-permute-start.17) | collective-permute-done | bytes 262176 | tf_op jit(solution)/shard_map/ppermute | solution.py:98
  131.6 4.2 %shard_map.87.p2 = bf16[512,256]{1,0:T(8,128)(2,1)} custom-call(bf16[512,2560]{1,0:T(8,128)(2,1)} %shard_map.82.band_ref, bf16[512,256]{1,0:T(8,128)(2,1)} %copy-done.25, bf16[512,256]{1,0:T(8,128)(2,1)} %copy-done.20, bf16[512,256]{1,0:T(8,128)(2,1)} %shard_map.86.p2, bf16[512,256]{1,0:T(8,128)(2,1)} %copy-done.31, bf16[512,256]{1,0:T(8,128)(2,1)} %copy-done.37, ...), custom_call_target="tpu_custom_call" | custom-call | flops 805306368 | bytes 4194304 | tf_op jit(solution)/shard_map/pallas_call | solution.py:57
  136.5 8.3 %collective-permute-done.21.p1 = bf16[512,256]{1,0:T(8,128)(2,1)S(1)} collective-permute-done((bf16[512,256]{1,0:T(8,128)(2,1)}, bf16[512,256]{1,0:T(8,128)(2,1)S(1)}, u32[]{:S(2)}, u32[]{:S(2)}) %collective-permute-start.21) | collective-permute-done | bytes 262176 | tf_op jit(solution)/shard_map/ppermute | solution.py:98
  145.7 3.4 %collective-permute-done.20.p0 = bf16[512,256]{1,0:T(8,128)(2,1)S(1)} collective-permute-done((bf16[512,256]{1,0:T(8,128)(2,1)}, bf16[512,256]{1,0:T(8,128)(2,1)S(1)}, u32[]{:S(2)}, u32[]{:S(2)}) %collective-permute-start.20) | collective-permute-done | bytes 262176 | tf_op jit(solution)/shard_map/ppermute | solution.py:98
  153.2 4.3 %shard_map.88.p2 = bf16[512,256]{1,0:T(8,128)(2,1)} custom-call(bf16[512,2560]{1,0:T(8,128)(2,1)} %shard_map.82.band_ref, bf16[512,256]{1,0:T(8,128)(2,1)} %copy-done.26, bf16[512,256]{1,0:T(8,128)(2,1)} %copy-done.21, bf16[512,256]{1,0:T(8,128)(2,1)} %shard_map.87.p2, bf16[512,256]{1,0:T(8,128)(2,1)} %copy-done.32, bf16[512,256]{1,0:T(8,128)(2,1)} %copy-done.38, ...), custom_call_target="tpu_custom_call" | custom-call | flops 805306368 | bytes 4194304 | tf_op jit(solution)/shard_map/pallas_call | solution.py:57
  158.2 8.3 %collective-permute-done.25.p1 = bf16[512,256]{1,0:T(8,128)(2,1)S(1)} collective-permute-done((bf16[512,256]{1,0:T(8,128)(2,1)}, bf16[512,256]{1,0:T(8,128)(2,1)S(1)}, u32[]{:S(2)}, u32[]{:S(2)}) %collective-permute-start.25) | collective-permute-done | bytes 262176 | tf_op jit(solution)/shard_map/ppermute | solution.py:98
  174.9 4.3 %shard_map.89 = bf16[512,256]{1,0:T(8,128)(2,1)} custom-call(bf16[512,2560]{1,0:T(8,128)(2,1)} %shard_map.82.band_ref, bf16[512,256]{1,0:T(8,128)(2,1)} %copy-done.12, bf16[512,256]{1,0:T(8,128)(2,1)} %copy-done.11, bf16[512,256]{1,0:T(8,128)(2,1)} %shard_map.88.p2, bf16[512,256]{1,0:T(8,128)(2,1)} %copy-done.27, bf16[512,256]{1,0:T(8,128)(2,1)} %copy-done.33, ...), custom_call_target="tpu_custom_call" | custom-call | flops 805306368 | bytes 4194304 | tf_op jit(solution)/shard_map/pallas_call | solution.py:57
  181.4 7.0 %collective-permute-done.29 = bf16[512,256]{1,0:T(8,128)(2,1)S(1)} collective-permute-done((bf16[512,256]{1,0:T(8,128)(2,1)}, bf16[512,256]{1,0:T(8,128)(2,1)S(1)}, u32[]{:S(2)}, u32[]{:S(2)}) %collective-permute-start.29) | collective-permute-done | bytes 262176 | tf_op jit(solution)/shard_map/ppermute | solution.py:98
  189.2 3.4 %collective-permute-done.28 = bf16[512,256]{1,0:T(8,128)(2,1)S(1)} collective-permute-done((bf16[512,256]{1,0:T(8,128)(2,1)}, bf16[512,256]{1,0:T(8,128)(2,1)S(1)}, u32[]{:S(2)}, u32[]{:S(2)}) %collective-permute-start.28) | collective-permute-done | bytes 262176 | tf_op jit(solution)/shard_map/ppermute | solution.py:98
  197.3 3.8 %shard_map.90 = bf16[8,512,256]{2,1,0:T(8,128)(2,1)} fusion(bf16[8,512,256]{2,1,0:T(8,128)(2,1)} %bitcast_dynamic-update-slice_fusion.1, bf16[512,2560]{1,0:T(8,128)(2,1)} %shard_map.82.band_ref, bf16[512,256]{1,0:T(8,128)(2,1)S(1)} %collective-permute-done.28, bf16[512,256]{1,0:T(8,128)(2,1)S(1)} %collective-permute-done.29, ...), kind=kCustom, calls=%fused_computation.4 | custom fusion | bytes 4458496 | tf_op jit(solution)/shard_map/pallas_call | solution.py:57
  206.3 5.4 %collective-permute-done.32 = bf16[512,256]{1,0:T(8,128)(2,1)S(1)} collective-permute-done((bf16[512,256]{1,0:T(8,128)(2,1)S(1)}, bf16[512,256]{1,0:T(8,128)(2,1)S(1)}, u32[]{:S(2)}, u32[]{:S(2)}) %collective-permute-start.32) | collective-permute-done | bytes 262176 | tf_op jit(solution)/shard_map/ppermute | solution.py:144
  211.7 5.1 %collective-permute-done.33 = bf16[512,256]{1,0:T(8,128)(2,1)S(1)} collective-permute-done((bf16[512,256]{1,0:T(8,128)(2,1)S(1)}, bf16[512,256]{1,0:T(8,128)(2,1)S(1)}, u32[]{:S(2)}, u32[]{:S(2)}) %collective-permute-start.33) | collective-permute-done | bytes 262176 | tf_op jit(solution)/shard_map/ppermute | solution.py:144
  (156 shorter events, 82.3 us)
Async XLA Ops:
  6.5 34.7 %all-gather.3.cloned.1.call-start = ((), (), s32[]{:S(2)}) async-start(), calls=%async_computation | async-start | bytes 2359296 | tf_op jit(solution)/shard_map/all_gather | solution.py:84
  8.4 18.8 %collective-permute-start.1 = (bf16[512,256]{1,0:T(8,128)(2,1)S(1)}, bf16[512,256]{1,0:T(8,128)(2,1)S(1)}, u32[]{:S(2)}, u32[]{:S(2)}) collective-permute-start(bf16[512,256]{1,0:T(8,128)(2,1)S(1)} %dynamic-slice_bitcast_fusion.4.p2), channel_id=1, source_target_pairs={{0,31},{1,0},{2,1},{3,2},{4,3},{5,4},{6,5},{7,6},{8,7},{9,8},{10,9... | collective-permute-start | bytes 786440 | tf_op jit(solution)/shard_map/ppermute | solution.py:98
  11.0 22.2 %collective-permute-start = (bf16[512,256]{1,0:T(8,128)(2,1)S(1)}, bf16[512,256]{1,0:T(8,128)(2,1)S(1)}, u32[]{:S(2)}, u32[]{:S(2)}) collective-permute-start(bf16[512,256]{1,0:T(8,128)(2,1)S(1)} %dynamic-slice_bitcast_fusion.4.p2), channel_id=1, source_target_pairs={{0,30},{1,31},{2,0},{3,1},{4,2},{5,3},{6,4},{7,5},{8,6},{9,7},{10,... | collective-permute-start | bytes 786440 | tf_op jit(solution)/shard_map/ppermute | solution.py:98
  27.2 17.0 %collective-permute-start.2 = (bf16[512,256]{1,0:T(8,128)(2,1)S(1)}, bf16[512,256]{1,0:T(8,128)(2,1)S(1)}, u32[]{:S(2)}, u32[]{:S(2)}) collective-permute-start(bf16[512,256]{1,0:T(8,128)(2,1)S(1)} %collective-permute-done.1.p1), channel_id=1, source_target_pairs={{0,32},{32,0},{64,96},{96,64},{128,160},{160,128},{192,224},{224,1... | collective-permute-start | bytes 786440 | tf_op jit(solution)/shard_map/ppermute | solution.py:102
  33.1 11.0 %collective-permute-start.3 = (bf16[512,256]{1,0:T(8,128)(2,1)S(1)}, bf16[512,256]{1,0:T(8,128)(2,1)S(1)}, u32[]{:S(2)}, u32[]{:S(2)}) collective-permute-start(bf16[512,256]{1,0:T(8,128)(2,1)S(1)} %collective-permute-done.p0), channel_id=1, source_target_pairs={{0,32},{32,0},{64,96},{96,64},{128,160},{160,128},{192,224},{224,1... | collective-permute-start | bytes 786440 | tf_op jit(solution)/shard_map/ppermute | solution.py:102
  49.2 9.2 %collective-permute-start.5 = (bf16[512,256]{1,0:T(8,128)(2,1)}, bf16[512,256]{1,0:T(8,128)(2,1)S(1)}, u32[]{:S(2)}, u32[]{:S(2)}) collective-permute-start(bf16[512,256]{1,0:T(8,128)(2,1)} %shard_map.83.p2), channel_id=1, source_target_pairs={{0,31},{1,0},{2,1},{3,2},{4,3},{5,4},{6,5},{7,6},{8,7},{9,8},{10,9... | collective-permute-start | bytes 786440 | tf_op jit(solution)/shard_map/ppermute | solution.py:98
  50.5 12.8 %collective-permute-start.4 = (bf16[512,256]{1,0:T(8,128)(2,1)}, bf16[512,256]{1,0:T(8,128)(2,1)S(1)}, u32[]{:S(2)}, u32[]{:S(2)}) collective-permute-start(bf16[512,256]{1,0:T(8,128)(2,1)} %shard_map.83.p2), channel_id=1, source_target_pairs={{0,30},{1,31},{2,0},{3,1},{4,2},{5,3},{6,4},{7,5},{8,6},{9,7},{10,... | collective-permute-start | bytes 786440 | tf_op jit(solution)/shard_map/ppermute | solution.py:98
  70.9 8.9 %collective-permute-start.9 = (bf16[512,256]{1,0:T(8,128)(2,1)}, bf16[512,256]{1,0:T(8,128)(2,1)S(1)}, u32[]{:S(2)}, u32[]{:S(2)}) collective-permute-start(bf16[512,256]{1,0:T(8,128)(2,1)} %shard_map.84.p2), channel_id=1, source_target_pairs={{0,31},{1,0},{2,1},{3,2},{4,3},{5,4},{6,5},{7,6},{8,7},{9,8},{10,9... | collective-permute-start | bytes 786440 | tf_op jit(solution)/shard_map/ppermute | solution.py:98
  71.7 12.4 %collective-permute-start.8 = (bf16[512,256]{1,0:T(8,128)(2,1)}, bf16[512,256]{1,0:T(8,128)(2,1)S(1)}, u32[]{:S(2)}, u32[]{:S(2)}) collective-permute-start(bf16[512,256]{1,0:T(8,128)(2,1)} %shard_map.84.p2), channel_id=1, source_target_pairs={{0,30},{1,31},{2,0},{3,1},{4,2},{5,3},{6,4},{7,5},{8,6},{9,7},{10,... | collective-permute-start | bytes 786440 | tf_op jit(solution)/shard_map/ppermute | solution.py:98
  92.5 9.1 %collective-permute-start.13 = (bf16[512,256]{1,0:T(8,128)(2,1)}, bf16[512,256]{1,0:T(8,128)(2,1)S(1)}, u32[]{:S(2)}, u32[]{:S(2)}) collective-permute-start(bf16[512,256]{1,0:T(8,128)(2,1)} %shard_map.85.p2), channel_id=1, source_target_pairs={{0,31},{1,0},{2,1},{3,2},{4,3},{5,4},{6,5},{7,6},{8,7},{9,8},{10,9... | collective-permute-start | bytes 786440 | tf_op jit(solution)/shard_map/ppermute | solution.py:98
  93.1 12.5 %collective-permute-start.12 = (bf16[512,256]{1,0:T(8,128)(2,1)}, bf16[512,256]{1,0:T(8,128)(2,1)S(1)}, u32[]{:S(2)}, u32[]{:S(2)}) collective-permute-start(bf16[512,256]{1,0:T(8,128)(2,1)} %shard_map.85.p2), channel_id=1, source_target_pairs={{0,30},{1,31},{2,0},{3,1},{4,2},{5,3},{6,4},{7,5},{8,6},{9,7},{10,... | collective-permute-start | bytes 786440 | tf_op jit(solution)/shard_map/ppermute | solution.py:98
  114.2 9.0 %collective-permute-start.17 = (bf16[512,256]{1,0:T(8,128)(2,1)}, bf16[512,256]{1,0:T(8,128)(2,1)S(1)}, u32[]{:S(2)}, u32[]{:S(2)}) collective-permute-start(bf16[512,256]{1,0:T(8,128)(2,1)} %shard_map.86.p2), channel_id=1, source_target_pairs={{0,31},{1,0},{2,1},{3,2},{4,3},{5,4},{6,5},{7,6},{8,7},{9,8},{10,9... | collective-permute-start | bytes 786440 | tf_op jit(solution)/shard_map/ppermute | solution.py:98
  114.8 12.5 %collective-permute-start.16 = (bf16[512,256]{1,0:T(8,128)(2,1)}, bf16[512,256]{1,0:T(8,128)(2,1)S(1)}, u32[]{:S(2)}, u32[]{:S(2)}) collective-permute-start(bf16[512,256]{1,0:T(8,128)(2,1)} %shard_map.86.p2), channel_id=1, source_target_pairs={{0,30},{1,31},{2,0},{3,1},{4,2},{5,3},{6,4},{7,5},{8,6},{9,7},{10,... | collective-permute-start | bytes 786440 | tf_op jit(solution)/shard_map/ppermute | solution.py:98
  135.9 8.9 %collective-permute-start.21 = (bf16[512,256]{1,0:T(8,128)(2,1)}, bf16[512,256]{1,0:T(8,128)(2,1)S(1)}, u32[]{:S(2)}, u32[]{:S(2)}) collective-permute-start(bf16[512,256]{1,0:T(8,128)(2,1)} %shard_map.87.p2), channel_id=1, source_target_pairs={{0,31},{1,0},{2,1},{3,2},{4,3},{5,4},{6,5},{7,6},{8,7},{9,8},{10,9... | collective-permute-start | bytes 786440 | tf_op jit(solution)/shard_map/ppermute | solution.py:98
  136.5 12.5 %collective-permute-start.20 = (bf16[512,256]{1,0:T(8,128)(2,1)}, bf16[512,256]{1,0:T(8,128)(2,1)S(1)}, u32[]{:S(2)}, u32[]{:S(2)}) collective-permute-start(bf16[512,256]{1,0:T(8,128)(2,1)} %shard_map.87.p2), channel_id=1, source_target_pairs={{0,30},{1,31},{2,0},{3,1},{4,2},{5,3},{6,4},{7,5},{8,6},{9,7},{10,... | collective-permute-start | bytes 786440 | tf_op jit(solution)/shard_map/ppermute | solution.py:98
  157.5 9.0 %collective-permute-start.25 = (bf16[512,256]{1,0:T(8,128)(2,1)}, bf16[512,256]{1,0:T(8,128)(2,1)S(1)}, u32[]{:S(2)}, u32[]{:S(2)}) collective-permute-start(bf16[512,256]{1,0:T(8,128)(2,1)} %shard_map.88.p2), channel_id=1, source_target_pairs={{0,31},{1,0},{2,1},{3,2},{4,3},{5,4},{6,5},{7,6},{8,7},{9,8},{10,9... | collective-permute-start | bytes 786440 | tf_op jit(solution)/shard_map/ppermute | solution.py:98
  158.1 12.5 %collective-permute-start.24 = (bf16[512,256]{1,0:T(8,128)(2,1)}, bf16[512,256]{1,0:T(8,128)(2,1)S(1)}, u32[]{:S(2)}, u32[]{:S(2)}) collective-permute-start(bf16[512,256]{1,0:T(8,128)(2,1)} %shard_map.88.p2), channel_id=1, source_target_pairs={{0,30},{1,31},{2,0},{3,1},{4,2},{5,3},{6,4},{7,5},{8,6},{9,7},{10,... | collective-permute-start | bytes 786440 | tf_op jit(solution)/shard_map/ppermute | solution.py:98
  166.5 6.6 %collective-permute-start.26 = (bf16[512,256]{1,0:T(8,128)(2,1)S(1)}, bf16[512,256]{1,0:T(8,128)(2,1)S(1)}, u32[]{:S(2)}, u32[]{:S(2)}) collective-permute-start(bf16[512,256]{1,0:T(8,128)(2,1)S(1)} %collective-permute-done.25.p1), channel_id=1, source_target_pairs={{0,32},{32,0},{64,96},{96,64},{128,160},{160,128},{192,224},{224,1... | collective-permute-start | bytes 786440 | tf_op jit(solution)/shard_map/ppermute | solution.py:102
  179.2 9.1 %collective-permute-start.29 = (bf16[512,256]{1,0:T(8,128)(2,1)}, bf16[512,256]{1,0:T(8,128)(2,1)S(1)}, u32[]{:S(2)}, u32[]{:S(2)}) collective-permute-start(bf16[512,256]{1,0:T(8,128)(2,1)} %shard_map.89), channel_id=1, source_target_pairs={{0,31},{1,0},{2,1},{3,2},{4,3},{5,4},{6,5},{7,6},{8,7},{9,8},{10,9... | collective-permute-start | bytes 786440 | tf_op jit(solution)/shard_map/ppermute | solution.py:98
  179.9 12.7 %collective-permute-start.28 = (bf16[512,256]{1,0:T(8,128)(2,1)}, bf16[512,256]{1,0:T(8,128)(2,1)S(1)}, u32[]{:S(2)}, u32[]{:S(2)}) collective-permute-start(bf16[512,256]{1,0:T(8,128)(2,1)} %shard_map.89), channel_id=1, source_target_pairs={{0,30},{1,31},{2,0},{3,1},{4,2},{5,3},{6,4},{7,5},{8,6},{9,7},{10,... | collective-permute-start | bytes 786440 | tf_op jit(solution)/shard_map/ppermute | solution.py:98
  188.3 8.9 %collective-permute-start.30 = (bf16[512,256]{1,0:T(8,128)(2,1)S(1)}, bf16[512,256]{1,0:T(8,128)(2,1)S(1)}, u32[]{:S(2)}, u32[]{:S(2)}) collective-permute-start(bf16[512,256]{1,0:T(8,128)(2,1)S(1)} %collective-permute-done.29), channel_id=1, source_target_pairs={{0,32},{32,0},{64,96},{96,64},{128,160},{160,128},{192,224},{224,1... | collective-permute-start | bytes 786440 | tf_op jit(solution)/shard_map/ppermute | solution.py:102
  202.3 9.4 %collective-permute-start.32 = (bf16[512,256]{1,0:T(8,128)(2,1)S(1)}, bf16[512,256]{1,0:T(8,128)(2,1)S(1)}, u32[]{:S(2)}, u32[]{:S(2)}) collective-permute-start(bf16[512,256]{1,0:T(8,128)(2,1)S(1)} %get-tuple-element.8), channel_id=1, source_target_pairs={{0,64},{32,96},{64,128},{96,160},{128,192},{160,224},{192,0},{224,... | collective-permute-start | bytes 786440 | tf_op jit(solution)/shard_map/ppermute | solution.py:144
  202.4 14.4 %collective-permute-start.33 = (bf16[512,256]{1,0:T(8,128)(2,1)S(1)}, bf16[512,256]{1,0:T(8,128)(2,1)S(1)}, u32[]{:S(2)}, u32[]{:S(2)}) collective-permute-start(bf16[512,256]{1,0:T(8,128)(2,1)S(1)} %get-tuple-element.7), channel_id=1, source_target_pairs={{0,128},{32,160},{64,192},{96,224},{128,0},{160,32},{192,64},{224,... | collective-permute-start | bytes 786440 | tf_op jit(solution)/shard_map/ppermute | solution.py:144
  204.8 12.6 %collective-permute-start.34 = (bf16[512,256]{1,0:T(8,128)(2,1)S(1)}, bf16[512,256]{1,0:T(8,128)(2,1)S(1)}, u32[]{:S(2)}, u32[]{:S(2)}) collective-permute-start(bf16[512,256]{1,0:T(8,128)(2,1)S(1)} %get-tuple-element.6), channel_id=1, source_target_pairs={{0,192},{32,224},{64,0},{96,32},{128,64},{160,96},{192,128},{224,1... | collective-permute-start | bytes 786440 | tf_op jit(solution)/shard_map/ppermute | solution.py:144
  (51 other events, 295.1 us)
Sparse Core Ops, SparseCore 0:
  9.2 31.9 all-gather.2

commit v8 on v7

--- a/solution.py
+++ b/solution.py
@@ -31,7 +31,7 @@
     )(row_local, column_local, count, values)
 
 
-def _layer_kernel(band_ref, p0, p1, p2, p3, p4, degree_ref, ws_ref, wn_ref, out_ref):
+def _layer_kernel(band_ref, p0, p1, p2, p3, p4, own_ref, degree_ref, ws_ref, wn_ref, out_ref):
     rows = p2.shape[0]
     parts = (p0, p1, p2, p3, p4)
     summed = jnp.dot(
@@ -44,7 +44,7 @@
             preferred_element_type=jnp.float32,
         )
     neighbour_mean = (summed / degree_ref[...]).astype(jnp.bfloat16)
-    combined = jnp.dot(p2[...], ws_ref[...], preferred_element_type=jnp.float32) + jnp.dot(
+    combined = jnp.dot(own_ref[...], ws_ref[...], preferred_element_type=jnp.float32) + jnp.dot(
         neighbour_mean, wn_ref[...], preferred_element_type=jnp.float32
     )
     active = jnp.maximum(combined, 0.0)
@@ -52,19 +52,33 @@
     out_ref[...] = (active * scale).astype(out_ref.dtype)
 
 
-def run_layer(band, parts, degree_f, ws, wn):
+def run_layer(band, parts, degree_f, weights_all, level, tile):
     rows, width = parts[2].shape
+    band_cols = band.shape[1]
+    whole = pl.BlockSpec((rows, width), lambda i: (0, 0))
     return pl.pallas_call(
         _layer_kernel,
         out_shape=jax.ShapeDtypeStruct((rows, width), jnp.bfloat16),
-        in_specs=[pl.BlockSpec(memory_space=pltpu.VMEM)] * 9,
-        out_specs=pl.BlockSpec(memory_space=pltpu.VMEM),
+        grid=(rows // tile,),
+        in_specs=[
+            pl.BlockSpec((tile, band_cols), lambda i: (i, 0)),
+            whole,
+            whole,
+            whole,
+            whole,
+            whole,
+            pl.BlockSpec((tile, width), lambda i: (i, 0)),
+            pl.BlockSpec((tile, 1), lambda i: (i, 0)),
+            pl.BlockSpec((None, None, width, width), lambda i: (level, 0, 0, 0)),
+            pl.BlockSpec((None, None, width, width), lambda i: (level, 1, 0, 0)),
+        ],
+        out_specs=pl.BlockSpec((tile, width), lambda i: (i, 0)),
         cost_estimate=pl.CostEstimate(
-            flops=2 * rows * band.shape[1] * width + 4 * rows * width * width,
+            flops=2 * rows * band_cols * width + 4 * rows * width * width,
             bytes_accessed=band.size * 2 + 6 * rows * width * 2,
             transcendentals=rows,
         ),
-    )(band, *parts, degree_f, ws, wn)
+    )(band, *parts, parts[2], degree_f, weights_all, weights_all)
 
 
 def body(
@@ -82,8 +96,6 @@
     section_index = lax.axis_index("section")
 
     weights_all = lax.all_gather(jnp.stack([self_weight[0], neighbour_weight[0]]), "section")
-    self_all = weights_all[:, 0]
-    neighbour_all = weights_all[:, 1]
 
     group = section_count // batch_total
     batch = section_index // group
@@ -128,7 +140,7 @@
         near = halo(hidden, 1)
         far = halo(hidden, 2)
         parts = [far, near, hidden, swap(near), swap(far)]
-        hidden = run_layer(band, parts, degree_f, self_all[level], neighbour_all[level])
+        hidden = run_layer(band, parts, degree_f, weights_all, level, block_size)
         outputs.append(hidden)
 
     stacked = jnp.stack(outputs)

time: 226 us -> 238 us (1.053)
  Pallas kernels: 33.5 us -> 42.6 us
  local copies, waits for them, and re-layouts: 21.5 us -> 25.1 us
  starting transfers between devices: 46.7 us -> 43.5 us
    pallas_call x7, Pallas kernels: 29.8 us -> 38.3 us  [run_layer(): pl.pallas_call(_layer_kernel, out_shape=jax.ShapeDtypeStruct((rows, width...]
    unnamed x85 -> x83, local copies, waits for them, and re-layouts: 8.99 us -> 13.8 us
    ppermute x16, waiting for transfers between devices: 76.1 us -> 80.3 us  [halo(): return lax.ppermute(x, ('section', 'blk'), pairs)]
    all_gather x1, waiting for transfers between devices: 7.98 us -> 4.18 us  [body(): lax.all_gather(jnp.stack([self_weight[0], neighbour_weight[0]]), 'section')]
    squeeze x1 -> x0, local copies, waits for them, and re-layouts: 2.91 us -> none  [body(): neighbour_all[level]]
    ppermute x3, waiting for transfers between devices: 11.1 us -> 13.9 us  [body(): arrived.append(lax.ppermute(sending, 'section', pairs))]
where the time goes in v8:
time: 238 us; the launch traced here: 237 us
  waiting for transfers between devices  104 us (44%)
  starting transfers between devices  43.5 us (18%)
  Pallas kernels  42.6 us (18%)
  local copies, waits for them, and re-layouts  25.1 us (11%)
  between operations  14.3 us (6%)
  other arithmetic  7.53 us (3%)
    ppermute x16, waiting for transfers between devices, halo(): return lax.ppermute(x, ('section', 'blk'), pairs)  80.3 us
    pallas_call x7, Pallas kernels, run_layer(): pl.pallas_call(_layer_kernel, out_shape=jax.ShapeDtypeStruct((rows, width...  38.3 us
    ppermute x16, starting transfers between devices, swap(): return lax.ppermute(x, 'section', pairs)  27.3 us
    ppermute x3, waiting for transfers between devices, body(): arrived.append(lax.ppermute(sending, 'section', pairs))  13.9 us
    unnamed x83, local copies, waits for them, and re-layouts  13.8 us
    ppermute x16, starting transfers between devices, halo(): return lax.ppermute(x, ('section', 'blk'), pairs)  13.4 us
    ppermute x16, waiting for transfers between devices, swap(): return lax.ppermute(x, 'section', pairs)  5.81 us
    pallas_call x1, local copies, waits for them, and re-layouts, run_layer(): pl.pallas_call(_layer_kernel, out_shape=jax.ShapeDtypeStruct((rows, width...  5.37 us
  transfers between devices with their start and end apart: 36, of which 24 were waited for; matrix products, arithmetic and copies ran while one was open for 7% of the time, Pallas kernels for 2%

profile of v8, /device:TPU:1, one launch (start us, length us, event | category | flops | bytes accessed | tf_op | source)
XLA Modules:
  0.0 237.1 jit_solution(6866352428146816156)
XLA Ops:
  21.1 3.4 %collective-permute-start.2 = (bf16[512,256]{1,0:T(8,128)(2,1)S(1)}, bf16[512,256]{1,0:T(8,128)(2,1)S(1)}, u32[]{:S(2)}, u32[]{:S(2)}) collective-permute-start(bf16[512,256]{1,0:T(8,128)(2,1)S(1)} %collective-permute-done.1.p1), channel_id=1, source_target_pairs={{0,32},{32,0},{64,96},{96,64},{128,160},{160,128},{192,224},{224,1... | collective-permute-start | bytes 786440 | tf_op jit(solution)/shard_map/ppermute | solution.py:114
  29.2 3.6 %dynamic-slice_bitcast_fusion.values_ref = bf16[80,128,128]{2,1,0:T(8,128)(2,1)} fusion(bf16[4,80,128,128]{3,2,1,0:T(8,128)(2,1)} %param.9, s32[]{:T(128)S(6)} %select_n.106), kind=kLoop, calls=%fused_computation | loop fusion | bytes 5242884 | tf_op jit(solution)/shard_map/jit(dynamic_index_in_dim)/squeeze | solution.py:116
  32.8 4.3 %shard_map.82.band_ref = bf16[512,2560]{1,0:T(8,128)(2,1)} custom-call(s32[80]{0:T(128)} %fusion.7.rows_ref, s32[80]{0:T(128)} %fusion.8.cols_ref, s32[1]{0:T(128)} %bitcast.2.count_ref, bf16[80,128,128]{2,1,0:T(8,128)(2,1)} %dynamic-slice_bitcast_fusion.values_ref), custom_call_target="tpu_custom_call" | custom-call | tf_op jit(solution)/shard_map/pallas_call | solution.py:25
  37.1 4.2 %all-gather.3.cloned.1.call-done = bf16[16,256,256]{2,1,0:T(8,128)(2,1)} async-done(((bf16[2,256,256]{2,1,0:T(8,128)(2,1)}), bf16[16,256,256]{2,1,0:T(8,128)(2,1)}) %all-gather.3.cloned.1.call-update) | async-done | bytes 2097168 | tf_op jit(solution)/shard_map/all_gather | solution.py:98
  41.2 5.5 %shard_map.83.p2.own_ref = bf16[512,256]{1,0:T(8,128)(2,1)} custom-call(bf16[512,2560]{1,0:T(8,128)(2,1)} %shard_map.82.band_ref, bf16[512,256]{1,0:T(8,128)(2,1)} %copy-done.11, bf16[512,256]{1,0:T(8,128)(2,1)} %copy-done.10, bf16[512,256]{1,0:T(8,128)(2,1)} %copy-done.6, bf16[512,256]{1,0:T(8,128)(2,1)} %copy-done.14, bf16[512,256]{1,0:T(8,128)(2,1)} %copy-done.15, ...), custom_call_target="tpu_custom_call" | custom-call | flops 805306368 | bytes 4194304 | tf_op jit(solution)/shard_map/pallas_call | solution.py:59
  50.3 5.6 %collective-permute-done.5.p1 = bf16[512,256]{1,0:T(8,128)(2,1)S(1)} collective-permute-done((bf16[512,256]{1,0:T(8,128)(2,1)}, bf16[512,256]{1,0:T(8,128)(2,1)S(1)}, u32[]{:S(2)}, u32[]{:S(2)}) %collective-permute-start.5) | collective-permute-done | bytes 262176 | tf_op jit(solution)/shard_map/ppermute | solution.py:110
  57.6 3.2 %collective-permute-done.4.p0 = bf16[512,256]{1,0:T(8,128)(2,1)S(1)} collective-permute-done((bf16[512,256]{1,0:T(8,128)(2,1)}, bf16[512,256]{1,0:T(8,128)(2,1)S(1)}, u32[]{:S(2)}, u32[]{:S(2)}) %collective-permute-start.4) | collective-permute-done | bytes 262176 | tf_op jit(solution)/shard_map/ppermute | solution.py:110
  64.2 5.5 %shard_map.84.p2.own_ref = bf16[512,256]{1,0:T(8,128)(2,1)} custom-call(bf16[512,2560]{1,0:T(8,128)(2,1)} %shard_map.82.band_ref, bf16[512,256]{1,0:T(8,128)(2,1)} %copy-done.22, bf16[512,256]{1,0:T(8,128)(2,1)} %copy-done.16, bf16[512,256]{1,0:T(8,128)(2,1)} %shard_map.83.p2.own_ref, bf16[512,256]{1,0:T(8,128)(2,1)} %copy-done.28, ...), custom_call_target="tpu_custom_call" | custom-call | flops 805306368 | bytes 4194304 | tf_op jit(solution)/shard_map/pallas_call | solution.py:59
  71.1 7.5 %collective-permute-done.9.p1 = bf16[512,256]{1,0:T(8,128)(2,1)S(1)} collective-permute-done((bf16[512,256]{1,0:T(8,128)(2,1)}, bf16[512,256]{1,0:T(8,128)(2,1)S(1)}, u32[]{:S(2)}, u32[]{:S(2)}) %collective-permute-start.9) | collective-permute-done | bytes 262176 | tf_op jit(solution)/shard_map/ppermute | solution.py:110
  79.5 3.4 %collective-permute-done.8.p0 = bf16[512,256]{1,0:T(8,128)(2,1)S(1)} collective-permute-done((bf16[512,256]{1,0:T(8,128)(2,1)}, bf16[512,256]{1,0:T(8,128)(2,1)S(1)}, u32[]{:S(2)}, u32[]{:S(2)}) %collective-permute-start.8) | collective-permute-done | bytes 262176 | tf_op jit(solution)/shard_map/ppermute | solution.py:110
  87.0 5.5 %shard_map.85.p2.own_ref = bf16[512,256]{1,0:T(8,128)(2,1)} custom-call(bf16[512,2560]{1,0:T(8,128)(2,1)} %shard_map.82.band_ref, bf16[512,256]{1,0:T(8,128)(2,1)} %copy-done.23, bf16[512,256]{1,0:T(8,128)(2,1)} %copy-done.17, bf16[512,256]{1,0:T(8,128)(2,1)} %shard_map.84.p2.own_ref, bf16[512,256]{1,0:T(8,128)(2,1)} %copy-done.29, ...), custom_call_target="tpu_custom_call" | custom-call | flops 805306368 | bytes 4194304 | tf_op jit(solution)/shard_map/pallas_call | solution.py:59
  93.1 8.4 %collective-permute-done.13.p1 = bf16[512,256]{1,0:T(8,128)(2,1)S(1)} collective-permute-done((bf16[512,256]{1,0:T(8,128)(2,1)}, bf16[512,256]{1,0:T(8,128)(2,1)S(1)}, u32[]{:S(2)}, u32[]{:S(2)}) %collective-permute-start.13) | collective-permute-done | bytes 262176 | tf_op jit(solution)/shard_map/ppermute | solution.py:110
  110.0 5.5 %shard_map.86.p2.own_ref = bf16[512,256]{1,0:T(8,128)(2,1)} custom-call(bf16[512,2560]{1,0:T(8,128)(2,1)} %shard_map.82.band_ref, bf16[512,256]{1,0:T(8,128)(2,1)} %copy-done.24, bf16[512,256]{1,0:T(8,128)(2,1)} %copy-done.18, bf16[512,256]{1,0:T(8,128)(2,1)} %shard_map.85.p2.own_ref, bf16[512,256]{1,0:T(8,128)(2,1)} %copy-done.30, ...), custom_call_target="tpu_custom_call" | custom-call | flops 805306368 | bytes 4194304 | tf_op jit(solution)/shard_map/pallas_call | solution.py:59
  116.1 8.4 %collective-permute-done.17.p1 = bf16[512,256]{1,0:T(8,128)(2,1)S(1)} collective-permute-done((bf16[512,256]{1,0:T(8,128)(2,1)}, bf16[512,256]{1,0:T(8,128)(2,1)S(1)}, u32[]{:S(2)}, u32[]{:S(2)}) %collective-permute-start.17) | collective-permute-done | bytes 262176 | tf_op jit(solution)/shard_map/ppermute | solution.py:110
  132.9 5.4 %shard_map.87.p2.own_ref = bf16[512,256]{1,0:T(8,128)(2,1)} custom-call(bf16[512,2560]{1,0:T(8,128)(2,1)} %shard_map.82.band_ref, bf16[512,256]{1,0:T(8,128)(2,1)} %copy-done.25, bf16[512,256]{1,0:T(8,128)(2,1)} %copy-done.19, bf16[512,256]{1,0:T(8,128)(2,1)} %shard_map.86.p2.own_ref, bf16[512,256]{1,0:T(8,128)(2,1)} %copy-done.31, ...), custom_call_target="tpu_custom_call" | custom-call | flops 805306368 | bytes 4194304 | tf_op jit(solution)/shard_map/pallas_call | solution.py:59
  139.1 8.3 %collective-permute-done.21.p1 = bf16[512,256]{1,0:T(8,128)(2,1)S(1)} collective-permute-done((bf16[512,256]{1,0:T(8,128)(2,1)}, bf16[512,256]{1,0:T(8,128)(2,1)S(1)}, u32[]{:S(2)}, u32[]{:S(2)}) %collective-permute-start.21) | collective-permute-done | bytes 262176 | tf_op jit(solution)/shard_map/ppermute | solution.py:110
  148.2 3.4 %collective-permute-done.20.p0 = bf16[512,256]{1,0:T(8,128)(2,1)S(1)} collective-permute-done((bf16[512,256]{1,0:T(8,128)(2,1)}, bf16[512,256]{1,0:T(8,128)(2,1)S(1)}, u32[]{:S(2)}, u32[]{:S(2)}) %collective-permute-start.20) | collective-permute-done | bytes 262176 | tf_op jit(solution)/shard_map/ppermute | solution.py:110
  155.8 5.5 %shard_map.88.p2.own_ref = bf16[512,256]{1,0:T(8,128)(2,1)} custom-call(bf16[512,2560]{1,0:T(8,128)(2,1)} %shard_map.82.band_ref, bf16[512,256]{1,0:T(8,128)(2,1)} %copy-done.26, bf16[512,256]{1,0:T(8,128)(2,1)} %copy-done.20, bf16[512,256]{1,0:T(8,128)(2,1)} %shard_map.87.p2.own_ref, bf16[512,256]{1,0:T(8,128)(2,1)} %copy-done.32, ...), custom_call_target="tpu_custom_call" | custom-call | flops 805306368 | bytes 4194304 | tf_op jit(solution)/shard_map/pallas_call | solution.py:59
  162.0 8.3 %collective-permute-done.25.p1 = bf16[512,256]{1,0:T(8,128)(2,1)S(1)} collective-permute-done((bf16[512,256]{1,0:T(8,128)(2,1)}, bf16[512,256]{1,0:T(8,128)(2,1)S(1)}, u32[]{:S(2)}, u32[]{:S(2)}) %collective-permute-start.25) | collective-permute-done | bytes 262176 | tf_op jit(solution)/shard_map/ppermute | solution.py:110
  178.9 5.5 %shard_map.89 = bf16[512,256]{1,0:T(8,128)(2,1)} custom-call(bf16[512,2560]{1,0:T(8,128)(2,1)} %shard_map.82.band_ref, bf16[512,256]{1,0:T(8,128)(2,1)} %copy-done.9, bf16[512,256]{1,0:T(8,128)(2,1)} %copy-done.8, bf16[512,256]{1,0:T(8,128)(2,1)} %shard_map.88.p2.own_ref, bf16[512,256]{1,0:T(8,128)(2,1)} %copy-done.27, ...), custom_call_target="tpu_custom_call" | custom-call | flops 805306368 | bytes 4194304 | tf_op jit(solution)/shard_map/pallas_call | solution.py:59
  188.2 11.0 %collective-permute-done.29 = bf16[512,256]{1,0:T(8,128)(2,1)S(1)} collective-permute-done((bf16[512,256]{1,0:T(8,128)(2,1)}, bf16[512,256]{1,0:T(8,128)(2,1)S(1)}, u32[]{:S(2)}, u32[]{:S(2)}) %collective-permute-start.29) | collective-permute-done | bytes 262176 | tf_op jit(solution)/shard_map/ppermute | solution.py:110
  205.7 5.4 %shard_map.90 = bf16[8,512,256]{2,1,0:T(8,128)(2,1)} fusion(bf16[8,512,256]{2,1,0:T(8,128)(2,1)} %bitcast_dynamic-update-slice_fusion.1, bf16[512,2560]{1,0:T(8,128)(2,1)} %shard_map.82.band_ref, bf16[512,256]{1,0:T(8,128)(2,1)} %copy-done.12, bf16[512,256]{1,0:T(8,128)(2,1)} %copy-done.13, bf16[512,256]{1,0:T(8,128)(2,1)} %shard_map.89, ...), kind=kCustom, calls=%fused_computation.4 | custom fusion | bytes 6293504 | tf_op jit(solution)/shard_map/pallas_call | solution.py:59
  215.1 4.7 %collective-permute-done.34 = bf16[512,256]{1,0:T(8,128)(2,1)S(1)} collective-permute-done((bf16[512,256]{1,0:T(8,128)(2,1)S(1)}, bf16[512,256]{1,0:T(8,128)(2,1)S(1)}, u32[]{:S(2)}, u32[]{:S(2)}) %collective-permute-start.34) | collective-permute-done | bytes 262176 | tf_op jit(solution)/shard_map/ppermute | solution.py:156
  222.3 6.7 %collective-permute-done.32 = bf16[512,256]{1,0:T(8,128)(2,1)S(1)} collective-permute-done((bf16[512,256]{1,0:T(8,128)(2,1)S(1)}, bf16[512,256]{1,0:T(8,128)(2,1)S(1)}, u32[]{:S(2)}, u32[]{:S(2)}) %collective-permute-start.32) | collective-permute-done | bytes 262176 | tf_op jit(solution)/shard_map/ppermute | solution.py:156
  (153 shorter events, 84.9 us)
Async XLA Ops:
  6.5 34.7 %all-gather.3.cloned.1.call-start = ((), (), s32[]{:S(2)}) async-start(), calls=%async_computation | async-start | bytes 2359296 | tf_op jit(solution)/shard_map/all_gather | solution.py:98
  8.4 12.7 %collective-permute-start.1 = (bf16[512,256]{1,0:T(8,128)(2,1)S(1)}, bf16[512,256]{1,0:T(8,128)(2,1)S(1)}, u32[]{:S(2)}, u32[]{:S(2)}) collective-permute-start(bf16[512,256]{1,0:T(8,128)(2,1)S(1)} %dynamic-slice_bitcast_fusion.4.p2.own_ref), channel_id=1, source_target_pairs={{0,31},{1,0},{2,1},{3,2},{4,3},{5,4},{6,5},{7,6},{8,7},{9,8},{10,9... | collective-permute-start | bytes 786440 | tf_op jit(solution)/shard_map/ppermute | solution.py:110
  11.0 14.7 %collective-permute-start = (bf16[512,256]{1,0:T(8,128)(2,1)S(1)}, bf16[512,256]{1,0:T(8,128)(2,1)S(1)}, u32[]{:S(2)}, u32[]{:S(2)}) collective-permute-start(bf16[512,256]{1,0:T(8,128)(2,1)S(1)} %dynamic-slice_bitcast_fusion.4.p2.own_ref), channel_id=1, source_target_pairs={{0,30},{1,31},{2,0},{3,1},{4,2},{5,3},{6,4},{7,5},{8,6},{9,7},{10,... | collective-permute-start | bytes 786440 | tf_op jit(solution)/shard_map/ppermute | solution.py:110
  21.1 15.9 %collective-permute-start.2 = (bf16[512,256]{1,0:T(8,128)(2,1)S(1)}, bf16[512,256]{1,0:T(8,128)(2,1)S(1)}, u32[]{:S(2)}, u32[]{:S(2)}) collective-permute-start(bf16[512,256]{1,0:T(8,128)(2,1)S(1)} %collective-permute-done.1.p1), channel_id=1, source_target_pairs={{0,32},{32,0},{64,96},{96,64},{128,160},{160,128},{192,224},{224,1... | collective-permute-start | bytes 786440 | tf_op jit(solution)/shard_map/ppermute | solution.py:114
  25.7 11.4 %collective-permute-start.3 = (bf16[512,256]{1,0:T(8,128)(2,1)S(1)}, bf16[512,256]{1,0:T(8,128)(2,1)S(1)}, u32[]{:S(2)}, u32[]{:S(2)}) collective-permute-start(bf16[512,256]{1,0:T(8,128)(2,1)S(1)} %collective-permute-done.p0), channel_id=1, source_target_pairs={{0,32},{32,0},{64,96},{96,64},{128,160},{160,128},{192,224},{224,1... | collective-permute-start | bytes 786440 | tf_op jit(solution)/shard_map/ppermute | solution.py:114
  46.7 9.2 %collective-permute-start.5 = (bf16[512,256]{1,0:T(8,128)(2,1)}, bf16[512,256]{1,0:T(8,128)(2,1)S(1)}, u32[]{:S(2)}, u32[]{:S(2)}) collective-permute-start(bf16[512,256]{1,0:T(8,128)(2,1)} %shard_map.83.p2.own_ref), channel_id=1, source_target_pairs={{0,31},{1,0},{2,1},{3,2},{4,3},{5,4},{6,5},{7,6},{8,7},{9,8},{10,9... | collective-permute-start | bytes 786440 | tf_op jit(solution)/shard_map/ppermute | solution.py:110
  48.0 12.8 %collective-permute-start.4 = (bf16[512,256]{1,0:T(8,128)(2,1)}, bf16[512,256]{1,0:T(8,128)(2,1)S(1)}, u32[]{:S(2)}, u32[]{:S(2)}) collective-permute-start(bf16[512,256]{1,0:T(8,128)(2,1)} %shard_map.83.p2.own_ref), channel_id=1, source_target_pairs={{0,30},{1,31},{2,0},{3,1},{4,2},{5,3},{6,4},{7,5},{8,6},{9,7},{10,... | collective-permute-start | bytes 786440 | tf_op jit(solution)/shard_map/ppermute | solution.py:110
  69.7 8.9 %collective-permute-start.9 = (bf16[512,256]{1,0:T(8,128)(2,1)}, bf16[512,256]{1,0:T(8,128)(2,1)S(1)}, u32[]{:S(2)}, u32[]{:S(2)}) collective-permute-start(bf16[512,256]{1,0:T(8,128)(2,1)} %shard_map.84.p2.own_ref), channel_id=1, source_target_pairs={{0,31},{1,0},{2,1},{3,2},{4,3},{5,4},{6,5},{7,6},{8,7},{9,8},{10,9... | collective-permute-start | bytes 786440 | tf_op jit(solution)/shard_map/ppermute | solution.py:110
  70.4 12.4 %collective-permute-start.8 = (bf16[512,256]{1,0:T(8,128)(2,1)}, bf16[512,256]{1,0:T(8,128)(2,1)S(1)}, u32[]{:S(2)}, u32[]{:S(2)}) collective-permute-start(bf16[512,256]{1,0:T(8,128)(2,1)} %shard_map.84.p2.own_ref), channel_id=1, source_target_pairs={{0,30},{1,31},{2,0},{3,1},{4,2},{5,3},{6,4},{7,5},{8,6},{9,7},{10,... | collective-permute-start | bytes 786440 | tf_op jit(solution)/shard_map/ppermute | solution.py:110
  92.5 9.1 %collective-permute-start.13 = (bf16[512,256]{1,0:T(8,128)(2,1)}, bf16[512,256]{1,0:T(8,128)(2,1)S(1)}, u32[]{:S(2)}, u32[]{:S(2)}) collective-permute-start(bf16[512,256]{1,0:T(8,128)(2,1)} %shard_map.85.p2.own_ref), channel_id=1, source_target_pairs={{0,31},{1,0},{2,1},{3,2},{4,3},{5,4},{6,5},{7,6},{8,7},{9,8},{10,9... | collective-permute-start | bytes 786440 | tf_op jit(solution)/shard_map/ppermute | solution.py:110
  93.1 12.5 %collective-permute-start.12 = (bf16[512,256]{1,0:T(8,128)(2,1)}, bf16[512,256]{1,0:T(8,128)(2,1)S(1)}, u32[]{:S(2)}, u32[]{:S(2)}) collective-permute-start(bf16[512,256]{1,0:T(8,128)(2,1)} %shard_map.85.p2.own_ref), channel_id=1, source_target_pairs={{0,30},{1,31},{2,0},{3,1},{4,2},{5,3},{6,4},{7,5},{8,6},{9,7},{10,... | collective-permute-start | bytes 786440 | tf_op jit(solution)/shard_map/ppermute | solution.py:110
  101.5 6.5 %collective-permute-start.14 = (bf16[512,256]{1,0:T(8,128)(2,1)S(1)}, bf16[512,256]{1,0:T(8,128)(2,1)S(1)}, u32[]{:S(2)}, u32[]{:S(2)}) collective-permute-start(bf16[512,256]{1,0:T(8,128)(2,1)S(1)} %collective-permute-done.13.p1), channel_id=1, source_target_pairs={{0,32},{32,0},{64,96},{96,64},{128,160},{160,128},{192,224},{224,1... | collective-permute-start | bytes 786440 | tf_op jit(solution)/shard_map/ppermute | solution.py:114
  115.5 9.0 %collective-permute-start.17 = (bf16[512,256]{1,0:T(8,128)(2,1)}, bf16[512,256]{1,0:T(8,128)(2,1)S(1)}, u32[]{:S(2)}, u32[]{:S(2)}) collective-permute-start(bf16[512,256]{1,0:T(8,128)(2,1)} %shard_map.86.p2.own_ref), channel_id=1, source_target_pairs={{0,31},{1,0},{2,1},{3,2},{4,3},{5,4},{6,5},{7,6},{8,7},{9,8},{10,9... | collective-permute-start | bytes 786440 | tf_op jit(solution)/shard_map/ppermute | solution.py:110
  116.1 12.5 %collective-permute-start.16 = (bf16[512,256]{1,0:T(8,128)(2,1)}, bf16[512,256]{1,0:T(8,128)(2,1)S(1)}, u32[]{:S(2)}, u32[]{:S(2)}) collective-permute-start(bf16[512,256]{1,0:T(8,128)(2,1)} %shard_map.86.p2.own_ref), channel_id=1, source_target_pairs={{0,30},{1,31},{2,0},{3,1},{4,2},{5,3},{6,4},{7,5},{8,6},{9,7},{10,... | collective-permute-start | bytes 786440 | tf_op jit(solution)/shard_map/ppermute | solution.py:110
  138.3 9.0 %collective-permute-start.21 = (bf16[512,256]{1,0:T(8,128)(2,1)}, bf16[512,256]{1,0:T(8,128)(2,1)S(1)}, u32[]{:S(2)}, u32[]{:S(2)}) collective-permute-start(bf16[512,256]{1,0:T(8,128)(2,1)} %shard_map.87.p2.own_ref), channel_id=1, source_target_pairs={{0,31},{1,0},{2,1},{3,2},{4,3},{5,4},{6,5},{7,6},{8,7},{9,8},{10,9... | collective-permute-start | bytes 786440 | tf_op jit(solution)/shard_map/ppermute | solution.py:110
  139.1 12.5 %collective-permute-start.20 = (bf16[512,256]{1,0:T(8,128)(2,1)}, bf16[512,256]{1,0:T(8,128)(2,1)S(1)}, u32[]{:S(2)}, u32[]{:S(2)}) collective-permute-start(bf16[512,256]{1,0:T(8,128)(2,1)} %shard_map.87.p2.own_ref), channel_id=1, source_target_pairs={{0,30},{1,31},{2,0},{3,1},{4,2},{5,3},{6,4},{7,5},{8,6},{9,7},{10,... | collective-permute-start | bytes 786440 | tf_op jit(solution)/shard_map/ppermute | solution.py:110
  161.3 9.0 %collective-permute-start.25 = (bf16[512,256]{1,0:T(8,128)(2,1)}, bf16[512,256]{1,0:T(8,128)(2,1)S(1)}, u32[]{:S(2)}, u32[]{:S(2)}) collective-permute-start(bf16[512,256]{1,0:T(8,128)(2,1)} %shard_map.88.p2.own_ref), channel_id=1, source_target_pairs={{0,31},{1,0},{2,1},{3,2},{4,3},{5,4},{6,5},{7,6},{8,7},{9,8},{10,9... | collective-permute-start | bytes 786440 | tf_op jit(solution)/shard_map/ppermute | solution.py:110
  161.9 12.5 %collective-permute-start.24 = (bf16[512,256]{1,0:T(8,128)(2,1)}, bf16[512,256]{1,0:T(8,128)(2,1)S(1)}, u32[]{:S(2)}, u32[]{:S(2)}) collective-permute-start(bf16[512,256]{1,0:T(8,128)(2,1)} %shard_map.88.p2.own_ref), channel_id=1, source_target_pairs={{0,30},{1,31},{2,0},{3,1},{4,2},{5,3},{6,4},{7,5},{8,6},{9,7},{10,... | collective-permute-start | bytes 786440 | tf_op jit(solution)/shard_map/ppermute | solution.py:110
  170.3 6.6 %collective-permute-start.26 = (bf16[512,256]{1,0:T(8,128)(2,1)S(1)}, bf16[512,256]{1,0:T(8,128)(2,1)S(1)}, u32[]{:S(2)}, u32[]{:S(2)}) collective-permute-start(bf16[512,256]{1,0:T(8,128)(2,1)S(1)} %collective-permute-done.25.p1), channel_id=1, source_target_pairs={{0,32},{32,0},{64,96},{96,64},{128,160},{160,128},{192,224},{224,1... | collective-permute-start | bytes 786440 | tf_op jit(solution)/shard_map/ppermute | solution.py:114
  184.5 16.4 %collective-permute-start.28 = (bf16[512,256]{1,0:T(8,128)(2,1)}, bf16[512,256]{1,0:T(8,128)(2,1)S(1)}, u32[]{:S(2)}, u32[]{:S(2)}) collective-permute-start(bf16[512,256]{1,0:T(8,128)(2,1)} %shard_map.89), channel_id=1, source_target_pairs={{0,30},{1,31},{2,0},{3,1},{4,2},{5,3},{6,4},{7,5},{8,6},{9,7},{10,... | collective-permute-start | bytes 786440 | tf_op jit(solution)/shard_map/ppermute | solution.py:110
  184.5 14.7 %collective-permute-start.29 = (bf16[512,256]{1,0:T(8,128)(2,1)}, bf16[512,256]{1,0:T(8,128)(2,1)S(1)}, u32[]{:S(2)}, u32[]{:S(2)}) collective-permute-start(bf16[512,256]{1,0:T(8,128)(2,1)} %shard_map.89), channel_id=1, source_target_pairs={{0,31},{1,0},{2,1},{3,2},{4,3},{5,4},{6,5},{7,6},{8,7},{9,8},{10,9... | collective-permute-start | bytes 786440 | tf_op jit(solution)/shard_map/ppermute | solution.py:110
  212.3 7.5 %collective-permute-start.34 = (bf16[512,256]{1,0:T(8,128)(2,1)S(1)}, bf16[512,256]{1,0:T(8,128)(2,1)S(1)}, u32[]{:S(2)}, u32[]{:S(2)}) collective-permute-start(bf16[512,256]{1,0:T(8,128)(2,1)S(1)} %get-tuple-element.6), channel_id=1, source_target_pairs={{0,192},{32,224},{64,0},{96,32},{128,64},{160,96},{192,128},{224,1... | collective-permute-start | bytes 786440 | tf_op jit(solution)/shard_map/ppermute | solution.py:156
  213.6 8.7 %collective-permute-start.33 = (bf16[512,256]{1,0:T(8,128)(2,1)S(1)}, bf16[512,256]{1,0:T(8,128)(2,1)S(1)}, u32[]{:S(2)}, u32[]{:S(2)}) collective-permute-start(bf16[512,256]{1,0:T(8,128)(2,1)S(1)} %get-tuple-element.7), channel_id=1, source_target_pairs={{0,128},{32,160},{64,192},{96,224},{128,0},{160,32},{192,64},{224,... | collective-permute-start | bytes 786440 | tf_op jit(solution)/shard_map/ppermute | solution.py:156
  214.3 14.6 %collective-permute-start.32 = (bf16[512,256]{1,0:T(8,128)(2,1)S(1)}, bf16[512,256]{1,0:T(8,128)(2,1)S(1)}, u32[]{:S(2)}, u32[]{:S(2)}) collective-permute-start(bf16[512,256]{1,0:T(8,128)(2,1)S(1)} %get-tuple-element.8), channel_id=1, source_target_pairs={{0,64},{32,96},{64,128},{96,160},{128,192},{160,224},{192,0},{224,... | collective-permute-start | bytes 786440 | tf_op jit(solution)/shard_map/ppermute | solution.py:156
  (50 other events, 340.9 us)
Sparse Core Ops, SparseCore 0:
  9.2 31.9 all-gather.2

commit v9 on v8

--- a/solution.py
+++ b/solution.py
@@ -52,9 +52,10 @@
     out_ref[...] = (active * scale).astype(out_ref.dtype)
 
 
-def run_layer(band, parts, degree_f, weights_all, level, tile):
+def run_layer(band, parts, degree_f, weights_all, level):
     rows, width = parts[2].shape
     band_cols = band.shape[1]
+    tile = rows
     whole = pl.BlockSpec((rows, width), lambda i: (0, 0))
     return pl.pallas_call(
         _layer_kernel,
@@ -140,7 +141,7 @@
         near = halo(hidden, 1)
         far = halo(hidden, 2)
         parts = [far, near, hidden, swap(near), swap(far)]
-        hidden = run_layer(band, parts, degree_f, weights_all, level, block_size)
+        hidden = run_layer(band, parts, degree_f, weights_all, level)
         outputs.append(hidden)
 
     stacked = jnp.stack(outputs)

time: 238 us -> 228 us (0.958)
  Pallas kernels: 42.6 us -> 34 us
    pallas_call x7, Pallas kernels: 38.3 us -> 30.4 us  [run_layer(): pl.pallas_call(_layer_kernel, out_shape=jax.ShapeDtypeStruct((rows, width...]
where the time goes in v9:
time: 228 us
  waiting for transfers between devices  105 us (46%)
  starting transfers between devices  43.5 us (19%)
  Pallas kernels  34 us (15%)
  local copies, waits for them, and re-layouts  23.9 us (10%)
  between operations  14.3 us (6%)
  other arithmetic  7.53 us (3%)
    ppermute x16, waiting for transfers between devices, halo(): return lax.ppermute(x, ('section', 'blk'), pairs)  80.3 us
    pallas_call x7, Pallas kernels, run_layer(): pl.pallas_call(_layer_kernel, out_shape=jax.ShapeDtypeStruct((rows, width...  30.4 us
    ppermute x16, starting transfers between devices, swap(): return lax.ppermute(x, 'section', pairs)  27.3 us
    ppermute x3, waiting for transfers between devices, body(): arrived.append(lax.ppermute(sending, 'section', pairs))  13.9 us
    unnamed x83, local copies, waits for them, and re-layouts  13.8 us
    ppermute x16, starting transfers between devices, halo(): return lax.ppermute(x, ('section', 'blk'), pairs)  13.4 us
    ppermute x16, waiting for transfers between devices, swap(): return lax.ppermute(x, 'section', pairs)  5.81 us
    all_gather x1, waiting for transfers between devices, body(): lax.all_gather(jnp.stack([self_weight[0], neighbour_weight[0]]), 'section')  4.83 us
  transfers between devices with their start and end apart: 36, of which 24 were waited for; matrix products, arithmetic and copies ran while one was open for 7% of the time, Pallas kernels for 2%

profile of v9, /device:TPU:1, one launch (start us, length us, event | category | flops | bytes accessed | tf_op | source)
XLA Modules:
  0.0 228.0 jit_solution(563411721197505329)
XLA Ops:
  21.1 3.4 %collective-permute-start.2 = (bf16[512,256]{1,0:T(8,128)(2,1)S(1)}, bf16[512,256]{1,0:T(8,128)(2,1)S(1)}, u32[]{:S(2)}, u32[]{:S(2)}) collective-permute-start(bf16[512,256]{1,0:T(8,128)(2,1)S(1)} %collective-permute-done.1.p1), channel_id=1, source_target_pairs={{0,32},{32,0},{64,96},{96,64},{128,160},{160,128},{192,224},{224,1... | collective-permute-start | bytes 786440 | tf_op jit(solution)/shard_map/ppermute | solution.py:115
  29.2 3.6 %dynamic-slice_bitcast_fusion.values_ref = bf16[80,128,128]{2,1,0:T(8,128)(2,1)} fusion(bf16[4,80,128,128]{3,2,1,0:T(8,128)(2,1)} %param.9, s32[]{:T(128)S(6)} %select_n.106), kind=kLoop, calls=%fused_computation | loop fusion | bytes 5242884 | tf_op jit(solution)/shard_map/jit(dynamic_index_in_dim)/squeeze | solution.py:117
  32.8 3.6 %shard_map.82.band_ref = bf16[512,2560]{1,0:T(8,128)(2,1)} custom-call(s32[80]{0:T(128)} %fusion.7.rows_ref, s32[80]{0:T(128)} %fusion.8.cols_ref, s32[1]{0:T(128)} %bitcast.2.count_ref, bf16[80,128,128]{2,1,0:T(8,128)(2,1)} %dynamic-slice_bitcast_fusion.values_ref), custom_call_target="tpu_custom_call" | custom-call | tf_op jit(solution)/shard_map/pallas_call | solution.py:25
  36.4 4.8 %all-gather.3.cloned.1.call-done = bf16[16,256,256]{2,1,0:T(8,128)(2,1)} async-done(((bf16[2,256,256]{2,1,0:T(8,128)(2,1)}), bf16[16,256,256]{2,1,0:T(8,128)(2,1)}) %all-gather.3.cloned.1.call-update) | async-done | bytes 2097168 | tf_op jit(solution)/shard_map/all_gather | solution.py:99
  41.2 4.3 %shard_map.83.p2.own_ref = bf16[512,256]{1,0:T(8,128)(2,1)} custom-call(bf16[512,2560]{1,0:T(8,128)(2,1)} %shard_map.82.band_ref, bf16[512,256]{1,0:T(8,128)(2,1)} %copy-done.11, bf16[512,256]{1,0:T(8,128)(2,1)} %copy-done.10, bf16[512,256]{1,0:T(8,128)(2,1)} %copy-done.6, bf16[512,256]{1,0:T(8,128)(2,1)} %copy-done.14, bf16[512,256]{1,0:T(8,128)(2,1)} %copy-done.15, ...), custom_call_target="tpu_custom_call" | custom-call | flops 805306368 | bytes 4194304 | tf_op jit(solution)/shard_map/pallas_call | solution.py:60
  49.1 5.6 %collective-permute-done.5.p1 = bf16[512,256]{1,0:T(8,128)(2,1)S(1)} collective-permute-done((bf16[512,256]{1,0:T(8,128)(2,1)}, bf16[512,256]{1,0:T(8,128)(2,1)S(1)}, u32[]{:S(2)}, u32[]{:S(2)}) %collective-permute-start.5) | collective-permute-done | bytes 262176 | tf_op jit(solution)/shard_map/ppermute | solution.py:111
  56.5 3.2 %collective-permute-done.4.p0 = bf16[512,256]{1,0:T(8,128)(2,1)S(1)} collective-permute-done((bf16[512,256]{1,0:T(8,128)(2,1)}, bf16[512,256]{1,0:T(8,128)(2,1)S(1)}, u32[]{:S(2)}, u32[]{:S(2)}) %collective-permute-start.4) | collective-permute-done | bytes 262176 | tf_op jit(solution)/shard_map/ppermute | solution.py:111
  63.1 4.3 %shard_map.84.p2.own_ref = bf16[512,256]{1,0:T(8,128)(2,1)} custom-call(bf16[512,2560]{1,0:T(8,128)(2,1)} %shard_map.82.band_ref, bf16[512,256]{1,0:T(8,128)(2,1)} %copy-done.22, bf16[512,256]{1,0:T(8,128)(2,1)} %copy-done.16, bf16[512,256]{1,0:T(8,128)(2,1)} %shard_map.83.p2.own_ref, bf16[512,256]{1,0:T(8,128)(2,1)} %copy-done.28, ...), custom_call_target="tpu_custom_call" | custom-call | flops 805306368 | bytes 4194304 | tf_op jit(solution)/shard_map/pallas_call | solution.py:60
  68.7 7.6 %collective-permute-done.9.p1 = bf16[512,256]{1,0:T(8,128)(2,1)S(1)} collective-permute-done((bf16[512,256]{1,0:T(8,128)(2,1)}, bf16[512,256]{1,0:T(8,128)(2,1)S(1)}, u32[]{:S(2)}, u32[]{:S(2)}) %collective-permute-start.9) | collective-permute-done | bytes 262176 | tf_op jit(solution)/shard_map/ppermute | solution.py:111
  77.2 3.4 %collective-permute-done.8.p0 = bf16[512,256]{1,0:T(8,128)(2,1)S(1)} collective-permute-done((bf16[512,256]{1,0:T(8,128)(2,1)}, bf16[512,256]{1,0:T(8,128)(2,1)S(1)}, u32[]{:S(2)}, u32[]{:S(2)}) %collective-permute-start.8) | collective-permute-done | bytes 262176 | tf_op jit(solution)/shard_map/ppermute | solution.py:111
  84.7 4.3 %shard_map.85.p2.own_ref = bf16[512,256]{1,0:T(8,128)(2,1)} custom-call(bf16[512,2560]{1,0:T(8,128)(2,1)} %shard_map.82.band_ref, bf16[512,256]{1,0:T(8,128)(2,1)} %copy-done.23, bf16[512,256]{1,0:T(8,128)(2,1)} %copy-done.17, bf16[512,256]{1,0:T(8,128)(2,1)} %shard_map.84.p2.own_ref, bf16[512,256]{1,0:T(8,128)(2,1)} %copy-done.29, ...), custom_call_target="tpu_custom_call" | custom-call | flops 805306368 | bytes 4194304 | tf_op jit(solution)/shard_map/pallas_call | solution.py:60
  89.7 8.4 %collective-permute-done.13.p1 = bf16[512,256]{1,0:T(8,128)(2,1)S(1)} collective-permute-done((bf16[512,256]{1,0:T(8,128)(2,1)}, bf16[512,256]{1,0:T(8,128)(2,1)S(1)}, u32[]{:S(2)}, u32[]{:S(2)}) %collective-permute-start.13) | collective-permute-done | bytes 262176 | tf_op jit(solution)/shard_map/ppermute | solution.py:111
  106.5 4.3 %shard_map.86.p2.own_ref = bf16[512,256]{1,0:T(8,128)(2,1)} custom-call(bf16[512,2560]{1,0:T(8,128)(2,1)} %shard_map.82.band_ref, bf16[512,256]{1,0:T(8,128)(2,1)} %copy-done.24, bf16[512,256]{1,0:T(8,128)(2,1)} %copy-done.18, bf16[512,256]{1,0:T(8,128)(2,1)} %shard_map.85.p2.own_ref, bf16[512,256]{1,0:T(8,128)(2,1)} %copy-done.30, ...), custom_call_target="tpu_custom_call" | custom-call | flops 805306368 | bytes 4194304 | tf_op jit(solution)/shard_map/pallas_call | solution.py:60
  111.5 8.4 %collective-permute-done.17.p1 = bf16[512,256]{1,0:T(8,128)(2,1)S(1)} collective-permute-done((bf16[512,256]{1,0:T(8,128)(2,1)}, bf16[512,256]{1,0:T(8,128)(2,1)S(1)}, u32[]{:S(2)}, u32[]{:S(2)}) %collective-permute-start.17) | collective-permute-done | bytes 262176 | tf_op jit(solution)/shard_map/ppermute | solution.py:111
  128.3 4.3 %shard_map.87.p2.own_ref = bf16[512,256]{1,0:T(8,128)(2,1)} custom-call(bf16[512,2560]{1,0:T(8,128)(2,1)} %shard_map.82.band_ref, bf16[512,256]{1,0:T(8,128)(2,1)} %copy-done.25, bf16[512,256]{1,0:T(8,128)(2,1)} %copy-done.19, bf16[512,256]{1,0:T(8,128)(2,1)} %shard_map.86.p2.own_ref, bf16[512,256]{1,0:T(8,128)(2,1)} %copy-done.31, ...), custom_call_target="tpu_custom_call" | custom-call | flops 805306368 | bytes 4194304 | tf_op jit(solution)/shard_map/pallas_call | solution.py:60
  133.3 8.3 %collective-permute-done.21.p1 = bf16[512,256]{1,0:T(8,128)(2,1)S(1)} collective-permute-done((bf16[512,256]{1,0:T(8,128)(2,1)}, bf16[512,256]{1,0:T(8,128)(2,1)S(1)}, u32[]{:S(2)}, u32[]{:S(2)}) %collective-permute-start.21) | collective-permute-done | bytes 262176 | tf_op jit(solution)/shard_map/ppermute | solution.py:111
  142.5 3.4 %collective-permute-done.20.p0 = bf16[512,256]{1,0:T(8,128)(2,1)S(1)} collective-permute-done((bf16[512,256]{1,0:T(8,128)(2,1)}, bf16[512,256]{1,0:T(8,128)(2,1)S(1)}, u32[]{:S(2)}, u32[]{:S(2)}) %collective-permute-start.20) | collective-permute-done | bytes 262176 | tf_op jit(solution)/shard_map/ppermute | solution.py:111
  150.0 4.3 %shard_map.88.p2.own_ref = bf16[512,256]{1,0:T(8,128)(2,1)} custom-call(bf16[512,2560]{1,0:T(8,128)(2,1)} %shard_map.82.band_ref, bf16[512,256]{1,0:T(8,128)(2,1)} %copy-done.26, bf16[512,256]{1,0:T(8,128)(2,1)} %copy-done.20, bf16[512,256]{1,0:T(8,128)(2,1)} %shard_map.87.p2.own_ref, bf16[512,256]{1,0:T(8,128)(2,1)} %copy-done.32, ...), custom_call_target="tpu_custom_call" | custom-call | flops 805306368 | bytes 4194304 | tf_op jit(solution)/shard_map/pallas_call | solution.py:60
  155.0 8.3 %collective-permute-done.25.p1 = bf16[512,256]{1,0:T(8,128)(2,1)S(1)} collective-permute-done((bf16[512,256]{1,0:T(8,128)(2,1)}, bf16[512,256]{1,0:T(8,128)(2,1)S(1)}, u32[]{:S(2)}, u32[]{:S(2)}) %collective-permute-start.25) | collective-permute-done | bytes 262176 | tf_op jit(solution)/shard_map/ppermute | solution.py:111
  172.0 4.5 %shard_map.89 = bf16[512,256]{1,0:T(8,128)(2,1)} custom-call(bf16[512,2560]{1,0:T(8,128)(2,1)} %shard_map.82.band_ref, bf16[512,256]{1,0:T(8,128)(2,1)} %copy-done.9, bf16[512,256]{1,0:T(8,128)(2,1)} %copy-done.8, bf16[512,256]{1,0:T(8,128)(2,1)} %shard_map.88.p2.own_ref, bf16[512,256]{1,0:T(8,128)(2,1)} %copy-done.27, ...), custom_call_target="tpu_custom_call" | custom-call | flops 805306368 | bytes 4194304 | tf_op jit(solution)/shard_map/pallas_call | solution.py:60
  180.2 11.0 %collective-permute-done.29 = bf16[512,256]{1,0:T(8,128)(2,1)S(1)} collective-permute-done((bf16[512,256]{1,0:T(8,128)(2,1)}, bf16[512,256]{1,0:T(8,128)(2,1)S(1)}, u32[]{:S(2)}, u32[]{:S(2)}) %collective-permute-start.29) | collective-permute-done | bytes 262176 | tf_op jit(solution)/shard_map/ppermute | solution.py:111
  197.7 4.2 %shard_map.90 = bf16[8,512,256]{2,1,0:T(8,128)(2,1)} fusion(bf16[8,512,256]{2,1,0:T(8,128)(2,1)} %bitcast_dynamic-update-slice_fusion.1, bf16[512,2560]{1,0:T(8,128)(2,1)} %shard_map.82.band_ref, bf16[512,256]{1,0:T(8,128)(2,1)} %copy-done.12, bf16[512,256]{1,0:T(8,128)(2,1)} %copy-done.13, bf16[512,256]{1,0:T(8,128)(2,1)} %shard_map.89, ...), kind=kCustom, calls=%fused_computation.4 | custom fusion | bytes 6293504 | tf_op jit(solution)/shard_map/pallas_call | solution.py:60
  205.9 4.7 %collective-permute-done.34 = bf16[512,256]{1,0:T(8,128)(2,1)S(1)} collective-permute-done((bf16[512,256]{1,0:T(8,128)(2,1)S(1)}, bf16[512,256]{1,0:T(8,128)(2,1)S(1)}, u32[]{:S(2)}, u32[]{:S(2)}) %collective-permute-start.34) | collective-permute-done | bytes 262176 | tf_op jit(solution)/shard_map/ppermute | solution.py:157
  213.1 6.7 %collective-permute-done.32 = bf16[512,256]{1,0:T(8,128)(2,1)S(1)} collective-permute-done((bf16[512,256]{1,0:T(8,128)(2,1)S(1)}, bf16[512,256]{1,0:T(8,128)(2,1)S(1)}, u32[]{:S(2)}, u32[]{:S(2)}) %collective-permute-start.32) | collective-permute-done | bytes 262176 | tf_op jit(solution)/shard_map/ppermute | solution.py:157
  (153 shorter events, 84.8 us)
Async XLA Ops:
  6.5 34.7 %all-gather.3.cloned.1.call-start = ((), (), s32[]{:S(2)}) async-start(), calls=%async_computation | async-start | bytes 2359296 | tf_op jit(solution)/shard_map/all_gather | solution.py:99
  8.4 12.7 %collective-permute-start.1 = (bf16[512,256]{1,0:T(8,128)(2,1)S(1)}, bf16[512,256]{1,0:T(8,128)(2,1)S(1)}, u32[]{:S(2)}, u32[]{:S(2)}) collective-permute-start(bf16[512,256]{1,0:T(8,128)(2,1)S(1)} %dynamic-slice_bitcast_fusion.4.p2.own_ref), channel_id=1, source_target_pairs={{0,31},{1,0},{2,1},{3,2},{4,3},{5,4},{6,5},{7,6},{8,7},{9,8},{10,9... | collective-permute-start | bytes 786440 | tf_op jit(solution)/shard_map/ppermute | solution.py:111
  11.0 14.7 %collective-permute-start = (bf16[512,256]{1,0:T(8,128)(2,1)S(1)}, bf16[512,256]{1,0:T(8,128)(2,1)S(1)}, u32[]{:S(2)}, u32[]{:S(2)}) collective-permute-start(bf16[512,256]{1,0:T(8,128)(2,1)S(1)} %dynamic-slice_bitcast_fusion.4.p2.own_ref), channel_id=1, source_target_pairs={{0,30},{1,31},{2,0},{3,1},{4,2},{5,3},{6,4},{7,5},{8,6},{9,7},{10,... | collective-permute-start | bytes 786440 | tf_op jit(solution)/shard_map/ppermute | solution.py:111
  21.1 15.3 %collective-permute-start.2 = (bf16[512,256]{1,0:T(8,128)(2,1)S(1)}, bf16[512,256]{1,0:T(8,128)(2,1)S(1)}, u32[]{:S(2)}, u32[]{:S(2)}) collective-permute-start(bf16[512,256]{1,0:T(8,128)(2,1)S(1)} %collective-permute-done.1.p1), channel_id=1, source_target_pairs={{0,32},{32,0},{64,96},{96,64},{128,160},{160,128},{192,224},{224,1... | collective-permute-start | bytes 786440 | tf_op jit(solution)/shard_map/ppermute | solution.py:115
  25.7 10.7 %collective-permute-start.3 = (bf16[512,256]{1,0:T(8,128)(2,1)S(1)}, bf16[512,256]{1,0:T(8,128)(2,1)S(1)}, u32[]{:S(2)}, u32[]{:S(2)}) collective-permute-start(bf16[512,256]{1,0:T(8,128)(2,1)S(1)} %collective-permute-done.p0), channel_id=1, source_target_pairs={{0,32},{32,0},{64,96},{96,64},{128,160},{160,128},{192,224},{224,1... | collective-permute-start | bytes 786440 | tf_op jit(solution)/shard_map/ppermute | solution.py:115
  45.6 9.2 %collective-permute-start.5 = (bf16[512,256]{1,0:T(8,128)(2,1)}, bf16[512,256]{1,0:T(8,128)(2,1)S(1)}, u32[]{:S(2)}, u32[]{:S(2)}) collective-permute-start(bf16[512,256]{1,0:T(8,128)(2,1)} %shard_map.83.p2.own_ref), channel_id=1, source_target_pairs={{0,31},{1,0},{2,1},{3,2},{4,3},{5,4},{6,5},{7,6},{8,7},{9,8},{10,9... | collective-permute-start | bytes 786440 | tf_op jit(solution)/shard_map/ppermute | solution.py:111
  46.8 12.8 %collective-permute-start.4 = (bf16[512,256]{1,0:T(8,128)(2,1)}, bf16[512,256]{1,0:T(8,128)(2,1)S(1)}, u32[]{:S(2)}, u32[]{:S(2)}) collective-permute-start(bf16[512,256]{1,0:T(8,128)(2,1)} %shard_map.83.p2.own_ref), channel_id=1, source_target_pairs={{0,30},{1,31},{2,0},{3,1},{4,2},{5,3},{6,4},{7,5},{8,6},{9,7},{10,... | collective-permute-start | bytes 786440 | tf_op jit(solution)/shard_map/ppermute | solution.py:111
  67.4 8.9 %collective-permute-start.9 = (bf16[512,256]{1,0:T(8,128)(2,1)}, bf16[512,256]{1,0:T(8,128)(2,1)S(1)}, u32[]{:S(2)}, u32[]{:S(2)}) collective-permute-start(bf16[512,256]{1,0:T(8,128)(2,1)} %shard_map.84.p2.own_ref), channel_id=1, source_target_pairs={{0,31},{1,0},{2,1},{3,2},{4,3},{5,4},{6,5},{7,6},{8,7},{9,8},{10,9... | collective-permute-start | bytes 786440 | tf_op jit(solution)/shard_map/ppermute | solution.py:111
  68.1 12.4 %collective-permute-start.8 = (bf16[512,256]{1,0:T(8,128)(2,1)}, bf16[512,256]{1,0:T(8,128)(2,1)S(1)}, u32[]{:S(2)}, u32[]{:S(2)}) collective-permute-start(bf16[512,256]{1,0:T(8,128)(2,1)} %shard_map.84.p2.own_ref), channel_id=1, source_target_pairs={{0,30},{1,31},{2,0},{3,1},{4,2},{5,3},{6,4},{7,5},{8,6},{9,7},{10,... | collective-permute-start | bytes 786440 | tf_op jit(solution)/shard_map/ppermute | solution.py:111
  89.0 9.1 %collective-permute-start.13 = (bf16[512,256]{1,0:T(8,128)(2,1)}, bf16[512,256]{1,0:T(8,128)(2,1)S(1)}, u32[]{:S(2)}, u32[]{:S(2)}) collective-permute-start(bf16[512,256]{1,0:T(8,128)(2,1)} %shard_map.85.p2.own_ref), channel_id=1, source_target_pairs={{0,31},{1,0},{2,1},{3,2},{4,3},{5,4},{6,5},{7,6},{8,7},{9,8},{10,9... | collective-permute-start | bytes 786440 | tf_op jit(solution)/shard_map/ppermute | solution.py:111
  89.7 12.5 %collective-permute-start.12 = (bf16[512,256]{1,0:T(8,128)(2,1)}, bf16[512,256]{1,0:T(8,128)(2,1)S(1)}, u32[]{:S(2)}, u32[]{:S(2)}) collective-permute-start(bf16[512,256]{1,0:T(8,128)(2,1)} %shard_map.85.p2.own_ref), channel_id=1, source_target_pairs={{0,30},{1,31},{2,0},{3,1},{4,2},{5,3},{6,4},{7,5},{8,6},{9,7},{10,... | collective-permute-start | bytes 786440 | tf_op jit(solution)/shard_map/ppermute | solution.py:111
  110.8 9.0 %collective-permute-start.17 = (bf16[512,256]{1,0:T(8,128)(2,1)}, bf16[512,256]{1,0:T(8,128)(2,1)S(1)}, u32[]{:S(2)}, u32[]{:S(2)}) collective-permute-start(bf16[512,256]{1,0:T(8,128)(2,1)} %shard_map.86.p2.own_ref), channel_id=1, source_target_pairs={{0,31},{1,0},{2,1},{3,2},{4,3},{5,4},{6,5},{7,6},{8,7},{9,8},{10,9... | collective-permute-start | bytes 786440 | tf_op jit(solution)/shard_map/ppermute | solution.py:111
  111.5 12.5 %collective-permute-start.16 = (bf16[512,256]{1,0:T(8,128)(2,1)}, bf16[512,256]{1,0:T(8,128)(2,1)S(1)}, u32[]{:S(2)}, u32[]{:S(2)}) collective-permute-start(bf16[512,256]{1,0:T(8,128)(2,1)} %shard_map.86.p2.own_ref), channel_id=1, source_target_pairs={{0,30},{1,31},{2,0},{3,1},{4,2},{5,3},{6,4},{7,5},{8,6},{9,7},{10,... | collective-permute-start | bytes 786440 | tf_op jit(solution)/shard_map/ppermute | solution.py:111
  119.9 6.5 %collective-permute-start.18 = (bf16[512,256]{1,0:T(8,128)(2,1)S(1)}, bf16[512,256]{1,0:T(8,128)(2,1)S(1)}, u32[]{:S(2)}, u32[]{:S(2)}) collective-permute-start(bf16[512,256]{1,0:T(8,128)(2,1)S(1)} %collective-permute-done.17.p1), channel_id=1, source_target_pairs={{0,32},{32,0},{64,96},{96,64},{128,160},{160,128},{192,224},{224,1... | collective-permute-start | bytes 786440 | tf_op jit(solution)/shard_map/ppermute | solution.py:115
  132.6 9.0 %collective-permute-start.21 = (bf16[512,256]{1,0:T(8,128)(2,1)}, bf16[512,256]{1,0:T(8,128)(2,1)S(1)}, u32[]{:S(2)}, u32[]{:S(2)}) collective-permute-start(bf16[512,256]{1,0:T(8,128)(2,1)} %shard_map.87.p2.own_ref), channel_id=1, source_target_pairs={{0,31},{1,0},{2,1},{3,2},{4,3},{5,4},{6,5},{7,6},{8,7},{9,8},{10,9... | collective-permute-start | bytes 786440 | tf_op jit(solution)/shard_map/ppermute | solution.py:111
  133.3 12.5 %collective-permute-start.20 = (bf16[512,256]{1,0:T(8,128)(2,1)}, bf16[512,256]{1,0:T(8,128)(2,1)S(1)}, u32[]{:S(2)}, u32[]{:S(2)}) collective-permute-start(bf16[512,256]{1,0:T(8,128)(2,1)} %shard_map.87.p2.own_ref), channel_id=1, source_target_pairs={{0,30},{1,31},{2,0},{3,1},{4,2},{5,3},{6,4},{7,5},{8,6},{9,7},{10,... | collective-permute-start | bytes 786440 | tf_op jit(solution)/shard_map/ppermute | solution.py:111
  154.4 9.0 %collective-permute-start.25 = (bf16[512,256]{1,0:T(8,128)(2,1)}, bf16[512,256]{1,0:T(8,128)(2,1)S(1)}, u32[]{:S(2)}, u32[]{:S(2)}) collective-permute-start(bf16[512,256]{1,0:T(8,128)(2,1)} %shard_map.88.p2.own_ref), channel_id=1, source_target_pairs={{0,31},{1,0},{2,1},{3,2},{4,3},{5,4},{6,5},{7,6},{8,7},{9,8},{10,9... | collective-permute-start | bytes 786440 | tf_op jit(solution)/shard_map/ppermute | solution.py:111
  155.0 12.5 %collective-permute-start.24 = (bf16[512,256]{1,0:T(8,128)(2,1)}, bf16[512,256]{1,0:T(8,128)(2,1)S(1)}, u32[]{:S(2)}, u32[]{:S(2)}) collective-permute-start(bf16[512,256]{1,0:T(8,128)(2,1)} %shard_map.88.p2.own_ref), channel_id=1, source_target_pairs={{0,30},{1,31},{2,0},{3,1},{4,2},{5,3},{6,4},{7,5},{8,6},{9,7},{10,... | collective-permute-start | bytes 786440 | tf_op jit(solution)/shard_map/ppermute | solution.py:111
  163.4 6.6 %collective-permute-start.26 = (bf16[512,256]{1,0:T(8,128)(2,1)S(1)}, bf16[512,256]{1,0:T(8,128)(2,1)S(1)}, u32[]{:S(2)}, u32[]{:S(2)}) collective-permute-start(bf16[512,256]{1,0:T(8,128)(2,1)S(1)} %collective-permute-done.25.p1), channel_id=1, source_target_pairs={{0,32},{32,0},{64,96},{96,64},{128,160},{160,128},{192,224},{224,1... | collective-permute-start | bytes 786440 | tf_op jit(solution)/shard_map/ppermute | solution.py:115
  176.5 16.4 %collective-permute-start.28 = (bf16[512,256]{1,0:T(8,128)(2,1)}, bf16[512,256]{1,0:T(8,128)(2,1)S(1)}, u32[]{:S(2)}, u32[]{:S(2)}) collective-permute-start(bf16[512,256]{1,0:T(8,128)(2,1)} %shard_map.89), channel_id=1, source_target_pairs={{0,30},{1,31},{2,0},{3,1},{4,2},{5,3},{6,4},{7,5},{8,6},{9,7},{10,... | collective-permute-start | bytes 786440 | tf_op jit(solution)/shard_map/ppermute | solution.py:111
  176.5 14.7 %collective-permute-start.29 = (bf16[512,256]{1,0:T(8,128)(2,1)}, bf16[512,256]{1,0:T(8,128)(2,1)S(1)}, u32[]{:S(2)}, u32[]{:S(2)}) collective-permute-start(bf16[512,256]{1,0:T(8,128)(2,1)} %shard_map.89), channel_id=1, source_target_pairs={{0,31},{1,0},{2,1},{3,2},{4,3},{5,4},{6,5},{7,6},{8,7},{9,8},{10,9... | collective-permute-start | bytes 786440 | tf_op jit(solution)/shard_map/ppermute | solution.py:111
  203.2 7.5 %collective-permute-start.34 = (bf16[512,256]{1,0:T(8,128)(2,1)S(1)}, bf16[512,256]{1,0:T(8,128)(2,1)S(1)}, u32[]{:S(2)}, u32[]{:S(2)}) collective-permute-start(bf16[512,256]{1,0:T(8,128)(2,1)S(1)} %get-tuple-element.6), channel_id=1, source_target_pairs={{0,192},{32,224},{64,0},{96,32},{128,64},{160,96},{192,128},{224,1... | collective-permute-start | bytes 786440 | tf_op jit(solution)/shard_map/ppermute | solution.py:157
  204.5 8.7 %collective-permute-start.33 = (bf16[512,256]{1,0:T(8,128)(2,1)S(1)}, bf16[512,256]{1,0:T(8,128)(2,1)S(1)}, u32[]{:S(2)}, u32[]{:S(2)}) collective-permute-start(bf16[512,256]{1,0:T(8,128)(2,1)S(1)} %get-tuple-element.7), channel_id=1, source_target_pairs={{0,128},{32,160},{64,192},{96,224},{128,0},{160,32},{192,64},{224,... | collective-permute-start | bytes 786440 | tf_op jit(solution)/shard_map/ppermute | solution.py:157
  205.2 14.6 %collective-permute-start.32 = (bf16[512,256]{1,0:T(8,128)(2,1)S(1)}, bf16[512,256]{1,0:T(8,128)(2,1)S(1)}, u32[]{:S(2)}, u32[]{:S(2)}) collective-permute-start(bf16[512,256]{1,0:T(8,128)(2,1)S(1)} %get-tuple-element.8), channel_id=1, source_target_pairs={{0,64},{32,96},{64,128},{96,160},{128,192},{160,224},{192,0},{224,... | collective-permute-start | bytes 786440 | tf_op jit(solution)/shard_map/ppermute | solution.py:157
  (50 other events, 337.6 us)
Sparse Core Ops, SparseCore 0:
  9.2 31.9 all-gather.2

commit v10 on v9

--- a/solution.py
+++ b/solution.py
@@ -144,23 +144,33 @@
         hidden = run_layer(band, parts, degree_f, weights_all, level)
         outputs.append(hidden)
 
-    stacked = jnp.stack(outputs)
-    arrived = []
-    for shift in range(0, section_count, group):
-        sending = lax.dynamic_index_in_dim(
-            stacked, (section_index + shift) % section_count, 0, keepdims=False
-        )
-        if shift == 0:
-            arrived.append(sending)
-        else:
-            pairs = [(s, (s + shift) % section_count) for s in range(section_count)]
-            arrived.append(lax.ppermute(sending, "section", pairs))
-    arrived = jnp.stack(arrived)
+    last = layer_total - 1
+
+    def pick(levels, at):
+        chosen = outputs[levels[0]]
+        for level in levels[1:]:
+            chosen = jnp.where(at == level, outputs[level], chosen)
+        return chosen
+
+    arrived = [pick(list(range(layer_total)), section_index)]
+    for shift in range(group, section_count, group):
+        at = (section_index + shift) % section_count
+        early_pairs = [
+            (s, (s + shift) % section_count)
+            for s in range(section_count)
+            if (s + shift) % section_count != last
+        ]
+        early = lax.ppermute(pick(list(range(last)), at), "section", early_pairs)
+        late = lax.ppermute(outputs[last], "section", [((last - shift) % section_count, last)])
+        arrived.append(jnp.where(section_index == last, late, early))
     chip = section_index // group
-    gathered = [
-        lax.dynamic_index_in_dim(arrived, (chip - m) % batch_total, 0, keepdims=False)
-        for m in range(batch_total)
-    ]
+    gathered = []
+    for m in range(batch_total):
+        which = (chip - m) % batch_total
+        chosen = arrived[0]
+        for j in range(1, batch_total):
+            chosen = jnp.where(which == j, arrived[j], chosen)
+        gathered.append(chosen)
     return jnp.stack(gathered)[None]
 
 

time: 228 us -> 226 us (level)
  local copies, waits for them, and re-layouts: 23.9 us -> 8.92 us
  starting transfers between devices: 43.5 us -> 56.3 us
  waiting for transfers between devices: 105 us -> 95.9 us
  Pallas kernels: 34 us -> 38.6 us
  other arithmetic: 7.53 us -> 11.2 us
    ppermute x3 -> x6, starting transfers between devices: 2.77 us -> 15 us  [the longest x3 7.93 us: body(): lax.ppermute(outputs[last], 'section', [((last - shift) % section_count,...]
    unnamed x83 -> x78, local copies, waits for them, and re-layouts: 13.8 us -> 4.4 us
    ppermute x3 -> x6, waiting for transfers between devices: 13.9 us -> 4.71 us  [the longest x3 4.7 us: body(): lax.ppermute(outputs[last], 'section', [((last - shift) % section_count,...]
    pallas_call x1 -> x0, local copies, waits for them, and re-layouts: 4.18 us -> none  [run_layer(): pl.pallas_call(_layer_kernel, out_shape=jax.ShapeDtypeStruct((rows, width...]
    pallas_call x7 -> x8, Pallas kernels: 30.4 us -> 34.5 us  [run_layer(): pl.pallas_call(_layer_kernel, out_shape=jax.ShapeDtypeStruct((rows, width...]
    select_n x0 -> x2, other arithmetic: none -> 2.68 us  [pick(): chosen = jnp.where(at == level, outputs[level], chosen)]
  transfers between devices with their start and end apart: 36 -> 39, of which waited for: 24 -> 23; matrix products, arithmetic and copies ran while one was open for 7% -> 5% of each run, Pallas kernels for 2% -> 4%
where the time goes in v10:
time: 226 us; the launch traced here: 225 us
  waiting for transfers between devices  95.9 us (42%)
  starting transfers between devices  56.3 us (25%)
  Pallas kernels  38.6 us (17%)
  between operations  14.3 us (6%)
  other arithmetic  11.2 us (5%)
  local copies, waits for them, and re-layouts  8.92 us (4%)
    ppermute x16, waiting for transfers between devices, halo(): return lax.ppermute(x, ('section', 'blk'), pairs)  79.7 us
    pallas_call x8, Pallas kernels, run_layer(): pl.pallas_call(_layer_kernel, out_shape=jax.ShapeDtypeStruct((rows, width...  34.5 us
    ppermute x16, starting transfers between devices, swap(): return lax.ppermute(x, 'section', pairs)  27.7 us
    ppermute x16, starting transfers between devices, halo(): return lax.ppermute(x, ('section', 'blk'), pairs)  13.6 us
    ppermute x3, starting transfers between devices, body(): lax.ppermute(outputs[last], 'section', [((last - shift) % section_count,...  7.93 us
    ppermute x3, starting transfers between devices, body(): early = lax.ppermute(pick(list(range(last)), at), 'section', early_pairs)  7.08 us
    ppermute x16, waiting for transfers between devices, swap(): return lax.ppermute(x, 'section', pairs)  7.05 us
    ppermute x3, waiting for transfers between devices, body(): lax.ppermute(outputs[last], 'section', [((last - shift) % section_count,...  4.7 us
  transfers between devices with their start and end apart: 39, of which 23 were waited for; matrix products, arithmetic and copies ran while one was open for 5% of the time, Pallas kernels for 4%

profile of v10, /device:TPU:1, one launch (start us, length us, event | category | flops | bytes accessed | tf_op | source)
XLA Modules:
  0.0 225.3 jit_solution(11231544925978630241)
XLA Ops:
  21.1 3.3 %collective-permute-start.2 = (bf16[512,256]{1,0:T(8,128)(2,1)S(1)}, bf16[512,256]{1,0:T(8,128)(2,1)S(1)}, u32[]{:S(2)}, u32[]{:S(2)}) collective-permute-start(bf16[512,256]{1,0:T(8,128)(2,1)S(1)} %collective-permute-done.1.p1), channel_id=1, source_target_pairs={{0,32},{32,0},{64,96},{96,64},{128,160},{160,128},{192,224},{224,1... | collective-permute-start | bytes 786440 | tf_op jit(solution)/shard_map/ppermute | solution.py:115
  29.1 3.6 %dynamic-slice_bitcast_fusion.values_ref = bf16[80,128,128]{2,1,0:T(8,128)(2,1)} fusion(bf16[4,80,128,128]{3,2,1,0:T(8,128)(2,1)} %param.9, s32[]{:T(128)S(6)} %select_n.316), kind=kLoop, calls=%fused_computation | loop fusion | bytes 5242884 | tf_op jit(solution)/shard_map/jit(dynamic_index_in_dim)/squeeze | solution.py:117
  32.7 4.1 %shard_map.82.band_ref = bf16[512,2560]{1,0:T(8,128)(2,1)} custom-call(s32[80]{0:T(128)} %fusion.5.rows_ref, s32[80]{0:T(128)} %fusion.6.cols_ref, s32[1]{0:T(128)} %bitcast.2.count_ref, bf16[80,128,128]{2,1,0:T(8,128)(2,1)} %dynamic-slice_bitcast_fusion.values_ref), custom_call_target="tpu_custom_call" | custom-call | tf_op jit(solution)/shard_map/pallas_call | solution.py:25
  36.8 4.4 %all-gather.3.cloned.1.call-done = bf16[16,256,256]{2,1,0:T(8,128)(2,1)} async-done(((bf16[2,256,256]{2,1,0:T(8,128)(2,1)}), bf16[16,256,256]{2,1,0:T(8,128)(2,1)}) %all-gather.3.cloned.1.call-update) | async-done | bytes 2097168 | tf_op jit(solution)/shard_map/all_gather | solution.py:99
  41.2 4.3 %shard_map.83.p2.own_ref = bf16[512,256]{1,0:T(8,128)(2,1)} custom-call(bf16[512,2560]{1,0:T(8,128)(2,1)} %shard_map.82.band_ref, bf16[512,256]{1,0:T(8,128)(2,1)} %copy-done.13, bf16[512,256]{1,0:T(8,128)(2,1)} %copy-done.12, bf16[512,256]{1,0:T(8,128)(2,1)} %copy-done.8, bf16[512,256]{1,0:T(8,128)(2,1)} %copy-done.17, bf16[512,256]{1,0:T(8,128)(2,1)} %copy-done.18, ...), custom_call_target="tpu_custom_call" | custom-call | flops 805306368 | bytes 4194304 | tf_op jit(solution)/shard_map/pallas_call | solution.py:60
  49.1 5.6 %collective-permute-done.5.p1 = bf16[512,256]{1,0:T(8,128)(2,1)S(1)} collective-permute-done((bf16[512,256]{1,0:T(8,128)(2,1)}, bf16[512,256]{1,0:T(8,128)(2,1)S(1)}, u32[]{:S(2)}, u32[]{:S(2)}) %collective-permute-start.5) | collective-permute-done | bytes 262176 | tf_op jit(solution)/shard_map/ppermute | solution.py:111
  63.1 4.3 %shard_map.84.p2.own_ref = bf16[512,256]{1,0:T(8,128)(2,1)} custom-call(bf16[512,2560]{1,0:T(8,128)(2,1)} %shard_map.82.band_ref, bf16[512,256]{1,0:T(8,128)(2,1)} %copy-done.24, bf16[512,256]{1,0:T(8,128)(2,1)} %copy-done.19, bf16[512,256]{1,0:T(8,128)(2,1)} %shard_map.83.p2.own_ref, bf16[512,256]{1,0:T(8,128)(2,1)} %copy-done.29, ...), custom_call_target="tpu_custom_call" | custom-call | flops 805306368 | bytes 4194304 | tf_op jit(solution)/shard_map/pallas_call | solution.py:60
  68.7 7.6 %collective-permute-done.9.p1 = bf16[512,256]{1,0:T(8,128)(2,1)S(1)} collective-permute-done((bf16[512,256]{1,0:T(8,128)(2,1)}, bf16[512,256]{1,0:T(8,128)(2,1)S(1)}, u32[]{:S(2)}, u32[]{:S(2)}) %collective-permute-start.9) | collective-permute-done | bytes 262176 | tf_op jit(solution)/shard_map/ppermute | solution.py:111
  77.2 3.4 %collective-permute-done.8.p0 = bf16[512,256]{1,0:T(8,128)(2,1)S(1)} collective-permute-done((bf16[512,256]{1,0:T(8,128)(2,1)}, bf16[512,256]{1,0:T(8,128)(2,1)S(1)}, u32[]{:S(2)}, u32[]{:S(2)}) %collective-permute-start.8) | collective-permute-done | bytes 262176 | tf_op jit(solution)/shard_map/ppermute | solution.py:111
  84.7 4.3 %shard_map.85.p2.own_ref = bf16[512,256]{1,0:T(8,128)(2,1)} custom-call(bf16[512,2560]{1,0:T(8,128)(2,1)} %shard_map.82.band_ref, bf16[512,256]{1,0:T(8,128)(2,1)} %copy-done.25, bf16[512,256]{1,0:T(8,128)(2,1)} %copy-done.20, bf16[512,256]{1,0:T(8,128)(2,1)} %shard_map.84.p2.own_ref, bf16[512,256]{1,0:T(8,128)(2,1)} %copy-done.30, ...), custom_call_target="tpu_custom_call" | custom-call | flops 805306368 | bytes 4194304 | tf_op jit(solution)/shard_map/pallas_call | solution.py:60
  89.7 8.4 %collective-permute-done.13.p1 = bf16[512,256]{1,0:T(8,128)(2,1)S(1)} collective-permute-done((bf16[512,256]{1,0:T(8,128)(2,1)}, bf16[512,256]{1,0:T(8,128)(2,1)S(1)}, u32[]{:S(2)}, u32[]{:S(2)}) %collective-permute-start.13) | collective-permute-done | bytes 262176 | tf_op jit(solution)/shard_map/ppermute | solution.py:111
  106.5 4.3 %shard_map.86.p2.own_ref = bf16[512,256]{1,0:T(8,128)(2,1)} custom-call(bf16[512,2560]{1,0:T(8,128)(2,1)} %shard_map.82.band_ref, bf16[512,256]{1,0:T(8,128)(2,1)} %copy-done.26, bf16[512,256]{1,0:T(8,128)(2,1)} %copy-done.21, bf16[512,256]{1,0:T(8,128)(2,1)} %shard_map.85.p2.own_ref, bf16[512,256]{1,0:T(8,128)(2,1)} %copy-done.31, ...), custom_call_target="tpu_custom_call" | custom-call | flops 805306368 | bytes 4194304 | tf_op jit(solution)/shard_map/pallas_call | solution.py:60
  111.5 8.4 %collective-permute-done.17.p1 = bf16[512,256]{1,0:T(8,128)(2,1)S(1)} collective-permute-done((bf16[512,256]{1,0:T(8,128)(2,1)}, bf16[512,256]{1,0:T(8,128)(2,1)S(1)}, u32[]{:S(2)}, u32[]{:S(2)}) %collective-permute-start.17) | collective-permute-done | bytes 262176 | tf_op jit(solution)/shard_map/ppermute | solution.py:111
  128.3 4.3 %shard_map.87.p2.own_ref = bf16[512,256]{1,0:T(8,128)(2,1)} custom-call(bf16[512,2560]{1,0:T(8,128)(2,1)} %shard_map.82.band_ref, bf16[512,256]{1,0:T(8,128)(2,1)} %copy-done.27, bf16[512,256]{1,0:T(8,128)(2,1)} %copy-done.22, bf16[512,256]{1,0:T(8,128)(2,1)} %shard_map.86.p2.own_ref, bf16[512,256]{1,0:T(8,128)(2,1)} %copy-done.32, ...), custom_call_target="tpu_custom_call" | custom-call | flops 805306368 | bytes 4194304 | tf_op jit(solution)/shard_map/pallas_call | solution.py:60
  133.2 8.3 %collective-permute-done.21.p1 = bf16[512,256]{1,0:T(8,128)(2,1)S(1)} collective-permute-done((bf16[512,256]{1,0:T(8,128)(2,1)}, bf16[512,256]{1,0:T(8,128)(2,1)S(1)}, u32[]{:S(2)}, u32[]{:S(2)}) %collective-permute-start.21) | collective-permute-done | bytes 262176 | tf_op jit(solution)/shard_map/ppermute | solution.py:111
  142.4 3.4 %collective-permute-done.20.p0 = bf16[512,256]{1,0:T(8,128)(2,1)S(1)} collective-permute-done((bf16[512,256]{1,0:T(8,128)(2,1)}, bf16[512,256]{1,0:T(8,128)(2,1)S(1)}, u32[]{:S(2)}, u32[]{:S(2)}) %collective-permute-start.20) | collective-permute-done | bytes 262176 | tf_op jit(solution)/shard_map/ppermute | solution.py:111
  149.9 4.3 %shard_map.88.p2.own_ref = bf16[512,256]{1,0:T(8,128)(2,1)} custom-call(bf16[512,2560]{1,0:T(8,128)(2,1)} %shard_map.82.band_ref, bf16[512,256]{1,0:T(8,128)(2,1)} %copy-done.28, bf16[512,256]{1,0:T(8,128)(2,1)} %copy-done.23, bf16[512,256]{1,0:T(8,128)(2,1)} %shard_map.87.p2.own_ref, bf16[512,256]{1,0:T(8,128)(2,1)} %copy-done.33, ...), custom_call_target="tpu_custom_call" | custom-call | flops 805306368 | bytes 4194304 | tf_op jit(solution)/shard_map/pallas_call | solution.py:60
  154.9 8.4 %collective-permute-done.25.p1 = bf16[512,256]{1,0:T(8,128)(2,1)S(1)} collective-permute-done((bf16[512,256]{1,0:T(8,128)(2,1)}, bf16[512,256]{1,0:T(8,128)(2,1)S(1)}, u32[]{:S(2)}, u32[]{:S(2)}) %collective-permute-start.25) | collective-permute-done | bytes 262176 | tf_op jit(solution)/shard_map/ppermute | solution.py:111
  171.2 4.3 %shard_map.89.p2.own_ref = bf16[512,256]{1,0:T(8,128)(2,1)} custom-call(bf16[512,2560]{1,0:T(8,128)(2,1)} %shard_map.82.band_ref, bf16[512,256]{1,0:T(8,128)(2,1)} %copy-done.10, bf16[512,256]{1,0:T(8,128)(2,1)} %copy-done.9, bf16[512,256]{1,0:T(8,128)(2,1)} %shard_map.88.p2.own_ref, bf16[512,256]{1,0:T(8,128)(2,1)} %copy-done.11, ...), custom_call_target="tpu_custom_call" | custom-call | flops 805306368 | bytes 4194304 | tf_op jit(solution)/shard_map/pallas_call | solution.py:60
  180.0 10.2 %collective-permute-done.29.p1 = bf16[512,256]{1,0:T(8,128)(2,1)S(1)} collective-permute-done((bf16[512,256]{1,0:T(8,128)(2,1)}, bf16[512,256]{1,0:T(8,128)(2,1)S(1)}, u32[]{:S(2)}, u32[]{:S(2)}) %collective-permute-start.29) | collective-permute-done | bytes 262176 | tf_op jit(solution)/shard_map/ppermute | solution.py:111
  193.2 3.7 %collective-permute-start.35 = (bf16[512,256]{1,0:T(8,128)(2,1)}, bf16[512,256]{1,0:T(8,128)(2,1)S(1)}, u32[]{:S(2)}, u32[]{:S(2)}) collective-permute-start(bf16[512,256]{1,0:T(8,128)(2,1)} %select_select_fusion.2), channel_id=1, source_target_pairs={{0,128},{32,160},{64,192},{128,0},{160,32},{192,64},{224,96},{1,12... | collective-permute-start | bytes 786440 | tf_op jit(solution)/shard_map/ppermute | solution.py:163
  199.1 4.3 %shard_map.90 = bf16[512,256]{1,0:T(8,128)(2,1)} custom-call(bf16[512,2560]{1,0:T(8,128)(2,1)} %shard_map.82.band_ref, bf16[512,256]{1,0:T(8,128)(2,1)} %copy-done.14, bf16[512,256]{1,0:T(8,128)(2,1)} %copy-done.15, bf16[512,256]{1,0:T(8,128)(2,1)} %shard_map.89.p2.own_ref, bf16[512,256]{1,0:T(8,128)(2,1)} %copy-done.16, ...), custom_call_target="tpu_custom_call" | custom-call | flops 805306368 | bytes 4194304 | tf_op jit(solution)/shard_map/pallas_call | solution.py:60
  206.2 5.2 %collective-permute-start.32 = (bf16[512,256]{1,0:T(8,128)(2,1)}, bf16[512,256]{1,0:T(8,128)(2,1)}, u32[]{:S(2)}, u32[]{:S(2)}) collective-permute-start(bf16[512,256]{1,0:T(8,128)(2,1)} %shard_map.90), channel_id=1, source_target_pairs={{32,224},{33,225},{34,226},{35,227},{36,228},{37,229},{38,230},{39... | collective-permute-start | bytes 786440 | tf_op jit(solution)/shard_map/ppermute | solution.py:164
  211.4 4.7 %collective-permute-done.32 = bf16[512,256]{1,0:T(8,128)(2,1)} collective-permute-done((bf16[512,256]{1,0:T(8,128)(2,1)}, bf16[512,256]{1,0:T(8,128)(2,1)}, u32[]{:S(2)}, u32[]{:S(2)}) %collective-permute-start.32) | collective-permute-done | bytes 262176 | tf_op jit(solution)/shard_map/ppermute | solution.py:164
  (155 shorter events, 83.7 us)
Async XLA Ops:
  6.5 34.7 %all-gather.3.cloned.1.call-start = ((), (), s32[]{:S(2)}) async-start(), calls=%async_computation | async-start | bytes 2359296 | tf_op jit(solution)/shard_map/all_gather | solution.py:99
  8.4 12.7 %collective-permute-start.1 = (bf16[512,256]{1,0:T(8,128)(2,1)S(1)}, bf16[512,256]{1,0:T(8,128)(2,1)S(1)}, u32[]{:S(2)}, u32[]{:S(2)}) collective-permute-start(bf16[512,256]{1,0:T(8,128)(2,1)S(1)} %dynamic-slice_bitcast_fusion.1.p2.own_ref), channel_id=1, source_target_pairs={{0,31},{1,0},{2,1},{3,2},{4,3},{5,4},{6,5},{7,6},{8,7},{9,8},{10,9... | collective-permute-start | bytes 786440 | tf_op jit(solution)/shard_map/ppermute | solution.py:111
  11.0 14.7 %collective-permute-start = (bf16[512,256]{1,0:T(8,128)(2,1)S(1)}, bf16[512,256]{1,0:T(8,128)(2,1)S(1)}, u32[]{:S(2)}, u32[]{:S(2)}) collective-permute-start(bf16[512,256]{1,0:T(8,128)(2,1)S(1)} %dynamic-slice_bitcast_fusion.1.p2.own_ref), channel_id=1, source_target_pairs={{0,30},{1,31},{2,0},{3,1},{4,2},{5,3},{6,4},{7,5},{8,6},{9,7},{10,... | collective-permute-start | bytes 786440 | tf_op jit(solution)/shard_map/ppermute | solution.py:111
  21.1 15.7 %collective-permute-start.2 = (bf16[512,256]{1,0:T(8,128)(2,1)S(1)}, bf16[512,256]{1,0:T(8,128)(2,1)S(1)}, u32[]{:S(2)}, u32[]{:S(2)}) collective-permute-start(bf16[512,256]{1,0:T(8,128)(2,1)S(1)} %collective-permute-done.1.p1), channel_id=1, source_target_pairs={{0,32},{32,0},{64,96},{96,64},{128,160},{160,128},{192,224},{224,1... | collective-permute-start | bytes 786440 | tf_op jit(solution)/shard_map/ppermute | solution.py:115
  25.7 11.1 %collective-permute-start.3 = (bf16[512,256]{1,0:T(8,128)(2,1)S(1)}, bf16[512,256]{1,0:T(8,128)(2,1)S(1)}, u32[]{:S(2)}, u32[]{:S(2)}) collective-permute-start(bf16[512,256]{1,0:T(8,128)(2,1)S(1)} %collective-permute-done.p0), channel_id=1, source_target_pairs={{0,32},{32,0},{64,96},{96,64},{128,160},{160,128},{192,224},{224,1... | collective-permute-start | bytes 786440 | tf_op jit(solution)/shard_map/ppermute | solution.py:115
  45.6 9.2 %collective-permute-start.5 = (bf16[512,256]{1,0:T(8,128)(2,1)}, bf16[512,256]{1,0:T(8,128)(2,1)S(1)}, u32[]{:S(2)}, u32[]{:S(2)}) collective-permute-start(bf16[512,256]{1,0:T(8,128)(2,1)} %shard_map.83.p2.own_ref), channel_id=1, source_target_pairs={{0,31},{1,0},{2,1},{3,2},{4,3},{5,4},{6,5},{7,6},{8,7},{9,8},{10,9... | collective-permute-start | bytes 786440 | tf_op jit(solution)/shard_map/ppermute | solution.py:111
  46.8 12.8 %collective-permute-start.4 = (bf16[512,256]{1,0:T(8,128)(2,1)}, bf16[512,256]{1,0:T(8,128)(2,1)S(1)}, u32[]{:S(2)}, u32[]{:S(2)}) collective-permute-start(bf16[512,256]{1,0:T(8,128)(2,1)} %shard_map.83.p2.own_ref), channel_id=1, source_target_pairs={{0,30},{1,31},{2,0},{3,1},{4,2},{5,3},{6,4},{7,5},{8,6},{9,7},{10,... | collective-permute-start | bytes 786440 | tf_op jit(solution)/shard_map/ppermute | solution.py:111
  67.4 8.9 %collective-permute-start.9 = (bf16[512,256]{1,0:T(8,128)(2,1)}, bf16[512,256]{1,0:T(8,128)(2,1)S(1)}, u32[]{:S(2)}, u32[]{:S(2)}) collective-permute-start(bf16[512,256]{1,0:T(8,128)(2,1)} %shard_map.84.p2.own_ref), channel_id=1, source_target_pairs={{0,31},{1,0},{2,1},{3,2},{4,3},{5,4},{6,5},{7,6},{8,7},{9,8},{10,9... | collective-permute-start | bytes 786440 | tf_op jit(solution)/shard_map/ppermute | solution.py:111
  68.1 12.4 %collective-permute-start.8 = (bf16[512,256]{1,0:T(8,128)(2,1)}, bf16[512,256]{1,0:T(8,128)(2,1)S(1)}, u32[]{:S(2)}, u32[]{:S(2)}) collective-permute-start(bf16[512,256]{1,0:T(8,128)(2,1)} %shard_map.84.p2.own_ref), channel_id=1, source_target_pairs={{0,30},{1,31},{2,0},{3,1},{4,2},{5,3},{6,4},{7,5},{8,6},{9,7},{10,... | collective-permute-start | bytes 786440 | tf_op jit(solution)/shard_map/ppermute | solution.py:111
  89.0 9.1 %collective-permute-start.13 = (bf16[512,256]{1,0:T(8,128)(2,1)}, bf16[512,256]{1,0:T(8,128)(2,1)S(1)}, u32[]{:S(2)}, u32[]{:S(2)}) collective-permute-start(bf16[512,256]{1,0:T(8,128)(2,1)} %shard_map.85.p2.own_ref), channel_id=1, source_target_pairs={{0,31},{1,0},{2,1},{3,2},{4,3},{5,4},{6,5},{7,6},{8,7},{9,8},{10,9... | collective-permute-start | bytes 786440 | tf_op jit(solution)/shard_map/ppermute | solution.py:111
  89.7 12.5 %collective-permute-start.12 = (bf16[512,256]{1,0:T(8,128)(2,1)}, bf16[512,256]{1,0:T(8,128)(2,1)S(1)}, u32[]{:S(2)}, u32[]{:S(2)}) collective-permute-start(bf16[512,256]{1,0:T(8,128)(2,1)} %shard_map.85.p2.own_ref), channel_id=1, source_target_pairs={{0,30},{1,31},{2,0},{3,1},{4,2},{5,3},{6,4},{7,5},{8,6},{9,7},{10,... | collective-permute-start | bytes 786440 | tf_op jit(solution)/shard_map/ppermute | solution.py:111
  110.9 9.0 %collective-permute-start.17 = (bf16[512,256]{1,0:T(8,128)(2,1)}, bf16[512,256]{1,0:T(8,128)(2,1)S(1)}, u32[]{:S(2)}, u32[]{:S(2)}) collective-permute-start(bf16[512,256]{1,0:T(8,128)(2,1)} %shard_map.86.p2.own_ref), channel_id=1, source_target_pairs={{0,31},{1,0},{2,1},{3,2},{4,3},{5,4},{6,5},{7,6},{8,7},{9,8},{10,9... | collective-permute-start | bytes 786440 | tf_op jit(solution)/shard_map/ppermute | solution.py:111
  111.5 12.5 %collective-permute-start.16 = (bf16[512,256]{1,0:T(8,128)(2,1)}, bf16[512,256]{1,0:T(8,128)(2,1)S(1)}, u32[]{:S(2)}, u32[]{:S(2)}) collective-permute-start(bf16[512,256]{1,0:T(8,128)(2,1)} %shard_map.86.p2.own_ref), channel_id=1, source_target_pairs={{0,30},{1,31},{2,0},{3,1},{4,2},{5,3},{6,4},{7,5},{8,6},{9,7},{10,... | collective-permute-start | bytes 786440 | tf_op jit(solution)/shard_map/ppermute | solution.py:111
  132.6 8.9 %collective-permute-start.21 = (bf16[512,256]{1,0:T(8,128)(2,1)}, bf16[512,256]{1,0:T(8,128)(2,1)S(1)}, u32[]{:S(2)}, u32[]{:S(2)}) collective-permute-start(bf16[512,256]{1,0:T(8,128)(2,1)} %shard_map.87.p2.own_ref), channel_id=1, source_target_pairs={{0,31},{1,0},{2,1},{3,2},{4,3},{5,4},{6,5},{7,6},{8,7},{9,8},{10,9... | collective-permute-start | bytes 786440 | tf_op jit(solution)/shard_map/ppermute | solution.py:111
  133.2 12.5 %collective-permute-start.20 = (bf16[512,256]{1,0:T(8,128)(2,1)}, bf16[512,256]{1,0:T(8,128)(2,1)S(1)}, u32[]{:S(2)}, u32[]{:S(2)}) collective-permute-start(bf16[512,256]{1,0:T(8,128)(2,1)} %shard_map.87.p2.own_ref), channel_id=1, source_target_pairs={{0,30},{1,31},{2,0},{3,1},{4,2},{5,3},{6,4},{7,5},{8,6},{9,7},{10,... | collective-permute-start | bytes 786440 | tf_op jit(solution)/shard_map/ppermute | solution.py:111
  154.3 9.0 %collective-permute-start.25 = (bf16[512,256]{1,0:T(8,128)(2,1)}, bf16[512,256]{1,0:T(8,128)(2,1)S(1)}, u32[]{:S(2)}, u32[]{:S(2)}) collective-permute-start(bf16[512,256]{1,0:T(8,128)(2,1)} %shard_map.88.p2.own_ref), channel_id=1, source_target_pairs={{0,31},{1,0},{2,1},{3,2},{4,3},{5,4},{6,5},{7,6},{8,7},{9,8},{10,9... | collective-permute-start | bytes 786440 | tf_op jit(solution)/shard_map/ppermute | solution.py:111
  154.9 12.5 %collective-permute-start.24 = (bf16[512,256]{1,0:T(8,128)(2,1)}, bf16[512,256]{1,0:T(8,128)(2,1)S(1)}, u32[]{:S(2)}, u32[]{:S(2)}) collective-permute-start(bf16[512,256]{1,0:T(8,128)(2,1)} %shard_map.88.p2.own_ref), channel_id=1, source_target_pairs={{0,30},{1,31},{2,0},{3,1},{4,2},{5,3},{6,4},{7,5},{8,6},{9,7},{10,... | collective-permute-start | bytes 786440 | tf_op jit(solution)/shard_map/ppermute | solution.py:111
  175.5 16.8 %collective-permute-start.28 = (bf16[512,256]{1,0:T(8,128)(2,1)}, bf16[512,256]{1,0:T(8,128)(2,1)S(1)}, u32[]{:S(2)}, u32[]{:S(2)}) collective-permute-start(bf16[512,256]{1,0:T(8,128)(2,1)} %shard_map.89.p2.own_ref), channel_id=1, source_target_pairs={{0,30},{1,31},{2,0},{3,1},{4,2},{5,3},{6,4},{7,5},{8,6},{9,7},{10,... | collective-permute-start | bytes 786440 | tf_op jit(solution)/shard_map/ppermute | solution.py:111
  175.5 14.7 %collective-permute-start.29 = (bf16[512,256]{1,0:T(8,128)(2,1)}, bf16[512,256]{1,0:T(8,128)(2,1)S(1)}, u32[]{:S(2)}, u32[]{:S(2)}) collective-permute-start(bf16[512,256]{1,0:T(8,128)(2,1)} %shard_map.89.p2.own_ref), channel_id=1, source_target_pairs={{0,31},{1,0},{2,1},{3,2},{4,3},{5,4},{6,5},{7,6},{8,7},{9,8},{10,9... | collective-permute-start | bytes 786440 | tf_op jit(solution)/shard_map/ppermute | solution.py:111
  178.0 28.1 %collective-permute-start.37 = (bf16[512,256]{1,0:T(8,128)(2,1)}, bf16[512,256]{1,0:T(8,128)(2,1)S(1)}, u32[]{:S(2)}, u32[]{:S(2)}) collective-permute-start(bf16[512,256]{1,0:T(8,128)(2,1)} %get-tuple-element.11), channel_id=1, source_target_pairs={{0,64},{32,96},{64,128},{96,160},{128,192},{192,0},{224,32},{1,65}... | collective-permute-start | bytes 786440 | tf_op jit(solution)/shard_map/ppermute | solution.py:163
  190.2 8.2 %collective-permute-start.30 = (bf16[512,256]{1,0:T(8,128)(2,1)S(1)}, bf16[512,256]{1,0:T(8,128)(2,1)S(1)}, u32[]{:S(2)}, u32[]{:S(2)}) collective-permute-start(bf16[512,256]{1,0:T(8,128)(2,1)S(1)} %collective-permute-done.29.p1), channel_id=1, source_target_pairs={{0,32},{32,0},{64,96},{96,64},{128,160},{160,128},{192,224},{224,1... | collective-permute-start | bytes 786440 | tf_op jit(solution)/shard_map/ppermute | solution.py:115
  193.2 18.2 %collective-permute-start.35 = (bf16[512,256]{1,0:T(8,128)(2,1)}, bf16[512,256]{1,0:T(8,128)(2,1)S(1)}, u32[]{:S(2)}, u32[]{:S(2)}) collective-permute-start(bf16[512,256]{1,0:T(8,128)(2,1)} %select_select_fusion.2), channel_id=1, source_target_pairs={{0,128},{32,160},{64,192},{128,0},{160,32},{192,64},{224,96},{1,12... | collective-permute-start | bytes 786440 | tf_op jit(solution)/shard_map/ppermute | solution.py:163
  196.9 14.4 %collective-permute-start.33 = (bf16[512,256]{1,0:T(8,128)(2,1)}, bf16[512,256]{1,0:T(8,128)(2,1)}, u32[]{:S(2)}, u32[]{:S(2)}) collective-permute-start(bf16[512,256]{1,0:T(8,128)(2,1)} %get-tuple-element.10), channel_id=1, source_target_pairs={{0,192},{64,0},{96,32},{128,64},{160,96},{192,128},{224,160},{1,19... | collective-permute-start | bytes 786440 | tf_op jit(solution)/shard_map/ppermute | solution.py:163
  206.2 9.9 %collective-permute-start.32 = (bf16[512,256]{1,0:T(8,128)(2,1)}, bf16[512,256]{1,0:T(8,128)(2,1)}, u32[]{:S(2)}, u32[]{:S(2)}) collective-permute-start(bf16[512,256]{1,0:T(8,128)(2,1)} %shard_map.90), channel_id=1, source_target_pairs={{32,224},{33,225},{34,226},{35,227},{36,228},{37,229},{38,230},{39... | collective-permute-start | bytes 786440 | tf_op jit(solution)/shard_map/ppermute | solution.py:164
  (54 other events, 280.9 us)
Sparse Core Ops, SparseCore 0:
  9.2 31.9 all-gather.2

commit v11 on v8

--- a/solution.py
+++ b/solution.py
@@ -31,18 +31,37 @@
     )(row_local, column_local, count, values)
 
 
-def _layer_kernel(band_ref, p0, p1, p2, p3, p4, own_ref, degree_ref, ws_ref, wn_ref, out_ref):
-    rows = p2.shape[0]
-    parts = (p0, p1, p2, p3, p4)
-    summed = jnp.dot(
-        band_ref[:, pl.ds(2 * rows, rows)], p2[...], preferred_element_type=jnp.float32
+def _partial_kernel(band_ref, far_ref, near_ref, out_ref):
+    rows = far_ref.shape[0]
+    out_ref[...] = jnp.dot(
+        band_ref[:, pl.ds(0, rows)], far_ref[...], preferred_element_type=jnp.float32
+    ) + jnp.dot(band_ref[:, pl.ds(rows, rows)], near_ref[...], preferred_element_type=jnp.float32)
+
+
+def side_part(band, far, near):
+    rows, width = far.shape
+    return pl.pallas_call(
+        _partial_kernel,
+        out_shape=jax.ShapeDtypeStruct((rows, width), jnp.float32),
+        grid=(1,),
+        in_specs=[
+            pl.BlockSpec((rows, REACH * rows), lambda i: (0, 0)),
+            pl.BlockSpec((rows, width), lambda i: (0, 0)),
+            pl.BlockSpec((rows, width), lambda i: (0, 0)),
+        ],
+        out_specs=pl.BlockSpec((rows, width), lambda i: (0, 0)),
+        cost_estimate=pl.CostEstimate(
+            flops=4 * rows * rows * width,
+            bytes_accessed=2 * rows * rows * 2 + 2 * rows * width * 2 + rows * width * 4,
+            transcendentals=0,
+        ),
+    )(band, far, near)
+
+
+def _layer_kernel(band_ref, own_ref, mine_ref, theirs_ref, degree_ref, ws_ref, wn_ref, out_ref):
+    summed = (mine_ref[...] + theirs_ref[...]) + jnp.dot(
+        band_ref[...], own_ref[...], preferred_element_type=jnp.float32
     )
-    for position in (1, 3, 0, 4):
-        summed = summed + jnp.dot(
-            band_ref[:, pl.ds(position * rows, rows)],
-            parts[position][...],
-            preferred_element_type=jnp.float32,
-        )
     neighbour_mean = (summed / degree_ref[...]).astype(jnp.bfloat16)
     combined = jnp.dot(own_ref[...], ws_ref[...], preferred_element_type=jnp.float32) + jnp.dot(
         neighbour_mean, wn_ref[...], preferred_element_type=jnp.float32
@@ -52,33 +71,29 @@
     out_ref[...] = (active * scale).astype(out_ref.dtype)
 
 
-def run_layer(band, parts, degree_f, weights_all, level, tile):
-    rows, width = parts[2].shape
-    band_cols = band.shape[1]
+def run_layer(band, own, mine, theirs, degree_f, weights_all, level):
+    rows, width = own.shape
     whole = pl.BlockSpec((rows, width), lambda i: (0, 0))
     return pl.pallas_call(
         _layer_kernel,
         out_shape=jax.ShapeDtypeStruct((rows, width), jnp.bfloat16),
-        grid=(rows // tile,),
+        grid=(1,),
         in_specs=[
-            pl.BlockSpec((tile, band_cols), lambda i: (i, 0)),
+            pl.BlockSpec((rows, rows), lambda i: (0, REACH)),
             whole,
             whole,
             whole,
-            whole,
-            whole,
-            pl.BlockSpec((tile, width), lambda i: (i, 0)),
-            pl.BlockSpec((tile, 1), lambda i: (i, 0)),
+            pl.BlockSpec((rows, 1), lambda i: (0, 0)),
             pl.BlockSpec((None, None, width, width), lambda i: (level, 0, 0, 0)),
             pl.BlockSpec((None, None, width, width), lambda i: (level, 1, 0, 0)),
         ],
-        out_specs=pl.BlockSpec((tile, width), lambda i: (i, 0)),
+        out_specs=whole,
         cost_estimate=pl.CostEstimate(
-            flops=2 * rows * band_cols * width + 4 * rows * width * width,
-            bytes_accessed=band.size * 2 + 6 * rows * width * 2,
+            flops=2 * rows * rows * width + 4 * rows * width * width,
+            bytes_accessed=rows * rows * 2 + 2 * rows * width * 2 + 2 * rows * width * 4,
             transcendentals=rows,
         ),
-    )(band, *parts, parts[2], degree_f, weights_all, weights_all)
+    )(band, own, mine, theirs, degree_f, weights_all, weights_all)
 
 
 def body(
@@ -139,8 +154,8 @@
     for level in range(layer_total):
         near = halo(hidden, 1)
         far = halo(hidden, 2)
-        parts = [far, near, hidden, swap(near), swap(far)]
-        hidden = run_layer(band, parts, degree_f, weights_all, level, block_size)
+        mine = side_part(band, far, near)
+        hidden = run_layer(band, hidden, mine, swap(mine), degree_f, weights_all, level)
         outputs.append(hidden)
 
     stacked = jnp.stack(outputs)

time: 238 us -> 238 us (level)
  starting transfers between devices: 43.5 us -> 22.2 us
  waiting for transfers between devices: 104 us -> 121 us
  Pallas kernels: 42.6 us -> 45.8 us
    pallas_call x0 -> x8, Pallas kernels: none -> 20.6 us  [side_part(): pl.pallas_call(_partial_kernel, out_shape=jax.ShapeDtypeStruct((rows, wid...]
    ppermute x16 -> x8, starting transfers between devices: 27.3 us -> 9.42 us  [swap(): return lax.ppermute(x, 'section', pairs)]
    pallas_call x7, Pallas kernels: 38.3 us -> 21.4 us  [run_layer(): pl.pallas_call(_layer_kernel, out_shape=jax.ShapeDtypeStruct((rows, width...]
    ppermute x16, waiting for transfers between devices: 80.3 us -> 93.5 us  [halo(): return lax.ppermute(x, ('section', 'blk'), pairs)]
    ppermute x16 -> x8, waiting for transfers between devices: 5.81 us -> 9.95 us  [swap(): return lax.ppermute(x, 'section', pairs)]
    unnamed x83 -> x65, local copies, waits for them, and re-layouts: 13.8 us -> 17.8 us
    ppermute x16, starting transfers between devices: 13.4 us -> 10.1 us  [halo(): return lax.ppermute(x, ('section', 'blk'), pairs)]
    pallas_call x1, local copies, waits for them, and re-layouts: 5.37 us -> 2.93 us  [run_layer(): pl.pallas_call(_layer_kernel, out_shape=jax.ShapeDtypeStruct((rows, width...]
  transfers between devices with their start and end apart: 36 -> 28, of which waited for: 24 -> 26; matrix products, arithmetic and copies ran while one was open for 7% -> 7% of each run, Pallas kernels for 2% -> 3%
where the time goes in v11:
time: 238 us; the launch traced here: 237 us
  waiting for transfers between devices  121 us (51%)
  Pallas kernels  45.8 us (19%)
  local copies, waits for them, and re-layouts  26.5 us (11%)
  starting transfers between devices  22.2 us (9%)
  between operations  14.2 us (6%)
  other arithmetic  7.45 us (3%)
    ppermute x16, waiting for transfers between devices, halo(): return lax.ppermute(x, ('section', 'blk'), pairs)  93.5 us
    pallas_call x7, Pallas kernels, run_layer(): pl.pallas_call(_layer_kernel, out_shape=jax.ShapeDtypeStruct((rows, width...  21.4 us
    pallas_call x8, Pallas kernels, side_part(): pl.pallas_call(_partial_kernel, out_shape=jax.ShapeDtypeStruct((rows, wid...  20.6 us
    unnamed x65, local copies, waits for them, and re-layouts  17.8 us
    ppermute x3, waiting for transfers between devices, body(): arrived.append(lax.ppermute(sending, 'section', pairs))  13.9 us
    ppermute x16, starting transfers between devices, halo(): return lax.ppermute(x, ('section', 'blk'), pairs)  10.1 us
    ppermute x8, waiting for transfers between devices, swap(): return lax.ppermute(x, 'section', pairs)  9.95 us
    ppermute x8, starting transfers between devices, swap(): return lax.ppermute(x, 'section', pairs)  9.42 us
  transfers between devices with their start and end apart: 28, of which 26 were waited for; matrix products, arithmetic and copies ran while one was open for 7% of the time, Pallas kernels for 3%

profile of v11, /device:TPU:1, one launch (start us, length us, event | category | flops | bytes accessed | tf_op | source)
XLA Modules:
  0.0 237.4 jit_solution(10725687348019358714)
XLA Ops:
  8.5 3.9 %collective-permute-start = (bf16[512,256]{1,0:T(8,128)(2,1)S(1)}, bf16[512,256]{1,0:T(8,128)(2,1)S(1)}, u32[]{:S(2)}, u32[]{:S(2)}) collective-permute-start(bf16[512,256]{1,0:T(8,128)(2,1)S(1)} %dynamic-slice_bitcast_fusion.4.own_ref), channel_id=1, source_target_pairs={{0,30},{1,31},{2,0},{3,1},{4,2},{5,3},{6,4},{7,5},{8,6},{9,7},{10,... | collective-permute-start | bytes 786440 | tf_op jit(solution)/shard_map/ppermute | solution.py:125
  18.3 3.6 %dynamic-slice_bitcast_fusion.values_ref = bf16[80,128,128]{2,1,0:T(8,128)(2,1)} fusion(bf16[4,80,128,128]{3,2,1,0:T(8,128)(2,1)} %param.9, s32[]{:T(128)S(6)} %select_n.106), kind=kLoop, calls=%fused_computation | loop fusion | bytes 5242884 | tf_op jit(solution)/shard_map/jit(dynamic_index_in_dim)/squeeze | solution.py:131
  21.9 3.7 %shard_map.82.band_ref = bf16[512,2560]{1,0:T(8,128)(2,1)} custom-call(s32[80]{0:T(128)} %fusion.7.rows_ref, s32[80]{0:T(128)} %fusion.8.cols_ref, s32[1]{0:T(128)} %bitcast.2.count_ref, bf16[80,128,128]{2,1,0:T(8,128)(2,1)} %dynamic-slice_bitcast_fusion.values_ref), custom_call_target="tpu_custom_call" | custom-call | tf_op jit(solution)/shard_map/pallas_call | solution.py:25
  30.1 5.5 %collective-permute-start.2 = (f32[512,256]{1,0:T(8,128)}, f32[512,256]{1,0:T(8,128)S(1)}, u32[]{:S(2)}, u32[]{:S(2)}) collective-permute-start(f32[512,256]{1,0:T(8,128)} %shard_map.83.mine_ref), channel_id=1, source_target_pairs={{0,32},{32,0},{64,96},{96,64},{128,160},{160,128},{192,224},{224,1... | collective-permute-start | bytes 1572872 | tf_op jit(solution)/shard_map/ppermute | solution.py:129
  37.4 3.8 %all-gather.3.cloned.1.call-done = bf16[16,256,256]{2,1,0:T(8,128)(2,1)} async-done(((bf16[2,256,256]{2,1,0:T(8,128)(2,1)}), bf16[16,256,256]{2,1,0:T(8,128)(2,1)}) %all-gather.3.cloned.1.call-update) | async-done | bytes 2097168 | tf_op jit(solution)/shard_map/all_gather | solution.py:113
  41.2 3.0 %shard_map.84.own_ref = bf16[512,256]{1,0:T(8,128)(2,1)} custom-call(bf16[512,2560]{1,0:T(8,128)(2,1)} %shard_map.82.band_ref, bf16[512,256]{1,0:T(8,128)(2,1)} %copy-done.7, f32[512,256]{1,0:T(8,128)} %shard_map.83.mine_ref, f32[512,256]{1,0:T(8,128)} %copy-done.9, f32[512,1]{1,0:T(8,128)} %copy.17.degree_ref, bf16[8,2,256,256]{3,2,1,0:T(8,128)(2,1)} %bitcast.43, ...), custom_call_target="tpu_custom_call" | custom-call | flops 268435456 | bytes 2097152 | tf_op jit(solution)/shard_map/pallas_call | solution.py:77
  47.8 7.4 %collective-permute-done.3.far_ref = bf16[512,256]{1,0:T(8,128)(2,1)S(1)} collective-permute-done((bf16[512,256]{1,0:T(8,128)(2,1)}, bf16[512,256]{1,0:T(8,128)(2,1)S(1)}, u32[]{:S(2)}, u32[]{:S(2)}) %collective-permute-start.3) | collective-permute-done | bytes 262176 | tf_op jit(solution)/shard_map/ppermute | solution.py:125
  55.2 4.4 %collective-permute-done.4.near_ref = bf16[512,256]{1,0:T(8,128)(2,1)S(1)} collective-permute-done((bf16[512,256]{1,0:T(8,128)(2,1)}, bf16[512,256]{1,0:T(8,128)(2,1)S(1)}, u32[]{:S(2)}, u32[]{:S(2)}) %collective-permute-start.4) | collective-permute-done | bytes 262176 | tf_op jit(solution)/shard_map/ppermute | solution.py:125
  66.5 3.1 %shard_map.86.own_ref = bf16[512,256]{1,0:T(8,128)(2,1)} custom-call(bf16[512,2560]{1,0:T(8,128)(2,1)} %shard_map.82.band_ref, bf16[512,256]{1,0:T(8,128)(2,1)} %shard_map.84.own_ref, f32[512,256]{1,0:T(8,128)} %shard_map.85.mine_ref, f32[512,256]{1,0:T(8,128)} %copy-done.10, f32[512,1]{1,0:T(8,128)} %copy.17.degree_ref, bf16[8,2,256,256]{3,2,1,0:T(8,128)(2,1)} %bitcast.45, ...), custom_call_target="tpu_custom_call" | custom-call | flops 268435456 | bytes 2097152 | tf_op jit(solution)/shard_map/pallas_call | solution.py:77
  70.4 9.0 %collective-permute-done.6.far_ref = bf16[512,256]{1,0:T(8,128)(2,1)S(1)} collective-permute-done((bf16[512,256]{1,0:T(8,128)(2,1)}, bf16[512,256]{1,0:T(8,128)(2,1)S(1)}, u32[]{:S(2)}, u32[]{:S(2)}) %collective-permute-start.6) | collective-permute-done | bytes 262176 | tf_op jit(solution)/shard_map/ppermute | solution.py:125
  79.4 5.2 %collective-permute-done.7.near_ref = bf16[512,256]{1,0:T(8,128)(2,1)S(1)} collective-permute-done((bf16[512,256]{1,0:T(8,128)(2,1)}, bf16[512,256]{1,0:T(8,128)(2,1)S(1)}, u32[]{:S(2)}, u32[]{:S(2)}) %collective-permute-start.7) | collective-permute-done | bytes 262176 | tf_op jit(solution)/shard_map/ppermute | solution.py:125
  90.8 3.1 %shard_map.88.own_ref = bf16[512,256]{1,0:T(8,128)(2,1)} custom-call(bf16[512,2560]{1,0:T(8,128)(2,1)} %shard_map.82.band_ref, bf16[512,256]{1,0:T(8,128)(2,1)} %shard_map.86.own_ref, f32[512,256]{1,0:T(8,128)} %shard_map.87.mine_ref, f32[512,256]{1,0:T(8,128)} %copy-done.11, f32[512,1]{1,0:T(8,128)} %copy.17.degree_ref, bf16[8,2,256,256]{3,2,1,0:T(8,128)(2,1)} %bitcast.47, ...), custom_call_target="tpu_custom_call" | custom-call | flops 268435456 | bytes 2097152 | tf_op jit(solution)/shard_map/pallas_call | solution.py:77
  93.9 12.5 %collective-permute-done.9.far_ref = bf16[512,256]{1,0:T(8,128)(2,1)S(1)} collective-permute-done((bf16[512,256]{1,0:T(8,128)(2,1)}, bf16[512,256]{1,0:T(8,128)(2,1)S(1)}, u32[]{:S(2)}, u32[]{:S(2)}) %collective-permute-start.9) | collective-permute-done | bytes 262176 | tf_op jit(solution)/shard_map/ppermute | solution.py:125
  115.2 3.1 %shard_map.90.own_ref = bf16[512,256]{1,0:T(8,128)(2,1)} custom-call(bf16[512,2560]{1,0:T(8,128)(2,1)} %shard_map.82.band_ref, bf16[512,256]{1,0:T(8,128)(2,1)} %shard_map.88.own_ref, f32[512,256]{1,0:T(8,128)} %shard_map.89.mine_ref, f32[512,256]{1,0:T(8,128)} %copy-done.12, f32[512,1]{1,0:T(8,128)} %copy.17.degree_ref, bf16[8,2,256,256]{3,2,1,0:T(8,128)(2,1)} %bitcast.49, ...), custom_call_target="tpu_custom_call" | custom-call | flops 268435456 | bytes 2097152 | tf_op jit(solution)/shard_map/pallas_call | solution.py:77
  118.3 12.6 %collective-permute-done.12.far_ref = bf16[512,256]{1,0:T(8,128)(2,1)S(1)} collective-permute-done((bf16[512,256]{1,0:T(8,128)(2,1)}, bf16[512,256]{1,0:T(8,128)(2,1)S(1)}, u32[]{:S(2)}, u32[]{:S(2)}) %collective-permute-start.12) | collective-permute-done | bytes 262176 | tf_op jit(solution)/shard_map/ppermute | solution.py:125
  138.4 3.1 %shard_map.92.own_ref = bf16[512,256]{1,0:T(8,128)(2,1)} custom-call(bf16[512,2560]{1,0:T(8,128)(2,1)} %shard_map.82.band_ref, bf16[512,256]{1,0:T(8,128)(2,1)} %shard_map.90.own_ref, f32[512,256]{1,0:T(8,128)} %shard_map.91.mine_ref, f32[512,256]{1,0:T(8,128)} %copy-done.13, f32[512,1]{1,0:T(8,128)} %copy.17.degree_ref, bf16[8,2,256,256]{3,2,1,0:T(8,128)(2,1)} %bitcast.51, ...), custom_call_target="tpu_custom_call" | custom-call | flops 268435456 | bytes 2097152 | tf_op jit(solution)/shard_map/pallas_call | solution.py:77
  141.4 12.5 %collective-permute-done.15.far_ref = bf16[512,256]{1,0:T(8,128)(2,1)S(1)} collective-permute-done((bf16[512,256]{1,0:T(8,128)(2,1)}, bf16[512,256]{1,0:T(8,128)(2,1)S(1)}, u32[]{:S(2)}, u32[]{:S(2)}) %collective-permute-start.15) | collective-permute-done | bytes 262176 | tf_op jit(solution)/shard_map/ppermute | solution.py:125
  161.1 3.1 %shard_map.94.own_ref = bf16[512,256]{1,0:T(8,128)(2,1)} custom-call(bf16[512,2560]{1,0:T(8,128)(2,1)} %shard_map.82.band_ref, bf16[512,256]{1,0:T(8,128)(2,1)} %shard_map.92.own_ref, f32[512,256]{1,0:T(8,128)} %shard_map.93.mine_ref, f32[512,256]{1,0:T(8,128)} %copy-done.14, f32[512,1]{1,0:T(8,128)} %copy.17.degree_ref, bf16[8,2,256,256]{3,2,1,0:T(8,128)(2,1)} %bitcast.53, ...), custom_call_target="tpu_custom_call" | custom-call | flops 268435456 | bytes 2097152 | tf_op jit(solution)/shard_map/pallas_call | solution.py:77
  164.3 12.3 %collective-permute-done.18.far_ref = bf16[512,256]{1,0:T(8,128)(2,1)S(1)} collective-permute-done((bf16[512,256]{1,0:T(8,128)(2,1)}, bf16[512,256]{1,0:T(8,128)(2,1)S(1)}, u32[]{:S(2)}, u32[]{:S(2)}) %collective-permute-start.18) | collective-permute-done | bytes 262176 | tf_op jit(solution)/shard_map/ppermute | solution.py:125
  183.6 3.1 %shard_map.96 = bf16[512,256]{1,0:T(8,128)(2,1)} custom-call(bf16[512,2560]{1,0:T(8,128)(2,1)} %shard_map.82.band_ref, bf16[512,256]{1,0:T(8,128)(2,1)} %shard_map.94.own_ref, f32[512,256]{1,0:T(8,128)} %shard_map.95.mine_ref, f32[512,256]{1,0:T(8,128)} %copy-done.8, f32[512,1]{1,0:T(8,128)} %copy.17.degree_ref, bf16[8,2,256,256]{3,2,1,0:T(8,128)(2,1)} %bitcast.55, ...), custom_call_target="tpu_custom_call" | custom-call | flops 268435456 | bytes 2097152 | tf_op jit(solution)/shard_map/pallas_call | solution.py:77
  188.3 11.0 %collective-permute-done.21.far_ref = bf16[512,256]{1,0:T(8,128)(2,1)} collective-permute-done((bf16[512,256]{1,0:T(8,128)(2,1)}, bf16[512,256]{1,0:T(8,128)(2,1)}, u32[]{:S(2)}, u32[]{:S(2)}) %collective-permute-start.21) | collective-permute-done | bytes 262176 | tf_op jit(solution)/shard_map/ppermute | solution.py:125
  208.4 2.9 %shard_map.98 = bf16[8,512,256]{2,1,0:T(8,128)(2,1)} fusion(bf16[8,512,256]{2,1,0:T(8,128)(2,1)} %bitcast_dynamic-update-slice_fusion.1, bf16[512,2560]{1,0:T(8,128)(2,1)} %shard_map.82.band_ref, bf16[512,256]{1,0:T(8,128)(2,1)} %shard_map.96, f32[512,256]{1,0:T(8,128)} %shard_map.97, f32[512,256]{1,0:T(8,128)} %collective-permute-done.23, ...), kind=kCustom, calls=%fused_computation.4 | custom fusion | bytes 6293504 | tf_op jit(solution)/shard_map/pallas_call | solution.py:77
  215.3 5.2 %collective-permute-done.26 = bf16[512,256]{1,0:T(8,128)(2,1)S(1)} collective-permute-done((bf16[512,256]{1,0:T(8,128)(2,1)S(1)}, bf16[512,256]{1,0:T(8,128)(2,1)S(1)}, u32[]{:S(2)}, u32[]{:S(2)}) %collective-permute-start.26) | collective-permute-done | bytes 262176 | tf_op jit(solution)/shard_map/ppermute | solution.py:171
  223.0 6.2 %collective-permute-done.24 = bf16[512,256]{1,0:T(8,128)(2,1)S(1)} collective-permute-done((bf16[512,256]{1,0:T(8,128)(2,1)S(1)}, bf16[512,256]{1,0:T(8,128)(2,1)S(1)}, u32[]{:S(2)}, u32[]{:S(2)}) %collective-permute-start.24) | collective-permute-done | bytes 262176 | tf_op jit(solution)/shard_map/ppermute | solution.py:171
  (127 shorter events, 80.0 us)
Async XLA Ops:
  6.5 34.7 %all-gather.3.cloned.1.call-start = ((), (), s32[]{:S(2)}) async-start(), calls=%async_computation | async-start | bytes 2359296 | tf_op jit(solution)/shard_map/all_gather | solution.py:113
  8.5 17.2 %collective-permute-start = (bf16[512,256]{1,0:T(8,128)(2,1)S(1)}, bf16[512,256]{1,0:T(8,128)(2,1)S(1)}, u32[]{:S(2)}, u32[]{:S(2)}) collective-permute-start(bf16[512,256]{1,0:T(8,128)(2,1)S(1)} %dynamic-slice_bitcast_fusion.4.own_ref), channel_id=1, source_target_pairs={{0,30},{1,31},{2,0},{3,1},{4,2},{5,3},{6,4},{7,5},{8,6},{9,7},{10,... | collective-permute-start | bytes 786440 | tf_op jit(solution)/shard_map/ppermute | solution.py:125
  12.3 14.4 %collective-permute-start.1 = (bf16[512,256]{1,0:T(8,128)(2,1)S(1)}, bf16[512,256]{1,0:T(8,128)(2,1)S(1)}, u32[]{:S(2)}, u32[]{:S(2)}) collective-permute-start(bf16[512,256]{1,0:T(8,128)(2,1)S(1)} %dynamic-slice_bitcast_fusion.4.own_ref), channel_id=1, source_target_pairs={{0,31},{1,0},{2,1},{3,2},{4,3},{5,4},{6,5},{7,6},{8,7},{9,8},{10,9... | collective-permute-start | bytes 786440 | tf_op jit(solution)/shard_map/ppermute | solution.py:125
  30.1 7.4 %collective-permute-start.2 = (f32[512,256]{1,0:T(8,128)}, f32[512,256]{1,0:T(8,128)S(1)}, u32[]{:S(2)}, u32[]{:S(2)}) collective-permute-start(f32[512,256]{1,0:T(8,128)} %shard_map.83.mine_ref), channel_id=1, source_target_pairs={{0,32},{32,0},{64,96},{96,64},{128,160},{160,128},{192,224},{224,1... | collective-permute-start | bytes 1572872 | tf_op jit(solution)/shard_map/ppermute | solution.py:129
  44.3 11.0 %collective-permute-start.3 = (bf16[512,256]{1,0:T(8,128)(2,1)}, bf16[512,256]{1,0:T(8,128)(2,1)S(1)}, u32[]{:S(2)}, u32[]{:S(2)}) collective-permute-start(bf16[512,256]{1,0:T(8,128)(2,1)} %shard_map.84.own_ref), channel_id=1, source_target_pairs={{0,30},{1,31},{2,0},{3,1},{4,2},{5,3},{6,4},{7,5},{8,6},{9,7},{10,... | collective-permute-start | bytes 786440 | tf_op jit(solution)/shard_map/ppermute | solution.py:125
  46.5 13.1 %collective-permute-start.4 = (bf16[512,256]{1,0:T(8,128)(2,1)}, bf16[512,256]{1,0:T(8,128)(2,1)S(1)}, u32[]{:S(2)}, u32[]{:S(2)}) collective-permute-start(bf16[512,256]{1,0:T(8,128)(2,1)} %shard_map.84.own_ref), channel_id=1, source_target_pairs={{0,31},{1,0},{2,1},{3,2},{4,3},{5,4},{6,5},{7,6},{8,7},{9,8},{10,9... | collective-permute-start | bytes 786440 | tf_op jit(solution)/shard_map/ppermute | solution.py:125
  62.9 2.8 %collective-permute-start.5 = (f32[512,256]{1,0:T(8,128)}, f32[512,256]{1,0:T(8,128)S(1)}, u32[]{:S(2)}, u32[]{:S(2)}) collective-permute-start(f32[512,256]{1,0:T(8,128)} %shard_map.85.mine_ref), channel_id=1, source_target_pairs={{0,32},{32,0},{64,96},{96,64},{128,160},{160,128},{192,224},{224,1... | collective-permute-start | bytes 1572872 | tf_op jit(solution)/shard_map/ppermute | solution.py:129
  69.6 9.8 %collective-permute-start.6 = (bf16[512,256]{1,0:T(8,128)(2,1)}, bf16[512,256]{1,0:T(8,128)(2,1)S(1)}, u32[]{:S(2)}, u32[]{:S(2)}) collective-permute-start(bf16[512,256]{1,0:T(8,128)(2,1)} %shard_map.86.own_ref), channel_id=1, source_target_pairs={{0,30},{1,31},{2,0},{3,1},{4,2},{5,3},{6,4},{7,5},{8,6},{9,7},{10,... | collective-permute-start | bytes 786440 | tf_op jit(solution)/shard_map/ppermute | solution.py:125
  69.6 15.0 %collective-permute-start.7 = (bf16[512,256]{1,0:T(8,128)(2,1)}, bf16[512,256]{1,0:T(8,128)(2,1)S(1)}, u32[]{:S(2)}, u32[]{:S(2)}) collective-permute-start(bf16[512,256]{1,0:T(8,128)(2,1)} %shard_map.86.own_ref), channel_id=1, source_target_pairs={{0,31},{1,0},{2,1},{3,2},{4,3},{5,4},{6,5},{7,6},{8,7},{9,8},{10,9... | collective-permute-start | bytes 786440 | tf_op jit(solution)/shard_map/ppermute | solution.py:125
  93.9 12.5 %collective-permute-start.9 = (bf16[512,256]{1,0:T(8,128)(2,1)}, bf16[512,256]{1,0:T(8,128)(2,1)S(1)}, u32[]{:S(2)}, u32[]{:S(2)}) collective-permute-start(bf16[512,256]{1,0:T(8,128)(2,1)} %shard_map.88.own_ref), channel_id=1, source_target_pairs={{0,30},{1,31},{2,0},{3,1},{4,2},{5,3},{6,4},{7,5},{8,6},{9,7},{10,... | collective-permute-start | bytes 786440 | tf_op jit(solution)/shard_map/ppermute | solution.py:125
  93.9 14.3 %collective-permute-start.10 = (bf16[512,256]{1,0:T(8,128)(2,1)}, bf16[512,256]{1,0:T(8,128)(2,1)S(1)}, u32[]{:S(2)}, u32[]{:S(2)}) collective-permute-start(bf16[512,256]{1,0:T(8,128)(2,1)} %shard_map.88.own_ref), channel_id=1, source_target_pairs={{0,31},{1,0},{2,1},{3,2},{4,3},{5,4},{6,5},{7,6},{8,7},{9,8},{10,9... | collective-permute-start | bytes 786440 | tf_op jit(solution)/shard_map/ppermute | solution.py:125
  111.5 2.9 %collective-permute-start.11 = (f32[512,256]{1,0:T(8,128)}, f32[512,256]{1,0:T(8,128)S(1)}, u32[]{:S(2)}, u32[]{:S(2)}) collective-permute-start(f32[512,256]{1,0:T(8,128)} %shard_map.89.mine_ref), channel_id=1, source_target_pairs={{0,32},{32,0},{64,96},{96,64},{128,160},{160,128},{192,224},{224,1... | collective-permute-start | bytes 1572872 | tf_op jit(solution)/shard_map/ppermute | solution.py:129
  118.3 12.6 %collective-permute-start.12 = (bf16[512,256]{1,0:T(8,128)(2,1)}, bf16[512,256]{1,0:T(8,128)(2,1)S(1)}, u32[]{:S(2)}, u32[]{:S(2)}) collective-permute-start(bf16[512,256]{1,0:T(8,128)(2,1)} %shard_map.90.own_ref), channel_id=1, source_target_pairs={{0,30},{1,31},{2,0},{3,1},{4,2},{5,3},{6,4},{7,5},{8,6},{9,7},{10,... | collective-permute-start | bytes 786440 | tf_op jit(solution)/shard_map/ppermute | solution.py:125
  118.3 13.6 %collective-permute-start.13 = (bf16[512,256]{1,0:T(8,128)(2,1)}, bf16[512,256]{1,0:T(8,128)(2,1)S(1)}, u32[]{:S(2)}, u32[]{:S(2)}) collective-permute-start(bf16[512,256]{1,0:T(8,128)(2,1)} %shard_map.90.own_ref), channel_id=1, source_target_pairs={{0,31},{1,0},{2,1},{3,2},{4,3},{5,4},{6,5},{7,6},{8,7},{9,8},{10,9... | collective-permute-start | bytes 786440 | tf_op jit(solution)/shard_map/ppermute | solution.py:125
  141.4 12.5 %collective-permute-start.15 = (bf16[512,256]{1,0:T(8,128)(2,1)}, bf16[512,256]{1,0:T(8,128)(2,1)S(1)}, u32[]{:S(2)}, u32[]{:S(2)}) collective-permute-start(bf16[512,256]{1,0:T(8,128)(2,1)} %shard_map.92.own_ref), channel_id=1, source_target_pairs={{0,30},{1,31},{2,0},{3,1},{4,2},{5,3},{6,4},{7,5},{8,6},{9,7},{10,... | collective-permute-start | bytes 786440 | tf_op jit(solution)/shard_map/ppermute | solution.py:125
  141.4 13.5 %collective-permute-start.16 = (bf16[512,256]{1,0:T(8,128)(2,1)}, bf16[512,256]{1,0:T(8,128)(2,1)S(1)}, u32[]{:S(2)}, u32[]{:S(2)}) collective-permute-start(bf16[512,256]{1,0:T(8,128)(2,1)} %shard_map.92.own_ref), channel_id=1, source_target_pairs={{0,31},{1,0},{2,1},{3,2},{4,3},{5,4},{6,5},{7,6},{8,7},{9,8},{10,9... | collective-permute-start | bytes 786440 | tf_op jit(solution)/shard_map/ppermute | solution.py:125
  164.2 12.4 %collective-permute-start.18 = (bf16[512,256]{1,0:T(8,128)(2,1)}, bf16[512,256]{1,0:T(8,128)(2,1)S(1)}, u32[]{:S(2)}, u32[]{:S(2)}) collective-permute-start(bf16[512,256]{1,0:T(8,128)(2,1)} %shard_map.94.own_ref), channel_id=1, source_target_pairs={{0,30},{1,31},{2,0},{3,1},{4,2},{5,3},{6,4},{7,5},{8,6},{9,7},{10,... | collective-permute-start | bytes 786440 | tf_op jit(solution)/shard_map/ppermute | solution.py:125
  164.2 13.2 %collective-permute-start.19 = (bf16[512,256]{1,0:T(8,128)(2,1)}, bf16[512,256]{1,0:T(8,128)(2,1)S(1)}, u32[]{:S(2)}, u32[]{:S(2)}) collective-permute-start(bf16[512,256]{1,0:T(8,128)(2,1)} %shard_map.94.own_ref), channel_id=1, source_target_pairs={{0,31},{1,0},{2,1},{3,2},{4,3},{5,4},{6,5},{7,6},{8,7},{9,8},{10,9... | collective-permute-start | bytes 786440 | tf_op jit(solution)/shard_map/ppermute | solution.py:125
  186.7 12.6 %collective-permute-start.21 = (bf16[512,256]{1,0:T(8,128)(2,1)}, bf16[512,256]{1,0:T(8,128)(2,1)}, u32[]{:S(2)}, u32[]{:S(2)}) collective-permute-start(bf16[512,256]{1,0:T(8,128)(2,1)} %shard_map.96), channel_id=1, source_target_pairs={{0,30},{1,31},{2,0},{3,1},{4,2},{5,3},{6,4},{7,5},{8,6},{9,7},{10,... | collective-permute-start | bytes 786440 | tf_op jit(solution)/shard_map/ppermute | solution.py:125
  186.7 13.6 %collective-permute-start.22 = (bf16[512,256]{1,0:T(8,128)(2,1)}, bf16[512,256]{1,0:T(8,128)(2,1)}, u32[]{:S(2)}, u32[]{:S(2)}) collective-permute-start(bf16[512,256]{1,0:T(8,128)(2,1)} %shard_map.96), channel_id=1, source_target_pairs={{0,31},{1,0},{2,1},{3,2},{4,3},{5,4},{6,5},{7,6},{8,7},{9,8},{10,9... | collective-permute-start | bytes 786440 | tf_op jit(solution)/shard_map/ppermute | solution.py:125
  202.8 5.6 %collective-permute-start.23 = (f32[512,256]{1,0:T(8,128)}, f32[512,256]{1,0:T(8,128)}, u32[]{:S(2)}, u32[]{:S(2)}) collective-permute-start(f32[512,256]{1,0:T(8,128)} %shard_map.97), channel_id=1, source_target_pairs={{0,32},{32,0},{64,96},{96,64},{128,160},{160,128},{192,224},{224,1... | collective-permute-start | bytes 1572872 | tf_op jit(solution)/shard_map/ppermute | solution.py:129
  212.6 7.9 %collective-permute-start.26 = (bf16[512,256]{1,0:T(8,128)(2,1)S(1)}, bf16[512,256]{1,0:T(8,128)(2,1)S(1)}, u32[]{:S(2)}, u32[]{:S(2)}) collective-permute-start(bf16[512,256]{1,0:T(8,128)(2,1)S(1)} %get-tuple-element.6), channel_id=1, source_target_pairs={{0,192},{32,224},{64,0},{96,32},{128,64},{160,96},{192,128},{224,1... | collective-permute-start | bytes 786440 | tf_op jit(solution)/shard_map/ppermute | solution.py:171
  213.9 9.1 %collective-permute-start.25 = (bf16[512,256]{1,0:T(8,128)(2,1)S(1)}, bf16[512,256]{1,0:T(8,128)(2,1)S(1)}, u32[]{:S(2)}, u32[]{:S(2)}) collective-permute-start(bf16[512,256]{1,0:T(8,128)(2,1)S(1)} %get-tuple-element.7), channel_id=1, source_target_pairs={{0,128},{32,160},{64,192},{96,224},{128,0},{160,32},{192,64},{224,... | collective-permute-start | bytes 786440 | tf_op jit(solution)/shard_map/ppermute | solution.py:171
  214.6 14.7 %collective-permute-start.24 = (bf16[512,256]{1,0:T(8,128)(2,1)S(1)}, bf16[512,256]{1,0:T(8,128)(2,1)S(1)}, u32[]{:S(2)}, u32[]{:S(2)}) collective-permute-start(bf16[512,256]{1,0:T(8,128)(2,1)S(1)} %get-tuple-element.8), channel_id=1, source_target_pairs={{0,64},{32,96},{64,128},{96,160},{128,192},{160,224},{192,0},{224,... | collective-permute-start | bytes 786440 | tf_op jit(solution)/shard_map/ppermute | solution.py:171
  (33 other events, 137.2 us)
Sparse Core Ops, SparseCore 0:
  9.2 31.9 all-gather.2

commit v12 on v5

--- a/solution.py
+++ b/solution.py
@@ -8,7 +8,7 @@
 REACH = 2
 
 
-def _band_kernel(rows_ref, cols_ref, count_ref, values_ref, band_ref):
+def _band_kernel(rows_ref, cols_ref, count_ref, batch_ref, values_ref, band_ref):
     block = values_ref.shape[1]
     band_ref[...] = jnp.zeros(band_ref.shape, band_ref.dtype)
 
@@ -21,14 +21,20 @@
     lax.fori_loop(0, count_ref[0], place, 0)
 
 
-def build_band(row_local, column_local, count, values, rows_dev, band_cols):
+def build_band(row_local, column_local, count, batch, tile_values, rows_dev, band_cols):
+    slots, block = tile_values.shape[1], tile_values.shape[2]
     return pl.pallas_call(
         _band_kernel,
-        out_shape=jax.ShapeDtypeStruct((rows_dev, band_cols), values.dtype),
-        in_specs=[pl.BlockSpec(memory_space=pltpu.SMEM)] * 3
-        + [pl.BlockSpec(memory_space=pltpu.VMEM)],
-        out_specs=pl.BlockSpec(memory_space=pltpu.VMEM),
-    )(row_local, column_local, count, values)
+        out_shape=jax.ShapeDtypeStruct((rows_dev, band_cols), tile_values.dtype),
+        grid_spec=pltpu.PrefetchScalarGridSpec(
+            num_scalar_prefetch=4,
+            grid=(1,),
+            in_specs=[
+                pl.BlockSpec((None, slots, block, block), lambda i, r, c, n, b: (b[0], 0, 0, 0))
+            ],
+            out_specs=pl.BlockSpec((rows_dev, band_cols), lambda i, r, c, n, b: (0, 0)),
+        ),
+    )(row_local, column_local, count, batch, tile_values)
 
 
 def _layer_kernel(band_ref, p0, p1, p2, p3, p4, degree_ref, ws_ref, wn_ref, out_ref):
@@ -101,7 +107,6 @@
         pairs = [(s, s ^ 1) for s in range(section_count)]
         return lax.ppermute(x, "section", pairs)
 
-    values = lax.dynamic_index_in_dim(tile_values, batch, 0, keepdims=False)
     rows = lax.dynamic_index_in_dim(tile_rows, batch, 0, keepdims=False)
     cols = lax.dynamic_index_in_dim(tile_cols, batch, 0, keepdims=False)
     count = lax.dynamic_index_in_dim(tile_count, batch, 0, keepdims=False)[0]
@@ -117,7 +122,8 @@
         jnp.clip(row_local, 0, blocks_dev - 1),
         jnp.clip(column_local, 0, band_width - 1),
         jnp.clip(count, 0, slot_total).reshape(1),
-        values,
+        jnp.clip(batch, 0, batch_total - 1).astype(jnp.int32).reshape(1),
+        tile_values,
         rows_dev,
         band_width * block_size,
     )

time: 225 us -> 226 us (level)
  local copies, waits for them, and re-layouts: 23.5 us -> 19.9 us
  waiting for transfers between devices: 127 us -> 130 us
    squeeze x1 -> x0, local copies, waits for them, and re-layouts: 3.63 us -> none  [body(): values = lax.dynamic_index_in_dim(tile_values, batch, 0, keepdims=False)]
    all_gather x1, waiting for transfers between devices: 0.01 us -> 2.45 us  [body(): lax.all_gather(jnp.stack([self_weight[0], neighbour_weight[0]]), 'section')]
  transfers between devices with their start and end apart: 28 -> 28, of which waited for: 25 -> 26; matrix products, arithmetic and copies ran while one was open for 6% -> 5% of each run, Pallas kernels for 2% -> 2%
where the time goes in v12:
time: 226 us; the launch traced here: 225 us
  waiting for transfers between devices  130 us (58%)
  Pallas kernels  34.1 us (15%)
  starting transfers between devices  20 us (9%)
  local copies, waits for them, and re-layouts  19.9 us (9%)
  between operations  14.3 us (6%)
  other arithmetic  7.09 us (3%)
    ppermute x16, waiting for transfers between devices, halo(): return lax.ppermute(x, ('section', 'blk'), pairs)  105 us
    pallas_call x7, Pallas kernels, run_layer(): pl.pallas_call(_layer_kernel, out_shape=jax.ShapeDtypeStruct((rows, width...  29.8 us
    ppermute x3, waiting for transfers between devices, body(): arrived.append(lax.ppermute(sending, 'section', pairs))  14.1 us
    ppermute x16, starting transfers between devices, halo(): return lax.ppermute(x, ('section', 'blk'), pairs)  9.99 us
    ppermute x8, waiting for transfers between devices, swap(): return lax.ppermute(x, 'section', pairs)  8.76 us
    ppermute x8, starting transfers between devices, swap(): return lax.ppermute(x, 'section', pairs)  7.29 us
    slice x8, local copies, waits for them, and re-layouts, body(): parts = [far, near, hidden, theirs[:rows_dev], theirs[rows_dev:]]  5.85 us
    unnamed x57, local copies, waits for them, and re-layouts  5.12 us
  transfers between devices with their start and end apart: 28, of which 26 were waited for; matrix products, arithmetic and copies ran while one was open for 5% of the time, Pallas kernels for 2%

profile of v12, /device:TPU:1, one launch (start us, length us, event | category | flops | bytes accessed | tf_op | source)
XLA Modules:
  0.0 225.2 jit_solution(2173663817277126188)
XLA Ops:
  8.4 3.9 %collective-permute-start = (bf16[512,256]{1,0:T(8,128)(2,1)S(1)}, bf16[512,256]{1,0:T(8,128)(2,1)S(1)}, u32[]{:S(2)}, u32[]{:S(2)}) collective-permute-start(bf16[512,256]{1,0:T(8,128)(2,1)S(1)} %dynamic-slice_bitcast_fusion.3.p2), channel_id=1, source_target_pairs={{0,30},{1,31},{2,0},{3,1},{4,2},{5,3},{6,4},{7,5},{8,6},{9,7},{10,... | collective-permute-start | bytes 786440 | tf_op jit(solution)/shard_map/ppermute | solution.py:104
  14.0 8.2 %collective-permute-done.p0 = bf16[512,256]{1,0:T(8,128)(2,1)S(1)} collective-permute-done((bf16[512,256]{1,0:T(8,128)(2,1)S(1)}, bf16[512,256]{1,0:T(8,128)(2,1)S(1)}, u32[]{:S(2)}, u32[]{:S(2)}) %collective-permute-start) | collective-permute-done | bytes 262176 | tf_op jit(solution)/shard_map/ppermute | solution.py:104
  22.2 4.6 %collective-permute-done.1.p1 = bf16[512,256]{1,0:T(8,128)(2,1)S(1)} collective-permute-done((bf16[512,256]{1,0:T(8,128)(2,1)S(1)}, bf16[512,256]{1,0:T(8,128)(2,1)S(1)}, u32[]{:S(2)}, u32[]{:S(2)}) %collective-permute-start.1) | collective-permute-done | bytes 262176 | tf_op jit(solution)/shard_map/ppermute | solution.py:104
  33.7 4.2 %shard_map.82.band_ref = bf16[512,2560]{1,0:T(8,128)(2,1)} custom-call(s32[80]{0:T(128)} %fusion.7.rows_ref, s32[80]{0:T(128)} %fusion.8.cols_ref, s32[1]{0:T(128)} %bitcast.2.count_ref, s32[1]{0:T(128)} %bitcast.3.batch_ref, bf16[4,80,128,128]{3,2,1,0:T(8,128)(2,1)} %values_ref.1), custom_call_target="tpu_custom_call" | custom-call | tf_op jit(solution)/shard_map/pallas_call | solution.py:26
  41.2 2.9 %slice_bitcast_fusion = (bf16[256,256]{1,0:T(8,128)(2,1)S(1)}, bf16[256,256]{1,0:T(8,128)(2,1)S(1)}, bf16[256,256]{1,0:T(8,128)(2,1)}, bf16[256,256]{1,0:T(8,128...) fusion(bf16[8,2,256,256]{3,2,1,0:T(8,128)(2,1)} %bitcast.74), kind=kLoop, calls=%fused_computation.23 | loop fusion | bytes 4194304 | tf_op jit(solution)/shard_map/squeeze | solution.py:138
  44.1 4.2 %shard_map.83.p2 = bf16[512,256]{1,0:T(8,128)(2,1)} custom-call(bf16[512,2560]{1,0:T(8,128)(2,1)} %shard_map.82.band_ref, bf16[512,256]{1,0:T(8,128)(2,1)} %copy-done.12, bf16[512,256]{1,0:T(8,128)(2,1)} %copy-done.13, bf16[512,256]{1,0:T(8,128)(2,1)} %copy-done.9, bf16[512,256]{1,0:T(8,128)(2,1)} %get-tuple-element.44.p3, ...), custom_call_target="tpu_custom_call" | custom-call | flops 805306368 | bytes 4194304 | tf_op jit(solution)/shard_map/pallas_call | solution.py:63
  51.9 7.4 %collective-permute-done.3.p0 = bf16[512,256]{1,0:T(8,128)(2,1)S(1)} collective-permute-done((bf16[512,256]{1,0:T(8,128)(2,1)}, bf16[512,256]{1,0:T(8,128)(2,1)S(1)}, u32[]{:S(2)}, u32[]{:S(2)}) %collective-permute-start.3) | collective-permute-done | bytes 262176 | tf_op jit(solution)/shard_map/ppermute | solution.py:104
  59.3 4.4 %collective-permute-done.4.p1 = bf16[512,256]{1,0:T(8,128)(2,1)S(1)} collective-permute-done((bf16[512,256]{1,0:T(8,128)(2,1)}, bf16[512,256]{1,0:T(8,128)(2,1)S(1)}, u32[]{:S(2)}, u32[]{:S(2)}) %collective-permute-start.4) | collective-permute-done | bytes 262176 | tf_op jit(solution)/shard_map/ppermute | solution.py:104
  67.3 4.2 %shard_map.84.p2 = bf16[512,256]{1,0:T(8,128)(2,1)} custom-call(bf16[512,2560]{1,0:T(8,128)(2,1)} %shard_map.82.band_ref, bf16[512,256]{1,0:T(8,128)(2,1)} %copy-done.14, bf16[512,256]{1,0:T(8,128)(2,1)} %copy-done.19, bf16[512,256]{1,0:T(8,128)(2,1)} %shard_map.83.p2, bf16[512,256]{1,0:T(8,128)(2,1)} %get-tuple-element.42.p3, ...), custom_call_target="tpu_custom_call" | custom-call | flops 805306368 | bytes 4194304 | tf_op jit(solution)/shard_map/pallas_call | solution.py:63
  72.2 9.1 %collective-permute-done.6.p0 = bf16[512,256]{1,0:T(8,128)(2,1)S(1)} collective-permute-done((bf16[512,256]{1,0:T(8,128)(2,1)}, bf16[512,256]{1,0:T(8,128)(2,1)S(1)}, u32[]{:S(2)}, u32[]{:S(2)}) %collective-permute-start.6) | collective-permute-done | bytes 262176 | tf_op jit(solution)/shard_map/ppermute | solution.py:104
  81.3 5.2 %collective-permute-done.7.p1 = bf16[512,256]{1,0:T(8,128)(2,1)S(1)} collective-permute-done((bf16[512,256]{1,0:T(8,128)(2,1)}, bf16[512,256]{1,0:T(8,128)(2,1)S(1)}, u32[]{:S(2)}, u32[]{:S(2)}) %collective-permute-start.7) | collective-permute-done | bytes 262176 | tf_op jit(solution)/shard_map/ppermute | solution.py:104
  89.4 4.2 %shard_map.85.p2 = bf16[512,256]{1,0:T(8,128)(2,1)} custom-call(bf16[512,2560]{1,0:T(8,128)(2,1)} %shard_map.82.band_ref, bf16[512,256]{1,0:T(8,128)(2,1)} %copy-done.15, bf16[512,256]{1,0:T(8,128)(2,1)} %copy-done.20, bf16[512,256]{1,0:T(8,128)(2,1)} %shard_map.84.p2, bf16[512,256]{1,0:T(8,128)(2,1)} %get-tuple-element.40.p3, ...), custom_call_target="tpu_custom_call" | custom-call | flops 805306368 | bytes 4194304 | tf_op jit(solution)/shard_map/pallas_call | solution.py:63
  93.6 12.6 %collective-permute-done.9.p0 = bf16[512,256]{1,0:T(8,128)(2,1)S(1)} collective-permute-done((bf16[512,256]{1,0:T(8,128)(2,1)}, bf16[512,256]{1,0:T(8,128)(2,1)S(1)}, u32[]{:S(2)}, u32[]{:S(2)}) %collective-permute-start.9) | collective-permute-done | bytes 262176 | tf_op jit(solution)/shard_map/ppermute | solution.py:104
  111.7 4.2 %shard_map.86.p2 = bf16[512,256]{1,0:T(8,128)(2,1)} custom-call(bf16[512,2560]{1,0:T(8,128)(2,1)} %shard_map.82.band_ref, bf16[512,256]{1,0:T(8,128)(2,1)} %copy-done.16, bf16[512,256]{1,0:T(8,128)(2,1)} %copy-done.21, bf16[512,256]{1,0:T(8,128)(2,1)} %shard_map.85.p2, bf16[512,256]{1,0:T(8,128)(2,1)} %get-tuple-element.38.p3, ...), custom_call_target="tpu_custom_call" | custom-call | flops 805306368 | bytes 4194304 | tf_op jit(solution)/shard_map/pallas_call | solution.py:63
  115.9 12.5 %collective-permute-done.12.p0 = bf16[512,256]{1,0:T(8,128)(2,1)S(1)} collective-permute-done((bf16[512,256]{1,0:T(8,128)(2,1)}, bf16[512,256]{1,0:T(8,128)(2,1)S(1)}, u32[]{:S(2)}, u32[]{:S(2)}) %collective-permute-start.12) | collective-permute-done | bytes 262176 | tf_op jit(solution)/shard_map/ppermute | solution.py:104
  133.1 4.3 %shard_map.87.p2 = bf16[512,256]{1,0:T(8,128)(2,1)} custom-call(bf16[512,2560]{1,0:T(8,128)(2,1)} %shard_map.82.band_ref, bf16[512,256]{1,0:T(8,128)(2,1)} %copy-done.17, bf16[512,256]{1,0:T(8,128)(2,1)} %copy-done.22, bf16[512,256]{1,0:T(8,128)(2,1)} %shard_map.86.p2, bf16[512,256]{1,0:T(8,128)(2,1)} %get-tuple-element.36.p3, ...), custom_call_target="tpu_custom_call" | custom-call | flops 805306368 | bytes 4194304 | tf_op jit(solution)/shard_map/pallas_call | solution.py:63
  137.4 12.5 %collective-permute-done.15.p0 = bf16[512,256]{1,0:T(8,128)(2,1)S(1)} collective-permute-done((bf16[512,256]{1,0:T(8,128)(2,1)}, bf16[512,256]{1,0:T(8,128)(2,1)S(1)}, u32[]{:S(2)}, u32[]{:S(2)}) %collective-permute-start.15) | collective-permute-done | bytes 262176 | tf_op jit(solution)/shard_map/ppermute | solution.py:104
  153.7 4.3 %shard_map.88.p2 = bf16[512,256]{1,0:T(8,128)(2,1)} custom-call(bf16[512,2560]{1,0:T(8,128)(2,1)} %shard_map.82.band_ref, bf16[512,256]{1,0:T(8,128)(2,1)} %copy-done.18, bf16[512,256]{1,0:T(8,128)(2,1)} %copy-done.23, bf16[512,256]{1,0:T(8,128)(2,1)} %shard_map.87.p2, bf16[512,256]{1,0:T(8,128)(2,1)} %get-tuple-element.34.p3, ...), custom_call_target="tpu_custom_call" | custom-call | flops 805306368 | bytes 4194304 | tf_op jit(solution)/shard_map/pallas_call | solution.py:63
  158.0 12.4 %collective-permute-done.18.p0 = bf16[512,256]{1,0:T(8,128)(2,1)S(1)} collective-permute-done((bf16[512,256]{1,0:T(8,128)(2,1)}, bf16[512,256]{1,0:T(8,128)(2,1)S(1)}, u32[]{:S(2)}, u32[]{:S(2)}) %collective-permute-start.18) | collective-permute-done | bytes 262176 | tf_op jit(solution)/shard_map/ppermute | solution.py:104
  174.5 4.3 %shard_map.89 = bf16[512,256]{1,0:T(8,128)(2,1)} custom-call(bf16[512,2560]{1,0:T(8,128)(2,1)} %shard_map.82.band_ref, bf16[512,256]{1,0:T(8,128)(2,1)} %copy-done.10, bf16[512,256]{1,0:T(8,128)(2,1)} %copy-done.11, bf16[512,256]{1,0:T(8,128)(2,1)} %shard_map.88.p2, bf16[512,256]{1,0:T(8,128)(2,1)} %get-tuple-element.32.p3, ...), custom_call_target="tpu_custom_call" | custom-call | flops 805306368 | bytes 4194304 | tf_op jit(solution)/shard_map/pallas_call | solution.py:63
  180.5 10.6 %collective-permute-done.21 = bf16[512,256]{1,0:T(8,128)(2,1)S(1)} collective-permute-done((bf16[512,256]{1,0:T(8,128)(2,1)}, bf16[512,256]{1,0:T(8,128)(2,1)S(1)}, u32[]{:S(2)}, u32[]{:S(2)}) %collective-permute-start.21) | collective-permute-done | bytes 262176 | tf_op jit(solution)/shard_map/ppermute | solution.py:104
  195.2 3.8 %shard_map.90 = bf16[8,512,256]{2,1,0:T(8,128)(2,1)} fusion(bf16[8,512,256]{2,1,0:T(8,128)(2,1)} %bitcast_dynamic-update-slice_fusion.1, bf16[512,2560]{1,0:T(8,128)(2,1)} %shard_map.82.band_ref, bf16[512,256]{1,0:T(8,128)(2,1)S(1)} %collective-permute-done.21, bf16[512,256]{1,0:T(8,128)(2,1)S(1)} %collective-permute-done.22, ...), kind=kCustom, calls=%fused_computation.11 | custom fusion | bytes 4458496 | tf_op jit(solution)/shard_map/pallas_call | solution.py:63
  203.0 5.2 %collective-permute-done.26 = bf16[512,256]{1,0:T(8,128)(2,1)S(1)} collective-permute-done((bf16[512,256]{1,0:T(8,128)(2,1)S(1)}, bf16[512,256]{1,0:T(8,128)(2,1)S(1)}, u32[]{:S(2)}, u32[]{:S(2)}) %collective-permute-start.26) | collective-permute-done | bytes 262176 | tf_op jit(solution)/shard_map/ppermute | solution.py:151
  210.8 6.2 %collective-permute-done.24 = bf16[512,256]{1,0:T(8,128)(2,1)S(1)} collective-permute-done((bf16[512,256]{1,0:T(8,128)(2,1)S(1)}, bf16[512,256]{1,0:T(8,128)(2,1)S(1)}, u32[]{:S(2)}, u32[]{:S(2)}) %collective-permute-start.24) | collective-permute-done | bytes 262176 | tf_op jit(solution)/shard_map/ppermute | solution.py:151
  (127 shorter events, 55.6 us)
Async XLA Ops:
  6.5 34.7 %all-gather.3.cloned.1.call-start = ((), (), s32[]{:S(2)}) async-start(), calls=%async_computation | async-start | bytes 2359296 | tf_op jit(solution)/shard_map/all_gather | solution.py:90
  8.4 13.7 %collective-permute-start = (bf16[512,256]{1,0:T(8,128)(2,1)S(1)}, bf16[512,256]{1,0:T(8,128)(2,1)S(1)}, u32[]{:S(2)}, u32[]{:S(2)}) collective-permute-start(bf16[512,256]{1,0:T(8,128)(2,1)S(1)} %dynamic-slice_bitcast_fusion.3.p2), channel_id=1, source_target_pairs={{0,30},{1,31},{2,0},{3,1},{4,2},{5,3},{6,4},{7,5},{8,6},{9,7},{10,... | collective-permute-start | bytes 786440 | tf_op jit(solution)/shard_map/ppermute | solution.py:104
  12.3 14.4 %collective-permute-start.1 = (bf16[512,256]{1,0:T(8,128)(2,1)S(1)}, bf16[512,256]{1,0:T(8,128)(2,1)S(1)}, u32[]{:S(2)}, u32[]{:S(2)}) collective-permute-start(bf16[512,256]{1,0:T(8,128)(2,1)S(1)} %dynamic-slice_bitcast_fusion.3.p2), channel_id=1, source_target_pairs={{0,31},{1,0},{2,1},{3,2},{4,3},{5,4},{6,5},{7,6},{8,7},{9,8},{10,9... | collective-permute-start | bytes 786440 | tf_op jit(solution)/shard_map/ppermute | solution.py:104
  26.8 11.2 %collective-permute-start.2 = (bf16[1024,256]{1,0:T(8,128)(2,1)S(1)}, bf16[1024,256]{1,0:T(8,128)(2,1)S(1)}, u32[]{:S(2)}, u32[]{:S(2)}) collective-permute-start(bf16[1024,256]{1,0:T(8,128)(2,1)S(1)} %pad_maximum_fusion.1), channel_id=1, source_target_pairs={{0,32},{32,0},{64,96},{96,64},{128,160},{160,128},{192,224},{224,1... | collective-permute-start | bytes 1572872 | tf_op jit(solution)/shard_map/ppermute | solution.py:108
  48.4 10.9 %collective-permute-start.3 = (bf16[512,256]{1,0:T(8,128)(2,1)}, bf16[512,256]{1,0:T(8,128)(2,1)S(1)}, u32[]{:S(2)}, u32[]{:S(2)}) collective-permute-start(bf16[512,256]{1,0:T(8,128)(2,1)} %shard_map.83.p2), channel_id=1, source_target_pairs={{0,30},{1,31},{2,0},{3,1},{4,2},{5,3},{6,4},{7,5},{8,6},{9,7},{10,... | collective-permute-start | bytes 786440 | tf_op jit(solution)/shard_map/ppermute | solution.py:104
  50.6 13.1 %collective-permute-start.4 = (bf16[512,256]{1,0:T(8,128)(2,1)}, bf16[512,256]{1,0:T(8,128)(2,1)S(1)}, u32[]{:S(2)}, u32[]{:S(2)}) collective-permute-start(bf16[512,256]{1,0:T(8,128)(2,1)} %shard_map.83.p2), channel_id=1, source_target_pairs={{0,31},{1,0},{2,1},{3,2},{4,3},{5,4},{6,5},{7,6},{8,7},{9,8},{10,9... | collective-permute-start | bytes 786440 | tf_op jit(solution)/shard_map/ppermute | solution.py:104
  71.5 9.8 %collective-permute-start.6 = (bf16[512,256]{1,0:T(8,128)(2,1)}, bf16[512,256]{1,0:T(8,128)(2,1)S(1)}, u32[]{:S(2)}, u32[]{:S(2)}) collective-permute-start(bf16[512,256]{1,0:T(8,128)(2,1)} %shard_map.84.p2), channel_id=1, source_target_pairs={{0,30},{1,31},{2,0},{3,1},{4,2},{5,3},{6,4},{7,5},{8,6},{9,7},{10,... | collective-permute-start | bytes 786440 | tf_op jit(solution)/shard_map/ppermute | solution.py:104
  71.5 15.0 %collective-permute-start.7 = (bf16[512,256]{1,0:T(8,128)(2,1)}, bf16[512,256]{1,0:T(8,128)(2,1)S(1)}, u32[]{:S(2)}, u32[]{:S(2)}) collective-permute-start(bf16[512,256]{1,0:T(8,128)(2,1)} %shard_map.84.p2), channel_id=1, source_target_pairs={{0,31},{1,0},{2,1},{3,2},{4,3},{5,4},{6,5},{7,6},{8,7},{9,8},{10,9... | collective-permute-start | bytes 786440 | tf_op jit(solution)/shard_map/ppermute | solution.py:104
  93.6 12.6 %collective-permute-start.9 = (bf16[512,256]{1,0:T(8,128)(2,1)}, bf16[512,256]{1,0:T(8,128)(2,1)S(1)}, u32[]{:S(2)}, u32[]{:S(2)}) collective-permute-start(bf16[512,256]{1,0:T(8,128)(2,1)} %shard_map.85.p2), channel_id=1, source_target_pairs={{0,30},{1,31},{2,0},{3,1},{4,2},{5,3},{6,4},{7,5},{8,6},{9,7},{10,... | collective-permute-start | bytes 786440 | tf_op jit(solution)/shard_map/ppermute | solution.py:104
  93.6 13.7 %collective-permute-start.10 = (bf16[512,256]{1,0:T(8,128)(2,1)}, bf16[512,256]{1,0:T(8,128)(2,1)S(1)}, u32[]{:S(2)}, u32[]{:S(2)}) collective-permute-start(bf16[512,256]{1,0:T(8,128)(2,1)} %shard_map.85.p2), channel_id=1, source_target_pairs={{0,31},{1,0},{2,1},{3,2},{4,3},{5,4},{6,5},{7,6},{8,7},{9,8},{10,9... | collective-permute-start | bytes 786440 | tf_op jit(solution)/shard_map/ppermute | solution.py:104
  107.3 3.5 %collective-permute-start.11 = (bf16[1024,256]{1,0:T(8,128)(2,1)S(1)}, bf16[1024,256]{1,0:T(8,128)(2,1)S(1)}, u32[]{:S(2)}, u32[]{:S(2)}) collective-permute-start(bf16[1024,256]{1,0:T(8,128)(2,1)S(1)} %pad_maximum_fusion.4), channel_id=1, source_target_pairs={{0,32},{32,0},{64,96},{96,64},{128,160},{160,128},{192,224},{224,1... | collective-permute-start | bytes 1572872 | tf_op jit(solution)/shard_map/ppermute | solution.py:108
  115.9 12.5 %collective-permute-start.12 = (bf16[512,256]{1,0:T(8,128)(2,1)}, bf16[512,256]{1,0:T(8,128)(2,1)S(1)}, u32[]{:S(2)}, u32[]{:S(2)}) collective-permute-start(bf16[512,256]{1,0:T(8,128)(2,1)} %shard_map.86.p2), channel_id=1, source_target_pairs={{0,30},{1,31},{2,0},{3,1},{4,2},{5,3},{6,4},{7,5},{8,6},{9,7},{10,... | collective-permute-start | bytes 786440 | tf_op jit(solution)/shard_map/ppermute | solution.py:104
  115.9 13.5 %collective-permute-start.13 = (bf16[512,256]{1,0:T(8,128)(2,1)}, bf16[512,256]{1,0:T(8,128)(2,1)S(1)}, u32[]{:S(2)}, u32[]{:S(2)}) collective-permute-start(bf16[512,256]{1,0:T(8,128)(2,1)} %shard_map.86.p2), channel_id=1, source_target_pairs={{0,31},{1,0},{2,1},{3,2},{4,3},{5,4},{6,5},{7,6},{8,7},{9,8},{10,9... | collective-permute-start | bytes 786440 | tf_op jit(solution)/shard_map/ppermute | solution.py:104
  129.4 2.9 %collective-permute-start.14 = (bf16[1024,256]{1,0:T(8,128)(2,1)S(1)}, bf16[1024,256]{1,0:T(8,128)(2,1)S(1)}, u32[]{:S(2)}, u32[]{:S(2)}) collective-permute-start(bf16[1024,256]{1,0:T(8,128)(2,1)S(1)} %pad_maximum_fusion.5), channel_id=1, source_target_pairs={{0,32},{32,0},{64,96},{96,64},{128,160},{160,128},{192,224},{224,1... | collective-permute-start | bytes 1572872 | tf_op jit(solution)/shard_map/ppermute | solution.py:108
  137.4 12.5 %collective-permute-start.15 = (bf16[512,256]{1,0:T(8,128)(2,1)}, bf16[512,256]{1,0:T(8,128)(2,1)S(1)}, u32[]{:S(2)}, u32[]{:S(2)}) collective-permute-start(bf16[512,256]{1,0:T(8,128)(2,1)} %shard_map.87.p2), channel_id=1, source_target_pairs={{0,30},{1,31},{2,0},{3,1},{4,2},{5,3},{6,4},{7,5},{8,6},{9,7},{10,... | collective-permute-start | bytes 786440 | tf_op jit(solution)/shard_map/ppermute | solution.py:104
  137.4 13.5 %collective-permute-start.16 = (bf16[512,256]{1,0:T(8,128)(2,1)}, bf16[512,256]{1,0:T(8,128)(2,1)S(1)}, u32[]{:S(2)}, u32[]{:S(2)}) collective-permute-start(bf16[512,256]{1,0:T(8,128)(2,1)} %shard_map.87.p2), channel_id=1, source_target_pairs={{0,31},{1,0},{2,1},{3,2},{4,3},{5,4},{6,5},{7,6},{8,7},{9,8},{10,9... | collective-permute-start | bytes 786440 | tf_op jit(solution)/shard_map/ppermute | solution.py:104
  158.0 12.4 %collective-permute-start.18 = (bf16[512,256]{1,0:T(8,128)(2,1)}, bf16[512,256]{1,0:T(8,128)(2,1)S(1)}, u32[]{:S(2)}, u32[]{:S(2)}) collective-permute-start(bf16[512,256]{1,0:T(8,128)(2,1)} %shard_map.88.p2), channel_id=1, source_target_pairs={{0,30},{1,31},{2,0},{3,1},{4,2},{5,3},{6,4},{7,5},{8,6},{9,7},{10,... | collective-permute-start | bytes 786440 | tf_op jit(solution)/shard_map/ppermute | solution.py:104
  158.0 13.6 %collective-permute-start.19 = (bf16[512,256]{1,0:T(8,128)(2,1)}, bf16[512,256]{1,0:T(8,128)(2,1)S(1)}, u32[]{:S(2)}, u32[]{:S(2)}) collective-permute-start(bf16[512,256]{1,0:T(8,128)(2,1)} %shard_map.88.p2), channel_id=1, source_target_pairs={{0,31},{1,0},{2,1},{3,2},{4,3},{5,4},{6,5},{7,6},{8,7},{9,8},{10,9... | collective-permute-start | bytes 786440 | tf_op jit(solution)/shard_map/ppermute | solution.py:104
  178.8 12.3 %collective-permute-start.21 = (bf16[512,256]{1,0:T(8,128)(2,1)}, bf16[512,256]{1,0:T(8,128)(2,1)S(1)}, u32[]{:S(2)}, u32[]{:S(2)}) collective-permute-start(bf16[512,256]{1,0:T(8,128)(2,1)} %shard_map.89), channel_id=1, source_target_pairs={{0,30},{1,31},{2,0},{3,1},{4,2},{5,3},{6,4},{7,5},{8,6},{9,7},{10,... | collective-permute-start | bytes 786440 | tf_op jit(solution)/shard_map/ppermute | solution.py:104
  178.9 13.1 %collective-permute-start.22 = (bf16[512,256]{1,0:T(8,128)(2,1)}, bf16[512,256]{1,0:T(8,128)(2,1)S(1)}, u32[]{:S(2)}, u32[]{:S(2)}) collective-permute-start(bf16[512,256]{1,0:T(8,128)(2,1)} %shard_map.89), channel_id=1, source_target_pairs={{0,31},{1,0},{2,1},{3,2},{4,3},{5,4},{6,5},{7,6},{8,7},{9,8},{10,9... | collective-permute-start | bytes 786440 | tf_op jit(solution)/shard_map/ppermute | solution.py:104
  192.0 3.1 %collective-permute-start.23 = (bf16[1024,256]{1,0:T(8,128)(2,1)S(1)}, bf16[1024,256]{1,0:T(8,128)(2,1)S(1)}, u32[]{:S(2)}, u32[]{:S(2)}) collective-permute-start(bf16[1024,256]{1,0:T(8,128)(2,1)S(1)} %pad_maximum_fusion.8), channel_id=1, source_target_pairs={{0,32},{32,0},{64,96},{96,64},{128,160},{160,128},{192,224},{224,1... | collective-permute-start | bytes 1572872 | tf_op jit(solution)/shard_map/ppermute | solution.py:108
  200.2 7.9 %collective-permute-start.26 = (bf16[512,256]{1,0:T(8,128)(2,1)S(1)}, bf16[512,256]{1,0:T(8,128)(2,1)S(1)}, u32[]{:S(2)}, u32[]{:S(2)}) collective-permute-start(bf16[512,256]{1,0:T(8,128)(2,1)S(1)} %get-tuple-element.6), channel_id=1, source_target_pairs={{0,192},{32,224},{64,0},{96,32},{128,64},{160,96},{192,128},{224,1... | collective-permute-start | bytes 786440 | tf_op jit(solution)/shard_map/ppermute | solution.py:151
  201.7 9.1 %collective-permute-start.25 = (bf16[512,256]{1,0:T(8,128)(2,1)S(1)}, bf16[512,256]{1,0:T(8,128)(2,1)S(1)}, u32[]{:S(2)}, u32[]{:S(2)}) collective-permute-start(bf16[512,256]{1,0:T(8,128)(2,1)S(1)} %get-tuple-element.7), channel_id=1, source_target_pairs={{0,128},{32,160},{64,192},{96,224},{128,0},{160,32},{192,64},{224,... | collective-permute-start | bytes 786440 | tf_op jit(solution)/shard_map/ppermute | solution.py:151
  202.3 14.8 %collective-permute-start.24 = (bf16[512,256]{1,0:T(8,128)(2,1)S(1)}, bf16[512,256]{1,0:T(8,128)(2,1)S(1)}, u32[]{:S(2)}, u32[]{:S(2)}) collective-permute-start(bf16[512,256]{1,0:T(8,128)(2,1)S(1)} %get-tuple-element.8), channel_id=1, source_target_pairs={{0,64},{32,96},{64,128},{96,160},{128,192},{160,224},{192,0},{224,... | collective-permute-start | bytes 786440 | tf_op jit(solution)/shard_map/ppermute | solution.py:151
  (29 other events, 250.0 us)
Sparse Core Ops, SparseCore 0:
  9.2 31.9 all-gather.2

commit v13 on v12

--- a/solution.py
+++ b/solution.py
@@ -73,6 +73,48 @@
     )(band, *parts, degree_f, ws, wn)
 
 
+def _sum_kernel(band_ref, p0, p1, p2, p3, p4, out_ref):
+    rows = p2.shape[0]
+    parts = (p0, p1, p2, p3, p4)
+    summed = jnp.dot(
+        band_ref[:, pl.ds(2 * rows, rows)], p2[...], preferred_element_type=jnp.float32
+    )
+    for position in (1, 3, 0, 4):
+        summed = summed + jnp.dot(
+            band_ref[:, pl.ds(position * rows, rows)],
+            parts[position][...],
+            preferred_element_type=jnp.float32,
+        )
+    out_ref[...] = summed
+
+
+def _combine_kernel(summed_ref, own_ref, degree_ref, ws_ref, wn_ref, out_ref):
+    neighbour_mean = (summed_ref[...] / degree_ref[...]).astype(jnp.bfloat16)
+    combined = jnp.dot(own_ref[...], ws_ref[...], preferred_element_type=jnp.float32) + jnp.dot(
+        neighbour_mean, wn_ref[...], preferred_element_type=jnp.float32
+    )
+    active = jnp.maximum(combined, 0.0)
+    scale = lax.rsqrt(jnp.mean(active * active, axis=-1, keepdims=True) + 1e-05)
+    out_ref[...] = (active * scale).astype(out_ref.dtype)
+
+
+def run_layer_split(band, parts, degree_f, ws, wn):
+    rows, width = parts[2].shape
+    vmem = pl.BlockSpec(memory_space=pltpu.VMEM)
+    summed = pl.pallas_call(
+        _sum_kernel,
+        out_shape=jax.ShapeDtypeStruct((rows, width), jnp.float32),
+        in_specs=[vmem] * 6,
+        out_specs=vmem,
+    )(band, *parts)
+    return pl.pallas_call(
+        _combine_kernel,
+        out_shape=jax.ShapeDtypeStruct((rows, width), jnp.bfloat16),
+        in_specs=[vmem] * 5,
+        out_specs=vmem,
+    )(summed, parts[2], degree_f, ws, wn)
+
+
 def body(
     features, tile_values, tile_rows, tile_cols, tile_count, degrees, self_weight, neighbour_weight
 ):
@@ -135,7 +177,8 @@
         far = halo(hidden, 2)
         theirs = swap(jnp.concatenate([near, far], axis=0))
         parts = [far, near, hidden, theirs[:rows_dev], theirs[rows_dev:]]
-        hidden = run_layer(band, parts, degree_f, self_all[level], neighbour_all[level])
+        layer_fn = run_layer_split if level == 0 else run_layer
+        hidden = layer_fn(band, parts, degree_f, self_all[level], neighbour_all[level])
         outputs.append(hidden)
 
     stacked = jnp.stack(outputs)

time: 226 us -> 224 us (level)
    pallas_call x0 -> x2, Pallas kernels: none -> 6.09 us  [the longest x1 3.69 us: run_layer_split(): pl.pallas_call(_sum_kernel, out_shape=jax.ShapeDtypeStruct((rows, width),...]
    pallas_call x7 -> x6, Pallas kernels: 29.8 us -> 25.6 us  [run_layer(): pl.pallas_call(_layer_kernel, out_shape=jax.ShapeDtypeStruct((rows, width...]
    all_gather x1, waiting for transfers between devices: 2.45 us -> 0.01 us  [body(): lax.all_gather(jnp.stack([self_weight[0], neighbour_weight[0]]), 'section')]
  transfers between devices with their start and end apart: 28 -> 28, of which waited for: 26 -> 25; matrix products, arithmetic and copies ran while one was open for 5% -> 5% of each run, Pallas kernels for 2% -> 4%
where the time goes in v13:
time: 224 us
  waiting for transfers between devices  128 us (57%)
  Pallas kernels  35.9 us (16%)
  local copies, waits for them, and re-layouts  19.9 us (9%)
  starting transfers between devices  18.9 us (8%)
  between operations  14.3 us (6%)
  other arithmetic  7.02 us (3%)
    ppermute x16, waiting for transfers between devices, halo(): return lax.ppermute(x, ('section', 'blk'), pairs)  105 us
    pallas_call x6, Pallas kernels, run_layer(): pl.pallas_call(_layer_kernel, out_shape=jax.ShapeDtypeStruct((rows, width...  25.6 us
    ppermute x3, waiting for transfers between devices, body(): arrived.append(lax.ppermute(sending, 'section', pairs))  14.3 us
    ppermute x8, waiting for transfers between devices, swap(): return lax.ppermute(x, 'section', pairs)  8.3 us
    ppermute x16, starting transfers between devices, halo(): return lax.ppermute(x, ('section', 'blk'), pairs)  8.09 us
    ppermute x8, starting transfers between devices, swap(): return lax.ppermute(x, 'section', pairs)  8.04 us
    slice x8, local copies, waits for them, and re-layouts, body(): parts = [far, near, hidden, theirs[:rows_dev], theirs[rows_dev:]]  5.83 us
    unnamed x57, local copies, waits for them, and re-layouts  5.12 us
  transfers between devices with their start and end apart: 28, of which 25 were waited for; matrix products, arithmetic and copies ran while one was open for 5% of the time, Pallas kernels for 4%

profile of v13, /device:TPU:1, one launch (start us, length us, event | category | flops | bytes accessed | tf_op | source)
XLA Modules:
  0.0 223.9 jit_solution(11960728846284926340)
XLA Ops:
  8.4 3.9 %collective-permute-start = (bf16[512,256]{1,0:T(8,128)(2,1)S(1)}, bf16[512,256]{1,0:T(8,128)(2,1)S(1)}, u32[]{:S(2)}, u32[]{:S(2)}) collective-permute-start(bf16[512,256]{1,0:T(8,128)(2,1)S(1)} %dynamic-slice_bitcast_fusion.3.p2.own_ref), channel_id=1, source_target_pairs={{0,30},{1,31},{2,0},{3,1},{4,2},{5,3},{6,4},{7,5},{8,6},{9,7},{10,... | collective-permute-start | bytes 786440 | tf_op jit(solution)/shard_map/ppermute | solution.py:146
  14.0 8.2 %collective-permute-done.p0 = bf16[512,256]{1,0:T(8,128)(2,1)S(1)} collective-permute-done((bf16[512,256]{1,0:T(8,128)(2,1)S(1)}, bf16[512,256]{1,0:T(8,128)(2,1)S(1)}, u32[]{:S(2)}, u32[]{:S(2)}) %collective-permute-start) | collective-permute-done | bytes 262176 | tf_op jit(solution)/shard_map/ppermute | solution.py:146
  22.2 4.6 %collective-permute-done.1.p1 = bf16[512,256]{1,0:T(8,128)(2,1)S(1)} collective-permute-done((bf16[512,256]{1,0:T(8,128)(2,1)S(1)}, bf16[512,256]{1,0:T(8,128)(2,1)S(1)}, u32[]{:S(2)}, u32[]{:S(2)}) %collective-permute-start.1) | collective-permute-done | bytes 262176 | tf_op jit(solution)/shard_map/ppermute | solution.py:146
  33.7 4.2 %shard_map.82.band_ref = bf16[512,2560]{1,0:T(8,128)(2,1)} custom-call(s32[80]{0:T(128)} %fusion.7.rows_ref, s32[80]{0:T(128)} %fusion.8.cols_ref, s32[1]{0:T(128)} %bitcast.2.count_ref, s32[1]{0:T(128)} %bitcast.3.batch_ref, bf16[4,80,128,128]{3,2,1,0:T(8,128)(2,1)} %values_ref.1), custom_call_target="tpu_custom_call" | custom-call | tf_op jit(solution)/shard_map/pallas_call | solution.py:26
  38.7 3.7 %shard_map.83.summed_ref = f32[512,256]{1,0:T(8,128)} custom-call(bf16[512,2560]{1,0:T(8,128)(2,1)} %shard_map.82.band_ref, bf16[512,256]{1,0:T(8,128)(2,1)} %copy-done.12, bf16[512,256]{1,0:T(8,128)(2,1)} %copy-done.13, bf16[512,256]{1,0:T(8,128)(2,1)} %copy-done.8, bf16[512,256]{1,0:T(8,128)(2,1)} %get-tuple-element.44.p3, ...), custom_call_target="tpu_custom_call" | custom-call | tf_op jit(solution)/shard_map/pallas_call | solution.py:104
  42.4 2.9 %slice_bitcast_fusion = (bf16[256,256]{1,0:T(8,128)(2,1)S(1)}, bf16[256,256]{1,0:T(8,128)(2,1)S(1)}, bf16[256,256]{1,0:T(8,128)(2,1)}, bf16[256,256]{1,0:T(8,128...) fusion(bf16[8,2,256,256]{3,2,1,0:T(8,128)(2,1)} %bitcast.74), kind=kLoop, calls=%fused_computation.23 | loop fusion | bytes 4194304 | tf_op jit(solution)/shard_map/squeeze | solution.py:181
  50.1 7.4 %collective-permute-done.3.p0 = bf16[512,256]{1,0:T(8,128)(2,1)S(1)} collective-permute-done((bf16[512,256]{1,0:T(8,128)(2,1)}, bf16[512,256]{1,0:T(8,128)(2,1)S(1)}, u32[]{:S(2)}, u32[]{:S(2)}) %collective-permute-start.3) | collective-permute-done | bytes 262176 | tf_op jit(solution)/shard_map/ppermute | solution.py:146
  57.4 5.6 %collective-permute-done.4.p1 = bf16[512,256]{1,0:T(8,128)(2,1)S(1)} collective-permute-done((bf16[512,256]{1,0:T(8,128)(2,1)}, bf16[512,256]{1,0:T(8,128)(2,1)S(1)}, u32[]{:S(2)}, u32[]{:S(2)}) %collective-permute-start.4) | collective-permute-done | bytes 262176 | tf_op jit(solution)/shard_map/ppermute | solution.py:146
  66.2 4.2 %shard_map.85.p2 = bf16[512,256]{1,0:T(8,128)(2,1)} custom-call(bf16[512,2560]{1,0:T(8,128)(2,1)} %shard_map.82.band_ref, bf16[512,256]{1,0:T(8,128)(2,1)} %copy-done.14, bf16[512,256]{1,0:T(8,128)(2,1)} %copy-done.19, bf16[512,256]{1,0:T(8,128)(2,1)} %shard_map.84.p2, bf16[512,256]{1,0:T(8,128)(2,1)} %get-tuple-element.42.p3, ...), custom_call_target="tpu_custom_call" | custom-call | flops 805306368 | bytes 4194304 | tf_op jit(solution)/shard_map/pallas_call | solution.py:63
  70.5 12.6 %collective-permute-done.6.p0 = bf16[512,256]{1,0:T(8,128)(2,1)S(1)} collective-permute-done((bf16[512,256]{1,0:T(8,128)(2,1)}, bf16[512,256]{1,0:T(8,128)(2,1)S(1)}, u32[]{:S(2)}, u32[]{:S(2)}) %collective-permute-start.6) | collective-permute-done | bytes 262176 | tf_op jit(solution)/shard_map/ppermute | solution.py:146
  88.2 4.2 %shard_map.86.p2 = bf16[512,256]{1,0:T(8,128)(2,1)} custom-call(bf16[512,2560]{1,0:T(8,128)(2,1)} %shard_map.82.band_ref, bf16[512,256]{1,0:T(8,128)(2,1)} %copy-done.15, bf16[512,256]{1,0:T(8,128)(2,1)} %copy-done.20, bf16[512,256]{1,0:T(8,128)(2,1)} %shard_map.85.p2, bf16[512,256]{1,0:T(8,128)(2,1)} %get-tuple-element.40.p3, ...), custom_call_target="tpu_custom_call" | custom-call | flops 805306368 | bytes 4194304 | tf_op jit(solution)/shard_map/pallas_call | solution.py:63
  92.4 12.5 %collective-permute-done.9.p0 = bf16[512,256]{1,0:T(8,128)(2,1)S(1)} collective-permute-done((bf16[512,256]{1,0:T(8,128)(2,1)}, bf16[512,256]{1,0:T(8,128)(2,1)S(1)}, u32[]{:S(2)}, u32[]{:S(2)}) %collective-permute-start.9) | collective-permute-done | bytes 262176 | tf_op jit(solution)/shard_map/ppermute | solution.py:146
  110.4 4.2 %shard_map.87.p2 = bf16[512,256]{1,0:T(8,128)(2,1)} custom-call(bf16[512,2560]{1,0:T(8,128)(2,1)} %shard_map.82.band_ref, bf16[512,256]{1,0:T(8,128)(2,1)} %copy-done.16, bf16[512,256]{1,0:T(8,128)(2,1)} %copy-done.21, bf16[512,256]{1,0:T(8,128)(2,1)} %shard_map.86.p2, bf16[512,256]{1,0:T(8,128)(2,1)} %get-tuple-element.38.p3, ...), custom_call_target="tpu_custom_call" | custom-call | flops 805306368 | bytes 4194304 | tf_op jit(solution)/shard_map/pallas_call | solution.py:63
  114.7 12.3 %collective-permute-done.12.p0 = bf16[512,256]{1,0:T(8,128)(2,1)S(1)} collective-permute-done((bf16[512,256]{1,0:T(8,128)(2,1)}, bf16[512,256]{1,0:T(8,128)(2,1)S(1)}, u32[]{:S(2)}, u32[]{:S(2)}) %collective-permute-start.12) | collective-permute-done | bytes 262176 | tf_op jit(solution)/shard_map/ppermute | solution.py:146
  131.3 4.3 %shard_map.88.p2 = bf16[512,256]{1,0:T(8,128)(2,1)} custom-call(bf16[512,2560]{1,0:T(8,128)(2,1)} %shard_map.82.band_ref, bf16[512,256]{1,0:T(8,128)(2,1)} %copy-done.17, bf16[512,256]{1,0:T(8,128)(2,1)} %copy-done.22, bf16[512,256]{1,0:T(8,128)(2,1)} %shard_map.87.p2, bf16[512,256]{1,0:T(8,128)(2,1)} %get-tuple-element.36.p3, ...), custom_call_target="tpu_custom_call" | custom-call | flops 805306368 | bytes 4194304 | tf_op jit(solution)/shard_map/pallas_call | solution.py:63
  135.6 12.5 %collective-permute-done.15.p0 = bf16[512,256]{1,0:T(8,128)(2,1)S(1)} collective-permute-done((bf16[512,256]{1,0:T(8,128)(2,1)}, bf16[512,256]{1,0:T(8,128)(2,1)S(1)}, u32[]{:S(2)}, u32[]{:S(2)}) %collective-permute-start.15) | collective-permute-done | bytes 262176 | tf_op jit(solution)/shard_map/ppermute | solution.py:146
  151.9 4.3 %shard_map.89.p2 = bf16[512,256]{1,0:T(8,128)(2,1)} custom-call(bf16[512,2560]{1,0:T(8,128)(2,1)} %shard_map.82.band_ref, bf16[512,256]{1,0:T(8,128)(2,1)} %copy-done.18, bf16[512,256]{1,0:T(8,128)(2,1)} %copy-done.23, bf16[512,256]{1,0:T(8,128)(2,1)} %shard_map.88.p2, bf16[512,256]{1,0:T(8,128)(2,1)} %get-tuple-element.34.p3, ...), custom_call_target="tpu_custom_call" | custom-call | flops 805306368 | bytes 4194304 | tf_op jit(solution)/shard_map/pallas_call | solution.py:63
  156.3 12.4 %collective-permute-done.18.p0 = bf16[512,256]{1,0:T(8,128)(2,1)S(1)} collective-permute-done((bf16[512,256]{1,0:T(8,128)(2,1)}, bf16[512,256]{1,0:T(8,128)(2,1)S(1)}, u32[]{:S(2)}, u32[]{:S(2)}) %collective-permute-start.18) | collective-permute-done | bytes 262176 | tf_op jit(solution)/shard_map/ppermute | solution.py:146
  172.5 4.3 %shard_map.90 = bf16[512,256]{1,0:T(8,128)(2,1)} custom-call(bf16[512,2560]{1,0:T(8,128)(2,1)} %shard_map.82.band_ref, bf16[512,256]{1,0:T(8,128)(2,1)} %copy-done.10, bf16[512,256]{1,0:T(8,128)(2,1)} %copy-done.11, bf16[512,256]{1,0:T(8,128)(2,1)} %shard_map.89.p2, bf16[512,256]{1,0:T(8,128)(2,1)} %get-tuple-element.32.p3, ...), custom_call_target="tpu_custom_call" | custom-call | flops 805306368 | bytes 4194304 | tf_op jit(solution)/shard_map/pallas_call | solution.py:63
  178.5 10.7 %collective-permute-done.21 = bf16[512,256]{1,0:T(8,128)(2,1)S(1)} collective-permute-done((bf16[512,256]{1,0:T(8,128)(2,1)}, bf16[512,256]{1,0:T(8,128)(2,1)S(1)}, u32[]{:S(2)}, u32[]{:S(2)}) %collective-permute-start.21) | collective-permute-done | bytes 262176 | tf_op jit(solution)/shard_map/ppermute | solution.py:146
  193.7 3.8 %shard_map.91 = bf16[8,512,256]{2,1,0:T(8,128)(2,1)} fusion(bf16[8,512,256]{2,1,0:T(8,128)(2,1)} %bitcast_dynamic-update-slice_fusion.1, bf16[512,2560]{1,0:T(8,128)(2,1)} %shard_map.82.band_ref, bf16[512,256]{1,0:T(8,128)(2,1)S(1)} %collective-permute-done.21, bf16[512,256]{1,0:T(8,128)(2,1)S(1)} %collective-permute-done.22, ...), kind=kCustom, calls=%fused_computation.11 | custom fusion | bytes 4458496 | tf_op jit(solution)/shard_map/pallas_call | solution.py:63
  201.4 5.2 %collective-permute-done.26 = bf16[512,256]{1,0:T(8,128)(2,1)S(1)} collective-permute-done((bf16[512,256]{1,0:T(8,128)(2,1)S(1)}, bf16[512,256]{1,0:T(8,128)(2,1)S(1)}, u32[]{:S(2)}, u32[]{:S(2)}) %collective-permute-start.26) | collective-permute-done | bytes 262176 | tf_op jit(solution)/shard_map/ppermute | solution.py:194
  206.6 2.8 %collective-permute-done.25 = bf16[512,256]{1,0:T(8,128)(2,1)S(1)} collective-permute-done((bf16[512,256]{1,0:T(8,128)(2,1)S(1)}, bf16[512,256]{1,0:T(8,128)(2,1)S(1)}, u32[]{:S(2)}, u32[]{:S(2)}) %collective-permute-start.25) | collective-permute-done | bytes 262176 | tf_op jit(solution)/shard_map/ppermute | solution.py:194
  209.5 6.2 %collective-permute-done.24 = bf16[512,256]{1,0:T(8,128)(2,1)S(1)} collective-permute-done((bf16[512,256]{1,0:T(8,128)(2,1)S(1)}, bf16[512,256]{1,0:T(8,128)(2,1)S(1)}, u32[]{:S(2)}, u32[]{:S(2)}) %collective-permute-start.24) | collective-permute-done | bytes 262176 | tf_op jit(solution)/shard_map/ppermute | solution.py:194
  (128 shorter events, 52.6 us)
Async XLA Ops:
  6.5 35.9 %all-gather.3.cloned.1.call-start = ((), (), s32[]{:S(2)}) async-start(), calls=%async_computation | async-start | bytes 2359296 | tf_op jit(solution)/shard_map/all_gather | solution.py:132
  8.4 13.7 %collective-permute-start = (bf16[512,256]{1,0:T(8,128)(2,1)S(1)}, bf16[512,256]{1,0:T(8,128)(2,1)S(1)}, u32[]{:S(2)}, u32[]{:S(2)}) collective-permute-start(bf16[512,256]{1,0:T(8,128)(2,1)S(1)} %dynamic-slice_bitcast_fusion.3.p2.own_ref), channel_id=1, source_target_pairs={{0,30},{1,31},{2,0},{3,1},{4,2},{5,3},{6,4},{7,5},{8,6},{9,7},{10,... | collective-permute-start | bytes 786440 | tf_op jit(solution)/shard_map/ppermute | solution.py:146
  12.3 14.4 %collective-permute-start.1 = (bf16[512,256]{1,0:T(8,128)(2,1)S(1)}, bf16[512,256]{1,0:T(8,128)(2,1)S(1)}, u32[]{:S(2)}, u32[]{:S(2)}) collective-permute-start(bf16[512,256]{1,0:T(8,128)(2,1)S(1)} %dynamic-slice_bitcast_fusion.3.p2.own_ref), channel_id=1, source_target_pairs={{0,31},{1,0},{2,1},{3,2},{4,3},{5,4},{6,5},{7,6},{8,7},{9,8},{10,9... | collective-permute-start | bytes 786440 | tf_op jit(solution)/shard_map/ppermute | solution.py:146
  26.8 11.1 %collective-permute-start.2 = (bf16[1024,256]{1,0:T(8,128)(2,1)S(1)}, bf16[1024,256]{1,0:T(8,128)(2,1)S(1)}, u32[]{:S(2)}, u32[]{:S(2)}) collective-permute-start(bf16[1024,256]{1,0:T(8,128)(2,1)S(1)} %pad_maximum_fusion.1), channel_id=1, source_target_pairs={{0,32},{32,0},{64,96},{96,64},{128,160},{160,128},{192,224},{224,1... | collective-permute-start | bytes 1572872 | tf_op jit(solution)/shard_map/ppermute | solution.py:150
  47.7 9.8 %collective-permute-start.3 = (bf16[512,256]{1,0:T(8,128)(2,1)}, bf16[512,256]{1,0:T(8,128)(2,1)S(1)}, u32[]{:S(2)}, u32[]{:S(2)}) collective-permute-start(bf16[512,256]{1,0:T(8,128)(2,1)} %shard_map.84.p2), channel_id=1, source_target_pairs={{0,30},{1,31},{2,0},{3,1},{4,2},{5,3},{6,4},{7,5},{8,6},{9,7},{10,... | collective-permute-start | bytes 786440 | tf_op jit(solution)/shard_map/ppermute | solution.py:146
  48.8 14.2 %collective-permute-start.4 = (bf16[512,256]{1,0:T(8,128)(2,1)}, bf16[512,256]{1,0:T(8,128)(2,1)S(1)}, u32[]{:S(2)}, u32[]{:S(2)}) collective-permute-start(bf16[512,256]{1,0:T(8,128)(2,1)} %shard_map.84.p2), channel_id=1, source_target_pairs={{0,31},{1,0},{2,1},{3,2},{4,3},{5,4},{6,5},{7,6},{8,7},{9,8},{10,9... | collective-permute-start | bytes 786440 | tf_op jit(solution)/shard_map/ppermute | solution.py:146
  70.5 12.6 %collective-permute-start.6 = (bf16[512,256]{1,0:T(8,128)(2,1)}, bf16[512,256]{1,0:T(8,128)(2,1)S(1)}, u32[]{:S(2)}, u32[]{:S(2)}) collective-permute-start(bf16[512,256]{1,0:T(8,128)(2,1)} %shard_map.85.p2), channel_id=1, source_target_pairs={{0,30},{1,31},{2,0},{3,1},{4,2},{5,3},{6,4},{7,5},{8,6},{9,7},{10,... | collective-permute-start | bytes 786440 | tf_op jit(solution)/shard_map/ppermute | solution.py:146
  70.5 14.2 %collective-permute-start.7 = (bf16[512,256]{1,0:T(8,128)(2,1)}, bf16[512,256]{1,0:T(8,128)(2,1)S(1)}, u32[]{:S(2)}, u32[]{:S(2)}) collective-permute-start(bf16[512,256]{1,0:T(8,128)(2,1)} %shard_map.85.p2), channel_id=1, source_target_pairs={{0,31},{1,0},{2,1},{3,2},{4,3},{5,4},{6,5},{7,6},{8,7},{9,8},{10,9... | collective-permute-start | bytes 786440 | tf_op jit(solution)/shard_map/ppermute | solution.py:146
  84.7 2.6 %collective-permute-start.8 = (bf16[1024,256]{1,0:T(8,128)(2,1)S(1)}, bf16[1024,256]{1,0:T(8,128)(2,1)S(1)}, u32[]{:S(2)}, u32[]{:S(2)}) collective-permute-start(bf16[1024,256]{1,0:T(8,128)(2,1)S(1)} %pad_maximum_fusion.3), channel_id=1, source_target_pairs={{0,32},{32,0},{64,96},{96,64},{128,160},{160,128},{192,224},{224,1... | collective-permute-start | bytes 1572872 | tf_op jit(solution)/shard_map/ppermute | solution.py:150
  92.4 12.6 %collective-permute-start.9 = (bf16[512,256]{1,0:T(8,128)(2,1)}, bf16[512,256]{1,0:T(8,128)(2,1)S(1)}, u32[]{:S(2)}, u32[]{:S(2)}) collective-permute-start(bf16[512,256]{1,0:T(8,128)(2,1)} %shard_map.86.p2), channel_id=1, source_target_pairs={{0,30},{1,31},{2,0},{3,1},{4,2},{5,3},{6,4},{7,5},{8,6},{9,7},{10,... | collective-permute-start | bytes 786440 | tf_op jit(solution)/shard_map/ppermute | solution.py:146
  92.4 13.5 %collective-permute-start.10 = (bf16[512,256]{1,0:T(8,128)(2,1)}, bf16[512,256]{1,0:T(8,128)(2,1)S(1)}, u32[]{:S(2)}, u32[]{:S(2)}) collective-permute-start(bf16[512,256]{1,0:T(8,128)(2,1)} %shard_map.86.p2), channel_id=1, source_target_pairs={{0,31},{1,0},{2,1},{3,2},{4,3},{5,4},{6,5},{7,6},{8,7},{9,8},{10,9... | collective-permute-start | bytes 786440 | tf_op jit(solution)/shard_map/ppermute | solution.py:146
  105.9 3.7 %collective-permute-start.11 = (bf16[1024,256]{1,0:T(8,128)(2,1)S(1)}, bf16[1024,256]{1,0:T(8,128)(2,1)S(1)}, u32[]{:S(2)}, u32[]{:S(2)}) collective-permute-start(bf16[1024,256]{1,0:T(8,128)(2,1)S(1)} %pad_maximum_fusion.4), channel_id=1, source_target_pairs={{0,32},{32,0},{64,96},{96,64},{128,160},{160,128},{192,224},{224,1... | collective-permute-start | bytes 1572872 | tf_op jit(solution)/shard_map/ppermute | solution.py:150
  114.7 12.3 %collective-permute-start.12 = (bf16[512,256]{1,0:T(8,128)(2,1)}, bf16[512,256]{1,0:T(8,128)(2,1)S(1)}, u32[]{:S(2)}, u32[]{:S(2)}) collective-permute-start(bf16[512,256]{1,0:T(8,128)(2,1)} %shard_map.87.p2), channel_id=1, source_target_pairs={{0,30},{1,31},{2,0},{3,1},{4,2},{5,3},{6,4},{7,5},{8,6},{9,7},{10,... | collective-permute-start | bytes 786440 | tf_op jit(solution)/shard_map/ppermute | solution.py:146
  114.7 13.5 %collective-permute-start.13 = (bf16[512,256]{1,0:T(8,128)(2,1)}, bf16[512,256]{1,0:T(8,128)(2,1)S(1)}, u32[]{:S(2)}, u32[]{:S(2)}) collective-permute-start(bf16[512,256]{1,0:T(8,128)(2,1)} %shard_map.87.p2), channel_id=1, source_target_pairs={{0,31},{1,0},{2,1},{3,2},{4,3},{5,4},{6,5},{7,6},{8,7},{9,8},{10,9... | collective-permute-start | bytes 786440 | tf_op jit(solution)/shard_map/ppermute | solution.py:146
  135.6 12.5 %collective-permute-start.15 = (bf16[512,256]{1,0:T(8,128)(2,1)}, bf16[512,256]{1,0:T(8,128)(2,1)S(1)}, u32[]{:S(2)}, u32[]{:S(2)}) collective-permute-start(bf16[512,256]{1,0:T(8,128)(2,1)} %shard_map.88.p2), channel_id=1, source_target_pairs={{0,30},{1,31},{2,0},{3,1},{4,2},{5,3},{6,4},{7,5},{8,6},{9,7},{10,... | collective-permute-start | bytes 786440 | tf_op jit(solution)/shard_map/ppermute | solution.py:146
  135.6 13.5 %collective-permute-start.16 = (bf16[512,256]{1,0:T(8,128)(2,1)}, bf16[512,256]{1,0:T(8,128)(2,1)S(1)}, u32[]{:S(2)}, u32[]{:S(2)}) collective-permute-start(bf16[512,256]{1,0:T(8,128)(2,1)} %shard_map.88.p2), channel_id=1, source_target_pairs={{0,31},{1,0},{2,1},{3,2},{4,3},{5,4},{6,5},{7,6},{8,7},{9,8},{10,9... | collective-permute-start | bytes 786440 | tf_op jit(solution)/shard_map/ppermute | solution.py:146
  156.3 12.4 %collective-permute-start.18 = (bf16[512,256]{1,0:T(8,128)(2,1)}, bf16[512,256]{1,0:T(8,128)(2,1)S(1)}, u32[]{:S(2)}, u32[]{:S(2)}) collective-permute-start(bf16[512,256]{1,0:T(8,128)(2,1)} %shard_map.89.p2), channel_id=1, source_target_pairs={{0,30},{1,31},{2,0},{3,1},{4,2},{5,3},{6,4},{7,5},{8,6},{9,7},{10,... | collective-permute-start | bytes 786440 | tf_op jit(solution)/shard_map/ppermute | solution.py:146
  156.3 13.4 %collective-permute-start.19 = (bf16[512,256]{1,0:T(8,128)(2,1)}, bf16[512,256]{1,0:T(8,128)(2,1)S(1)}, u32[]{:S(2)}, u32[]{:S(2)}) collective-permute-start(bf16[512,256]{1,0:T(8,128)(2,1)} %shard_map.89.p2), channel_id=1, source_target_pairs={{0,31},{1,0},{2,1},{3,2},{4,3},{5,4},{6,5},{7,6},{8,7},{9,8},{10,9... | collective-permute-start | bytes 786440 | tf_op jit(solution)/shard_map/ppermute | solution.py:146
  176.8 12.3 %collective-permute-start.21 = (bf16[512,256]{1,0:T(8,128)(2,1)}, bf16[512,256]{1,0:T(8,128)(2,1)S(1)}, u32[]{:S(2)}, u32[]{:S(2)}) collective-permute-start(bf16[512,256]{1,0:T(8,128)(2,1)} %shard_map.90), channel_id=1, source_target_pairs={{0,30},{1,31},{2,0},{3,1},{4,2},{5,3},{6,4},{7,5},{8,6},{9,7},{10,... | collective-permute-start | bytes 786440 | tf_op jit(solution)/shard_map/ppermute | solution.py:146
  176.9 13.3 %collective-permute-start.22 = (bf16[512,256]{1,0:T(8,128)(2,1)}, bf16[512,256]{1,0:T(8,128)(2,1)S(1)}, u32[]{:S(2)}, u32[]{:S(2)}) collective-permute-start(bf16[512,256]{1,0:T(8,128)(2,1)} %shard_map.90), channel_id=1, source_target_pairs={{0,31},{1,0},{2,1},{3,2},{4,3},{5,4},{6,5},{7,6},{8,7},{9,8},{10,9... | collective-permute-start | bytes 786440 | tf_op jit(solution)/shard_map/ppermute | solution.py:146
  190.2 3.4 %collective-permute-start.23 = (bf16[1024,256]{1,0:T(8,128)(2,1)S(1)}, bf16[1024,256]{1,0:T(8,128)(2,1)S(1)}, u32[]{:S(2)}, u32[]{:S(2)}) collective-permute-start(bf16[1024,256]{1,0:T(8,128)(2,1)S(1)} %pad_maximum_fusion.8), channel_id=1, source_target_pairs={{0,32},{32,0},{64,96},{96,64},{128,160},{160,128},{192,224},{224,1... | collective-permute-start | bytes 1572872 | tf_op jit(solution)/shard_map/ppermute | solution.py:150
  198.7 7.9 %collective-permute-start.26 = (bf16[512,256]{1,0:T(8,128)(2,1)S(1)}, bf16[512,256]{1,0:T(8,128)(2,1)S(1)}, u32[]{:S(2)}, u32[]{:S(2)}) collective-permute-start(bf16[512,256]{1,0:T(8,128)(2,1)S(1)} %get-tuple-element.6), channel_id=1, source_target_pairs={{0,192},{32,224},{64,0},{96,32},{128,64},{160,96},{192,128},{224,1... | collective-permute-start | bytes 786440 | tf_op jit(solution)/shard_map/ppermute | solution.py:194
  200.4 9.1 %collective-permute-start.25 = (bf16[512,256]{1,0:T(8,128)(2,1)S(1)}, bf16[512,256]{1,0:T(8,128)(2,1)S(1)}, u32[]{:S(2)}, u32[]{:S(2)}) collective-permute-start(bf16[512,256]{1,0:T(8,128)(2,1)S(1)} %get-tuple-element.7), channel_id=1, source_target_pairs={{0,128},{32,160},{64,192},{96,224},{128,0},{160,32},{192,64},{224,... | collective-permute-start | bytes 786440 | tf_op jit(solution)/shard_map/ppermute | solution.py:194
  200.8 14.9 %collective-permute-start.24 = (bf16[512,256]{1,0:T(8,128)(2,1)S(1)}, bf16[512,256]{1,0:T(8,128)(2,1)S(1)}, u32[]{:S(2)}, u32[]{:S(2)}) collective-permute-start(bf16[512,256]{1,0:T(8,128)(2,1)S(1)} %get-tuple-element.8), channel_id=1, source_target_pairs={{0,64},{32,96},{64,128},{96,160},{128,192},{160,224},{192,0},{224,... | collective-permute-start | bytes 786440 | tf_op jit(solution)/shard_map/ppermute | solution.py:194
  (29 other events, 248.7 us)
Sparse Core Ops, SparseCore 0:
  9.2 31.9 all-gather.2

commit v14 on v13

--- a/solution.py
+++ b/solution.py
@@ -58,19 +58,34 @@
     out_ref[...] = (active * scale).astype(out_ref.dtype)
 
 
-def run_layer(band, parts, degree_f, ws, wn):
+def weight_specs(level, width):
+    return [
+        pl.BlockSpec((None, None, width, width), lambda i: (level, 0, 0, 0)),
+        pl.BlockSpec((None, None, width, width), lambda i: (level, 1, 0, 0)),
+    ]
+
+
+def whole_spec(shape):
+    return pl.BlockSpec(shape, lambda i: (0,) * len(shape))
+
+
+def run_layer(band, parts, degree_f, weights_all, level):
     rows, width = parts[2].shape
     return pl.pallas_call(
         _layer_kernel,
         out_shape=jax.ShapeDtypeStruct((rows, width), jnp.bfloat16),
-        in_specs=[pl.BlockSpec(memory_space=pltpu.VMEM)] * 9,
-        out_specs=pl.BlockSpec(memory_space=pltpu.VMEM),
+        grid=(1,),
+        in_specs=[whole_spec(band.shape)]
+        + [whole_spec((rows, width))] * 5
+        + [whole_spec(degree_f.shape)]
+        + weight_specs(level, width),
+        out_specs=whole_spec((rows, width)),
         cost_estimate=pl.CostEstimate(
             flops=2 * rows * band.shape[1] * width + 4 * rows * width * width,
             bytes_accessed=band.size * 2 + 6 * rows * width * 2,
             transcendentals=rows,
         ),
-    )(band, *parts, degree_f, ws, wn)
+    )(band, *parts, degree_f, weights_all, weights_all)
 
 
 def _sum_kernel(band_ref, p0, p1, p2, p3, p4, out_ref):
@@ -98,7 +113,7 @@
     out_ref[...] = (active * scale).astype(out_ref.dtype)
 
 
-def run_layer_split(band, parts, degree_f, ws, wn):
+def run_layer_split(band, parts, degree_f, weights_all, level):
     rows, width = parts[2].shape
     vmem = pl.BlockSpec(memory_space=pltpu.VMEM)
     summed = pl.pallas_call(
@@ -110,9 +125,12 @@
     return pl.pallas_call(
         _combine_kernel,
         out_shape=jax.ShapeDtypeStruct((rows, width), jnp.bfloat16),
-        in_specs=[vmem] * 5,
-        out_specs=vmem,
-    )(summed, parts[2], degree_f, ws, wn)
+        grid=(1,),
+        in_specs=[whole_spec((rows, width))] * 2
+        + [whole_spec(degree_f.shape)]
+        + weight_specs(level, width),
+        out_specs=whole_spec((rows, width)),
+    )(summed, parts[2], degree_f, weights_all, weights_all)
 
 
 def body(
@@ -130,8 +148,6 @@
     section_index = lax.axis_index("section")
 
     weights_all = lax.all_gather(jnp.stack([self_weight[0], neighbour_weight[0]]), "section")
-    self_all = weights_all[:, 0]
-    neighbour_all = weights_all[:, 1]
 
     group = section_count // batch_total
     batch = section_index // group
@@ -178,7 +194,7 @@
         theirs = swap(jnp.concatenate([near, far], axis=0))
         parts = [far, near, hidden, theirs[:rows_dev], theirs[rows_dev:]]
         layer_fn = run_layer_split if level == 0 else run_layer
-        hidden = layer_fn(band, parts, degree_f, self_all[level], neighbour_all[level])
+        hidden = layer_fn(band, parts, degree_f, weights_all, level)
         outputs.append(hidden)
 
     stacked = jnp.stack(outputs)

time: 224 us -> 223 us (level)
    squeeze x1 -> x0, local copies, waits for them, and re-layouts: 2.88 us -> none  [body(): neighbour_all[level]]
    unnamed x57 -> x61, local copies, waits for them, and re-layouts: 5.12 us -> 6.31 us
where the time goes in v14:
time: 223 us; the launch traced here: 222 us
  waiting for transfers between devices  127 us (57%)
  Pallas kernels  36 us (16%)
  local copies, waits for them, and re-layouts  19.4 us (9%)
  starting transfers between devices  19.1 us (9%)
  between operations  14.3 us (6%)
  other arithmetic  7.03 us (3%)
    ppermute x16, waiting for transfers between devices, halo(): return lax.ppermute(x, ('section', 'blk'), pairs)  104 us
    pallas_call x6, Pallas kernels, run_layer(): pl.pallas_call(_layer_kernel, out_shape=jax.ShapeDtypeStruct((rows, width...  25.6 us
    ppermute x3, waiting for transfers between devices, body(): arrived.append(lax.ppermute(sending, 'section', pairs))  14.4 us
    ppermute x8, waiting for transfers between devices, swap(): return lax.ppermute(x, 'section', pairs)  8.2 us
    ppermute x8, starting transfers between devices, swap(): return lax.ppermute(x, 'section', pairs)  8.19 us
    ppermute x16, starting transfers between devices, halo(): return lax.ppermute(x, ('section', 'blk'), pairs)  8.16 us
    slice x8, local copies, waits for them, and re-layouts, body(): parts = [far, near, hidden, theirs[:rows_dev], theirs[rows_dev:]]  6.74 us
    unnamed x61, local copies, waits for them, and re-layouts  6.31 us
  transfers between devices with their start and end apart: 28, of which 25 were waited for; matrix products, arithmetic and copies ran while one was open for 5% of the time, Pallas kernels for 4%

profile of v14, /device:TPU:1, one launch (start us, length us, event | category | flops | bytes accessed | tf_op | source)
XLA Modules:
  0.0 222.4 jit_solution(8102799990700262721)
XLA Ops:
  8.4 3.9 %collective-permute-start = (bf16[512,256]{1,0:T(8,128)(2,1)S(1)}, bf16[512,256]{1,0:T(8,128)(2,1)S(1)}, u32[]{:S(2)}, u32[]{:S(2)}) collective-permute-start(bf16[512,256]{1,0:T(8,128)(2,1)S(1)} %dynamic-slice_bitcast_fusion.3.p2.own_ref), channel_id=1, source_target_pairs={{0,30},{1,31},{2,0},{3,1},{4,2},{5,3},{6,4},{7,5},{8,6},{9,7},{10,... | collective-permute-start | bytes 786440 | tf_op jit(solution)/shard_map/ppermute | solution.py:162
  14.0 8.2 %collective-permute-done.p0 = bf16[512,256]{1,0:T(8,128)(2,1)S(1)} collective-permute-done((bf16[512,256]{1,0:T(8,128)(2,1)S(1)}, bf16[512,256]{1,0:T(8,128)(2,1)S(1)}, u32[]{:S(2)}, u32[]{:S(2)}) %collective-permute-start) | collective-permute-done | bytes 262176 | tf_op jit(solution)/shard_map/ppermute | solution.py:162
  22.2 4.6 %collective-permute-done.1.p1 = bf16[512,256]{1,0:T(8,128)(2,1)S(1)} collective-permute-done((bf16[512,256]{1,0:T(8,128)(2,1)S(1)}, bf16[512,256]{1,0:T(8,128)(2,1)S(1)}, u32[]{:S(2)}, u32[]{:S(2)}) %collective-permute-start.1) | collective-permute-done | bytes 262176 | tf_op jit(solution)/shard_map/ppermute | solution.py:162
  33.7 4.2 %shard_map.82.band_ref = bf16[512,2560]{1,0:T(8,128)(2,1)} custom-call(s32[80]{0:T(128)} %fusion.7.rows_ref, s32[80]{0:T(128)} %fusion.8.cols_ref, s32[1]{0:T(128)} %bitcast.2.count_ref, s32[1]{0:T(128)} %bitcast.3.batch_ref, bf16[4,80,128,128]{3,2,1,0:T(8,128)(2,1)} %values_ref.1), custom_call_target="tpu_custom_call" | custom-call | tf_op jit(solution)/shard_map/pallas_call | solution.py:26
  38.7 3.7 %shard_map.83.summed_ref = f32[512,256]{1,0:T(8,128)} custom-call(bf16[512,2560]{1,0:T(8,128)(2,1)} %shard_map.82.band_ref, bf16[512,256]{1,0:T(8,128)(2,1)} %copy-done.12, bf16[512,256]{1,0:T(8,128)(2,1)} %copy-done.13, bf16[512,256]{1,0:T(8,128)(2,1)} %copy-done.8, bf16[512,256]{1,0:T(8,128)(2,1)} %get-tuple-element.28.p3, ...), custom_call_target="tpu_custom_call" | custom-call | tf_op jit(solution)/shard_map/pallas_call | solution.py:119
  42.4 2.4 %shard_map.84.p2 = bf16[512,256]{1,0:T(8,128)(2,1)} custom-call(f32[512,256]{1,0:T(8,128)} %shard_map.83.summed_ref, bf16[512,256]{1,0:T(8,128)(2,1)} %copy-done.8, f32[512,1]{1,0:T(8,128)} %copy.17.degree_ref, bf16[8,2,256,256]{3,2,1,0:T(8,128)(2,1)} %bitcast.42, bf16[8,2,256,256]{3,2,1,0:T(8,128)(2,1)} %bitcast.43), custom_call_target="tpu_custom_call" | custom-call | tf_op jit(solution)/shard_map/pallas_call | solution.py:125
  47.2 7.5 %collective-permute-done.3.p0 = bf16[512,256]{1,0:T(8,128)(2,1)S(1)} collective-permute-done((bf16[512,256]{1,0:T(8,128)(2,1)}, bf16[512,256]{1,0:T(8,128)(2,1)S(1)}, u32[]{:S(2)}, u32[]{:S(2)}) %collective-permute-start.3) | collective-permute-done | bytes 262176 | tf_op jit(solution)/shard_map/ppermute | solution.py:162
  54.6 5.5 %collective-permute-done.4.p1 = bf16[512,256]{1,0:T(8,128)(2,1)S(1)} collective-permute-done((bf16[512,256]{1,0:T(8,128)(2,1)}, bf16[512,256]{1,0:T(8,128)(2,1)S(1)}, u32[]{:S(2)}, u32[]{:S(2)}) %collective-permute-start.4) | collective-permute-done | bytes 262176 | tf_op jit(solution)/shard_map/ppermute | solution.py:162
  63.4 4.3 %shard_map.85.p2 = bf16[512,256]{1,0:T(8,128)(2,1)} custom-call(bf16[512,2560]{1,0:T(8,128)(2,1)} %shard_map.82.band_ref, bf16[512,256]{1,0:T(8,128)(2,1)} %copy-done.16, bf16[512,256]{1,0:T(8,128)(2,1)} %copy-done.21, bf16[512,256]{1,0:T(8,128)(2,1)} %shard_map.84.p2, bf16[512,256]{1,0:T(8,128)(2,1)} %get-tuple-element.26.p3, ...), custom_call_target="tpu_custom_call" | custom-call | flops 805306368 | bytes 4194304 | tf_op jit(solution)/shard_map/pallas_call | solution.py:74
  67.7 12.6 %collective-permute-done.6.p0 = bf16[512,256]{1,0:T(8,128)(2,1)S(1)} collective-permute-done((bf16[512,256]{1,0:T(8,128)(2,1)}, bf16[512,256]{1,0:T(8,128)(2,1)S(1)}, u32[]{:S(2)}, u32[]{:S(2)}) %collective-permute-start.6) | collective-permute-done | bytes 262176 | tf_op jit(solution)/shard_map/ppermute | solution.py:162
  85.4 4.3 %shard_map.86.p2 = bf16[512,256]{1,0:T(8,128)(2,1)} custom-call(bf16[512,2560]{1,0:T(8,128)(2,1)} %shard_map.82.band_ref, bf16[512,256]{1,0:T(8,128)(2,1)} %copy-done.17, bf16[512,256]{1,0:T(8,128)(2,1)} %copy-done.22, bf16[512,256]{1,0:T(8,128)(2,1)} %shard_map.85.p2, bf16[512,256]{1,0:T(8,128)(2,1)} %get-tuple-element.24.p3, ...), custom_call_target="tpu_custom_call" | custom-call | flops 805306368 | bytes 4194304 | tf_op jit(solution)/shard_map/pallas_call | solution.py:74
  89.7 12.5 %collective-permute-done.9.p0 = bf16[512,256]{1,0:T(8,128)(2,1)S(1)} collective-permute-done((bf16[512,256]{1,0:T(8,128)(2,1)}, bf16[512,256]{1,0:T(8,128)(2,1)S(1)}, u32[]{:S(2)}, u32[]{:S(2)}) %collective-permute-start.9) | collective-permute-done | bytes 262176 | tf_op jit(solution)/shard_map/ppermute | solution.py:162
  107.7 4.2 %shard_map.87.p2 = bf16[512,256]{1,0:T(8,128)(2,1)} custom-call(bf16[512,2560]{1,0:T(8,128)(2,1)} %shard_map.82.band_ref, bf16[512,256]{1,0:T(8,128)(2,1)} %copy-done.18, bf16[512,256]{1,0:T(8,128)(2,1)} %copy-done.23, bf16[512,256]{1,0:T(8,128)(2,1)} %shard_map.86.p2, bf16[512,256]{1,0:T(8,128)(2,1)} %get-tuple-element.22.p3, ...), custom_call_target="tpu_custom_call" | custom-call | flops 805306368 | bytes 4194304 | tf_op jit(solution)/shard_map/pallas_call | solution.py:74
  112.0 12.3 %collective-permute-done.12.p0 = bf16[512,256]{1,0:T(8,128)(2,1)S(1)} collective-permute-done((bf16[512,256]{1,0:T(8,128)(2,1)}, bf16[512,256]{1,0:T(8,128)(2,1)S(1)}, u32[]{:S(2)}, u32[]{:S(2)}) %collective-permute-start.12) | collective-permute-done | bytes 262176 | tf_op jit(solution)/shard_map/ppermute | solution.py:162
  128.6 4.2 %shard_map.88.p2 = bf16[512,256]{1,0:T(8,128)(2,1)} custom-call(bf16[512,2560]{1,0:T(8,128)(2,1)} %shard_map.82.band_ref, bf16[512,256]{1,0:T(8,128)(2,1)} %copy-done.19, bf16[512,256]{1,0:T(8,128)(2,1)} %copy-done.24, bf16[512,256]{1,0:T(8,128)(2,1)} %shard_map.87.p2, bf16[512,256]{1,0:T(8,128)(2,1)} %get-tuple-element.20.p3, ...), custom_call_target="tpu_custom_call" | custom-call | flops 805306368 | bytes 4194304 | tf_op jit(solution)/shard_map/pallas_call | solution.py:74
  132.8 12.5 %collective-permute-done.15.p0 = bf16[512,256]{1,0:T(8,128)(2,1)S(1)} collective-permute-done((bf16[512,256]{1,0:T(8,128)(2,1)}, bf16[512,256]{1,0:T(8,128)(2,1)S(1)}, u32[]{:S(2)}, u32[]{:S(2)}) %collective-permute-start.15) | collective-permute-done | bytes 262176 | tf_op jit(solution)/shard_map/ppermute | solution.py:162
  149.2 4.3 %shard_map.89.p2 = bf16[512,256]{1,0:T(8,128)(2,1)} custom-call(bf16[512,2560]{1,0:T(8,128)(2,1)} %shard_map.82.band_ref, bf16[512,256]{1,0:T(8,128)(2,1)} %copy-done.20, bf16[512,256]{1,0:T(8,128)(2,1)} %copy-done.25, bf16[512,256]{1,0:T(8,128)(2,1)} %shard_map.88.p2, bf16[512,256]{1,0:T(8,128)(2,1)} %get-tuple-element.18.p3, ...), custom_call_target="tpu_custom_call" | custom-call | flops 805306368 | bytes 4194304 | tf_op jit(solution)/shard_map/pallas_call | solution.py:74
  153.5 12.4 %collective-permute-done.18.p0 = bf16[512,256]{1,0:T(8,128)(2,1)S(1)} collective-permute-done((bf16[512,256]{1,0:T(8,128)(2,1)}, bf16[512,256]{1,0:T(8,128)(2,1)S(1)}, u32[]{:S(2)}, u32[]{:S(2)}) %collective-permute-start.18) | collective-permute-done | bytes 262176 | tf_op jit(solution)/shard_map/ppermute | solution.py:162
  169.7 4.3 %shard_map.90 = bf16[512,256]{1,0:T(8,128)(2,1)} custom-call(bf16[512,2560]{1,0:T(8,128)(2,1)} %shard_map.82.band_ref, bf16[512,256]{1,0:T(8,128)(2,1)} %copy-done.10, bf16[512,256]{1,0:T(8,128)(2,1)} %copy-done.11, bf16[512,256]{1,0:T(8,128)(2,1)} %shard_map.89.p2, bf16[512,256]{1,0:T(8,128)(2,1)} %get-tuple-element.16.p3, ...), custom_call_target="tpu_custom_call" | custom-call | flops 805306368 | bytes 4194304 | tf_op jit(solution)/shard_map/pallas_call | solution.py:74
  176.9 9.6 %collective-permute-done.21 = bf16[512,256]{1,0:T(8,128)(2,1)S(1)} collective-permute-done((bf16[512,256]{1,0:T(8,128)(2,1)}, bf16[512,256]{1,0:T(8,128)(2,1)S(1)}, u32[]{:S(2)}, u32[]{:S(2)}) %collective-permute-start.21) | collective-permute-done | bytes 262176 | tf_op jit(solution)/shard_map/ppermute | solution.py:162
  191.7 4.1 %shard_map.91 = bf16[8,512,256]{2,1,0:T(8,128)(2,1)} fusion(bf16[8,512,256]{2,1,0:T(8,128)(2,1)} %bitcast_dynamic-update-slice_fusion.1, bf16[512,2560]{1,0:T(8,128)(2,1)} %shard_map.82.band_ref, bf16[512,256]{1,0:T(8,128)(2,1)} %copy-done.14, bf16[512,256]{1,0:T(8,128)(2,1)} %copy-done.15, bf16[512,256]{1,0:T(8,128)(2,1)} %shard_map.90, ...), kind=kCustom, calls=%fused_computation.11 | custom fusion | bytes 6293504 | tf_op jit(solution)/shard_map/pallas_call | solution.py:74
  199.8 5.2 %collective-permute-done.26 = bf16[512,256]{1,0:T(8,128)(2,1)S(1)} collective-permute-done((bf16[512,256]{1,0:T(8,128)(2,1)S(1)}, bf16[512,256]{1,0:T(8,128)(2,1)S(1)}, u32[]{:S(2)}, u32[]{:S(2)}) %collective-permute-start.26) | collective-permute-done | bytes 262176 | tf_op jit(solution)/shard_map/ppermute | solution.py:210
  205.0 3.2 %collective-permute-done.25 = bf16[512,256]{1,0:T(8,128)(2,1)S(1)} collective-permute-done((bf16[512,256]{1,0:T(8,128)(2,1)S(1)}, bf16[512,256]{1,0:T(8,128)(2,1)S(1)}, u32[]{:S(2)}, u32[]{:S(2)}) %collective-permute-start.25) | collective-permute-done | bytes 262176 | tf_op jit(solution)/shard_map/ppermute | solution.py:210
  208.2 6.0 %collective-permute-done.24 = bf16[512,256]{1,0:T(8,128)(2,1)S(1)} collective-permute-done((bf16[512,256]{1,0:T(8,128)(2,1)S(1)}, bf16[512,256]{1,0:T(8,128)(2,1)S(1)}, u32[]{:S(2)}, u32[]{:S(2)}) %collective-permute-start.24) | collective-permute-done | bytes 262176 | tf_op jit(solution)/shard_map/ppermute | solution.py:210
  (131 shorter events, 52.3 us)
Async XLA Ops:
  6.5 35.9 %all-gather.3.cloned.1.call-start = ((), (), s32[]{:S(2)}) async-start(), calls=%async_computation | async-start | bytes 2359296 | tf_op jit(solution)/shard_map/all_gather | solution.py:150
  8.4 13.7 %collective-permute-start = (bf16[512,256]{1,0:T(8,128)(2,1)S(1)}, bf16[512,256]{1,0:T(8,128)(2,1)S(1)}, u32[]{:S(2)}, u32[]{:S(2)}) collective-permute-start(bf16[512,256]{1,0:T(8,128)(2,1)S(1)} %dynamic-slice_bitcast_fusion.3.p2.own_ref), channel_id=1, source_target_pairs={{0,30},{1,31},{2,0},{3,1},{4,2},{5,3},{6,4},{7,5},{8,6},{9,7},{10,... | collective-permute-start | bytes 786440 | tf_op jit(solution)/shard_map/ppermute | solution.py:162
  12.3 14.4 %collective-permute-start.1 = (bf16[512,256]{1,0:T(8,128)(2,1)S(1)}, bf16[512,256]{1,0:T(8,128)(2,1)S(1)}, u32[]{:S(2)}, u32[]{:S(2)}) collective-permute-start(bf16[512,256]{1,0:T(8,128)(2,1)S(1)} %dynamic-slice_bitcast_fusion.3.p2.own_ref), channel_id=1, source_target_pairs={{0,31},{1,0},{2,1},{3,2},{4,3},{5,4},{6,5},{7,6},{8,7},{9,8},{10,9... | collective-permute-start | bytes 786440 | tf_op jit(solution)/shard_map/ppermute | solution.py:162
  26.8 11.1 %collective-permute-start.2 = (bf16[1024,256]{1,0:T(8,128)(2,1)S(1)}, bf16[1024,256]{1,0:T(8,128)(2,1)S(1)}, u32[]{:S(2)}, u32[]{:S(2)}) collective-permute-start(bf16[1024,256]{1,0:T(8,128)(2,1)S(1)} %pad_maximum_fusion.1), channel_id=1, source_target_pairs={{0,32},{32,0},{64,96},{96,64},{128,160},{160,128},{192,224},{224,1... | collective-permute-start | bytes 1572872 | tf_op jit(solution)/shard_map/ppermute | solution.py:166
  44.9 9.8 %collective-permute-start.3 = (bf16[512,256]{1,0:T(8,128)(2,1)}, bf16[512,256]{1,0:T(8,128)(2,1)S(1)}, u32[]{:S(2)}, u32[]{:S(2)}) collective-permute-start(bf16[512,256]{1,0:T(8,128)(2,1)} %shard_map.84.p2), channel_id=1, source_target_pairs={{0,30},{1,31},{2,0},{3,1},{4,2},{5,3},{6,4},{7,5},{8,6},{9,7},{10,... | collective-permute-start | bytes 786440 | tf_op jit(solution)/shard_map/ppermute | solution.py:162
  45.9 14.2 %collective-permute-start.4 = (bf16[512,256]{1,0:T(8,128)(2,1)}, bf16[512,256]{1,0:T(8,128)(2,1)S(1)}, u32[]{:S(2)}, u32[]{:S(2)}) collective-permute-start(bf16[512,256]{1,0:T(8,128)(2,1)} %shard_map.84.p2), channel_id=1, source_target_pairs={{0,31},{1,0},{2,1},{3,2},{4,3},{5,4},{6,5},{7,6},{8,7},{9,8},{10,9... | collective-permute-start | bytes 786440 | tf_op jit(solution)/shard_map/ppermute | solution.py:162
  67.6 12.6 %collective-permute-start.6 = (bf16[512,256]{1,0:T(8,128)(2,1)}, bf16[512,256]{1,0:T(8,128)(2,1)S(1)}, u32[]{:S(2)}, u32[]{:S(2)}) collective-permute-start(bf16[512,256]{1,0:T(8,128)(2,1)} %shard_map.85.p2), channel_id=1, source_target_pairs={{0,30},{1,31},{2,0},{3,1},{4,2},{5,3},{6,4},{7,5},{8,6},{9,7},{10,... | collective-permute-start | bytes 786440 | tf_op jit(solution)/shard_map/ppermute | solution.py:162
  67.7 14.2 %collective-permute-start.7 = (bf16[512,256]{1,0:T(8,128)(2,1)}, bf16[512,256]{1,0:T(8,128)(2,1)S(1)}, u32[]{:S(2)}, u32[]{:S(2)}) collective-permute-start(bf16[512,256]{1,0:T(8,128)(2,1)} %shard_map.85.p2), channel_id=1, source_target_pairs={{0,31},{1,0},{2,1},{3,2},{4,3},{5,4},{6,5},{7,6},{8,7},{9,8},{10,9... | collective-permute-start | bytes 786440 | tf_op jit(solution)/shard_map/ppermute | solution.py:162
  81.9 2.7 %collective-permute-start.8 = (bf16[1024,256]{1,0:T(8,128)(2,1)S(1)}, bf16[1024,256]{1,0:T(8,128)(2,1)S(1)}, u32[]{:S(2)}, u32[]{:S(2)}) collective-permute-start(bf16[1024,256]{1,0:T(8,128)(2,1)S(1)} %pad_maximum_fusion.3), channel_id=1, source_target_pairs={{0,32},{32,0},{64,96},{96,64},{128,160},{160,128},{192,224},{224,1... | collective-permute-start | bytes 1572872 | tf_op jit(solution)/shard_map/ppermute | solution.py:166
  89.7 12.5 %collective-permute-start.9 = (bf16[512,256]{1,0:T(8,128)(2,1)}, bf16[512,256]{1,0:T(8,128)(2,1)S(1)}, u32[]{:S(2)}, u32[]{:S(2)}) collective-permute-start(bf16[512,256]{1,0:T(8,128)(2,1)} %shard_map.86.p2), channel_id=1, source_target_pairs={{0,30},{1,31},{2,0},{3,1},{4,2},{5,3},{6,4},{7,5},{8,6},{9,7},{10,... | collective-permute-start | bytes 786440 | tf_op jit(solution)/shard_map/ppermute | solution.py:162
  89.7 13.5 %collective-permute-start.10 = (bf16[512,256]{1,0:T(8,128)(2,1)}, bf16[512,256]{1,0:T(8,128)(2,1)S(1)}, u32[]{:S(2)}, u32[]{:S(2)}) collective-permute-start(bf16[512,256]{1,0:T(8,128)(2,1)} %shard_map.86.p2), channel_id=1, source_target_pairs={{0,31},{1,0},{2,1},{3,2},{4,3},{5,4},{6,5},{7,6},{8,7},{9,8},{10,9... | collective-permute-start | bytes 786440 | tf_op jit(solution)/shard_map/ppermute | solution.py:162
  103.2 3.7 %collective-permute-start.11 = (bf16[1024,256]{1,0:T(8,128)(2,1)S(1)}, bf16[1024,256]{1,0:T(8,128)(2,1)S(1)}, u32[]{:S(2)}, u32[]{:S(2)}) collective-permute-start(bf16[1024,256]{1,0:T(8,128)(2,1)S(1)} %pad_maximum_fusion.4), channel_id=1, source_target_pairs={{0,32},{32,0},{64,96},{96,64},{128,160},{160,128},{192,224},{224,1... | collective-permute-start | bytes 1572872 | tf_op jit(solution)/shard_map/ppermute | solution.py:166
  112.0 12.3 %collective-permute-start.12 = (bf16[512,256]{1,0:T(8,128)(2,1)}, bf16[512,256]{1,0:T(8,128)(2,1)S(1)}, u32[]{:S(2)}, u32[]{:S(2)}) collective-permute-start(bf16[512,256]{1,0:T(8,128)(2,1)} %shard_map.87.p2), channel_id=1, source_target_pairs={{0,30},{1,31},{2,0},{3,1},{4,2},{5,3},{6,4},{7,5},{8,6},{9,7},{10,... | collective-permute-start | bytes 786440 | tf_op jit(solution)/shard_map/ppermute | solution.py:162
  112.0 13.5 %collective-permute-start.13 = (bf16[512,256]{1,0:T(8,128)(2,1)}, bf16[512,256]{1,0:T(8,128)(2,1)S(1)}, u32[]{:S(2)}, u32[]{:S(2)}) collective-permute-start(bf16[512,256]{1,0:T(8,128)(2,1)} %shard_map.87.p2), channel_id=1, source_target_pairs={{0,31},{1,0},{2,1},{3,2},{4,3},{5,4},{6,5},{7,6},{8,7},{9,8},{10,9... | collective-permute-start | bytes 786440 | tf_op jit(solution)/shard_map/ppermute | solution.py:162
  132.8 12.5 %collective-permute-start.15 = (bf16[512,256]{1,0:T(8,128)(2,1)}, bf16[512,256]{1,0:T(8,128)(2,1)S(1)}, u32[]{:S(2)}, u32[]{:S(2)}) collective-permute-start(bf16[512,256]{1,0:T(8,128)(2,1)} %shard_map.88.p2), channel_id=1, source_target_pairs={{0,30},{1,31},{2,0},{3,1},{4,2},{5,3},{6,4},{7,5},{8,6},{9,7},{10,... | collective-permute-start | bytes 786440 | tf_op jit(solution)/shard_map/ppermute | solution.py:162
  132.8 13.5 %collective-permute-start.16 = (bf16[512,256]{1,0:T(8,128)(2,1)}, bf16[512,256]{1,0:T(8,128)(2,1)S(1)}, u32[]{:S(2)}, u32[]{:S(2)}) collective-permute-start(bf16[512,256]{1,0:T(8,128)(2,1)} %shard_map.88.p2), channel_id=1, source_target_pairs={{0,31},{1,0},{2,1},{3,2},{4,3},{5,4},{6,5},{7,6},{8,7},{9,8},{10,9... | collective-permute-start | bytes 786440 | tf_op jit(solution)/shard_map/ppermute | solution.py:162
  153.5 12.4 %collective-permute-start.18 = (bf16[512,256]{1,0:T(8,128)(2,1)}, bf16[512,256]{1,0:T(8,128)(2,1)S(1)}, u32[]{:S(2)}, u32[]{:S(2)}) collective-permute-start(bf16[512,256]{1,0:T(8,128)(2,1)} %shard_map.89.p2), channel_id=1, source_target_pairs={{0,30},{1,31},{2,0},{3,1},{4,2},{5,3},{6,4},{7,5},{8,6},{9,7},{10,... | collective-permute-start | bytes 786440 | tf_op jit(solution)/shard_map/ppermute | solution.py:162
  153.5 13.3 %collective-permute-start.19 = (bf16[512,256]{1,0:T(8,128)(2,1)}, bf16[512,256]{1,0:T(8,128)(2,1)S(1)}, u32[]{:S(2)}, u32[]{:S(2)}) collective-permute-start(bf16[512,256]{1,0:T(8,128)(2,1)} %shard_map.89.p2), channel_id=1, source_target_pairs={{0,31},{1,0},{2,1},{3,2},{4,3},{5,4},{6,5},{7,6},{8,7},{9,8},{10,9... | collective-permute-start | bytes 786440 | tf_op jit(solution)/shard_map/ppermute | solution.py:162
  174.0 12.4 %collective-permute-start.21 = (bf16[512,256]{1,0:T(8,128)(2,1)}, bf16[512,256]{1,0:T(8,128)(2,1)S(1)}, u32[]{:S(2)}, u32[]{:S(2)}) collective-permute-start(bf16[512,256]{1,0:T(8,128)(2,1)} %shard_map.90), channel_id=1, source_target_pairs={{0,30},{1,31},{2,0},{3,1},{4,2},{5,3},{6,4},{7,5},{8,6},{9,7},{10,... | collective-permute-start | bytes 786440 | tf_op jit(solution)/shard_map/ppermute | solution.py:162
  174.1 13.3 %collective-permute-start.22 = (bf16[512,256]{1,0:T(8,128)(2,1)}, bf16[512,256]{1,0:T(8,128)(2,1)S(1)}, u32[]{:S(2)}, u32[]{:S(2)}) collective-permute-start(bf16[512,256]{1,0:T(8,128)(2,1)} %shard_map.90), channel_id=1, source_target_pairs={{0,31},{1,0},{2,1},{3,2},{4,3},{5,4},{6,5},{7,6},{8,7},{9,8},{10,9... | collective-permute-start | bytes 786440 | tf_op jit(solution)/shard_map/ppermute | solution.py:162
  187.5 3.3 %collective-permute-start.23 = (bf16[1024,256]{1,0:T(8,128)(2,1)S(1)}, bf16[1024,256]{1,0:T(8,128)(2,1)S(1)}, u32[]{:S(2)}, u32[]{:S(2)}) collective-permute-start(bf16[1024,256]{1,0:T(8,128)(2,1)S(1)} %pad_maximum_fusion.8), channel_id=1, source_target_pairs={{0,32},{32,0},{64,96},{96,64},{128,160},{160,128},{192,224},{224,1... | collective-permute-start | bytes 1572872 | tf_op jit(solution)/shard_map/ppermute | solution.py:166
  197.0 8.0 %collective-permute-start.26 = (bf16[512,256]{1,0:T(8,128)(2,1)S(1)}, bf16[512,256]{1,0:T(8,128)(2,1)S(1)}, u32[]{:S(2)}, u32[]{:S(2)}) collective-permute-start(bf16[512,256]{1,0:T(8,128)(2,1)S(1)} %get-tuple-element.6), channel_id=1, source_target_pairs={{0,192},{32,224},{64,0},{96,32},{128,64},{160,96},{192,128},{224,1... | collective-permute-start | bytes 786440 | tf_op jit(solution)/shard_map/ppermute | solution.py:210
  199.1 9.1 %collective-permute-start.25 = (bf16[512,256]{1,0:T(8,128)(2,1)S(1)}, bf16[512,256]{1,0:T(8,128)(2,1)S(1)}, u32[]{:S(2)}, u32[]{:S(2)}) collective-permute-start(bf16[512,256]{1,0:T(8,128)(2,1)S(1)} %get-tuple-element.7), channel_id=1, source_target_pairs={{0,128},{32,160},{64,192},{96,224},{128,0},{160,32},{192,64},{224,... | collective-permute-start | bytes 786440 | tf_op jit(solution)/shard_map/ppermute | solution.py:210
  199.3 15.0 %collective-permute-start.24 = (bf16[512,256]{1,0:T(8,128)(2,1)S(1)}, bf16[512,256]{1,0:T(8,128)(2,1)S(1)}, u32[]{:S(2)}, u32[]{:S(2)}) collective-permute-start(bf16[512,256]{1,0:T(8,128)(2,1)S(1)} %get-tuple-element.8), channel_id=1, source_target_pairs={{0,64},{32,96},{64,128},{96,160},{128,192},{160,224},{192,0},{224,... | collective-permute-start | bytes 786440 | tf_op jit(solution)/shard_map/ppermute | solution.py:210
  (31 other events, 268.9 us)
Sparse Core Ops, SparseCore 0:
  9.2 31.9 all-gather.2
